TPU v7x, 256 devices: a whole 4x4x8 slice. The times are simulated.
256 devices in a mesh: dp: 16 (over y_lo, z), tm: 16 (over x, y_hi, core).
Axes of the slice: x: 4, y: 4 (y_hi: 2, y_lo: 2; y = y_hi * 2 + y_lo), z: 8, core: 2. Of those that a mesh axis runs over, the one named last changes fastest.
Arguments:
- frames: bfloat16 [16, 2048, 1024], P('dp', 'tm'), may hold values from -6 to 6
- cotangent: bfloat16 [16, 2048, 1024], P('dp', 'tm'), may hold values from -6 to 6
- lengths: int32 [16], P('dp'), may hold values from 512 to 2048, as said below
- w_proj: bfloat16 [1024, 2048], replicated
- gain_attn: float32 [1024], replicated, may hold values from 0.25 to 1.75
- gain_conv: float32 [1024], replicated, may hold values from 0.25 to 1.75
- w_conv: bfloat16 [31, 1024], replicated, may hold values from -1 to 1
Outputs:
- grad_frames: bfloat16 [16, 2048, 1024], P('dp', 'tm')
- grad_proj: float32 [1024, 2048], P(('dp', 'tm'))
- grad_conv: float32 [31, 1024], replicated
- grad_gains: float32 [2, 1024], replicated
Inputs may be any that keep to these rules, and one draw needn't show every extreme that they name: lengths[r] counts the valid frames of recording r; later frames are padding. Some recording has exactly 2048 and some exactly 512.
All inputs are finite; a program needn't handle non-finite values.
Results may differ from a plain program's by a relative error of at most 0.035.
Values may be sent and summed in bfloat16 or wider, within the bound.
No kernel may reach another device: no remote copies, remote signals or barrier semaphores. Data moves between devices by JAX's collectives and lax.ppermute only.
A program may use at most 128 MiB of HBM per device.

v0:
```python
import math

import jax
import jax.numpy as jnp
from jax import lax
from jax.sharding import PartitionSpec as P

HEADS = 8
HDIM = 64
KER = 31


epsilon = 1e-05
negative = -1e30


def padded_2(value, sides, width):
    for axis, dim in sides:
        size, length = (lax.axis_size(axis), value.shape[dim])
        up = [(i, (i + 1) % size) for i in range(size - 1)]
        down = [(j, i) for i, j in up]
        last = lax.slice_in_dim(value, length - width, length, axis=dim)
        first = lax.slice_in_dim(value, 0, width, axis=dim)
        before = lax.ppermute(last, axis, up)
        after = lax.ppermute(first, axis, down)
        value = jnp.concatenate([before, value, after], axis=dim)
    return value


def normalize(inputs, gain):
    centre = inputs - jnp.mean(inputs, axis=-1, keepdims=True)
    spread = jnp.mean(centre * centre, axis=-1, keepdims=True)
    return centre * lax.rsqrt(spread + epsilon) * gain


def split_heads(matrix):
    return matrix.reshape(matrix.shape[0], HEADS, HDIM)


def over_blocks(advance, carried, members):
    total_rows = members[0].shape[0]
    stride = math.gcd(total_rows, 1024)

    def one_block(block_index, inner_state):
        offset = block_index * stride
        sliced = tuple((lax.dynamic_slice_in_dim(member, offset, stride, 0) for member in members))
        return advance(inner_state, sliced, offset)

    return lax.fori_loop(0, total_rows // stride, one_block, carried)


def forward_step(query_heads, length, scaling):

    def advance(carried, sliced, first_row):
        key_heads = split_heads(sliced[0])
        value_heads = split_heads(sliced[1])
        positions = first_row + jnp.arange(key_heads.shape[0], dtype=jnp.int32)
        living = (positions < length)[None, None, :]
        scores = (
            jnp.einsum("bhd,lhd->hbl", query_heads, key_heads, preferred_element_type=jnp.float32)
            * scaling
        )
        scores = jnp.where(living, scores, negative)
        top_old, total_old, accumulated = carried
        top_new = jnp.maximum(top_old, jnp.max(scores, axis=-1))
        weights = jnp.where(living, jnp.exp(scores - top_new[:, :, None]), 0.0)
        fading = jnp.exp(top_old - top_new)
        total_new = total_old * fading + jnp.sum(weights, axis=-1)
        update = jnp.einsum(
            "hbl,lhd->bhd",
            weights.astype(jnp.bfloat16),
            value_heads,
            preferred_element_type=jnp.float32,
        )
        return (top_new, total_new, accumulated * fading.T[:, :, None] + update)

    return advance


def query_side(query_heads, grad_heads, logsum, delta, length, scaling):

    def advance(carried, sliced, first_row):
        key_heads = split_heads(sliced[0])
        value_heads = split_heads(sliced[1])
        count_here = key_heads.shape[0]
        positions = first_row + jnp.arange(count_here, dtype=jnp.int32)
        living = (positions < length)[None, None, :]
        scores = (
            jnp.einsum("bhd,lhd->hbl", query_heads, key_heads, preferred_element_type=jnp.float32)
            * scaling
        )
        scores = jnp.where(living, scores, negative)
        probs = jnp.where(living, jnp.exp(scores - logsum.T[:, :, None]), 0.0)
        dprobs = jnp.einsum(
            "bhd,lhd->hbl", grad_heads, value_heads, preferred_element_type=jnp.float32
        )
        grad_scores = (probs * (dprobs - delta.T[:, :, None])).astype(jnp.bfloat16)
        grad_query = (
            carried[0]
            + jnp.einsum("hbl,lhd->bhd", grad_scores, key_heads, preferred_element_type=jnp.float32)
            * scaling
        )
        return (grad_query,)

    return advance


def key_side(key_heads, value_heads, own_living, scaling):

    def advance(carried, sliced, first_row):
        query_heads = split_heads(sliced[0].astype(jnp.bfloat16))
        grad_heads = split_heads(sliced[1].astype(jnp.bfloat16))
        logsum_block = sliced[2]
        delta_block = sliced[3]
        scores = (
            jnp.einsum("bhd,lhd->hbl", query_heads, key_heads, preferred_element_type=jnp.float32)
            * scaling
        )
        scores = jnp.where(own_living, scores, negative)
        probs = jnp.where(own_living, jnp.exp(scores - logsum_block.T[:, :, None]), 0.0)
        dprobs = jnp.einsum(
            "bhd,lhd->hbl", grad_heads, value_heads, preferred_element_type=jnp.float32
        )
        grad_scores = (probs * (dprobs - delta_block.T[:, :, None])).astype(jnp.bfloat16)
        grad_key = (
            carried[0]
            + jnp.einsum(
                "hbl,bhd->lhd", grad_scores, query_heads, preferred_element_type=jnp.float32
            )
            * scaling
        )
        grad_value = carried[1] + jnp.einsum(
            "hbl,bhd->lhd",
            probs.astype(jnp.bfloat16),
            grad_heads,
            preferred_element_type=jnp.float32,
        )
        return (grad_key, grad_value)

    return advance


def per_device(frames, cotangent, lengths, w_proj, gain_attn, gain_conv, w_conv):
    frame_count = frames.shape[1]
    width = HEADS * HDIM
    cycle_size = lax.axis_size("tm")
    own_start = lax.axis_index("tm") * frame_count
    length = lengths[0]
    scaling = 1.0 / math.sqrt(HDIM)
    total_frames = lax.axis_size("dp") * frames.shape[0] * frame_count * cycle_size
    grad_scale = 1.0 / math.sqrt(total_frames)
    contract_last = (((1,), (1,)), ((), ()))
    contract_first = (((0,), (0,)), ((), ()))
    inputs = frames[0].astype(jnp.float32)
    normed_attn = normalize(inputs, gain_attn).astype(jnp.bfloat16)
    projected = jnp.dot(
        normed_attn, w_proj[:, : 3 * width], preferred_element_type=jnp.float32
    ).astype(jnp.bfloat16)
    queries = projected[:, :width]
    key_rows = projected[:, width : 2 * width]
    value_rows = projected[:, 2 * width :]
    query_heads = split_heads(queries)
    start_state = (
        jnp.full((HEADS, frame_count), negative, jnp.float32),
        jnp.zeros((HEADS, frame_count), jnp.float32),
        jnp.zeros((frame_count, HEADS, HDIM), jnp.float32),
    )
    advance_forward = forward_step(query_heads, length, scaling)
    top_all, total_all, accumulated = over_blocks(
        advance_forward,
        start_state,
        (
            lax.all_gather(key_rows, "tm", axis=0, tiled=True),
            lax.all_gather(value_rows, "tm", axis=0, tiled=True),
        ),
    )
    attended = (
        (accumulated / total_all.T[:, :, None]).reshape(frame_count, width).astype(jnp.bfloat16)
    )
    logsum = (top_all + jnp.log(total_all)).T
    w_out = w_proj[:, 3 * width :]
    mixed = inputs + lax.dot_general(
        attended, w_out, contract_last, preferred_element_type=jnp.float32
    )
    resid_f = mixed.astype(jnp.bfloat16).astype(jnp.float32)
    positions = own_start + jnp.arange(frame_count, dtype=jnp.int32)
    valid = (positions < length)[:, None]
    normed_conv = jnp.where(valid, normalize(resid_f, gain_conv), 0.0).astype(jnp.bfloat16)
    reach = KER // 2
    padded = padded_2(normed_conv, (("tm", 0),), reach).astype(jnp.float32)
    kernel = w_conv.astype(jnp.float32)
    conv = jnp.zeros((frame_count, padded.shape[1]), jnp.float32)
    for shift_index in range(KER):
        conv = conv + kernel[shift_index] * padded[shift_index : shift_index + frame_count]
    upstream = cotangent[0].astype(jnp.float32)
    gate = jax.nn.sigmoid(conv)
    grad_conv_in = upstream * gate * (1.0 + conv * (1.0 - gate))
    conv_term = jnp.stack(
        [
            jnp.sum(grad_conv_in * padded[shift_index : shift_index + frame_count], axis=0)
            for shift_index in range(KER)
        ]
    )
    grad_padded = padded_2(grad_conv_in.astype(jnp.bfloat16), (("tm", 0),), reach).astype(
        grad_conv_in.dtype
    )
    grad_normed = jnp.zeros_like(grad_conv_in)
    for shift_index in range(KER):
        begin = 2 * reach - shift_index
        grad_normed = grad_normed + kernel[shift_index] * grad_padded[begin : begin + frame_count]
    grad_normed = jnp.where(valid, grad_normed, 0.0)
    unused_conv, pull_conv = jax.vjp(normalize, resid_f, gain_conv)
    back_resid, gain_conv_term = pull_conv(grad_normed)
    grad_resid = upstream + back_resid
    grad_resid_low = grad_resid.astype(jnp.bfloat16)
    grad_attended = jnp.dot(grad_resid_low, w_out, preferred_element_type=jnp.float32).astype(
        jnp.bfloat16
    )
    grad_heads = split_heads(grad_attended)
    delta = jnp.sum(
        grad_heads.astype(jnp.float32) * split_heads(attended).astype(jnp.float32), axis=-1
    )
    zero_heads = jnp.zeros((frame_count, HEADS, HDIM), jnp.float32)
    back_start = (zero_heads,)
    advance_back = query_side(query_heads, grad_heads, logsum, delta, length, scaling)
    back_state = over_blocks(
        advance_back,
        back_start,
        (
            lax.all_gather(key_rows, "tm", axis=0, tiled=True),
            lax.all_gather(value_rows, "tm", axis=0, tiled=True),
        ),
    )
    own_living = valid[:, 0][None, None, :]
    advance_keys = key_side(split_heads(key_rows), split_heads(value_rows), own_living, scaling)
    travelling = (queries.astype(jnp.float32), grad_attended.astype(jnp.float32), logsum, delta)
    grad_keys, grad_values = over_blocks(
        advance_keys,
        (zero_heads, zero_heads),
        (
            lax.all_gather(travelling[0], "tm", axis=0, tiled=True),
            lax.all_gather(travelling[1], "tm", axis=0, tiled=True),
            lax.all_gather(travelling[2], "tm", axis=0, tiled=True),
            lax.all_gather(travelling[3], "tm", axis=0, tiled=True),
        ),
    )
    grad_qkv = jnp.concatenate(
        [
            back_state[0].reshape(frame_count, width).astype(jnp.bfloat16),
            grad_keys.reshape(frame_count, width).astype(jnp.bfloat16),
            grad_values.reshape(frame_count, width).astype(jnp.bfloat16),
        ],
        axis=1,
    )
    back_normed = lax.dot_general(
        grad_qkv, w_proj[:, : 3 * width], contract_last, preferred_element_type=jnp.float32
    )
    unused_attn, pull_attn = jax.vjp(normalize, inputs, gain_attn)
    back_inputs, gain_attn_term = pull_attn(back_normed)
    grad_frames = (grad_resid + back_inputs).astype(jnp.bfloat16)[None]
    inner_part = lax.dot_general(
        normed_attn, grad_qkv, contract_first, preferred_element_type=jnp.float32
    )
    outer_part = lax.dot_general(
        grad_resid_low, attended, contract_first, preferred_element_type=jnp.float32
    )
    grad_proj = lax.psum_scatter(
        jnp.concatenate([inner_part, outer_part], axis=1),
        ("dp", "tm"),
        scatter_dimension=0,
        tiled=True,
    )
    conv_sum, gains_sum = lax.psum(
        (conv_term, jnp.stack([gain_attn_term, gain_conv_term])), ("dp", "tm")
    )
    return (grad_frames, grad_proj * grad_scale, conv_sum * grad_scale, gains_sum * grad_scale)


def solution(mesh):
    return jax.shard_map(
        per_device,
        mesh=mesh,
        in_specs=(P("dp", "tm", None), P("dp", "tm", None), P("dp"), P(), P(), P(), P()),
        out_specs=(P("dp", "tm", None), P(("dp", "tm"), None), P(), P()),
        check_vma=False,
    )
```

profile of v0, /device:TPU:1, one launch (start us, length us, event | category | flops | bytes accessed | tf_op | source)
XLA Modules:
  0.0 585.6 jit_solution(8436438792059377084)
XLA Ops:
  7.2 1.1 convert_reduce_fusion
  8.3 1.2 fusion.68
  10.1 2.7 fusion.52
  15.8 1.0 copy.38
  16.9 54.3 %all-gather.7.cloned.1.call-done = bf16[2048,512]{1,0:T(8,128)(2,1)} async-done(((bf16[128,512]{1,0:T(8,128)(2,1)}), bf16[2048,512]{1,0:T(8,128)(2,1)}) %all-gather.7.cloned.1.call-update) | async-done | bytes 2097168 | tf_op jit(solution)/shard_map/all_gather | solution.py:174
  71.1 2.9 copy.40
  74.1 52.0 %all-gather.5.cloned.1.call-done = bf16[2048,512]{1,0:T(8,128)(2,1)} async-done(((bf16[128,512]{1,0:T(8,128)(2,1)}), bf16[2048,512]{1,0:T(8,128)(2,1)}) %all-gather.5.cloned.1.call-update) | async-done | bytes 2097168 | tf_op jit(solution)/shard_map/all_gather | solution.py:173
  126.1 4.0 copy.39
  130.1 12.4 %while.48 = (s32[]{:T(128)}, f32[8,128]{1,0:T(8,128)S(1)}, f32[8,128]{1,0:T(8,128)S(1)}, f32[128,8,64]{0,2,1:T(8,128)S(1)}, s32[]{:T(128)}, /*index=5*/bf16[2048...) while((s32[]{:T(128)}, f32[8,128]{1,0:T(8,128)S(1)}, ...), condition=%wide.region_5.6_spmd.clone, body=%wide.region_2.5_spmd.clone.sunk | while | flops 282271744 | bytes 19599556 | solution.py:49
  130.8 1.4 constant_dynamic-slice_fusion.9
  132.2 1.2 bitcast_reduce_fusion.2
  133.4 1.4 fusion.174
  134.8 1.4 fusion.172
  137.0 1.4 constant_dynamic-slice_fusion.9
  138.4 1.2 bitcast_reduce_fusion.2
  139.6 1.4 fusion.174
  141.0 1.4 fusion.172
  142.5 1.8 fusion.120
  144.8 2.4 collective-permute-start
  147.2 2.0 collective-permute-start.1
  149.2 4.7 collective-permute-done.1
  154.1 4.8 multiply_reduce_fusion.1
  158.9 1.4 multiply_reduce_fusion.19
  160.3 1.9 collective-permute-start.2
  162.2 2.6 collective-permute-start.3
  164.8 6.9 %collective-permute-done.3 = bf16[15,1024]{1,0:T(8,128)(2,1)S(1)} collective-permute-done((bf16[15,1024]{1,0:T(8,128)(2,1)S(1)}, bf16[15,1024]{1,0:T(8,128)(2,1)S(1)}, u32[]{:S(2)}, u32[]{:S(2)}) %collective-permute-start.3) | collective-permute-done | bytes 30752 | tf_op jit(solution)/shard_map/ppermute | solution.py:25
  171.7 4.2 multiply_reduce_fusion
  177.3 2.4 convolution_convert_fusion
  182.0 21.1 %all_gather.23 = f32[2048,8]{0,1:T(8,128)} all-gather(f32[128,8]{0,1:T(8,128)} %bitcast.41), channel_id=1, replica_groups=mesh['dp'=16,'tm'=16] {'tm'}, dimensions={0}, use_global_device_ids=true | all-gather | bytes 69632 | tf_op jit(solution)/shard_map/all_gather | solution.py:243
  203.2 2.6 stack.132
  205.8 1.6 copy.41
  207.5 1.0 multiply_reduce_fusion.34
  208.4 22.9 %while.49 = (s32[]{:T(128)}, f32[128,8,64]{0,2,1:T(8,128)}, bf16[2048,512]{0,1:T(8,128)(2,1)}, s32[]{:T(128)}, bf16[128,8,64]{0,2,1:T(8,128)(2,1)S(1)}, /*index=...) while((s32[]{:T(128)}, f32[128,8,64]{0,2,1:T(8,128)}, ...), condition=%wide.region_12.13_spmd.clone, body=%wide.region_11.12_spmd.clone.sunk | while | flops 410191872 | bytes 16525513 | solution.py:49
  209.1 2.4 constant_dynamic-slice_fusion.10
  211.6 2.7 fusion.180
  214.3 5.6 fusion.181
  220.5 2.4 constant_dynamic-slice_fusion.10
  223.0 2.7 fusion.180
  225.7 5.6 fusion.181
  231.4 1.6 convert_element_type.146
  233.0 22.3 %all_gather.25 = f32[2048,8]{0,1:T(8,128)} all-gather(f32[128,8]{0,1:T(8,128)S(1)} %get-tuple-element.1160), channel_id=1, replica_groups=mesh['dp'=16,'tm'=16] {'tm'}, dimensions={0}, use_global_device_ids=true | all-gather | bytes 69632 | tf_op jit(solution)/shard_map/all_gather | solution.py:244
  255.3 2.8 fusion.123
  258.2 34.1 %while.50 = (s32[]{:T(128)}, f32[128,8,64]{0,2,1:T(8,128)}, f32[128,8,64]{0,2,1:T(8,128)}, bf16[2048,512]{1,0:T(8,128)(2,1)}, bf16[128,8,64]{0,2,1:T(8,128)(2,1)...) while((s32[]{:T(128)}, f32[128,8,64]{0,2,1:T(8,128)}, ...), condition=%wide.region_14.15_spmd.clone, body=%wide.region_13.14_spmd.clone.sunk | while | flops 549781760 | bytes 32211772 | solution.py:49
  258.9 1.4 dynamic-slice_bitcast_fusion.3
  260.3 1.7 constant_dynamic-slice_fusion.11
  263.1 2.7 fusion.189
  265.9 5.3 fusion.190
  271.2 3.3 fusion.191
  275.9 1.4 dynamic-slice_bitcast_fusion.3
  277.3 1.7 constant_dynamic-slice_fusion.11
  280.2 2.7 fusion.189
  283.0 5.3 fusion.190
  288.3 3.3 fusion.191
  292.3 1.0 convert_element_type.152
  293.3 1.0 convert_element_type.150
  294.3 2.2 fusion.104
  296.5 4.0 pad_maximum_fusion
  300.6 0.8 copy-done.13
  301.4 3.1 fusion.69
  304.9 75.8 %psum.15 = f32[2,1024]{1,0:T(2,128)S(1)} all-reduce(f32[2,1024]{1,0:T(2,128)S(1)} %pad_maximum_fusion.4), channel_id=1, replica_groups=mesh['dp'=16,'tm'=16] {'dp','tm'}, use_global_device_ids=true, to_apply=%region_52.53 | all-reduce | flops 2048 | bytes 16384 | tf_op jit(solution)/shard_map/psum | solution.py:273
  381.3 1.0 fusion.103
  382.3 193.7 %all-reduce.4.cloned.1.call-done = (f32[1024,2048]{1,0:T(8,128)}, f32[31,1024]{1,0:T(8,128)}) async-done(((f32[1024,2048]{1,0:T(8,128)}, f32[31,1024]{1,0:T(8,128)}), (f32[1024,2048]{1,0:T(8,128)}, f32[31,1024]{1,0:T(8,128)})) %all-reduce.4.cloned.1.call-update) | async-done | bytes 8515600
  576.1 1.6 broadcast_multiply_fusion
  577.6 1.5 dynamic-slice_multiply_fusion
  (182 shorter events, 15.8 us)
Async XLA Ops:
  7.2 8.6 %copy-start.18 = (bf16[31,1024]{1,0:T(8,128)(2,1)S(1)}, bf16[31,1024]{1,0:T(8,128)(2,1)}, u32[]{:S(2)}) copy-start(bf16[31,1024]{1,0:T(8,128)(2,1)} %param.19) | copy-start | bytes 190468
  7.2 63.9 %all-gather.7.cloned.1.call-start = ((), (), s32[]{:S(2)}) async-start(), calls=%async_computation.1 | async-start | bytes 2228224 | tf_op jit(solution)/shard_map/all_gather | solution.py:174
  8.3 8.6 %copy-start.44 = (f32[128]{0:T(128)}, f32[128]{0:T(128)S(1)}, u32[]{:S(2)}) copy-start(f32[128]{0:T(128)S(1)} %broadcast_multiply_fusion.3) | copy-start | bytes 1540
  10.1 6.8 %copy-start.46 = (f32[128]{0:T(128)}, f32[128]{0:T(128)S(1)}, u32[]{:S(2)}) copy-start(f32[128]{0:T(128)S(1)} %fusion.105) | copy-start | bytes 1540
  13.5 112.6 %all-gather.5.cloned.1.call-start = ((), (), s32[]{:S(2)}) async-start(), calls=%async_computation | async-start | bytes 2228224 | tf_op jit(solution)/shard_map/all_gather | solution.py:173
  14.3 243.9 %all-gather.9.cloned.1.call-start = ((), (), s32[]{:S(2)}) async-start(), calls=%async_computation.2 | async-start | bytes 2228224 | tf_op jit(solution)/shard_map/all_gather | solution.py:241
  15.0 243.2 %all-gather.11.cloned.1.call-start = ((), (), s32[]{:S(2)}) async-start(), calls=%async_computation.3 | async-start | bytes 2228224 | tf_op jit(solution)/shard_map/all_gather | solution.py:242
  130.1 12.5 %copy-start = (bf16[1,128,1024]{2,1,0:T(8,128)(2,1)S(1)}, bf16[1,128,1024]{2,1,0:T(8,128)(2,1)}, u32[]{:S(2)}) copy-start(bf16[1,128,1024]{2,1,0:T(8,128)(2,1)} %param.13) | copy-start | bytes 786436
  130.1 14.5 %copy-start.21 = (f32[1024]{0:T(1024)S(1)}, f32[1024]{0:T(1024)}, u32[]{:S(2)}) copy-start(f32[1024]{0:T(1024)} %param.18) | copy-start | bytes 12292
  142.5 11.6 %copy-start.5 = (bf16[1,128,1024]{2,1,0:T(8,128)(2,1)S(1)}, bf16[1,128,1024]{2,1,0:T(8,128)(2,1)}, u32[]{:S(2)}) copy-start(bf16[1,128,1024]{2,1,0:T(8,128)(2,1)} %param.14) | copy-start | bytes 786436
  142.5 11.5 %copy-start.7 = (bf16[128,8,64]{0,2,1:T(8,128)(2,1)}, bf16[128,8,64]{0,2,1:T(8,128)(2,1)S(1)}, u32[]{:S(2)}) copy-start(bf16[128,8,64]{0,2,1:T(8,128)(2,1)S(1)} %divide_convert_fusion) | copy-start | bytes 393220
  144.8 4.4 collective-permute-start
  147.2 6.7 %collective-permute-start.1 = (bf16[15,1024]{1,0:T(8,128)(2,1)S(1)}, bf16[15,1024]{1,0:T(8,128)(2,1)S(1)}, u32[]{:S(2)}, u32[]{:S(2)}) collective-permute-start(bf16[15,1024]{1,0:T(8,128)(2,1)S(1)} %get-tuple-element.773), channel_id=1, source_target_pairs={{1,0},{2,1},{3,2},{4,3},{5,4},{6,5},{7,6},{8,7},{9,8},{10,9},{11,1... | collective-permute-start | bytes 92168 | tf_op jit(solution)/shard_map/ppermute | solution.py:25
  160.3 4.5 collective-permute-start.2
  162.2 9.5 %collective-permute-start.3 = (bf16[15,1024]{1,0:T(8,128)(2,1)S(1)}, bf16[15,1024]{1,0:T(8,128)(2,1)S(1)}, u32[]{:S(2)}, u32[]{:S(2)}) collective-permute-start(bf16[15,1024]{1,0:T(8,128)(2,1)S(1)} %get-tuple-element.771), channel_id=1, source_target_pairs={{1,0},{2,1},{3,2},{4,3},{5,4},{6,5},{7,6},{8,7},{9,8},{10,9},{11,1... | collective-permute-start | bytes 92168 | tf_op jit(solution)/shard_map/ppermute | solution.py:25
  175.9 3.9 copy-start.9
  175.9 4.7 copy-start.8
  175.9 27.1 %copy-start.22 = (f32[1024]{0:T(1024)S(1)}, f32[1024]{0:T(1024)}, u32[]{:S(2)}) copy-start(f32[1024]{0:T(1024)} %get-tuple-element.684) | copy-start | bytes 12292
  175.9 27.1 %copy-start.23 = (f32[1024]{0:T(1024)S(1)}, f32[1024]{0:T(1024)}, u32[]{:S(2)}) copy-start(f32[1024]{0:T(1024)} %get-tuple-element.685) | copy-start | bytes 12292
  175.9 27.1 %copy-start.24 = (f32[1024]{0:T(1024)S(1)}, f32[1024]{0:T(1024)}, u32[]{:S(2)}) copy-start(f32[1024]{0:T(1024)} %get-tuple-element.686) | copy-start | bytes 12292
  175.9 27.1 %copy-start.25 = (f32[1024]{0:T(1024)S(1)}, f32[1024]{0:T(1024)}, u32[]{:S(2)}) copy-start(f32[1024]{0:T(1024)} %get-tuple-element.656) | copy-start | bytes 12292
  175.9 27.1 %copy-start.26 = (f32[1024]{0:T(1024)S(1)}, f32[1024]{0:T(1024)}, u32[]{:S(2)}) copy-start(f32[1024]{0:T(1024)} %get-tuple-element.657) | copy-start | bytes 12292
  176.0 27.1 %copy-start.27 = (f32[1024]{0:T(1024)S(1)}, f32[1024]{0:T(1024)}, u32[]{:S(2)}) copy-start(f32[1024]{0:T(1024)} %get-tuple-element.658) | copy-start | bytes 12292
  176.0 27.1 %copy-start.28 = (f32[1024]{0:T(1024)S(1)}, f32[1024]{0:T(1024)}, u32[]{:S(2)}) copy-start(f32[1024]{0:T(1024)} %get-tuple-element.659) | copy-start | bytes 12292
  176.0 27.1 %copy-start.29 = (f32[1024]{0:T(1024)S(1)}, f32[1024]{0:T(1024)}, u32[]{:S(2)}) copy-start(f32[1024]{0:T(1024)} %get-tuple-element.660) | copy-start | bytes 12292
  176.0 27.1 %copy-start.30 = (f32[1024]{0:T(1024)S(1)}, f32[1024]{0:T(1024)}, u32[]{:S(2)}) copy-start(f32[1024]{0:T(1024)} %get-tuple-element.661) | copy-start | bytes 12292
  176.0 27.1 %copy-start.31 = (f32[1024]{0:T(1024)S(1)}, f32[1024]{0:T(1024)}, u32[]{:S(2)}) copy-start(f32[1024]{0:T(1024)} %get-tuple-element.662) | copy-start | bytes 12292
  176.0 27.1 %copy-start.32 = (f32[1024]{0:T(1024)S(1)}, f32[1024]{0:T(1024)}, u32[]{:S(2)}) copy-start(f32[1024]{0:T(1024)} %get-tuple-element.663) | copy-start | bytes 12292
  176.0 27.1 %copy-start.33 = (f32[1024]{0:T(1024)S(1)}, f32[1024]{0:T(1024)}, u32[]{:S(2)}) copy-start(f32[1024]{0:T(1024)} %get-tuple-element.664) | copy-start | bytes 12292
  176.0 27.1 %copy-start.34 = (f32[1024]{0:T(1024)S(1)}, f32[1024]{0:T(1024)}, u32[]{:S(2)}) copy-start(f32[1024]{0:T(1024)} %get-tuple-element.665) | copy-start | bytes 12292
  176.0 27.1 %copy-start.35 = (f32[1024]{0:T(1024)S(1)}, f32[1024]{0:T(1024)}, u32[]{:S(2)}) copy-start(f32[1024]{0:T(1024)} %get-tuple-element.666) | copy-start | bytes 12292
  176.0 27.1 %copy-start.36 = (f32[1024]{0:T(1024)S(1)}, f32[1024]{0:T(1024)}, u32[]{:S(2)}) copy-start(f32[1024]{0:T(1024)} %get-tuple-element.667) | copy-start | bytes 12292
  176.1 27.1 %copy-start.37 = (f32[1024]{0:T(1024)S(1)}, f32[1024]{0:T(1024)}, u32[]{:S(2)}) copy-start(f32[1024]{0:T(1024)} %get-tuple-element.668) | copy-start | bytes 12292
  176.1 27.1 %copy-start.38 = (f32[1024]{0:T(1024)S(1)}, f32[1024]{0:T(1024)}, u32[]{:S(2)}) copy-start(f32[1024]{0:T(1024)} %get-tuple-element.669) | copy-start | bytes 12292
  176.1 27.1 %copy-start.39 = (f32[1024]{0:T(1024)S(1)}, f32[1024]{0:T(1024)}, u32[]{:S(2)}) copy-start(f32[1024]{0:T(1024)} %get-tuple-element.670) | copy-start | bytes 12292
  176.1 27.1 %copy-start.40 = (f32[1024]{0:T(1024)S(1)}, f32[1024]{0:T(1024)}, u32[]{:S(2)}) copy-start(f32[1024]{0:T(1024)} %get-tuple-element.671) | copy-start | bytes 12292
  176.1 27.1 %copy-start.41 = (f32[1024]{0:T(1024)S(1)}, f32[1024]{0:T(1024)}, u32[]{:S(2)}) copy-start(f32[1024]{0:T(1024)} %get-tuple-element.672) | copy-start | bytes 12292
  176.1 27.1 %copy-start.42 = (f32[1024]{0:T(1024)S(1)}, f32[1024]{0:T(1024)}, u32[]{:S(2)}) copy-start(f32[1024]{0:T(1024)} %get-tuple-element.673) | copy-start | bytes 12292
  176.4 32.0 %copy-start.48 = (f32[128]{0:T(128)}, f32[128]{0:T(128)S(1)}, u32[]{:S(2)}) copy-start(f32[128]{0:T(128)S(1)} %negate_multiply_fusion.1) | copy-start | bytes 1540
  177.3 31.1 %copy-start.10 = (bf16[128,1024]{1,0:T(8,128)(2,1)}, bf16[128,1024]{1,0:T(8,128)(2,1)S(1)}, u32[]{:S(2)}) copy-start(bf16[128,1024]{1,0:T(8,128)(2,1)S(1)} %fusion.102) | copy-start | bytes 786436
  179.7 396.3 %all-reduce.4.cloned.1.call-start = ((), (), s32[]{:S(2)}) async-start(), calls=%async_computation.4 | async-start | bytes 17039360
  258.2 36.1 %copy-start.19 = (f32[1024]{0:T(1024)S(1)}, f32[1024]{0:T(1024)}, u32[]{:S(2)}) copy-start(f32[1024]{0:T(1024)} %param.17) | copy-start | bytes 12292
  258.2 36.1 %copy-start.45 = (f32[128]{0:T(128)S(1)}, f32[128]{0:T(128)}, u32[]{:S(2)}) copy-start(f32[128]{0:T(128)} %copy-done.44) | copy-start | bytes 1540
  258.2 36.1 %copy-start.47 = (f32[128]{0:T(128)S(1)}, f32[128]{0:T(128)}, u32[]{:S(2)}) copy-start(f32[128]{0:T(128)} %copy-done.46) | copy-start | bytes 1540
  260.3 2.9 copy-start.4
  263.1 2.8 copy-start.11
  263.1 2.8 copy-start.12
  263.1 2.8 copy-start.16
  263.1 2.8 copy-start.20
  265.9 5.3 copy-start.14
  271.2 3.3 copy-start.17
  277.3 2.9 copy-start.4
  280.1 2.8 copy-start.11
  280.2 2.8 copy-start.12
  280.2 2.8 copy-start.16
  280.2 2.8 copy-start.20
  283.0 5.3 copy-start.14
  288.3 3.3 copy-start.17
  294.3 2.2 copy-start.1
  300.6 4.0 copy-start.51
  300.6 4.3 copy-start.43
  300.6 80.7 %copy-start.3 = (f32[128,1024]{1,0:T(8,128)S(1)}, f32[128,1024]{1,0:T(8,128)}, u32[]{:S(2)}) copy-start(f32[128,1024]{1,0:T(8,128)} %copy-done.2) | copy-start | bytes 1572868
  300.6 80.7 %copy-start.6 = (bf16[1,128,1024]{2,1,0:T(8,128)(2,1)S(1)}, bf16[1,128,1024]{2,1,0:T(8,128)(2,1)}, u32[]{:S(2)}) copy-start(bf16[1,128,1024]{2,1,0:T(8,128)(2,1)} %param.14) | copy-start | bytes 786436
  300.6 80.7 %copy-start.49 = (f32[128]{0:T(128)S(1)}, f32[128]{0:T(128)}, u32[]{:S(2)}) copy-start(f32[128]{0:T(128)} %copy-done.48) | copy-start | bytes 1540
  (5 other events, 3.7 us)
Sparse Core Ops, SparseCore 0:
  13.6 57.4 all-gather.6
  73.8 52.2 all-gather.4
  129.4 52.7 all-gather.8
  184.7 51.7 all-gather.10
  300.7 275.3 all-reduce.3
where the time goes:
time: 588 us; the launch traced here: 586 us
  waiting for transfers between devices  313 us (53%)
  blocking collectives  119 us (20%)
  matrix products  59.7 us (10%)
  other arithmetic  34.6 us (6%)
  local copies, waits for them, and re-layouts  34.5 us (6%)
  between operations  15.2 us (3%)
  starting transfers between devices  9.03 us (2%)
    unnamed x6, waiting for transfers between devices  195 us
    psum x1, blocking collectives, per_device(): lax.psum((conv_term, jnp.stack([gain_attn_term, gain_conv_term])), ('dp',...  75.8 us
    all_gather x1, waiting for transfers between devices, per_device(): lax.all_gather(value_rows, 'tm', axis=0, tiled=True)  54.3 us
    all_gather x1, waiting for transfers between devices, per_device(): lax.all_gather(key_rows, 'tm', axis=0, tiled=True)  52 us
    all_gather x1, blocking collectives, per_device(): lax.all_gather(travelling[3], 'tm', axis=0, tiled=True)  22.3 us
    all_gather x1, blocking collectives, per_device(): lax.all_gather(travelling[2], 'tm', axis=0, tiled=True)  21.1 us
    dot_general x6, matrix products, advance(): jnp.einsum('bhd,lhd->hbl', query_heads, key_heads, preferred_element_type...  13.4 us
    dynamic_slice x10, local copies, waits for them, and re-layouts, one_block(): lax.dynamic_slice_in_dim(member, offset, stride, 0)  13.2 us
  transfers between devices with their start and end apart: 9, of which 5 were waited for; matrix products, arithmetic and copies ran while one was open for 13% of the time, Pallas kernels for 0%

commit v1 on v0

--- a/solution.py
+++ b/solution.py
@@ -166,13 +166,13 @@
         jnp.zeros((frame_count, HEADS, HDIM), jnp.float32),
     )
     advance_forward = forward_step(query_heads, length, scaling)
+    key_value_all = lax.all_gather(projected[:, width:], "tm", axis=0, tiled=True)
+    keys_all = key_value_all[:, :width]
+    values_all = key_value_all[:, width:]
     top_all, total_all, accumulated = over_blocks(
         advance_forward,
         start_state,
-        (
-            lax.all_gather(key_rows, "tm", axis=0, tiled=True),
-            lax.all_gather(value_rows, "tm", axis=0, tiled=True),
-        ),
+        (keys_all, values_all),
     )
     attended = (
         (accumulated / total_all.T[:, :, None]).reshape(frame_count, width).astype(jnp.bfloat16)
@@ -226,23 +226,18 @@
     back_state = over_blocks(
         advance_back,
         back_start,
-        (
-            lax.all_gather(key_rows, "tm", axis=0, tiled=True),
-            lax.all_gather(value_rows, "tm", axis=0, tiled=True),
-        ),
+        (keys_all, values_all),
     )
     own_living = valid[:, 0][None, None, :]
     advance_keys = key_side(split_heads(key_rows), split_heads(value_rows), own_living, scaling)
-    travelling = (queries.astype(jnp.float32), grad_attended.astype(jnp.float32), logsum, delta)
+    rows_all = lax.all_gather(
+        jnp.concatenate([queries, grad_attended], axis=1), "tm", axis=0, tiled=True
+    )
+    stats_all = lax.all_gather(jnp.concatenate([logsum, delta], axis=1), "tm", axis=0, tiled=True)
     grad_keys, grad_values = over_blocks(
         advance_keys,
         (zero_heads, zero_heads),
-        (
-            lax.all_gather(travelling[0], "tm", axis=0, tiled=True),
-            lax.all_gather(travelling[1], "tm", axis=0, tiled=True),
-            lax.all_gather(travelling[2], "tm", axis=0, tiled=True),
-            lax.all_gather(travelling[3], "tm", axis=0, tiled=True),
-        ),
+        (rows_all[:, :width], rows_all[:, width:], stats_all[:, :HEADS], stats_all[:, HEADS:]),
     )
     grad_qkv = jnp.concatenate(
         [
@@ -264,15 +259,26 @@
     outer_part = lax.dot_general(
         grad_resid_low, attended, contract_first, preferred_element_type=jnp.float32
     )
-    grad_proj = lax.psum_scatter(
-        jnp.concatenate([inner_part, outer_part], axis=1),
-        ("dp", "tm"),
-        scatter_dimension=0,
-        tiled=True,
-    )
-    conv_sum, gains_sum = lax.psum(
-        (conv_term, jnp.stack([gain_attn_term, gain_conv_term])), ("dp", "tm")
-    )
+    axes = ("dp", "tm")
+    devices = lax.axis_size(axes)
+    rows = inner_part.shape[0]
+    small = jnp.concatenate([conv_term, gain_attn_term[None], gain_conv_term[None]], axis=0)
+    small_count = small.size
+    small_width = -(-small_count // rows)
+    small_flat = jnp.pad(small.reshape(-1), (0, small_width * rows - small_count))
+    packed = jnp.concatenate(
+        [inner_part, outer_part, small_flat.reshape(rows, small_width)], axis=1
+    )
+    packed = packed.reshape(devices, rows // devices, packed.shape[1]).astype(jnp.bfloat16)
+    reduced = lax.all_to_all(packed, axes, 0, 0, tiled=True).astype(jnp.float32).sum(0)
+    grad_proj = reduced[:, : 4 * width]
+    small_part = reduced[:, 4 * width :].reshape(1, -1)
+    small_all = lax.all_to_all(
+        jnp.broadcast_to(small_part, (devices, small_part.shape[1])), axes, 0, 0, tiled=True
+    )
+    small_sum = small_all.reshape(-1)[:small_count]
+    conv_sum = small_sum[: conv_term.size].reshape(conv_term.shape)
+    gains_sum = small_sum[conv_term.size :].reshape(2, -1)
     return (grad_frames, grad_proj * grad_scale, conv_sum * grad_scale, gains_sum * grad_scale)
 
 

time: 588 us -> 434 us (0.74)
  waiting for transfers between devices: 313 us -> 88.6 us
  local copies, waits for them, and re-layouts: 34.5 us -> 87.7 us
  blocking collectives: 119 us -> 132 us
  starting transfers between devices: 9.03 us -> 17.2 us
    unnamed x6 -> x2, waiting for transfers between devices: 195 us -> 0.03 us
    all_to_all x0 -> x1, blocking collectives: none -> 112 us  [per_device(): lax.all_to_all(packed, axes, 0, 0, tiled=True).astype(jnp.float32).sum(0)]
    psum x1 -> x0, blocking collectives: 75.8 us -> none  [per_device(): lax.psum((conv_term, jnp.stack([gain_attn_term, gain_conv_term])), ('dp',...]
    all_gather x4 -> x2, waiting for transfers between devices: 106 us -> 63.3 us  [the longest x1 63.3 us: per_device(): lax.all_gather(projected[:, width:], 'tm', axis=0, tiled=True)]
    another operation x1 -> x31, local copies, waits for them, and re-layouts: 2.61 us -> 38 us  [per_device(): jnp.stack([jnp.sum(grad_conv_in * padded[shift_index:shift_index + frame_...]
    all_gather x2 -> x1, blocking collectives: 43.4 us -> 20.2 us  [per_device(): lax.all_gather(jnp.concatenate([logsum, delta], axis=1), 'tm', axis=0, ti...]
    all_to_all x0 -> x1, waiting for transfers between devices: none -> 15 us  [per_device(): lax.all_to_all(jnp.broadcast_to(small_part, (devices, small_part.shape[1]...]
    slice x0 -> x6, local copies, waits for them, and re-layouts: none -> 10.6 us  [the longest x1 4.5 us: per_device(): rows_all[:, width:]]
  transfers between devices with their start and end apart: 9 -> 7, of which waited for: 5 -> 4; matrix products, arithmetic and copies ran while one was open for 13% -> 18% of each run, Pallas kernels for 0% -> 0%
where the time goes in v1:
time: 434 us; the launch traced here: 432 us
  blocking collectives  132 us (30%)
  waiting for transfers between devices  88.6 us (20%)
  local copies, waits for them, and re-layouts  87.7 us (20%)
  matrix products  57.4 us (13%)
  other arithmetic  32.9 us (8%)
  starting transfers between devices  17.2 us (4%)
  between operations  16.1 us (4%)
    all_to_all x1, blocking collectives, per_device(): lax.all_to_all(packed, axes, 0, 0, tiled=True).astype(jnp.float32).sum(0)  112 us
    all_gather x1, waiting for transfers between devices, per_device(): lax.all_gather(projected[:, width:], 'tm', axis=0, tiled=True)  63.3 us
    another operation x31, local copies, waits for them, and re-layouts, per_device(): jnp.stack([jnp.sum(grad_conv_in * padded[shift_index:shift_index + frame_...  38 us
    all_gather x1, blocking collectives, per_device(): lax.all_gather(jnp.concatenate([logsum, delta], axis=1), 'tm', axis=0, ti...  20.2 us
    all_to_all x1, waiting for transfers between devices, per_device(): lax.all_to_all(jnp.broadcast_to(small_part, (devices, small_part.shape[1]...  15 us
    dot_general x6, matrix products, advance(): jnp.einsum('bhd,lhd->hbl', query_heads, key_heads, preferred_element_type...  13.5 us
    dynamic_slice x10, local copies, waits for them, and re-layouts, one_block(): lax.dynamic_slice_in_dim(member, offset, stride, 0)  13.2 us
    dot_general x2, matrix products, advance(): jnp.einsum('hbl,lhd->bhd', grad_scores, key_heads, preferred_element_type...  11.2 us
  transfers between devices with their start and end apart: 7, of which 4 were waited for; matrix products, arithmetic and copies ran while one was open for 18% of the time, Pallas kernels for 0%

profile of v1, /device:TPU:1, one launch (start us, length us, event | category | flops | bytes accessed | tf_op | source)
XLA Modules:
  0.0 432.2 jit_solution(11173725838518039456)
XLA Ops:
  9.5 2.6 fusion.52
  15.2 63.3 %all-gather.3.cloned.1.call-done = bf16[2048,1024]{1,0:T(8,128)(2,1)} async-done(((bf16[128,1024]{1,0:T(8,128)(2,1)}), bf16[2048,1024]{1,0:T(8,128)(2,1)}) %all-gather.3.cloned.1.call-update) | async-done | bytes 4194320 | tf_op jit(solution)/shard_map/all_gather | solution.py:169
  78.5 4.5 %fusion.118 = (bf16[2048,512]{1,0:T(8,128)(2,1)}, bf16[2048,512]{1,0:T(8,128)(2,1)}) fusion(bf16[2048,1024]{1,0:T(8,128)(2,1)} %all-gather.3.cloned.1.call-done), kind=kLoop, calls=%fused_computation.222 | loop fusion | bytes 8388608 | tf_op jit(solution)/shard_map/slice | solution.py:171
  83.0 2.9 copy.52
  86.0 4.0 copy.51
  90.0 12.4 %while.48 = (s32[]{:T(128)}, f32[8,128]{1,0:T(8,128)S(1)}, f32[8,128]{1,0:T(8,128)S(1)}, f32[128,8,64]{0,2,1:T(8,128)S(1)}, s32[]{:T(128)}, /*index=5*/bf16[2048...) while((s32[]{:T(128)}, f32[8,128]{1,0:T(8,128)S(1)}, ...), condition=%wide.region_5.6_spmd.clone, body=%wide.region_2.5_spmd.clone.sunk | while | flops 282271744 | bytes 19599556 | solution.py:49
  90.7 1.4 constant_dynamic-slice_fusion.9
  93.3 1.4 fusion.177
  94.8 1.4 fusion.175
  96.9 1.4 constant_dynamic-slice_fusion.9
  99.5 1.4 fusion.177
  100.9 1.4 fusion.175
  102.6 1.8 fusion.125
  105.0 2.3 collective-permute-start
  107.3 2.0 collective-permute-start.1
  109.4 4.7 %collective-permute-done.1 = bf16[15,1024]{1,0:T(8,128)(2,1)S(1)} collective-permute-done((bf16[15,1024]{1,0:T(8,128)(2,1)S(1)}, bf16[15,1024]{1,0:T(8,128)(2,1)S(1)}, u32[]{:S(2)}, u32[]{:S(2)}) %collective-permute-start.1) | collective-permute-done | bytes 30752 | tf_op jit(solution)/shard_map/ppermute | solution.py:25
  114.3 4.8 %multiply_reduce_fusion.1 = (bf16[1024]{0:T(1024)(128)(2,1)}, bf16[1024]{0:T(1024)(128)(2,1)}, bf16[1024]{0:T(1024)(128)(2,1)}, bf16[1024]{0:T(1024)(128)(2,1)},...) fusion(f32[158,1024]{1,0:T(8,128)S(1)} %maximum_convert_fusion,, ...), kind=kLoop, calls=%fused_computation.154 | loop fusion | flops 13875200 | bytes 17203200 | tf_op jit(solution)/shard_map/reduce_sum | solution.py:200
  119.1 1.4 multiply_reduce_fusion.19
  120.6 1.9 collective-permute-start.2
  122.5 2.6 collective-permute-start.3
  125.1 5.5 %collective-permute-done.3 = bf16[15,1024]{1,0:T(8,128)(2,1)S(1)} collective-permute-done((bf16[15,1024]{1,0:T(8,128)(2,1)S(1)}, bf16[15,1024]{1,0:T(8,128)(2,1)S(1)}, u32[]{:S(2)}, u32[]{:S(2)}) %collective-permute-start.3) | collective-permute-done | bytes 30752 | tf_op jit(solution)/shard_map/ppermute | solution.py:25
  130.7 4.1 multiply_reduce_fusion
  135.9 1.6 convolution_convert_fusion.2
  138.3 1.7 copy.57
  140.0 1.7 copy.56
  142.9 1.3 stack.136
  149.0 1.3 stack.149
  150.3 1.3 stack.148
  156.5 1.3 stack.143
  157.8 1.3 stack.142
  160.2 1.3 stack.140
  167.6 1.3 stack.133
  168.9 1.3 stack.132
  170.2 1.3 stack.131
  171.4 1.3 stack.130
  177.7 1.3 stack.125
  179.0 1.3 stack.124
  182.7 23.0 %while.49 = (s32[]{:T(128)}, f32[128,8,64]{0,2,1:T(8,128)}, bf16[2048,512]{0,1:T(8,128)(2,1)}, s32[]{:T(128)}, bf16[128,8,64]{0,2,1:T(8,128)(2,1)S(1)}, /*index=...) while((s32[]{:T(128)}, f32[128,8,64]{0,2,1:T(8,128)}, ...), condition=%wide.region_12.13_spmd.clone, body=%wide.region_11.12_spmd.clone.sunk | while | flops 410191872 | bytes 16541925 | solution.py:49
  183.4 2.4 constant_dynamic-slice_fusion.10
  185.9 2.8 fusion.183
  188.7 5.6 %fusion.184 = f32[128,8,64]{0,2,1:T(8,128)} fusion(bf16[1024,8,64]{0,2,1:T(8,128)(2,1)S(1)} %bitcast.225, f32[8,1024,128]{2,1,0:T(8,128)} %fusion.183, bf16[1024,8,64]{0,2,1:T(8,128)(2,1)} %bitcast.229, bf16[128,8,64]{0,2,1:T(8,128)(2,1)} %get-tuple-element.1123, f32[8,128]{1,0:T(8,128)S(1)} %bitcast.307, f32[8,128]{1,0:T(8,128)S(1)} %copy-done.72, ...), kind=kOutput, calls=%fused_computation.29.clone.1 | convolution fusion | flops 275972096 | bytes 6956033 | tf_op jit(solution)/shard_map/while/body/eval_jaxpr/hbl,lhd->bhd/dot_general | solution.py:100
  195.0 2.4 constant_dynamic-slice_fusion.10
  197.4 2.8 fusion.183
  200.2 5.6 %fusion.184 = f32[128,8,64]{0,2,1:T(8,128)} fusion(bf16[1024,8,64]{0,2,1:T(8,128)(2,1)S(1)} %bitcast.225, f32[8,1024,128]{2,1,0:T(8,128)} %fusion.183, bf16[1024,8,64]{0,2,1:T(8,128)(2,1)} %bitcast.229, bf16[128,8,64]{0,2,1:T(8,128)(2,1)} %get-tuple-element.1123, f32[8,128]{1,0:T(8,128)S(1)} %bitcast.307, f32[8,128]{1,0:T(8,128)S(1)} %copy-done.72, ...), kind=kOutput, calls=%fused_computation.29.clone.1 | convolution fusion | flops 275972096 | bytes 6956033 | tf_op jit(solution)/shard_map/while/body/eval_jaxpr/hbl,lhd->bhd/dot_general | solution.py:100
  209.3 20.2 %all_gather.11 = f32[2048,16]{0,1:T(8,128)S(1)} all-gather(f32[128,16]{0,1:T(8,128)S(1)} %pad_maximum_fusion.5), channel_id=1, replica_groups=mesh['dp'=16,'tm'=16] {'tm'}, dimensions={0}, use_global_device_ids=true | all-gather | bytes 139264 | tf_op jit(solution)/shard_map/all_gather | solution.py:236
  229.5 2.4 convolution_convert_fusion.1
  232.6 4.5 %fusion.117 = (bf16[2048,512]{1,0:T(8,128)(2,1)}, bf16[2048,512]{1,0:T(8,128)(2,1)}) fusion(bf16[2048,1024]{1,0:T(8,128)(2,1)} %all-gather.5.cloned.1.call-done), kind=kLoop, calls=%fused_computation.221 | loop fusion | bytes 8388608 | tf_op jit(solution)/shard_map/slice | solution.py:240
  237.1 34.0 %while.50 = (s32[]{:T(128)}, f32[128,8,64]{0,2,1:T(8,128)}, f32[128,8,64]{0,2,1:T(8,128)}, bf16[2048,512]{1,0:T(8,128)(2,1)}, bf16[128,8,64]{0,2,1:T(8,128)(2,1)...) while((s32[]{:T(128)}, f32[128,8,64]{0,2,1:T(8,128)}, ...), condition=%wide.region_14.15_spmd.clone, body=%wide.region_13.14_spmd.clone.sunk | while | flops 549781760 | bytes 31687456 | solution.py:49
  237.8 1.4 dynamic-slice_bitcast_fusion.3
  239.2 1.7 constant_dynamic-slice_fusion.11
  242.0 2.7 fusion.192
  244.7 5.3 %fusion.193 = f32[128,8,64]{0,2,1:T(8,128)S(1)} fusion(bf16[1024,8,64]{0,2,1:T(8,128)(2,1)S(1)} %bitcast.227, f32[8,1024,128]{2,1,0:T(8,128)} %fusion.192, bf16[1024,8,64]{0,2,1:T(8,128)(2,1)S(1)} %bitcast.230, bf16[128,8,64]{0,2,1:T(8,128)(2,1)S(1)} %copy-done.20, f32[8,1024]{1,0:T(8,128)S(1)} %copy-done.13, f32[8,1024]{1,0:T(8,128)S(1)} %copy-done.12, ...), kind=kOutput, calls=%fused_computation.46.clone.1 | convolution fusion | flops 275972096 | bytes 7012481 | tf_op jit(solution)/shard_map/while/body/eval_jaxpr/hbl,bhd->lhd/dot_general | solution.py:127
  250.1 3.3 fusion.194
  254.8 1.4 dynamic-slice_bitcast_fusion.3
  256.2 1.7 constant_dynamic-slice_fusion.11
  259.0 2.7 fusion.192
  261.8 5.3 %fusion.193 = f32[128,8,64]{0,2,1:T(8,128)S(1)} fusion(bf16[1024,8,64]{0,2,1:T(8,128)(2,1)S(1)} %bitcast.227, f32[8,1024,128]{2,1,0:T(8,128)} %fusion.192, bf16[1024,8,64]{0,2,1:T(8,128)(2,1)S(1)} %bitcast.230, bf16[128,8,64]{0,2,1:T(8,128)(2,1)S(1)} %copy-done.20, f32[8,1024]{1,0:T(8,128)S(1)} %copy-done.13, f32[8,1024]{1,0:T(8,128)S(1)} %copy-done.12, ...), kind=kOutput, calls=%fused_computation.46.clone.1 | convolution fusion | flops 275972096 | bytes 7012481 | tf_op jit(solution)/shard_map/while/body/eval_jaxpr/hbl,bhd->lhd/dot_general | solution.py:127
  267.1 3.3 fusion.194
  273.8 3.1 fusion.69
  281.4 3.4 copy.69
  284.8 111.7 %all_to_all.11 = bf16[256,4,2081]{2,1,0:T(4,128)(2,1)S(1)} all-to-all(bf16[256,4,2081]{2,1,0:T(4,128)(2,1)S(1)} %copy.69), channel_id=1, replica_groups=mesh['dp'=16,'tm'=16] {'dp','tm'}, dimensions={0} | all-to-all | bytes 8523776 | tf_op jit(solution)/shard_map/all_to_all | solution.py:273
  396.5 1.8 convert_reduce_fusion
  399.2 8.3 %all-to-all-start.1 = ((f32[256,1,132]{2,1,0:T(1,128)}), f32[256,1,132]{2,1,0:T(1,128)S(1)}, u32[]{:S(2)}, u32[]{:S(2)}) async-start(f32[256,1,132]{2,1,0:T(1,128)} %broadcast_in_dim.206), calls=%async_computation.1 | async-start | bytes 524288 | tf_op jit(solution)/shard_map/all_to_all | solution.py:276
  408.1 15.0 %all-to-all-done.1 = f32[256,1,132]{2,1,0:T(1,128)S(1)} async-done(((f32[256,1,132]{2,1,0:T(1,128)}), f32[256,1,132]{2,1,0:T(1,128)S(1)}, u32[]{:S(2)}, u32[]{:S(2)}) %all-to-all-start.1) | async-done | bytes 135200 | tf_op jit(solution)/shard_map/all_to_all | solution.py:276
  (290 shorter events, 57.4 us)
Async XLA Ops:
  7.2 7.4 %copy-start.19 = (bf16[31,1024]{1,0:T(8,128)(2,1)S(1)}, bf16[31,1024]{1,0:T(8,128)(2,1)}, u32[]{:S(2)}) copy-start(bf16[31,1024]{1,0:T(8,128)(2,1)} %param.19) | copy-start | bytes 190468
  7.2 71.4 %all-gather.3.cloned.1.call-start = ((), (), s32[]{:S(2)}) async-start(), calls=%async_computation.2 | async-start | bytes 4456448 | tf_op jit(solution)/shard_map/all_gather | solution.py:169
  8.3 74.7 %copy-start.74 = (f32[128]{0:T(128)}, f32[128]{0:T(128)S(1)}, u32[]{:S(2)}) copy-start(f32[128]{0:T(128)S(1)} %broadcast_multiply_fusion.1) | copy-start | bytes 1540
  9.5 73.6 %copy-start.82 = (f32[128]{0:T(128)}, f32[128]{0:T(128)S(1)}, u32[]{:S(2)}) copy-start(f32[128]{0:T(128)S(1)} %fusion.68) | copy-start | bytes 1540
  9.5 73.5 %copy-start.78 = (f32[128]{0:T(128)}, f32[128]{0:T(128)S(1)}, u32[]{:S(2)}) copy-start(f32[128]{0:T(128)S(1)} %fusion.107) | copy-start | bytes 1540
  12.9 219.7 %all-gather.5.cloned.1.call-start = ((), (), s32[]{:S(2)}) async-start(), calls=%async_computation.3 | async-start | bytes 4456448 | tf_op jit(solution)/shard_map/all_gather | solution.py:233
  14.4 68.7 %copy-start.8 = (bf16[128,512]{1,0:T(8,128)(2,1)}, bf16[128,512]{1,0:T(8,128)(2,1)S(1)}, u32[]{:S(2)}) copy-start(bf16[128,512]{1,0:T(8,128)(2,1)S(1)} %get-tuple-element.770) | copy-start | bytes 393220
  14.5 90.2 %copy-start.76 = (pred[128]{0:T(512)(128)(4,1)}, pred[128]{0:T(512)(128)(4,1)S(1)}, u32[]{:S(2)}) copy-start(pred[128]{0:T(512)(128)(4,1)S(1)} %add_compare_fusion.2) | copy-start | bytes 388
  90.0 12.7 %copy-start = (bf16[1,128,1024]{2,1,0:T(8,128)(2,1)S(1)}, bf16[1,128,1024]{2,1,0:T(8,128)(2,1)}, u32[]{:S(2)}) copy-start(bf16[1,128,1024]{2,1,0:T(8,128)(2,1)} %param.13) | copy-start | bytes 786436
  90.0 14.8 %copy-start.21 = (f32[1024]{0:T(1024)S(1)}, f32[1024]{0:T(1024)}, u32[]{:S(2)}) copy-start(f32[1024]{0:T(1024)} %param.18) | copy-start | bytes 12292
  102.4 11.8 %copy-start.5 = (bf16[1,128,1024]{2,1,0:T(8,128)(2,1)S(1)}, bf16[1,128,1024]{2,1,0:T(8,128)(2,1)}, u32[]{:S(2)}) copy-start(bf16[1,128,1024]{2,1,0:T(8,128)(2,1)} %param.14) | copy-start | bytes 786436
  102.4 11.8 %copy-start.22 = (f32[1,1024]{1,0:T(1,128)S(1)}, f32[1,1024]{1,0:T(1,128)}, u32[]{:S(2)}) copy-start(f32[1,1024]{1,0:T(1,128)} %get-tuple-element.780) | copy-start | bytes 12292
  102.4 11.8 %copy-start.23 = (f32[1,1024]{1,0:T(1,128)S(1)}, f32[1,1024]{1,0:T(1,128)}, u32[]{:S(2)}) copy-start(f32[1,1024]{1,0:T(1,128)} %get-tuple-element.781) | copy-start | bytes 12292
  102.4 11.7 %copy-start.24 = (f32[1,1024]{1,0:T(1,128)S(1)}, f32[1,1024]{1,0:T(1,128)}, u32[]{:S(2)}) copy-start(f32[1,1024]{1,0:T(1,128)} %get-tuple-element.782) | copy-start | bytes 12292
  102.4 11.7 %copy-start.25 = (f32[1,1024]{1,0:T(1,128)S(1)}, f32[1,1024]{1,0:T(1,128)}, u32[]{:S(2)}) copy-start(f32[1,1024]{1,0:T(1,128)} %get-tuple-element.783) | copy-start | bytes 12292
  102.4 11.7 %copy-start.26 = (f32[1,1024]{1,0:T(1,128)S(1)}, f32[1,1024]{1,0:T(1,128)}, u32[]{:S(2)}) copy-start(f32[1,1024]{1,0:T(1,128)} %get-tuple-element.784) | copy-start | bytes 12292
  102.4 11.7 %copy-start.27 = (f32[1,1024]{1,0:T(1,128)S(1)}, f32[1,1024]{1,0:T(1,128)}, u32[]{:S(2)}) copy-start(f32[1,1024]{1,0:T(1,128)} %get-tuple-element.785) | copy-start | bytes 12292
  102.5 11.7 %copy-start.28 = (f32[1,1024]{1,0:T(1,128)S(1)}, f32[1,1024]{1,0:T(1,128)}, u32[]{:S(2)}) copy-start(f32[1,1024]{1,0:T(1,128)} %get-tuple-element.786) | copy-start | bytes 12292
  102.5 11.7 %copy-start.29 = (f32[1,1024]{1,0:T(1,128)S(1)}, f32[1,1024]{1,0:T(1,128)}, u32[]{:S(2)}) copy-start(f32[1,1024]{1,0:T(1,128)} %get-tuple-element.787) | copy-start | bytes 12292
  102.5 11.7 %copy-start.30 = (f32[1,1024]{1,0:T(1,128)S(1)}, f32[1,1024]{1,0:T(1,128)}, u32[]{:S(2)}) copy-start(f32[1,1024]{1,0:T(1,128)} %get-tuple-element.788) | copy-start | bytes 12292
  102.5 11.7 %copy-start.31 = (f32[1,1024]{1,0:T(1,128)S(1)}, f32[1,1024]{1,0:T(1,128)}, u32[]{:S(2)}) copy-start(f32[1,1024]{1,0:T(1,128)} %get-tuple-element.789) | copy-start | bytes 12292
  102.5 11.7 %copy-start.32 = (f32[1,1024]{1,0:T(1,128)S(1)}, f32[1,1024]{1,0:T(1,128)}, u32[]{:S(2)}) copy-start(f32[1,1024]{1,0:T(1,128)} %get-tuple-element.790) | copy-start | bytes 12292
  102.5 11.7 %copy-start.33 = (f32[1,1024]{1,0:T(1,128)S(1)}, f32[1,1024]{1,0:T(1,128)}, u32[]{:S(2)}) copy-start(f32[1,1024]{1,0:T(1,128)} %get-tuple-element.791) | copy-start | bytes 12292
  102.5 11.7 %copy-start.34 = (f32[1,1024]{1,0:T(1,128)S(1)}, f32[1,1024]{1,0:T(1,128)}, u32[]{:S(2)}) copy-start(f32[1,1024]{1,0:T(1,128)} %get-tuple-element.792) | copy-start | bytes 12292
  102.5 11.7 %copy-start.35 = (f32[1,1024]{1,0:T(1,128)S(1)}, f32[1,1024]{1,0:T(1,128)}, u32[]{:S(2)}) copy-start(f32[1,1024]{1,0:T(1,128)} %get-tuple-element.793) | copy-start | bytes 12292
  102.5 11.7 %copy-start.36 = (f32[1,1024]{1,0:T(1,128)S(1)}, f32[1,1024]{1,0:T(1,128)}, u32[]{:S(2)}) copy-start(f32[1,1024]{1,0:T(1,128)} %get-tuple-element.794) | copy-start | bytes 12292
  102.5 11.7 %copy-start.37 = (f32[1,1024]{1,0:T(1,128)S(1)}, f32[1,1024]{1,0:T(1,128)}, u32[]{:S(2)}) copy-start(f32[1,1024]{1,0:T(1,128)} %get-tuple-element.795) | copy-start | bytes 12292
  102.6 11.7 %copy-start.38 = (f32[1,1024]{1,0:T(1,128)S(1)}, f32[1,1024]{1,0:T(1,128)}, u32[]{:S(2)}) copy-start(f32[1,1024]{1,0:T(1,128)} %get-tuple-element.796) | copy-start | bytes 12292
  102.6 11.7 %copy-start.39 = (f32[1,1024]{1,0:T(1,128)S(1)}, f32[1,1024]{1,0:T(1,128)}, u32[]{:S(2)}) copy-start(f32[1,1024]{1,0:T(1,128)} %get-tuple-element.797) | copy-start | bytes 12292
  105.0 4.4 %collective-permute-start = (bf16[15,1024]{1,0:T(8,128)(2,1)S(1)}, bf16[15,1024]{1,0:T(8,128)(2,1)S(1)}, u32[]{:S(2)}, u32[]{:S(2)}) collective-permute-start(bf16[15,1024]{1,0:T(8,128)(2,1)S(1)} %get-tuple-element.775), channel_id=1, source_target_pairs={{0,1},{1,2},{2,3},{3,4},{4,5},{5,6},{6,7},{7,8},{8,9},{9,10},{10,1... | collective-permute-start | bytes 92168 | tf_op jit(solution)/shard_map/ppermute | solution.py:24
  107.3 6.7 %collective-permute-start.1 = (bf16[15,1024]{1,0:T(8,128)(2,1)S(1)}, bf16[15,1024]{1,0:T(8,128)(2,1)S(1)}, u32[]{:S(2)}, u32[]{:S(2)}) collective-permute-start(bf16[15,1024]{1,0:T(8,128)(2,1)S(1)} %get-tuple-element.776), channel_id=1, source_target_pairs={{1,0},{2,1},{3,2},{4,3},{5,4},{6,5},{7,6},{8,7},{9,8},{10,9},{11,1... | collective-permute-start | bytes 92168 | tf_op jit(solution)/shard_map/ppermute | solution.py:25
  119.1 11.6 %copy-start.77 = (pred[128]{0:T(512)(128)(4,1)S(1)}, pred[128]{0:T(512)(128)(4,1)}, u32[]{:S(2)}) copy-start(pred[128]{0:T(512)(128)(4,1)} %copy-done.76) | copy-start | bytes 388
  120.6 4.5 %collective-permute-start.2 = (bf16[15,1024]{1,0:T(8,128)(2,1)S(1)}, bf16[15,1024]{1,0:T(8,128)(2,1)S(1)}, u32[]{:S(2)}, u32[]{:S(2)}) collective-permute-start(bf16[15,1024]{1,0:T(8,128)(2,1)S(1)} %get-tuple-element.773), channel_id=1, source_target_pairs={{0,1},{1,2},{2,3},{3,4},{4,5},{5,6},{6,7},{7,8},{8,9},{9,10},{10,1... | collective-permute-start | bytes 92168 | tf_op jit(solution)/shard_map/ppermute | solution.py:24
  122.5 8.1 %collective-permute-start.3 = (bf16[15,1024]{1,0:T(8,128)(2,1)S(1)}, bf16[15,1024]{1,0:T(8,128)(2,1)S(1)}, u32[]{:S(2)}, u32[]{:S(2)}) collective-permute-start(bf16[15,1024]{1,0:T(8,128)(2,1)S(1)} %get-tuple-element.774), channel_id=1, source_target_pairs={{1,0},{2,1},{3,2},{4,3},{5,4},{6,5},{7,6},{8,7},{9,8},{10,9},{11,1... | collective-permute-start | bytes 92168 | tf_op jit(solution)/shard_map/ppermute | solution.py:25
  135.1 47.6 %copy-start.1 = (f32[128,1024]{1,0:T(8,128)}, f32[128,1024]{1,0:T(8,128)S(1)}, u32[]{:S(2)}) copy-start(f32[128,1024]{1,0:T(8,128)S(1)} %get-tuple-element.751) | copy-start | bytes 1572868
  135.1 46.0 %copy-start.73 = (bf16[1024]{0:T(1024)(128)(2,1)S(1)}, bf16[1024]{0:T(1024)(128)(2,1)}, u32[]{:S(2)}) copy-start(bf16[1024]{0:T(1024)(128)(2,1)} %get-tuple-element.687) | copy-start | bytes 6148
  135.9 46.9 %copy-start.11 = (bf16[128,1024]{1,0:T(8,128)(2,1)}, bf16[128,1024]{1,0:T(8,128)(2,1)S(1)}, u32[]{:S(2)}) copy-start(bf16[128,1024]{1,0:T(8,128)(2,1)S(1)} %fusion.103) | copy-start | bytes 786436
  183.4 5.2 %copy-start.72 = (f32[8,128]{1,0:T(8,128)S(1)}, f32[8,128]{1,0:T(8,128)}, u32[]{:S(2)}) copy-start(f32[8,128]{1,0:T(8,128)} %get-tuple-element.1121) | copy-start | bytes 12292 | tf_op jit(solution)/shard_map/while
  195.0 5.2 %copy-start.72 = (f32[8,128]{1,0:T(8,128)S(1)}, f32[8,128]{1,0:T(8,128)}, u32[]{:S(2)}) copy-start(f32[8,128]{1,0:T(8,128)} %get-tuple-element.1121) | copy-start | bytes 12292 | tf_op jit(solution)/shard_map/while
  237.1 36.3 %copy-start.40 = (f32[1024]{0:T(1024)S(1)}, f32[1024]{0:T(1024)}, u32[]{:S(2)}) copy-start(f32[1024]{0:T(1024)} %param.17) | copy-start | bytes 12292
  244.7 5.3 %copy-start.15 = (f32[128,8,64]{0,2,1:T(8,128)S(1)}, f32[128,8,64]{0,2,1:T(8,128)}, u32[]{:S(2)}) copy-start(f32[128,8,64]{0,2,1:T(8,128)} %get-tuple-element.1062) | copy-start | bytes 786436 | tf_op jit(solution)/shard_map/while
  261.7 5.3 %copy-start.15 = (f32[128,8,64]{0,2,1:T(8,128)S(1)}, f32[128,8,64]{0,2,1:T(8,128)}, u32[]{:S(2)}) copy-start(f32[128,8,64]{0,2,1:T(8,128)} %get-tuple-element.1062) | copy-start | bytes 786436 | tf_op jit(solution)/shard_map/while
  271.1 5.8 %copy-start.83 = (f32[128]{0:T(128)S(1)}, f32[128]{0:T(128)}, u32[]{:S(2)}) copy-start(f32[128]{0:T(128)} %copy-done.82) | copy-start | bytes 1540
  271.1 5.8 %copy-start.75 = (f32[128]{0:T(128)S(1)}, f32[128]{0:T(128)}, u32[]{:S(2)}) copy-start(f32[128]{0:T(128)} %copy-done.74) | copy-start | bytes 1540
  271.1 5.8 %copy-start.79 = (f32[128]{0:T(128)S(1)}, f32[128]{0:T(128)}, u32[]{:S(2)}) copy-start(f32[128]{0:T(128)} %copy-done.78) | copy-start | bytes 1540
  271.1 6.2 %copy-start.2 = (f32[128,1024]{1,0:T(8,128)S(1)}, f32[128,1024]{1,0:T(8,128)}, u32[]{:S(2)}) copy-start(f32[128,1024]{1,0:T(8,128)} %copy-done.1) | copy-start | bytes 1572868
  271.1 6.2 %copy-start.6 = (bf16[1,128,1024]{2,1,0:T(8,128)(2,1)S(1)}, bf16[1,128,1024]{2,1,0:T(8,128)(2,1)}, u32[]{:S(2)}) copy-start(bf16[1,128,1024]{2,1,0:T(8,128)(2,1)} %param.14) | copy-start | bytes 786436
  271.2 6.2 %copy-start.81 = (f32[128]{0:T(128)S(1)}, f32[128]{0:T(128)}, u32[]{:S(2)}) copy-start(f32[128]{0:T(128)} %copy-done.80) | copy-start | bytes 1540
  273.4 5.1 %copy-start.41 = (bf16[1,1024]{1,0:T(2,128)(2,1)S(1)}, bf16[1,1024]{1,0:T(2,128)(2,1)}, u32[]{:S(2)}) copy-start(bf16[1,1024]{1,0:T(2,128)(2,1)} %stack.136) | copy-start | bytes 6148
  273.4 5.1 %copy-start.42 = (bf16[1,1024]{1,0:T(2,128)(2,1)S(1)}, bf16[1,1024]{1,0:T(2,128)(2,1)}, u32[]{:S(2)}) copy-start(bf16[1,1024]{1,0:T(2,128)(2,1)} %stack.153) | copy-start | bytes 6148
  273.5 5.1 %copy-start.43 = (bf16[1,1024]{1,0:T(2,128)(2,1)S(1)}, bf16[1,1024]{1,0:T(2,128)(2,1)}, u32[]{:S(2)}) copy-start(bf16[1,1024]{1,0:T(2,128)(2,1)} %stack.152) | copy-start | bytes 6148
  273.5 5.1 %copy-start.44 = (bf16[1,1024]{1,0:T(2,128)(2,1)S(1)}, bf16[1,1024]{1,0:T(2,128)(2,1)}, u32[]{:S(2)}) copy-start(bf16[1,1024]{1,0:T(2,128)(2,1)} %stack.151) | copy-start | bytes 6148
  273.5 5.1 %copy-start.45 = (bf16[1,1024]{1,0:T(2,128)(2,1)S(1)}, bf16[1,1024]{1,0:T(2,128)(2,1)}, u32[]{:S(2)}) copy-start(bf16[1,1024]{1,0:T(2,128)(2,1)} %stack.150) | copy-start | bytes 6148
  273.5 5.1 %copy-start.46 = (bf16[1,1024]{1,0:T(2,128)(2,1)S(1)}, bf16[1,1024]{1,0:T(2,128)(2,1)}, u32[]{:S(2)}) copy-start(bf16[1,1024]{1,0:T(2,128)(2,1)} %stack.149) | copy-start | bytes 6148
  273.5 5.1 %copy-start.47 = (bf16[1,1024]{1,0:T(2,128)(2,1)S(1)}, bf16[1,1024]{1,0:T(2,128)(2,1)}, u32[]{:S(2)}) copy-start(bf16[1,1024]{1,0:T(2,128)(2,1)} %stack.148) | copy-start | bytes 6148
  273.5 5.1 %copy-start.48 = (bf16[1,1024]{1,0:T(2,128)(2,1)S(1)}, bf16[1,1024]{1,0:T(2,128)(2,1)}, u32[]{:S(2)}) copy-start(bf16[1,1024]{1,0:T(2,128)(2,1)} %stack.147) | copy-start | bytes 6148
  273.5 5.1 %copy-start.49 = (bf16[1,1024]{1,0:T(2,128)(2,1)S(1)}, bf16[1,1024]{1,0:T(2,128)(2,1)}, u32[]{:S(2)}) copy-start(bf16[1,1024]{1,0:T(2,128)(2,1)} %stack.146) | copy-start | bytes 6148
  273.5 5.1 %copy-start.50 = (bf16[1,1024]{1,0:T(2,128)(2,1)S(1)}, bf16[1,1024]{1,0:T(2,128)(2,1)}, u32[]{:S(2)}) copy-start(bf16[1,1024]{1,0:T(2,128)(2,1)} %stack.145) | copy-start | bytes 6148
  273.5 5.1 %copy-start.51 = (bf16[1,1024]{1,0:T(2,128)(2,1)S(1)}, bf16[1,1024]{1,0:T(2,128)(2,1)}, u32[]{:S(2)}) copy-start(bf16[1,1024]{1,0:T(2,128)(2,1)} %stack.144) | copy-start | bytes 6148
  273.5 5.1 %copy-start.52 = (bf16[1,1024]{1,0:T(2,128)(2,1)S(1)}, bf16[1,1024]{1,0:T(2,128)(2,1)}, u32[]{:S(2)}) copy-start(bf16[1,1024]{1,0:T(2,128)(2,1)} %stack.143) | copy-start | bytes 6148
  273.6 5.1 %copy-start.53 = (bf16[1,1024]{1,0:T(2,128)(2,1)S(1)}, bf16[1,1024]{1,0:T(2,128)(2,1)}, u32[]{:S(2)}) copy-start(bf16[1,1024]{1,0:T(2,128)(2,1)} %stack.142) | copy-start | bytes 6148
  273.6 5.1 %copy-start.54 = (bf16[1,1024]{1,0:T(2,128)(2,1)S(1)}, bf16[1,1024]{1,0:T(2,128)(2,1)}, u32[]{:S(2)}) copy-start(bf16[1,1024]{1,0:T(2,128)(2,1)} %stack.141) | copy-start | bytes 6148
  273.7 6.0 %copy-start.14 = (bf16[128,512]{1,0:T(8,128)(2,1)S(1)}, bf16[128,512]{1,0:T(8,128)(2,1)}, u32[]{:S(2)}) copy-start(bf16[128,512]{1,0:T(8,128)(2,1)} %copy.60) | copy-start | bytes 393220
  399.2 23.9 %all-to-all-start.1 = ((f32[256,1,132]{2,1,0:T(1,128)}), f32[256,1,132]{2,1,0:T(1,128)S(1)}, u32[]{:S(2)}, u32[]{:S(2)}) async-start(f32[256,1,132]{2,1,0:T(1,128)} %broadcast_in_dim.206), calls=%async_computation.1 | async-start | bytes 524288 | tf_op jit(solution)/shard_map/all_to_all | solution.py:276
  (35 other events, 133.3 us)
Sparse Core Ops, SparseCore 0:
  13.0 65.4 all-gather.2
  138.4 63.1 all-gather.4

commit v2 on v1

--- a/solution.py
+++ b/solution.py
@@ -156,28 +156,38 @@
     projected = jnp.dot(
         normed_attn, w_proj[:, : 3 * width], preferred_element_type=jnp.float32
     ).astype(jnp.bfloat16)
-    queries = projected[:, :width]
-    key_rows = projected[:, width : 2 * width]
-    value_rows = projected[:, 2 * width :]
-    query_heads = split_heads(queries)
-    start_state = (
-        jnp.full((HEADS, frame_count), negative, jnp.float32),
-        jnp.zeros((HEADS, frame_count), jnp.float32),
-        jnp.zeros((frame_count, HEADS, HDIM), jnp.float32),
-    )
-    advance_forward = forward_step(query_heads, length, scaling)
-    key_value_all = lax.all_gather(projected[:, width:], "tm", axis=0, tiled=True)
-    keys_all = key_value_all[:, :width]
-    values_all = key_value_all[:, width:]
-    top_all, total_all, accumulated = over_blocks(
-        advance_forward,
-        start_state,
-        (keys_all, values_all),
-    )
-    attended = (
-        (accumulated / total_all.T[:, :, None]).reshape(frame_count, width).astype(jnp.bfloat16)
-    )
-    logsum = (top_all + jnp.log(total_all)).T
+    tm_count = lax.axis_size("tm")
+    halves = tm_count // HEADS
+    me = lax.axis_index("tm")
+    half = me // HEADS
+    span = frame_count * HEADS
+    total = frame_count * tm_count
+    key_live = (jnp.arange(total, dtype=jnp.int32) < length)[None, :]
+    half_live = lax.dynamic_slice_in_dim(key_live, half * span, span, 1)
+    mine = (jnp.arange(halves) == half).reshape(halves, 1, 1, 1, 1)
+    qkv = projected.reshape(frame_count, 3, HEADS, HDIM).transpose(2, 0, 1, 3)
+    got = lax.all_to_all(jnp.tile(qkv, (halves, 1, 1, 1)), "tm", 0, 0, tiled=True)
+    got = got.reshape(total, 3, HDIM)
+    q_all, k_all, v_all = got[:, 0], got[:, 1], got[:, 2]
+    q_half = lax.dynamic_slice_in_dim(q_all, half * span, span, 0)
+    scores = lax.dot_general(q_half, k_all, contract_last, preferred_element_type=jnp.float32)
+    scores = jnp.where(key_live, scores * scaling, negative)
+    top = jnp.max(scores, axis=-1)
+    weights = jnp.where(key_live, jnp.exp(scores - top[:, None]), 0.0)
+    summed = jnp.sum(weights, axis=-1)
+    acc = jnp.dot(weights.astype(jnp.bfloat16), v_all, preferred_element_type=jnp.float32)
+    a_half = (acc / summed[:, None]).astype(jnp.bfloat16)
+    lse_half = top + jnp.log(summed)
+
+    def to_frames(rows):
+        blocks = rows.reshape((1, HEADS, frame_count) + rows.shape[1:])
+        placed = jnp.where(mine.reshape((halves,) + (1,) * (blocks.ndim - 1)), blocks, 0)
+        placed = placed.reshape((tm_count, frame_count) + rows.shape[1:])
+        back = lax.all_to_all(placed, "tm", 0, 0, tiled=True)
+        back = back.reshape((halves, HEADS, frame_count) + rows.shape[1:])
+        return jnp.sum(back.astype(jnp.float32), axis=0).astype(rows.dtype)
+
+    attended = to_frames(a_half).transpose(1, 0, 2).reshape(frame_count, width)
     w_out = w_proj[:, 3 * width :]
     mixed = inputs + lax.dot_general(
         attended, w_out, contract_last, preferred_element_type=jnp.float32
@@ -216,37 +226,44 @@
     grad_attended = jnp.dot(grad_resid_low, w_out, preferred_element_type=jnp.float32).astype(
         jnp.bfloat16
     )
-    grad_heads = split_heads(grad_attended)
-    delta = jnp.sum(
-        grad_heads.astype(jnp.float32) * split_heads(attended).astype(jnp.float32), axis=-1
-    )
-    zero_heads = jnp.zeros((frame_count, HEADS, HDIM), jnp.float32)
-    back_start = (zero_heads,)
-    advance_back = query_side(query_heads, grad_heads, logsum, delta, length, scaling)
-    back_state = over_blocks(
-        advance_back,
-        back_start,
-        (keys_all, values_all),
-    )
-    own_living = valid[:, 0][None, None, :]
-    advance_keys = key_side(split_heads(key_rows), split_heads(value_rows), own_living, scaling)
-    rows_all = lax.all_gather(
-        jnp.concatenate([queries, grad_attended], axis=1), "tm", axis=0, tiled=True
-    )
-    stats_all = lax.all_gather(jnp.concatenate([logsum, delta], axis=1), "tm", axis=0, tiled=True)
-    grad_keys, grad_values = over_blocks(
-        advance_keys,
-        (zero_heads, zero_heads),
-        (rows_all[:, :width], rows_all[:, width:], stats_all[:, :HEADS], stats_all[:, HEADS:]),
-    )
-    grad_qkv = jnp.concatenate(
-        [
-            back_state[0].reshape(frame_count, width).astype(jnp.bfloat16),
-            grad_keys.reshape(frame_count, width).astype(jnp.bfloat16),
-            grad_values.reshape(frame_count, width).astype(jnp.bfloat16),
-        ],
-        axis=1,
-    )
+    send_grad = grad_attended.reshape(frame_count, HEADS, HDIM).transpose(1, 0, 2)
+    da_all = lax.all_to_all(jnp.tile(send_grad, (halves, 1, 1)), "tm", 0, 0, tiled=True)
+    da_all = da_all.reshape(total, HDIM)
+    da_half = lax.dynamic_slice_in_dim(da_all, half * span, span, 0)
+    delta_half = jnp.sum(da_half.astype(jnp.float32) * a_half.astype(jnp.float32), axis=-1)
+    stats_half = jnp.stack([lse_half, delta_half], axis=0)
+    partner = lax.ppermute(
+        stats_half, "tm", [(i, (i + HEADS) % tm_count) for i in range(tm_count)]
+    )
+    stats_all = jnp.where(
+        half == 0,
+        jnp.concatenate([stats_half, partner], axis=1),
+        jnp.concatenate([partner, stats_half], axis=1),
+    )
+    lse_all = stats_all[0][:, None]
+    delta_all = stats_all[1][:, None]
+    scores = lax.dot_general(q_half, k_all, contract_last, preferred_element_type=jnp.float32)
+    scores = jnp.where(key_live, scores * scaling, negative)
+    probs = jnp.where(key_live, jnp.exp(scores - lse_half[:, None]), 0.0)
+    dprobs = lax.dot_general(da_half, v_all, contract_last, preferred_element_type=jnp.float32)
+    grad_scores = (probs * (dprobs - delta_half[:, None])).astype(jnp.bfloat16)
+    grad_q = jnp.dot(grad_scores, k_all, preferred_element_type=jnp.float32) * scaling
+    k_half = lax.dynamic_slice_in_dim(k_all, half * span, span, 0)
+    v_half = lax.dynamic_slice_in_dim(v_all, half * span, span, 0)
+    scores = lax.dot_general(q_all, k_half, contract_last, preferred_element_type=jnp.float32)
+    scores = jnp.where(half_live, scores * scaling, negative)
+    probs = jnp.where(half_live, jnp.exp(scores - lse_all), 0.0)
+    dprobs = lax.dot_general(da_all, v_half, contract_last, preferred_element_type=jnp.float32)
+    grad_scores = (probs * (dprobs - delta_all)).astype(jnp.bfloat16)
+    grad_k = (
+        lax.dot_general(grad_scores, q_all, contract_first, preferred_element_type=jnp.float32)
+        * scaling
+    )
+    grad_v = lax.dot_general(
+        probs.astype(jnp.bfloat16), da_all, contract_first, preferred_element_type=jnp.float32
+    )
+    grad_rows = jnp.stack([grad_q, grad_k, grad_v], axis=1).astype(jnp.bfloat16)
+    grad_qkv = to_frames(grad_rows).transpose(1, 2, 0, 3).reshape(frame_count, 3 * width)
     back_normed = lax.dot_general(
         grad_qkv, w_proj[:, : 3 * width], contract_last, preferred_element_type=jnp.float32
     )

time: 434 us -> 319 us (0.74)
  blocking collectives: 132 us -> 0 us
  waiting for transfers between devices: 88.6 us -> 166 us
  local copies, waits for them, and re-layouts: 87.7 us -> 14.8 us
  starting transfers between devices: 17.2 us -> 65.8 us
  matrix products: 57.4 us -> 39 us
  between operations: 16.1 us -> 2.4 us
  other arithmetic: 32.9 us -> 27.3 us
    all_to_all x0 -> x5, waiting for transfers between devices: none -> 142 us  [the longest x1 100 us: per_device(): lax.all_to_all(packed, axes, 0, 0, tiled=True).astype(jnp.float32).sum(0)]
    all_to_all x1 -> x0, blocking collectives: 112 us -> none  [per_device(): lax.all_to_all(packed, axes, 0, 0, tiled=True).astype(jnp.float32).sum(0)]
    all_gather x2 -> x0, waiting for transfers between devices: 63.3 us -> none  [the longest x1 63.3 us: per_device(): lax.all_gather(projected[:, width:], 'tm', axis=0, tiled=True)]
    all_to_all x0 -> x5, starting transfers between devices: none -> 47.5 us  [the longest x2 19 us: to_frames(): back = lax.all_to_all(placed, 'tm', 0, 0, tiled=True)]
    another operation x31, local copies, waits for them, and re-layouts: 38 us -> 0.16 us  [per_device(): jnp.stack([jnp.sum(grad_conv_in * padded[shift_index:shift_index + frame_...]
    all_gather x1 -> x0, blocking collectives: 20.2 us -> none  [per_device(): lax.all_gather(jnp.concatenate([logsum, delta], axis=1), 'tm', axis=0, ti...]
    dot_general x14 -> x6, matrix products: 44.8 us -> 27.5 us  [the longest x1 7.11 us: per_device(): lax.dot_general(grad_scores, q_all, contract_first, preferred_element_typ...]
    slice x8 -> x2, local copies, waits for them, and re-layouts: 14.5 us -> 0.78 us  [the longest x1 0.77 us: per_device(): q_all, k_all, v_all = (got[:, 0], got[:, 1], got[:, 2])]
  transfers between devices with their start and end apart: 7 -> 11, of which waited for: 4 -> 8; matrix products, arithmetic and copies ran while one was open for 18% -> 3% of each run, Pallas kernels for 0% -> 0%
where the time goes in v2:
time: 319 us; the launch traced here: 315 us
  waiting for transfers between devices  166 us (52%)
  starting transfers between devices  65.8 us (21%)
  matrix products  39 us (12%)
  other arithmetic  27.3 us (9%)
  local copies, waits for them, and re-layouts  14.8 us (5%)
    all_to_all x1, waiting for transfers between devices, per_device(): lax.all_to_all(packed, axes, 0, 0, tiled=True).astype(jnp.float32).sum(0)  100 us
    all_to_all x2, waiting for transfers between devices, to_frames(): back = lax.all_to_all(placed, 'tm', 0, 0, tiled=True)  20.2 us
    all_to_all x2, starting transfers between devices, to_frames(): back = lax.all_to_all(placed, 'tm', 0, 0, tiled=True)  19 us
    all_to_all x1, waiting for transfers between devices, per_device(): lax.all_to_all(jnp.broadcast_to(small_part, (devices, small_part.shape[1]...  15 us
    all_to_all x1, waiting for transfers between devices, per_device(): lax.all_to_all(jnp.tile(qkv, (halves, 1, 1, 1)), 'tm', 0, 0, tiled=True)  12.7 us
    all_to_all x1, starting transfers between devices, per_device(): lax.all_to_all(packed, axes, 0, 0, tiled=True).astype(jnp.float32).sum(0)  12.4 us
    all_to_all x1, waiting for transfers between devices, per_device(): lax.all_to_all(jnp.tile(send_grad, (halves, 1, 1)), 'tm', 0, 0, tiled=True)  8.82 us
    ppermute x2, waiting for transfers between devices, padded_2(): after = lax.ppermute(first, axis, down)  8.81 us
  transfers between devices with their start and end apart: 11, of which 8 were waited for; matrix products, arithmetic and copies ran while one was open for 3% of the time, Pallas kernels for 0%

profile of v2, /device:TPU:1, one launch (start us, length us, event | category | flops | bytes accessed | tf_op | source)
XLA Modules:
  0.0 315.1 jit_solution(15232076435269318697)
XLA Ops:
  0.6 1.1 convert_reduce_fusion.1
  1.7 1.2 fusion.42
  2.9 0.6 copy-done.18
  3.5 0.5 copy-done.9
  4.0 2.6 fusion.10
  6.9 1.1 tile.8
  8.0 8.4 %all-to-all-start = ((bf16[16,128,3,64]{1,3,2,0:T(8,128)(2,1)}), bf16[16,128,3,64]{1,3,2,0:T(8,128)(2,1)S(1)}, u32[]{:S(2)}, u32[]{:S(2)}) async-start(bf16[16,128,3,64]{1,3,2,0:T(8,128)(2,1)} %bitcast.7), calls=%async_computation | async-start | bytes 1572864 | tf_op jit(solution)/shard_map/all_to_all | solution.py:169
  17.3 12.7 %all-to-all-done = bf16[16,128,3,64]{1,3,2,0:T(8,128)(2,1)S(1)} async-done(((bf16[16,128,3,64]{1,3,2,0:T(8,128)(2,1)}), bf16[16,128,3,64]{1,3,2,0:T(8,128)(2,1)S(1)}, u32[]{:S(2)}, u32[]{:S(2)}) %all-to-all-start) | async-done | bytes 786464 | tf_op jit(solution)/shard_map/all_to_all | solution.py:169
  30.1 0.8 fusion.134
  30.9 1.4 fusion.3
  32.3 2.5 fusion
  34.8 1.9 fusion.27
  36.8 0.8 bitcast_select_fusion.1
  37.6 5.0 %all-to-all-start.1 = ((bf16[16,128,64]{1,2,0:T(8,128)(2,1)}), bf16[16,128,64]{1,2,0:T(8,128)(2,1)S(1)}, u32[]{:S(2)}, u32[]{:S(2)}) async-start(bf16[16,128,64]{1,2,0:T(8,128)(2,1)} %bitcast_select_fusion.1), calls=%async_computation.1 | async-start | bytes 524288 | tf_op jit(solution)/shard_map/all_to_all | solution.py:186
  42.7 8.9 %all-to-all-done.1 = bf16[16,128,64]{1,2,0:T(8,128)(2,1)S(1)} async-done(((bf16[16,128,64]{1,2,0:T(8,128)(2,1)}), bf16[16,128,64]{1,2,0:T(8,128)(2,1)S(1)}, u32[]{:S(2)}, u32[]{:S(2)}) %all-to-all-start.1) | async-done | bytes 262176 | tf_op jit(solution)/shard_map/all_to_all | solution.py:186
  51.6 1.8 fusion.140
  53.6 0.2 select_convert_fusion
  53.8 2.5 collective-permute-start
  56.4 1.9 collective-permute-start.1
  58.4 4.8 %collective-permute-done.1 = bf16[15,1024]{1,0:T(8,128)(2,1)S(1)} collective-permute-done((bf16[15,1024]{1,0:T(8,128)(2,1)S(1)}, bf16[15,1024]{1,0:T(8,128)(2,1)S(1)}, u32[]{:S(2)}, u32[]{:S(2)}) %collective-permute-start.1) | collective-permute-done | bytes 30752 | tf_op jit(solution)/shard_map/ppermute | solution.py:25
  63.2 4.2 %multiply_reduce_fusion.1 = (bf16[1024]{0:T(1024)(128)(2,1)S(1)}, bf16[1024]{0:T(1024)(128)(2,1)S(1)}, bf16[1024]{0:T(1024)(128)(2,1)S(1)}, bf16[1024]{0:T(1024)...) fusion(f32[158,1024]{1,0:T(8,128)S(1)} %maximum_convert_fusion,, ...), kind=kLoop, calls=%fused_computation.124 | loop fusion | flops 13875200 | bytes 17203200 | tf_op jit(solution)/shard_map/reduce_sum | solution.py:210
  67.4 0.8 multiply_reduce_fusion.19
  68.2 1.9 collective-permute-start.2
  70.2 2.7 collective-permute-start.3
  72.8 4.1 %collective-permute-done.3 = bf16[15,1024]{1,0:T(8,128)(2,1)S(1)} collective-permute-done((bf16[15,1024]{1,0:T(8,128)(2,1)S(1)}, bf16[15,1024]{1,0:T(8,128)(2,1)S(1)}, u32[]{:S(2)}, u32[]{:S(2)}) %collective-permute-start.3) | collective-permute-done | bytes 30752 | tf_op jit(solution)/shard_map/ppermute | solution.py:25
  77.0 3.6 %multiply_reduce_fusion = (bf16[1024]{0:T(1024)(128)(2,1)S(1)}, f32[128]{0:T(128)S(1)}, f32[128,1024]{1,0:T(8,128)S(1)}) fusion(f32[128,1024]{1,0:T(8,128)S(1)} %get-tuple-element.87, f32[128]{0:T(128)S(1)} %fusion.113, f32[128]{0:T(128)S(1)} %broadcast_multiply_fusion, f32[1024]{0:T(1024)S(1)} %copy-done.4, f32[158,1024]{1,0:T(8,128)S(1)} %maximum_convert_fusion.1, ...), kind=kLoop, calls=%fused_computation.123 | loop fusion | flops 9042816 | bytes 17436288 | tf_op jit(solution)/shard_map/transpose(jvp())/reduce_sum | solution.py:33
  80.6 0.3 fusion.132
  81.0 1.5 convolution_convert_fusion.3
  82.7 0.8 tile.20
  83.4 7.7 %all-to-all-start.2 = ((bf16[16,128,64]{1,2,0:T(8,128)(2,1)}), bf16[16,128,64]{1,2,0:T(8,128)(2,1)S(1)}, u32[]{:S(2)}, u32[]{:S(2)}) async-start(bf16[16,128,64]{1,2,0:T(8,128)(2,1)} %bitcast.47), calls=%async_computation.2 | async-start | bytes 524288 | tf_op jit(solution)/shard_map/all_to_all | solution.py:230
  91.2 8.8 %all-to-all-done.2 = bf16[16,128,64]{1,2,0:T(8,128)(2,1)S(1)} async-done(((bf16[16,128,64]{1,2,0:T(8,128)(2,1)}), bf16[16,128,64]{1,2,0:T(8,128)(2,1)S(1)}, u32[]{:S(2)}, u32[]{:S(2)}) %all-to-all-start.2) | async-done | bytes 262176 | tf_op jit(solution)/shard_map/all_to_all | solution.py:230
  100.1 0.6 pad_maximum_fusion.2
  100.7 1.1 collective-permute-start.4
  101.8 6.9 %fusion.23 = bf16[8,8,8,128]{3,1,2,0:T(8,128)(2,1)S(1)} fusion(f32[1024,2048]{1,0:T(8,128)} %copy-done, f32[1024]{0:T(1024)S(1)} %multiply_reduce_fusion.34, f32[1024]{0:T(1024)S(1)} %log_add_fusion, pred[2048]{0:T(1024)(128)(4,1)S(1)} %iota_compare_fusion, bf16[2048,64]{0,1:T(8,128)(2,1)S(1)} %copy_bitcast_fusion.1, s32[]{:T(128)S(6)} %select_n.61, ...), kind=kOutput, calls=%fused_computation.32 | convolution fusion | flops 551682048 | bytes 9185284 | tf_op jit(solution)/shard_map/dot_general | solution.py:250
  109.0 0.8 maximum_select_fusion
  109.9 6.7 %fusion.2 = (bf16[2048,1024]{0,1:T(8,128)(2,1)}, f32[2048,1024]{0,1:T(8,128)}) fusion(f32[2048]{0:T(1024)S(1)} %bitcast.272, pred[1024]{0:T(1024)(128)(4,1)S(1)} %dynamic-slice.6, bf16[2048,1,64]{0,2,1:T(8,128)(2,1)} %get-tuple-element.44, s32[]{:T(128)S(6)} %select_n.61, bf16[2048,3,64]{0,2,1:T(8,128)(2,1)S(1)} %copy_bitcast_fusion), kind=kOutput, calls=%fused_computation.8 | convolution fusion | flops 278921216 | bytes 12985348 | tf_op jit(solution)/shard_map/dot_general | solution.py:253
  116.5 7.1 %fusion.22 = bf16[8,8,8,128]{3,1,2,0:T(8,128)(2,1)S(1)} fusion(f32[2048,1024]{0,1:T(8,128)} %get-tuple-element.89, f32[2048]{0:T(1024)S(1)} %bitcast.271, f32[2048]{0:T(1024)S(1)} %bitcast.273, pred[1024]{0:T(1024)(128)(4,1)} %copy-done.17, bf16[2048,1,64]{0,2,1:T(8,128)(2,1)S(1)} %get-tuple-element.43, s32[]{:T(128)S(6)} %select_n.61, ...), kind=kOutput, calls=%fused_computation.31 | convolution fusion | flops 551682048 | bytes 9192452 | tf_op jit(solution)/shard_map/dot_general | solution.py:259
  123.7 3.6 %fusion.21 = bf16[8,128,1,64]{1,3,0,2:T(8,128)(2,1)S(1)} fusion(bf16[8,128,2048]{2,1,0:T(8,128)(2,1)} %bitcast.190, bf16[2048,64,1]{0,1,2:T(8,128)(2,1)S(1)} %reshape.259), kind=kOutput, calls=%fused_computation.30 | convolution fusion | flops 268500992 | bytes 4587520 | tf_op jit(solution)/shard_map/dot_general | solution.py:262
  127.3 1.2 bitcast_select_fusion
  128.5 14.0 %all-to-all-start.3 = ((bf16[16,128,3,64]{1,3,2,0:T(8,128)(2,1)}), bf16[16,128,3,64]{1,3,2,0:T(8,128)(2,1)S(1)}, u32[]{:S(2)}, u32[]{:S(2)}) async-start(bf16[16,128,3,64]{1,3,2,0:T(8,128)(2,1)} %bitcast_select_fusion), calls=%async_computation.3 | async-start | bytes 1572864 | tf_op jit(solution)/shard_map/all_to_all | solution.py:186
  142.7 0.8 copy.63
  144.1 0.4 convolution_convert_fusion.1
  144.6 11.3 %all-to-all-done.3 = bf16[16,128,3,64]{1,3,2,0:T(8,128)(2,1)S(1)} async-done(((bf16[16,128,3,64]{1,3,2,0:T(8,128)(2,1)}), bf16[16,128,3,64]{1,3,2,0:T(8,128)(2,1)S(1)}, u32[]{:S(2)}, u32[]{:S(2)}) %all-to-all-start.3) | async-done | bytes 786464 | tf_op jit(solution)/shard_map/all_to_all | solution.py:186
  155.9 1.0 reduce_sum.469
  156.9 1.0 copy.62
  157.9 3.1 fusion.43
  161.1 0.3 fusion.40
  161.4 0.3 concatenate.32
  161.7 0.6 concatenate.33
  162.3 1.9 convolution_convert_fusion
  164.3 0.4 pad_maximum_fusion
  164.7 5.5 %copy.70 = bf16[256,4,2081]{2,1,0:T(4,128)(2,1)} copy(bf16[256,4,2081]{2,0,1:T(8,128)(2,1)S(1)} %pad_maximum_fusion) | data formatting | bytes 8523776 | tf_op jit(solution)/shard_map/concatenate | solution.py:286
  170.2 12.4 %all-to-all-start.4 = ((bf16[256,4,2081]{2,1,0:T(4,128)(2,1)}), bf16[256,4,2081]{2,1,0:T(4,128)(2,1)}, u32[]{:S(2)}, u32[]{:S(2)}) async-start(bf16[256,4,2081]{2,1,0:T(4,128)(2,1)} %copy.70), calls=%async_computation.4 | async-start | bytes 8912896 | tf_op jit(solution)/shard_map/all_to_all | solution.py:290
  182.6 1.0 fusion.79
  183.6 100.2 %all-to-all-done.4 = bf16[256,4,2081]{2,1,0:T(4,128)(2,1)} async-done(((bf16[256,4,2081]{2,1,0:T(4,128)(2,1)}), bf16[256,4,2081]{2,1,0:T(4,128)(2,1)}, u32[]{:S(2)}, u32[]{:S(2)}) %all-to-all-start.4) | async-done | bytes 4261920 | tf_op jit(solution)/shard_map/all_to_all | solution.py:290
  283.8 4.1 %convert_reduce_fusion = f32[4,2081]{1,0:T(4,128)S(1)} fusion(bf16[256,4,2081]{2,1,0:T(4,128)(2,1)} %all-to-all-done.4), kind=kLoop, calls=%fused_computation | loop fusion | flops 4253564 | bytes 4295184 | tf_op jit(solution)/shard_map/reduce_sum | solution.py:290
  288.0 0.8 broadcast_in_dim.182
  288.8 8.3 %all-to-all-start.5 = ((f32[256,1,132]{2,1,0:T(1,128)}), f32[256,1,132]{2,1,0:T(1,128)S(1)}, u32[]{:S(2)}, u32[]{:S(2)}) async-start(f32[256,1,132]{2,1,0:T(1,128)} %broadcast_in_dim.182), calls=%async_computation.5 | async-start | bytes 524288 | tf_op jit(solution)/shard_map/all_to_all | solution.py:293
  297.1 0.6 slice_multiply_fusion.32
  297.7 15.0 %all-to-all-done.5 = f32[256,1,132]{2,1,0:T(1,128)S(1)} async-done(((f32[256,1,132]{2,1,0:T(1,128)}), f32[256,1,132]{2,1,0:T(1,128)S(1)}, u32[]{:S(2)}, u32[]{:S(2)}) %all-to-all-start.5) | async-done | bytes 135200 | tf_op jit(solution)/shard_map/all_to_all | solution.py:293
  312.8 0.6 reduce.3
  313.4 0.2 slice.497
  313.7 0.7 slice_multiply_fusion.31
  314.3 0.6 slice_multiply_fusion.33
  (117 shorter events, 2.7 us)
Async XLA Ops:
  1.7 1.2 copy-start.6
  2.9 0.6 copy-start.18
  3.5 0.5 copy-start.9
  8.0 22.0 %all-to-all-start = ((bf16[16,128,3,64]{1,3,2,0:T(8,128)(2,1)}), bf16[16,128,3,64]{1,3,2,0:T(8,128)(2,1)S(1)}, u32[]{:S(2)}, u32[]{:S(2)}) async-start(bf16[16,128,3,64]{1,3,2,0:T(8,128)(2,1)} %bitcast.7), calls=%async_computation | async-start | bytes 1572864 | tf_op jit(solution)/shard_map/all_to_all | solution.py:169
  17.3 19.5 %copy-start.13 = (pred[16]{0:T(512)(128)(4,1)}, pred[16]{0:T(512)(128)(4,1)S(1)}, u32[]{:S(2)}) copy-start(pred[16]{0:T(512)(128)(4,1)S(1)} %broadcast_in_dim.158) | copy-start | bytes 52
  32.3 4.4 %copy-start = (f32[1024,2048]{1,0:T(8,128)}, f32[1024,2048]{1,0:T(8,128)S(1)}, u32[]{:S(2)}) copy-start(f32[1024,2048]{1,0:T(8,128)S(1)} %get-tuple-element.85) | copy-start | bytes 25165828
  34.8 7.8 %copy-start.3 = (bf16[31,1024]{1,0:T(8,128)(2,1)S(1)}, bf16[31,1024]{1,0:T(8,128)(2,1)}, u32[]{:S(2)}) copy-start(bf16[31,1024]{1,0:T(8,128)(2,1)} %param.13) | copy-start | bytes 190468
  34.8 16.8 %copy-start.1 = (bf16[1,128,1024]{2,1,0:T(8,128)(2,1)S(1)}, bf16[1,128,1024]{2,1,0:T(8,128)(2,1)}, u32[]{:S(2)}) copy-start(bf16[1,128,1024]{2,1,0:T(8,128)(2,1)} %param.7) | copy-start | bytes 786436
  34.8 18.8 %copy-start.4 = (f32[1024]{0:T(1024)S(1)}, f32[1024]{0:T(1024)}, u32[]{:S(2)}) copy-start(f32[1024]{0:T(1024)} %param.12) | copy-start | bytes 12292
  34.8 28.4 %copy-start.2 = (bf16[1,128,1024]{2,1,0:T(8,128)(2,1)S(1)}, bf16[1,128,1024]{2,1,0:T(8,128)(2,1)}, u32[]{:S(2)}) copy-start(bf16[1,128,1024]{2,1,0:T(8,128)(2,1)} %param.8) | copy-start | bytes 786436
  37.6 13.9 %all-to-all-start.1 = ((bf16[16,128,64]{1,2,0:T(8,128)(2,1)}), bf16[16,128,64]{1,2,0:T(8,128)(2,1)S(1)}, u32[]{:S(2)}, u32[]{:S(2)}) async-start(bf16[16,128,64]{1,2,0:T(8,128)(2,1)} %bitcast_select_fusion.1), calls=%async_computation.1 | async-start | bytes 524288 | tf_op jit(solution)/shard_map/all_to_all | solution.py:186
  53.8 4.5 %collective-permute-start = (bf16[15,1024]{1,0:T(8,128)(2,1)S(1)}, bf16[15,1024]{1,0:T(8,128)(2,1)S(1)}, u32[]{:S(2)}, u32[]{:S(2)}) collective-permute-start(bf16[15,1024]{1,0:T(8,128)(2,1)S(1)} %get-tuple-element.49), channel_id=1, source_target_pairs={{0,1},{1,2},{2,3},{3,4},{4,5},{5,6},{6,7},{7,8},{8,9},{9,10},{10,1... | collective-permute-start | bytes 92168 | tf_op jit(solution)/shard_map/ppermute | solution.py:24
  56.4 6.7 %collective-permute-start.1 = (bf16[15,1024]{1,0:T(8,128)(2,1)S(1)}, bf16[15,1024]{1,0:T(8,128)(2,1)S(1)}, u32[]{:S(2)}, u32[]{:S(2)}) collective-permute-start(bf16[15,1024]{1,0:T(8,128)(2,1)S(1)} %get-tuple-element.50), channel_id=1, source_target_pairs={{1,0},{2,1},{3,2},{4,3},{5,4},{6,5},{7,6},{8,7},{9,8},{10,9},{11,1... | collective-permute-start | bytes 92168 | tf_op jit(solution)/shard_map/ppermute | solution.py:25
  68.2 4.6 %collective-permute-start.2 = (bf16[15,1024]{1,0:T(8,128)(2,1)S(1)}, bf16[15,1024]{1,0:T(8,128)(2,1)S(1)}, u32[]{:S(2)}, u32[]{:S(2)}) collective-permute-start(bf16[15,1024]{1,0:T(8,128)(2,1)S(1)} %get-tuple-element.47), channel_id=1, source_target_pairs={{0,1},{1,2},{2,3},{3,4},{4,5},{5,6},{6,7},{7,8},{8,9},{9,10},{10,1... | collective-permute-start | bytes 92168 | tf_op jit(solution)/shard_map/ppermute | solution.py:24
  70.2 6.7 %collective-permute-start.3 = (bf16[15,1024]{1,0:T(8,128)(2,1)S(1)}, bf16[15,1024]{1,0:T(8,128)(2,1)S(1)}, u32[]{:S(2)}, u32[]{:S(2)}) collective-permute-start(bf16[15,1024]{1,0:T(8,128)(2,1)S(1)} %get-tuple-element.48), channel_id=1, source_target_pairs={{1,0},{2,1},{3,2},{4,3},{5,4},{6,5},{7,6},{8,7},{9,8},{10,9},{11,1... | collective-permute-start | bytes 92168 | tf_op jit(solution)/shard_map/ppermute | solution.py:25
  80.8 10.3 %copy-start.15 = (f32[128]{0:T(128)}, f32[128]{0:T(128)S(1)}, u32[]{:S(2)}) copy-start(f32[128]{0:T(128)S(1)} %negate_multiply_fusion.1) | copy-start | bytes 1540
  83.4 16.6 %all-to-all-start.2 = ((bf16[16,128,64]{1,2,0:T(8,128)(2,1)}), bf16[16,128,64]{1,2,0:T(8,128)(2,1)S(1)}, u32[]{:S(2)}, u32[]{:S(2)}) async-start(bf16[16,128,64]{1,2,0:T(8,128)(2,1)} %bitcast.47), calls=%async_computation.2 | async-start | bytes 524288 | tf_op jit(solution)/shard_map/all_to_all | solution.py:230
  91.2 18.7 %copy-start.17 = (pred[1024]{0:T(1024)(128)(4,1)}, pred[1024]{0:T(1024)(128)(4,1)S(1)}, u32[]{:S(2)}) copy-start(pred[1024]{0:T(1024)(128)(4,1)S(1)} %dynamic-slice.6) | copy-start | bytes 3076
  100.7 8.3 %collective-permute-start.4 = (f32[2,1024]{1,0:T(2,128)}, f32[2,1024]{1,0:T(2,128)}, u32[]{:S(2)}, u32[]{:S(2)}) collective-permute-start(f32[2,1024]{1,0:T(2,128)} %pad_maximum_fusion.2), channel_id=1, source_target_pairs={{0,8},{1,9},{2,10},{3,11},{4,12},{5,13},{6,14},{7,15},{8,0},{9,1},... | collective-permute-start | bytes 24584 | tf_op jit(solution)/shard_map/ppermute | solution.py:235
  116.5 10.8 %copy-start.14 = (pred[16]{0:T(512)(128)(4,1)S(1)}, pred[16]{0:T(512)(128)(4,1)}, u32[]{:S(2)}) copy-start(pred[16]{0:T(512)(128)(4,1)} %copy-done.13) | copy-start | bytes 52
  116.5 25.9 %copy-start.5 = (f32[1024]{0:T(1024)S(1)}, f32[1024]{0:T(1024)}, u32[]{:S(2)}) copy-start(f32[1024]{0:T(1024)} %param.11) | copy-start | bytes 12292
  116.5 25.9 %copy-start.7 = (f32[128]{0:T(128)S(1)}, f32[128]{0:T(128)}, u32[]{:S(2)}) copy-start(f32[128]{0:T(128)} %copy-done.6) | copy-start | bytes 1540
  116.5 26.0 %copy-start.10 = (f32[128]{0:T(128)S(1)}, f32[128]{0:T(128)}, u32[]{:S(2)}) copy-start(f32[128]{0:T(128)} %copy-done.9) | copy-start | bytes 1540
  123.7 37.4 %copy-start.19 = (f32[128]{0:T(128)S(1)}, f32[128]{0:T(128)}, u32[]{:S(2)}) copy-start(f32[128]{0:T(128)} %copy-done.18) | copy-start | bytes 1540
  123.7 37.4 %copy-start.11 = (f32[128]{0:T(128)S(1)}, f32[128]{0:T(128)}, u32[]{:S(2)}) copy-start(f32[128]{0:T(128)} %copy-done.9) | copy-start | bytes 1540
  128.5 27.5 %all-to-all-start.3 = ((bf16[16,128,3,64]{1,3,2,0:T(8,128)(2,1)}), bf16[16,128,3,64]{1,3,2,0:T(8,128)(2,1)S(1)}, u32[]{:S(2)}, u32[]{:S(2)}) async-start(bf16[16,128,3,64]{1,3,2,0:T(8,128)(2,1)} %bitcast_select_fusion), calls=%async_computation.3 | async-start | bytes 1572864 | tf_op jit(solution)/shard_map/all_to_all | solution.py:186
  164.7 17.9 %copy-start.8 = (f32[128]{0:T(128)S(1)}, f32[128]{0:T(128)}, u32[]{:S(2)}) copy-start(f32[128]{0:T(128)} %copy-done.6) | copy-start | bytes 1540
  164.7 17.9 %copy-start.12 = (f32[128]{0:T(128)S(1)}, f32[128]{0:T(128)}, u32[]{:S(2)}) copy-start(f32[128]{0:T(128)} %copy-done.9) | copy-start | bytes 1540
  164.7 17.9 %copy-start.16 = (f32[128]{0:T(128)S(1)}, f32[128]{0:T(128)}, u32[]{:S(2)}) copy-start(f32[128]{0:T(128)} %copy-done.15) | copy-start | bytes 1540
  170.2 113.6 %all-to-all-start.4 = ((bf16[256,4,2081]{2,1,0:T(4,128)(2,1)}), bf16[256,4,2081]{2,1,0:T(4,128)(2,1)}, u32[]{:S(2)}, u32[]{:S(2)}) async-start(bf16[256,4,2081]{2,1,0:T(4,128)(2,1)} %copy.70), calls=%async_computation.4 | async-start | bytes 8912896 | tf_op jit(solution)/shard_map/all_to_all | solution.py:290
  288.8 23.9 %all-to-all-start.5 = ((f32[256,1,132]{2,1,0:T(1,128)}), f32[256,1,132]{2,1,0:T(1,128)S(1)}, u32[]{:S(2)}, u32[]{:S(2)}) async-start(f32[256,1,132]{2,1,0:T(1,128)} %broadcast_in_dim.182), calls=%async_computation.5 | async-start | bytes 524288 | tf_op jit(solution)/shard_map/all_to_all | solution.py:293

commit v3 on v2

--- a/solution.py
+++ b/solution.py
@@ -286,8 +286,12 @@
     packed = jnp.concatenate(
         [inner_part, outer_part, small_flat.reshape(rows, small_width)], axis=1
     )
-    packed = packed.reshape(devices, rows // devices, packed.shape[1]).astype(jnp.bfloat16)
-    reduced = lax.all_to_all(packed, axes, 0, 0, tiled=True).astype(jnp.float32).sum(0)
+    outer_count = lax.axis_size("dp")
+    packed = packed.reshape(outer_count, tm_count, rows // devices, packed.shape[1])
+    packed = packed.transpose(1, 0, 2, 3).astype(jnp.bfloat16)
+    reduced = lax.all_to_all(packed, "tm", 0, 0, tiled=True).astype(jnp.float32).sum(0)
+    reduced = lax.all_to_all(reduced.astype(jnp.bfloat16), "dp", 0, 0, tiled=True)
+    reduced = reduced.astype(jnp.float32).sum(0)
     grad_proj = reduced[:, : 4 * width]
     small_part = reduced[:, 4 * width :].reshape(1, -1)
     small_all = lax.all_to_all(

time: 319 us -> 267 us (0.84)
  waiting for transfers between devices: 166 us -> 74.1 us
  blocking collectives: 0 us -> 58.7 us
  starting transfers between devices: 65.8 us -> 52.3 us
  local copies, waits for them, and re-layouts: 14.8 us -> 11.4 us
    all_to_all x1, waiting for transfers between devices: 100 us -> 8.27 us  [per_device(): lax.all_to_all(reduced.astype(jnp.bfloat16), 'dp', 0, 0, tiled=True)]
    all_to_all x0 -> x1, blocking collectives: none -> 58.7 us  [per_device(): lax.all_to_all(packed, 'tm', 0, 0, tiled=True).astype(jnp.float32).sum(0)]
    all_to_all x2, starting transfers between devices: 19 us -> 9.2 us  [to_frames(): back = lax.all_to_all(placed, 'tm', 0, 0, tiled=True)]
    concatenate x3 -> x2, local copies, waits for them, and re-layouts: 6.15 us -> 0.62 us  [per_device(): jnp.concatenate([inner_part, outer_part, small_flat.reshape(rows, small_w...]
    all_to_all x1, starting transfers between devices: 12.4 us -> 8.4 us  [per_device(): lax.all_to_all(reduced.astype(jnp.bfloat16), 'dp', 0, 0, tiled=True)]
  transfers between devices with their start and end apart: 11 -> 11, of which waited for: 8 -> 8; matrix products, arithmetic and copies ran while one was open for 3% -> 4% of each run, Pallas kernels for 0% -> 0%
where the time goes in v3:
time: 267 us; the launch traced here: 266 us
  waiting for transfers between devices  74.1 us (28%)
  blocking collectives  58.7 us (22%)
  starting transfers between devices  52.3 us (20%)
  matrix products  39 us (15%)
  other arithmetic  28.4 us (11%)
  local copies, waits for them, and re-layouts  11.4 us (4%)
    all_to_all x1, blocking collectives, per_device(): lax.all_to_all(packed, 'tm', 0, 0, tiled=True).astype(jnp.float32).sum(0)  58.7 us
    all_to_all x2, waiting for transfers between devices, to_frames(): back = lax.all_to_all(placed, 'tm', 0, 0, tiled=True)  20.3 us
    all_to_all x1, waiting for transfers between devices, per_device(): lax.all_to_all(jnp.broadcast_to(small_part, (devices, small_part.shape[1]...  15 us
    all_to_all x1, waiting for transfers between devices, per_device(): lax.all_to_all(jnp.tile(qkv, (halves, 1, 1, 1)), 'tm', 0, 0, tiled=True)  12.7 us
    all_to_all x2, starting transfers between devices, to_frames(): back = lax.all_to_all(placed, 'tm', 0, 0, tiled=True)  9.2 us
    ppermute x2, waiting for transfers between devices, padded_2(): after = lax.ppermute(first, axis, down)  8.89 us
    all_to_all x1, waiting for transfers between devices, per_device(): lax.all_to_all(jnp.tile(send_grad, (halves, 1, 1)), 'tm', 0, 0, tiled=True)  8.82 us
    all_to_all x1, starting transfers between devices, per_device(): lax.all_to_all(jnp.broadcast_to(small_part, (devices, small_part.shape[1]...  8.53 us
  transfers between devices with their start and end apart: 11, of which 8 were waited for; matrix products, arithmetic and copies ran while one was open for 4% of the time, Pallas kernels for 0%

profile of v3, /device:TPU:1, one launch (start us, length us, event | category | flops | bytes accessed | tf_op | source)
XLA Modules:
  0.0 266.2 jit_solution(5975073754013254939)
XLA Ops:
  0.6 1.1 convert_reduce_fusion
  1.7 1.2 fusion.42
  2.9 0.6 copy-done.18
  3.5 0.5 copy-done.9
  4.0 2.6 fusion.10
  6.9 1.1 tile.8
  8.0 8.4 %all-to-all-start = ((bf16[16,128,3,64]{1,3,2,0:T(8,128)(2,1)}), bf16[16,128,3,64]{1,3,2,0:T(8,128)(2,1)S(1)}, u32[]{:S(2)}, u32[]{:S(2)}) async-start(bf16[16,128,3,64]{1,3,2,0:T(8,128)(2,1)} %bitcast.7), calls=%async_computation | async-start | bytes 1572864 | tf_op jit(solution)/shard_map/all_to_all | solution.py:169
  17.3 12.7 %all-to-all-done = bf16[16,128,3,64]{1,3,2,0:T(8,128)(2,1)S(1)} async-done(((bf16[16,128,3,64]{1,3,2,0:T(8,128)(2,1)}), bf16[16,128,3,64]{1,3,2,0:T(8,128)(2,1)S(1)}, u32[]{:S(2)}, u32[]{:S(2)}) %all-to-all-start) | async-done | bytes 786464 | tf_op jit(solution)/shard_map/all_to_all | solution.py:169
  30.1 0.8 fusion.134
  30.9 1.4 fusion.3
  32.3 2.5 fusion
  34.8 1.9 fusion.27
  36.8 0.8 bitcast_select_fusion.1
  37.6 5.0 %all-to-all-start.1 = ((bf16[16,128,64]{1,2,0:T(8,128)(2,1)}), bf16[16,128,64]{1,2,0:T(8,128)(2,1)S(1)}, u32[]{:S(2)}, u32[]{:S(2)}) async-start(bf16[16,128,64]{1,2,0:T(8,128)(2,1)} %bitcast_select_fusion.1), calls=%async_computation.1 | async-start | bytes 524288 | tf_op jit(solution)/shard_map/all_to_all | solution.py:186
  42.7 8.9 %all-to-all-done.1 = bf16[16,128,64]{1,2,0:T(8,128)(2,1)S(1)} async-done(((bf16[16,128,64]{1,2,0:T(8,128)(2,1)}), bf16[16,128,64]{1,2,0:T(8,128)(2,1)S(1)}, u32[]{:S(2)}, u32[]{:S(2)}) %all-to-all-start.1) | async-done | bytes 262176 | tf_op jit(solution)/shard_map/all_to_all | solution.py:186
  51.6 1.8 fusion.140
  53.8 2.5 collective-permute-start
  56.4 1.9 collective-permute-start.1
  58.4 4.8 %collective-permute-done.1 = bf16[15,1024]{1,0:T(8,128)(2,1)S(1)} collective-permute-done((bf16[15,1024]{1,0:T(8,128)(2,1)S(1)}, bf16[15,1024]{1,0:T(8,128)(2,1)S(1)}, u32[]{:S(2)}, u32[]{:S(2)}) %collective-permute-start.1) | collective-permute-done | bytes 30752 | tf_op jit(solution)/shard_map/ppermute | solution.py:25
  63.2 4.2 %multiply_reduce_fusion.1 = (bf16[1024]{0:T(1024)(128)(2,1)S(1)}, bf16[1024]{0:T(1024)(128)(2,1)S(1)}, bf16[1024]{0:T(1024)(128)(2,1)S(1)}, bf16[1024]{0:T(1024)...) fusion(f32[158,1024]{1,0:T(8,128)S(1)} %maximum_convert_fusion,, ...), kind=kLoop, calls=%fused_computation.124 | loop fusion | flops 13875200 | bytes 17203200 | tf_op jit(solution)/shard_map/reduce_sum | solution.py:210
  67.4 0.8 multiply_reduce_fusion.19
  68.2 1.9 collective-permute-start.2
  70.2 2.6 collective-permute-start.3
  72.8 4.1 %collective-permute-done.3 = bf16[15,1024]{1,0:T(8,128)(2,1)S(1)} collective-permute-done((bf16[15,1024]{1,0:T(8,128)(2,1)S(1)}, bf16[15,1024]{1,0:T(8,128)(2,1)S(1)}, u32[]{:S(2)}, u32[]{:S(2)}) %collective-permute-start.3) | collective-permute-done | bytes 30752 | tf_op jit(solution)/shard_map/ppermute | solution.py:25
  77.0 3.6 %multiply_reduce_fusion = (bf16[1024]{0:T(1024)(128)(2,1)S(1)}, f32[128]{0:T(128)S(1)}, f32[128,1024]{1,0:T(8,128)S(1)}) fusion(f32[128,1024]{1,0:T(8,128)S(1)} %get-tuple-element.87, f32[128]{0:T(128)S(1)} %fusion.113, f32[128]{0:T(128)S(1)} %broadcast_multiply_fusion, f32[1024]{0:T(1024)S(1)} %copy-done.4, f32[158,1024]{1,0:T(8,128)S(1)} %maximum_convert_fusion.1, ...), kind=kLoop, calls=%fused_computation.123 | loop fusion | flops 9042816 | bytes 17436288 | tf_op jit(solution)/shard_map/transpose(jvp())/reduce_sum | solution.py:33
  80.6 0.3 fusion.132
  81.0 1.5 convolution_convert_fusion.3
  82.7 0.8 tile.20
  83.4 7.7 %all-to-all-start.2 = ((bf16[16,128,64]{1,2,0:T(8,128)(2,1)}), bf16[16,128,64]{1,2,0:T(8,128)(2,1)S(1)}, u32[]{:S(2)}, u32[]{:S(2)}) async-start(bf16[16,128,64]{1,2,0:T(8,128)(2,1)} %bitcast.47), calls=%async_computation.2 | async-start | bytes 524288 | tf_op jit(solution)/shard_map/all_to_all | solution.py:230
  91.2 8.8 %all-to-all-done.2 = bf16[16,128,64]{1,2,0:T(8,128)(2,1)S(1)} async-done(((bf16[16,128,64]{1,2,0:T(8,128)(2,1)}), bf16[16,128,64]{1,2,0:T(8,128)(2,1)S(1)}, u32[]{:S(2)}, u32[]{:S(2)}) %all-to-all-start.2) | async-done | bytes 262176 | tf_op jit(solution)/shard_map/all_to_all | solution.py:230
  100.1 0.6 pad_maximum_fusion.1
  100.7 1.1 collective-permute-start.4
  101.8 6.9 %fusion.23 = bf16[8,8,8,128]{3,1,2,0:T(8,128)(2,1)S(1)} fusion(f32[1024,2048]{1,0:T(8,128)} %copy-done, f32[1024]{0:T(1024)S(1)} %multiply_reduce_fusion.34, f32[1024]{0:T(1024)S(1)} %log_add_fusion, pred[2048]{0:T(1024)(128)(4,1)S(1)} %iota_compare_fusion, bf16[2048,64]{0,1:T(8,128)(2,1)S(1)} %copy_bitcast_fusion.1, s32[]{:T(128)S(6)} %select_n.61, ...), kind=kOutput, calls=%fused_computation.31 | convolution fusion | flops 551682048 | bytes 9185284 | tf_op jit(solution)/shard_map/dot_general | solution.py:250
  109.0 0.8 maximum_select_fusion
  109.9 6.7 %fusion.2 = (bf16[2048,1024]{0,1:T(8,128)(2,1)}, f32[2048,1024]{0,1:T(8,128)}) fusion(f32[2048]{0:T(1024)S(1)} %bitcast.274, pred[1024]{0:T(1024)(128)(4,1)S(1)} %dynamic-slice.6, bf16[2048,1,64]{0,2,1:T(8,128)(2,1)} %get-tuple-element.44, s32[]{:T(128)S(6)} %select_n.61, bf16[2048,3,64]{0,2,1:T(8,128)(2,1)S(1)} %copy_bitcast_fusion), kind=kOutput, calls=%fused_computation.7 | convolution fusion | flops 278921216 | bytes 12985348 | tf_op jit(solution)/shard_map/dot_general | solution.py:253
  116.5 7.1 %fusion.22 = bf16[8,8,8,128]{3,1,2,0:T(8,128)(2,1)S(1)} fusion(f32[2048,1024]{0,1:T(8,128)} %get-tuple-element.89, f32[2048]{0:T(1024)S(1)} %bitcast.273, f32[2048]{0:T(1024)S(1)} %bitcast.275, pred[1024]{0:T(1024)(128)(4,1)} %copy-done.17, bf16[2048,1,64]{0,2,1:T(8,128)(2,1)S(1)} %get-tuple-element.43, s32[]{:T(128)S(6)} %select_n.61, ...), kind=kOutput, calls=%fused_computation.30 | convolution fusion | flops 551682048 | bytes 9192452 | tf_op jit(solution)/shard_map/dot_general | solution.py:259
  123.7 3.6 %fusion.21 = bf16[8,128,1,64]{1,3,0,2:T(8,128)(2,1)S(1)} fusion(bf16[8,128,2048]{2,1,0:T(8,128)(2,1)} %bitcast.192, bf16[2048,64,1]{0,1,2:T(8,128)(2,1)S(1)} %reshape.259), kind=kOutput, calls=%fused_computation.29 | convolution fusion | flops 268500992 | bytes 4587520 | tf_op jit(solution)/shard_map/dot_general | solution.py:262
  127.3 1.2 bitcast_select_fusion
  128.5 4.2 %all-to-all-start.3 = ((bf16[16,128,3,64]{1,3,2,0:T(8,128)(2,1)}), bf16[16,128,3,64]{1,3,2,0:T(8,128)(2,1)S(1)}, u32[]{:S(2)}, u32[]{:S(2)}) async-start(bf16[16,128,3,64]{1,3,2,0:T(8,128)(2,1)} %bitcast_select_fusion), calls=%async_computation.3 | async-start | bytes 1572864 | tf_op jit(solution)/shard_map/all_to_all | solution.py:186
  132.9 0.8 copy.121
  134.4 0.4 convolution_convert_fusion.1
  134.8 11.5 %all-to-all-done.3 = bf16[16,128,3,64]{1,3,2,0:T(8,128)(2,1)S(1)} async-done(((bf16[16,128,3,64]{1,3,2,0:T(8,128)(2,1)}), bf16[16,128,3,64]{1,3,2,0:T(8,128)(2,1)S(1)}, u32[]{:S(2)}, u32[]{:S(2)}) %all-to-all-start.3) | async-done | bytes 786464 | tf_op jit(solution)/shard_map/all_to_all | solution.py:186
  146.3 1.0 reduce_sum.481
  147.3 1.0 copy.120
  148.3 3.1 %fusion.43 = (f32[128]{0:T(128)S(1)}, f32[128,1024]{1,0:T(8,128)S(1)}) fusion(bf16[1,128,1024]{2,1,0:T(8,128)(2,1)S(1)} %copy-done.1, f32[1024]{0:T(1024)S(1)} %copy-done.5, f32[128]{0:T(128)S(1)} %copy-done.7, bf16[128,1536]{0,1:T(8,128)(2,1)S(1)} %bitcast.194, bf16[1024,2048]{1,0:T(8,128)(2,1)} %param.10), kind=kOutput, calls=%fused_computation.57 | convolution fusion | flops 403308416 | bytes 4330496 | tf_op jit(solution)/shard_map/dot_general | solution.py:267
  151.4 0.3 fusion.40
  151.8 0.3 concatenate.32
  152.1 0.6 concatenate.33
  152.7 1.9 convolution_convert_fusion
  154.7 0.5 maximum_bitcast_fusion
  155.2 2.1 copy.128
  157.4 58.7 %all_to_all.36 = bf16[16,16,4,2081]{3,2,1,0:T(4,128)(2,1)} all-to-all(bf16[16,16,4,2081]{3,2,1,0:T(4,128)(2,1)S(1)} %copy.128), channel_id=1, replica_groups=mesh['dp'=16,'tm'=16] {'tm'}, dimensions={0} | all-to-all | bytes 8523776 | tf_op jit(solution)/shard_map/all_to_all | solution.py:292
  216.1 5.0 %reduce_sum.517 = bf16[16,4,2081]{2,1,0:T(4,128)(2,1)} reduce(bf16[16,16,4,2081]{3,2,1,0:T(4,128)(2,1)} %all_to_all.36, bf16[]{:T(256)} %constant.62.clone.1), dimensions={0}, to_apply=%region_46.47 | reduce | flops 1997760 | bytes 4528258 | tf_op jit(solution)/shard_map/reduce_sum | solution.py:292
  221.1 8.4 %all-to-all-start.5 = ((bf16[16,4,2081]{2,1,0:T(4,128)(2,1)}), bf16[16,4,2081]{2,1,0:T(4,128)(2,1)S(1)}, u32[]{:S(2)}, u32[]{:S(2)}) async-start(bf16[16,4,2081]{2,1,0:T(4,128)(2,1)} %reduce_sum.517), calls=%async_computation.5 | async-start | bytes 557056 | tf_op jit(solution)/shard_map/all_to_all | solution.py:293
  229.5 1.0 fusion.79
  230.5 8.3 %all-to-all-done.5 = bf16[16,4,2081]{2,1,0:T(4,128)(2,1)S(1)} async-done(((bf16[16,4,2081]{2,1,0:T(4,128)(2,1)}), bf16[16,4,2081]{2,1,0:T(4,128)(2,1)S(1)}, u32[]{:S(2)}, u32[]{:S(2)}) %all-to-all-start.5) | async-done | bytes 266400 | tf_op jit(solution)/shard_map/all_to_all | solution.py:293
  239.0 0.8 broadcast_in_dim.182
  239.8 8.5 %all-to-all-start.6 = ((f32[256,1,132]{2,1,0:T(1,128)}), f32[256,1,132]{2,1,0:T(1,128)S(1)}, u32[]{:S(2)}, u32[]{:S(2)}) async-start(f32[256,1,132]{2,1,0:T(1,128)} %broadcast_in_dim.182), calls=%async_computation.6 | async-start | bytes 524288 | tf_op jit(solution)/shard_map/all_to_all | solution.py:297
  248.3 0.6 slice_multiply_fusion.32
  249.0 15.0 %all-to-all-done.6 = f32[256,1,132]{2,1,0:T(1,128)S(1)} async-done(((f32[256,1,132]{2,1,0:T(1,128)}), f32[256,1,132]{2,1,0:T(1,128)S(1)}, u32[]{:S(2)}, u32[]{:S(2)}) %all-to-all-start.6) | async-done | bytes 135200 | tf_op jit(solution)/shard_map/all_to_all | solution.py:297
  264.0 0.6 reduce.4
  264.6 0.2 slice.497
  264.9 0.7 slice_multiply_fusion.31
  265.6 0.6 slice_multiply_fusion.33
  (119 shorter events, 3.0 us)
Async XLA Ops:
  1.7 1.2 copy-start.6
  2.9 0.6 copy-start.18
  3.5 0.5 copy-start.9
  8.0 22.0 %all-to-all-start = ((bf16[16,128,3,64]{1,3,2,0:T(8,128)(2,1)}), bf16[16,128,3,64]{1,3,2,0:T(8,128)(2,1)S(1)}, u32[]{:S(2)}, u32[]{:S(2)}) async-start(bf16[16,128,3,64]{1,3,2,0:T(8,128)(2,1)} %bitcast.7), calls=%async_computation | async-start | bytes 1572864 | tf_op jit(solution)/shard_map/all_to_all | solution.py:169
  17.3 19.5 %copy-start.13 = (pred[16]{0:T(512)(128)(4,1)}, pred[16]{0:T(512)(128)(4,1)S(1)}, u32[]{:S(2)}) copy-start(pred[16]{0:T(512)(128)(4,1)S(1)} %broadcast_in_dim.158) | copy-start | bytes 52
  32.3 4.4 %copy-start = (f32[1024,2048]{1,0:T(8,128)}, f32[1024,2048]{1,0:T(8,128)S(1)}, u32[]{:S(2)}) copy-start(f32[1024,2048]{1,0:T(8,128)S(1)} %get-tuple-element.85) | copy-start | bytes 25165828
  34.8 7.8 %copy-start.3 = (bf16[31,1024]{1,0:T(8,128)(2,1)S(1)}, bf16[31,1024]{1,0:T(8,128)(2,1)}, u32[]{:S(2)}) copy-start(bf16[31,1024]{1,0:T(8,128)(2,1)} %param.13) | copy-start | bytes 190468
  34.8 16.8 %copy-start.1 = (bf16[1,128,1024]{2,1,0:T(8,128)(2,1)S(1)}, bf16[1,128,1024]{2,1,0:T(8,128)(2,1)}, u32[]{:S(2)}) copy-start(bf16[1,128,1024]{2,1,0:T(8,128)(2,1)} %param.7) | copy-start | bytes 786436
  34.8 18.8 %copy-start.4 = (f32[1024]{0:T(1024)S(1)}, f32[1024]{0:T(1024)}, u32[]{:S(2)}) copy-start(f32[1024]{0:T(1024)} %param.12) | copy-start | bytes 12292
  34.8 28.4 %copy-start.2 = (bf16[1,128,1024]{2,1,0:T(8,128)(2,1)S(1)}, bf16[1,128,1024]{2,1,0:T(8,128)(2,1)}, u32[]{:S(2)}) copy-start(bf16[1,128,1024]{2,1,0:T(8,128)(2,1)} %param.8) | copy-start | bytes 786436
  37.6 13.9 %all-to-all-start.1 = ((bf16[16,128,64]{1,2,0:T(8,128)(2,1)}), bf16[16,128,64]{1,2,0:T(8,128)(2,1)S(1)}, u32[]{:S(2)}, u32[]{:S(2)}) async-start(bf16[16,128,64]{1,2,0:T(8,128)(2,1)} %bitcast_select_fusion.1), calls=%async_computation.1 | async-start | bytes 524288 | tf_op jit(solution)/shard_map/all_to_all | solution.py:186
  53.8 4.5 %collective-permute-start = (bf16[15,1024]{1,0:T(8,128)(2,1)S(1)}, bf16[15,1024]{1,0:T(8,128)(2,1)S(1)}, u32[]{:S(2)}, u32[]{:S(2)}) collective-permute-start(bf16[15,1024]{1,0:T(8,128)(2,1)S(1)} %get-tuple-element.49), channel_id=1, source_target_pairs={{0,1},{1,2},{2,3},{3,4},{4,5},{5,6},{6,7},{7,8},{8,9},{9,10},{10,1... | collective-permute-start | bytes 92168 | tf_op jit(solution)/shard_map/ppermute | solution.py:24
  56.4 6.7 %collective-permute-start.1 = (bf16[15,1024]{1,0:T(8,128)(2,1)S(1)}, bf16[15,1024]{1,0:T(8,128)(2,1)S(1)}, u32[]{:S(2)}, u32[]{:S(2)}) collective-permute-start(bf16[15,1024]{1,0:T(8,128)(2,1)S(1)} %get-tuple-element.50), channel_id=1, source_target_pairs={{1,0},{2,1},{3,2},{4,3},{5,4},{6,5},{7,6},{8,7},{9,8},{10,9},{11,1... | collective-permute-start | bytes 92168 | tf_op jit(solution)/shard_map/ppermute | solution.py:25
  68.2 4.5 %collective-permute-start.2 = (bf16[15,1024]{1,0:T(8,128)(2,1)S(1)}, bf16[15,1024]{1,0:T(8,128)(2,1)S(1)}, u32[]{:S(2)}, u32[]{:S(2)}) collective-permute-start(bf16[15,1024]{1,0:T(8,128)(2,1)S(1)} %get-tuple-element.47), channel_id=1, source_target_pairs={{0,1},{1,2},{2,3},{3,4},{4,5},{5,6},{6,7},{7,8},{8,9},{9,10},{10,1... | collective-permute-start | bytes 92168 | tf_op jit(solution)/shard_map/ppermute | solution.py:24
  70.2 6.7 %collective-permute-start.3 = (bf16[15,1024]{1,0:T(8,128)(2,1)S(1)}, bf16[15,1024]{1,0:T(8,128)(2,1)S(1)}, u32[]{:S(2)}, u32[]{:S(2)}) collective-permute-start(bf16[15,1024]{1,0:T(8,128)(2,1)S(1)} %get-tuple-element.48), channel_id=1, source_target_pairs={{1,0},{2,1},{3,2},{4,3},{5,4},{6,5},{7,6},{8,7},{9,8},{10,9},{11,1... | collective-permute-start | bytes 92168 | tf_op jit(solution)/shard_map/ppermute | solution.py:25
  80.8 10.3 %copy-start.15 = (f32[128]{0:T(128)}, f32[128]{0:T(128)S(1)}, u32[]{:S(2)}) copy-start(f32[128]{0:T(128)S(1)} %negate_multiply_fusion.1) | copy-start | bytes 1540
  83.4 16.6 %all-to-all-start.2 = ((bf16[16,128,64]{1,2,0:T(8,128)(2,1)}), bf16[16,128,64]{1,2,0:T(8,128)(2,1)S(1)}, u32[]{:S(2)}, u32[]{:S(2)}) async-start(bf16[16,128,64]{1,2,0:T(8,128)(2,1)} %bitcast.47), calls=%async_computation.2 | async-start | bytes 524288 | tf_op jit(solution)/shard_map/all_to_all | solution.py:230
  91.2 18.7 %copy-start.17 = (pred[1024]{0:T(1024)(128)(4,1)}, pred[1024]{0:T(1024)(128)(4,1)S(1)}, u32[]{:S(2)}) copy-start(pred[1024]{0:T(1024)(128)(4,1)S(1)} %dynamic-slice.6) | copy-start | bytes 3076
  100.7 8.3 %collective-permute-start.4 = (f32[2,1024]{1,0:T(2,128)}, f32[2,1024]{1,0:T(2,128)}, u32[]{:S(2)}, u32[]{:S(2)}) collective-permute-start(f32[2,1024]{1,0:T(2,128)} %pad_maximum_fusion.1), channel_id=1, source_target_pairs={{0,8},{1,9},{2,10},{3,11},{4,12},{5,13},{6,14},{7,15},{8,0},{9,1},... | collective-permute-start | bytes 24584 | tf_op jit(solution)/shard_map/ppermute | solution.py:235
  116.5 10.8 %copy-start.14 = (pred[16]{0:T(512)(128)(4,1)S(1)}, pred[16]{0:T(512)(128)(4,1)}, u32[]{:S(2)}) copy-start(pred[16]{0:T(512)(128)(4,1)} %copy-done.13) | copy-start | bytes 52
  116.5 16.2 %copy-start.5 = (f32[1024]{0:T(1024)S(1)}, f32[1024]{0:T(1024)}, u32[]{:S(2)}) copy-start(f32[1024]{0:T(1024)} %param.11) | copy-start | bytes 12292
  116.5 16.2 %copy-start.7 = (f32[128]{0:T(128)S(1)}, f32[128]{0:T(128)}, u32[]{:S(2)}) copy-start(f32[128]{0:T(128)} %copy-done.6) | copy-start | bytes 1540
  116.5 16.2 %copy-start.10 = (f32[128]{0:T(128)S(1)}, f32[128]{0:T(128)}, u32[]{:S(2)}) copy-start(f32[128]{0:T(128)} %copy-done.9) | copy-start | bytes 1540
  123.7 27.7 %copy-start.19 = (f32[128]{0:T(128)S(1)}, f32[128]{0:T(128)}, u32[]{:S(2)}) copy-start(f32[128]{0:T(128)} %copy-done.18) | copy-start | bytes 1540
  123.7 27.7 %copy-start.11 = (f32[128]{0:T(128)S(1)}, f32[128]{0:T(128)}, u32[]{:S(2)}) copy-start(f32[128]{0:T(128)} %copy-done.9) | copy-start | bytes 1540
  128.5 17.8 %all-to-all-start.3 = ((bf16[16,128,3,64]{1,3,2,0:T(8,128)(2,1)}), bf16[16,128,3,64]{1,3,2,0:T(8,128)(2,1)S(1)}, u32[]{:S(2)}, u32[]{:S(2)}) async-start(bf16[16,128,3,64]{1,3,2,0:T(8,128)(2,1)} %bitcast_select_fusion), calls=%async_computation.3 | async-start | bytes 1572864 | tf_op jit(solution)/shard_map/all_to_all | solution.py:186
  157.3 72.2 %copy-start.8 = (f32[128]{0:T(128)S(1)}, f32[128]{0:T(128)}, u32[]{:S(2)}) copy-start(f32[128]{0:T(128)} %copy-done.6) | copy-start | bytes 1540
  157.3 72.2 %copy-start.12 = (f32[128]{0:T(128)S(1)}, f32[128]{0:T(128)}, u32[]{:S(2)}) copy-start(f32[128]{0:T(128)} %copy-done.9) | copy-start | bytes 1540
  157.4 72.2 %copy-start.16 = (f32[128]{0:T(128)S(1)}, f32[128]{0:T(128)}, u32[]{:S(2)}) copy-start(f32[128]{0:T(128)} %copy-done.15) | copy-start | bytes 1540
  221.1 17.7 %all-to-all-start.5 = ((bf16[16,4,2081]{2,1,0:T(4,128)(2,1)}), bf16[16,4,2081]{2,1,0:T(4,128)(2,1)S(1)}, u32[]{:S(2)}, u32[]{:S(2)}) async-start(bf16[16,4,2081]{2,1,0:T(4,128)(2,1)} %reduce_sum.517), calls=%async_computation.5 | async-start | bytes 557056 | tf_op jit(solution)/shard_map/all_to_all | solution.py:293
  239.8 24.2 %all-to-all-start.6 = ((f32[256,1,132]{2,1,0:T(1,128)}), f32[256,1,132]{2,1,0:T(1,128)S(1)}, u32[]{:S(2)}, u32[]{:S(2)}) async-start(f32[256,1,132]{2,1,0:T(1,128)} %broadcast_in_dim.182), calls=%async_computation.6 | async-start | bytes 524288 | tf_op jit(solution)/shard_map/all_to_all | solution.py:297

commit v4 on v3

--- a/solution.py
+++ b/solution.py
@@ -164,7 +164,6 @@
     total = frame_count * tm_count
     key_live = (jnp.arange(total, dtype=jnp.int32) < length)[None, :]
     half_live = lax.dynamic_slice_in_dim(key_live, half * span, span, 1)
-    mine = (jnp.arange(halves) == half).reshape(halves, 1, 1, 1, 1)
     qkv = projected.reshape(frame_count, 3, HEADS, HDIM).transpose(2, 0, 1, 3)
     got = lax.all_to_all(jnp.tile(qkv, (halves, 1, 1, 1)), "tm", 0, 0, tiled=True)
     got = got.reshape(total, 3, HDIM)
@@ -179,13 +178,11 @@
     a_half = (acc / summed[:, None]).astype(jnp.bfloat16)
     lse_half = top + jnp.log(summed)
 
+    half_groups = [[part * HEADS + k for k in range(HEADS)] for part in range(halves)]
+
     def to_frames(rows):
-        blocks = rows.reshape((1, HEADS, frame_count) + rows.shape[1:])
-        placed = jnp.where(mine.reshape((halves,) + (1,) * (blocks.ndim - 1)), blocks, 0)
-        placed = placed.reshape((tm_count, frame_count) + rows.shape[1:])
-        back = lax.all_to_all(placed, "tm", 0, 0, tiled=True)
-        back = back.reshape((halves, HEADS, frame_count) + rows.shape[1:])
-        return jnp.sum(back.astype(jnp.float32), axis=0).astype(rows.dtype)
+        blocks = rows.reshape((HEADS, frame_count) + rows.shape[1:])
+        return lax.all_to_all(blocks, "tm", 0, 0, tiled=True, axis_index_groups=half_groups)
 
     attended = to_frames(a_half).transpose(1, 0, 2).reshape(frame_count, width)
     w_out = w_proj[:, 3 * width :]

time: 267 us -> 257 us (0.963)
  waiting for transfers between devices: 74.1 us -> 66.3 us
    all_to_all x2, waiting for transfers between devices: 20.3 us -> 11.6 us  [to_frames(): lax.all_to_all(blocks, 'tm', 0, 0, tiled=True, axis_index_groups=half_gro...]
where the time goes in v4:
time: 257 us; the launch traced here: 255 us
  waiting for transfers between devices  66.3 us (26%)
  blocking collectives  59.2 us (23%)
  starting transfers between devices  51 us (20%)
  matrix products  39 us (15%)
  other arithmetic  26 us (10%)
  local copies, waits for them, and re-layouts  11.7 us (5%)
    all_to_all x1, blocking collectives, per_device(): lax.all_to_all(packed, 'tm', 0, 0, tiled=True).astype(jnp.float32).sum(0)  59.2 us
    all_to_all x1, waiting for transfers between devices, per_device(): lax.all_to_all(jnp.broadcast_to(small_part, (devices, small_part.shape[1]...  15 us
    all_to_all x1, waiting for transfers between devices, per_device(): lax.all_to_all(jnp.tile(qkv, (halves, 1, 1, 1)), 'tm', 0, 0, tiled=True)  12.9 us
    all_to_all x2, waiting for transfers between devices, to_frames(): lax.all_to_all(blocks, 'tm', 0, 0, tiled=True, axis_index_groups=half_gro...  11.6 us
    ppermute x2, waiting for transfers between devices, padded_2(): after = lax.ppermute(first, axis, down)  9.62 us
    all_to_all x2, starting transfers between devices, to_frames(): lax.all_to_all(blocks, 'tm', 0, 0, tiled=True, axis_index_groups=half_gro...  8.83 us
    all_to_all x1, waiting for transfers between devices, per_device(): lax.all_to_all(jnp.tile(send_grad, (halves, 1, 1)), 'tm', 0, 0, tiled=True)  8.82 us
    all_to_all x1, starting transfers between devices, per_device(): lax.all_to_all(jnp.broadcast_to(small_part, (devices, small_part.shape[1]...  8.6 us
  transfers between devices with their start and end apart: 11, of which 8 were waited for; matrix products, arithmetic and copies ran while one was open for 4% of the time, Pallas kernels for 0%

profile of v4, /device:TPU:1, one launch (start us, length us, event | category | flops | bytes accessed | tf_op | source)
XLA Modules:
  0.0 255.5 jit_solution(10173526774747268324)
XLA Ops:
  0.6 1.1 convert_reduce_fusion
  1.7 1.2 fusion.42
  2.9 0.6 copy-done.18
  3.5 0.6 copy-done.11
  4.0 2.6 %fusion.10 = bf16[128,1536]{1,0:T(8,128)(2,1)S(1)} fusion(bf16[1024,2048]{1,0:T(8,128)(2,1)} %param.10, bf16[1,128,1024]{2,1,0:T(8,128)(2,1)} %param.7, f32[1024]{0:T(1024)} %param.11, f32[128]{0:T(128)S(1)} %fusion.112, f32[128]{0:T(128)S(1)} %broadcast_multiply_fusion.1), kind=kOutput, calls=%fused_computation.16 | convolution fusion | flops 403505152 | bytes 3806208 | tf_op jit(solution)/shard_map/dot_general | solution.py:156
  7.0 1.1 tile.8
  8.0 8.4 %all-to-all-start = ((bf16[16,128,3,64]{1,3,2,0:T(8,128)(2,1)}), bf16[16,128,3,64]{1,3,2,0:T(8,128)(2,1)S(1)}, u32[]{:S(2)}, u32[]{:S(2)}) async-start(bf16[16,128,3,64]{1,3,2,0:T(8,128)(2,1)} %bitcast.7), calls=%async_computation | async-start | bytes 1572864 | tf_op jit(solution)/shard_map/all_to_all | solution.py:168
  17.1 12.9 %all-to-all-done = bf16[16,128,3,64]{1,3,2,0:T(8,128)(2,1)S(1)} async-done(((bf16[16,128,3,64]{1,3,2,0:T(8,128)(2,1)}), bf16[16,128,3,64]{1,3,2,0:T(8,128)(2,1)S(1)}, u32[]{:S(2)}, u32[]{:S(2)}) %all-to-all-start) | async-done | bytes 786464 | tf_op jit(solution)/shard_map/all_to_all | solution.py:168
  30.2 0.8 fusion.134
  30.9 1.4 fusion.3
  32.4 2.5 fusion
  34.9 1.9 fusion.27
  36.8 0.7 copy_bitcast_fusion.2
  37.5 4.9 %all-to-all-start.1 = ((bf16[8,128,64]{1,2,0:T(8,128)(2,1)}), bf16[8,128,64]{1,2,0:T(8,128)(2,1)S(1)}, u32[]{:S(2)}, u32[]{:S(2)}) async-start(bf16[8,128,64]{1,2,0:T(8,128)(2,1)} %copy_bitcast_fusion.2), calls=%async_computation.1 | async-start | bytes 262144 | tf_op jit(solution)/shard_map/all_to_all | solution.py:185
  42.5 5.8 %all-to-all-done.1 = bf16[8,128,64]{1,2,0:T(8,128)(2,1)S(1)} async-done(((bf16[8,128,64]{1,2,0:T(8,128)(2,1)}), bf16[8,128,64]{1,2,0:T(8,128)(2,1)S(1)}, u32[]{:S(2)}, u32[]{:S(2)}) %all-to-all-start.1) | async-done | bytes 131104 | tf_op jit(solution)/shard_map/all_to_all | solution.py:185
  48.3 1.8 fusion.140
  50.3 0.2 select_convert_fusion
  50.5 3.3 %collective-permute-start = (bf16[15,1024]{1,0:T(8,128)(2,1)S(1)}, bf16[15,1024]{1,0:T(8,128)(2,1)S(1)}, u32[]{:S(2)}, u32[]{:S(2)}) collective-permute-start(bf16[15,1024]{1,0:T(8,128)(2,1)S(1)} %get-tuple-element.49), channel_id=1, source_target_pairs={{0,1},{1,2},{2,3},{3,4},{4,5},{5,6},{6,7},{7,8},{8,9},{9,10},{10,1... | collective-permute-start | bytes 92168 | tf_op jit(solution)/shard_map/ppermute | solution.py:24
  53.8 1.9 collective-permute-start.1
  55.8 4.8 %collective-permute-done.1 = bf16[15,1024]{1,0:T(8,128)(2,1)S(1)} collective-permute-done((bf16[15,1024]{1,0:T(8,128)(2,1)S(1)}, bf16[15,1024]{1,0:T(8,128)(2,1)S(1)}, u32[]{:S(2)}, u32[]{:S(2)}) %collective-permute-start.1) | collective-permute-done | bytes 30752 | tf_op jit(solution)/shard_map/ppermute | solution.py:25
  60.7 4.1 %multiply_reduce_fusion.1 = (bf16[1024]{0:T(1024)(128)(2,1)S(1)}, bf16[1024]{0:T(1024)(128)(2,1)S(1)}, bf16[1024]{0:T(1024)(128)(2,1)S(1)}, bf16[1024]{0:T(1024)...) fusion(f32[158,1024]{1,0:T(8,128)S(1)} %maximum_convert_fusion,, ...), kind=kLoop, calls=%fused_computation.123 | loop fusion | flops 13875200 | bytes 17203200 | tf_op jit(solution)/shard_map/reduce_sum | solution.py:207
  64.8 1.4 multiply_reduce_fusion.19
  66.2 1.9 collective-permute-start.2
  68.2 2.6 %collective-permute-start.3 = (bf16[15,1024]{1,0:T(8,128)(2,1)S(1)}, bf16[15,1024]{1,0:T(8,128)(2,1)S(1)}, u32[]{:S(2)}, u32[]{:S(2)}) collective-permute-start(bf16[15,1024]{1,0:T(8,128)(2,1)S(1)} %get-tuple-element.48), channel_id=1, source_target_pairs={{1,0},{2,1},{3,2},{4,3},{5,4},{6,5},{7,6},{8,7},{9,8},{10,9},{11,1... | collective-permute-start | bytes 92168 | tf_op jit(solution)/shard_map/ppermute | solution.py:25
  70.8 4.9 %collective-permute-done.3 = bf16[15,1024]{1,0:T(8,128)(2,1)S(1)} collective-permute-done((bf16[15,1024]{1,0:T(8,128)(2,1)S(1)}, bf16[15,1024]{1,0:T(8,128)(2,1)S(1)}, u32[]{:S(2)}, u32[]{:S(2)}) %collective-permute-start.3) | collective-permute-done | bytes 30752 | tf_op jit(solution)/shard_map/ppermute | solution.py:25
  75.7 3.6 %multiply_reduce_fusion = (bf16[1024]{0:T(1024)(128)(2,1)S(1)}, f32[128]{0:T(128)S(1)}, f32[128,1024]{1,0:T(8,128)S(1)}) fusion(f32[128,1024]{1,0:T(8,128)S(1)} %get-tuple-element.87, f32[128]{0:T(128)S(1)} %fusion.113, f32[128]{0:T(128)S(1)} %broadcast_multiply_fusion, f32[1024]{0:T(1024)S(1)} %copy-done.4, f32[158,1024]{1,0:T(8,128)S(1)} %maximum_convert_fusion.1, ...), kind=kLoop, calls=%fused_computation.122 | loop fusion | flops 9042816 | bytes 17436288 | tf_op jit(solution)/shard_map/transpose(jvp())/reduce_sum | solution.py:33
  79.3 0.3 fusion.132
  79.7 1.5 convolution_convert_fusion.3
  81.4 0.8 tile.20
  82.1 6.0 %all-to-all-start.2 = ((bf16[16,128,64]{1,2,0:T(8,128)(2,1)}), bf16[16,128,64]{1,2,0:T(8,128)(2,1)S(1)}, u32[]{:S(2)}, u32[]{:S(2)}) async-start(bf16[16,128,64]{1,2,0:T(8,128)(2,1)} %bitcast.45), calls=%async_computation.2 | async-start | bytes 524288 | tf_op jit(solution)/shard_map/all_to_all | solution.py:227
  88.1 8.8 %all-to-all-done.2 = bf16[16,128,64]{1,2,0:T(8,128)(2,1)S(1)} async-done(((bf16[16,128,64]{1,2,0:T(8,128)(2,1)}), bf16[16,128,64]{1,2,0:T(8,128)(2,1)S(1)}, u32[]{:S(2)}, u32[]{:S(2)}) %all-to-all-start.2) | async-done | bytes 262176 | tf_op jit(solution)/shard_map/all_to_all | solution.py:227
  97.1 0.6 pad_maximum_fusion.1
  97.7 1.1 collective-permute-start.4
  98.7 6.9 %fusion.23 = bf16[8,8,8,128]{3,1,2,0:T(8,128)(2,1)S(1)} fusion(f32[1024,2048]{1,0:T(8,128)} %copy-done, f32[1024]{0:T(1024)S(1)} %multiply_reduce_fusion.34, f32[1024]{0:T(1024)S(1)} %log_add_fusion, pred[2048]{0:T(1024)(128)(4,1)S(1)} %iota_compare_fusion, bf16[2048,64]{0,1:T(8,128)(2,1)S(1)} %copy_bitcast_fusion.1, s32[]{:T(128)S(6)} %select_n.51, ...), kind=kOutput, calls=%fused_computation.31 | convolution fusion | flops 551682048 | bytes 9185284 | tf_op jit(solution)/shard_map/dot_general | solution.py:247
  106.0 0.8 maximum_select_fusion
  106.8 6.7 %fusion.2 = (bf16[2048,1024]{0,1:T(8,128)(2,1)}, f32[2048,1024]{0,1:T(8,128)}) fusion(f32[2048]{0:T(1024)S(1)} %bitcast.266, pred[1024]{0:T(1024)(128)(4,1)S(1)} %dynamic-slice.6, bf16[2048,1,64]{0,2,1:T(8,128)(2,1)} %get-tuple-element.44, s32[]{:T(128)S(6)} %select_n.51, bf16[2048,3,64]{0,2,1:T(8,128)(2,1)S(1)} %copy_bitcast_fusion), kind=kOutput, calls=%fused_computation.7 | convolution fusion | flops 278921216 | bytes 12985348 | tf_op jit(solution)/shard_map/dot_general | solution.py:250
  113.5 7.1 %fusion.22 = bf16[8,8,8,128]{3,1,2,0:T(8,128)(2,1)S(1)} fusion(f32[2048,1024]{0,1:T(8,128)} %get-tuple-element.89, f32[2048]{0:T(1024)S(1)} %bitcast.265, f32[2048]{0:T(1024)S(1)} %bitcast.267, pred[1024]{0:T(1024)(128)(4,1)} %copy-done.17, bf16[2048,1,64]{0,2,1:T(8,128)(2,1)S(1)} %get-tuple-element.43, s32[]{:T(128)S(6)} %select_n.51, ...), kind=kOutput, calls=%fused_computation.30 | convolution fusion | flops 551682048 | bytes 9192452 | tf_op jit(solution)/shard_map/dot_general | solution.py:256
  120.7 3.6 %fusion.21 = bf16[8,128,1,64]{1,3,0,2:T(8,128)(2,1)S(1)} fusion(bf16[8,128,2048]{2,1,0:T(8,128)(2,1)} %bitcast.187, bf16[2048,64,1]{0,1,2:T(8,128)(2,1)S(1)} %reshape.214), kind=kOutput, calls=%fused_computation.29 | convolution fusion | flops 268500992 | bytes 4587520 | tf_op jit(solution)/shard_map/dot_general | solution.py:259
  124.3 0.8 copy.118
  125.1 3.9 %all-to-all-start.3 = ((bf16[8,128,3,64]{1,3,2,0:T(8,128)(2,1)}), bf16[8,128,3,64]{1,3,2,0:T(8,128)(2,1)S(1)}, u32[]{:S(2)}, u32[]{:S(2)}) async-start(bf16[8,128,3,64]{1,3,2,0:T(8,128)(2,1)} %copy.118), calls=%async_computation.3 | async-start | bytes 786432 | tf_op jit(solution)/shard_map/all_to_all | solution.py:185
  129.0 0.2 fusion.80
  129.3 0.8 copy.120
  130.7 0.4 convolution_convert_fusion.1
  131.1 5.8 %all-to-all-done.3 = bf16[8,128,3,64]{1,3,2,0:T(8,128)(2,1)S(1)} async-done(((bf16[8,128,3,64]{1,3,2,0:T(8,128)(2,1)}), bf16[8,128,3,64]{1,3,2,0:T(8,128)(2,1)S(1)}, u32[]{:S(2)}, u32[]{:S(2)}) %all-to-all-start.3) | async-done | bytes 393248 | tf_op jit(solution)/shard_map/all_to_all | solution.py:185
  137.0 3.1 %fusion.43 = (f32[128]{0:T(128)S(1)}, f32[128,1024]{1,0:T(8,128)S(1)}) fusion(bf16[1,128,1024]{2,1,0:T(8,128)(2,1)S(1)} %copy-done.1, f32[1024]{0:T(1024)S(1)} %copy-done.5, f32[128]{0:T(128)S(1)} %copy-done.9, bf16[128,1536]{0,1:T(8,128)(2,1)S(1)} %bitcast.188, bf16[1024,2048]{1,0:T(8,128)(2,1)} %param.10), kind=kOutput, calls=%fused_computation.56 | convolution fusion | flops 403308416 | bytes 4330496 | tf_op jit(solution)/shard_map/dot_general | solution.py:264
  140.2 0.3 fusion.40
  140.5 0.3 concatenate.29
  140.8 0.6 concatenate.30
  141.4 1.9 convolution_convert_fusion
  143.4 0.5 maximum_bitcast_fusion
  143.9 2.1 copy.127
  146.1 59.2 %all_to_all.36 = bf16[16,16,4,2081]{3,2,1,0:T(4,128)(2,1)} all-to-all(bf16[16,16,4,2081]{3,2,1,0:T(4,128)(2,1)S(1)} %copy.127), channel_id=1, replica_groups=mesh['dp'=16,'tm'=16] {'tm'}, dimensions={0} | all-to-all | bytes 8523776 | tf_op jit(solution)/shard_map/all_to_all | solution.py:289
  205.3 5.0 %reduce_sum.491 = bf16[16,4,2081]{2,1,0:T(4,128)(2,1)} reduce(bf16[16,16,4,2081]{3,2,1,0:T(4,128)(2,1)} %all_to_all.36, bf16[]{:T(256)} %constant.60.clone.1), dimensions={0}, to_apply=%region_44.45 | reduce | flops 1997760 | bytes 4528258 | tf_op jit(solution)/shard_map/reduce_sum | solution.py:289
  210.3 8.4 %all-to-all-start.5 = ((bf16[16,4,2081]{2,1,0:T(4,128)(2,1)}), bf16[16,4,2081]{2,1,0:T(4,128)(2,1)S(1)}, u32[]{:S(2)}, u32[]{:S(2)}) async-start(bf16[16,4,2081]{2,1,0:T(4,128)(2,1)} %reduce_sum.491), calls=%async_computation.5 | async-start | bytes 557056 | tf_op jit(solution)/shard_map/all_to_all | solution.py:290
  218.8 1.0 fusion.79
  219.8 8.3 %all-to-all-done.5 = bf16[16,4,2081]{2,1,0:T(4,128)(2,1)S(1)} async-done(((bf16[16,4,2081]{2,1,0:T(4,128)(2,1)}), bf16[16,4,2081]{2,1,0:T(4,128)(2,1)S(1)}, u32[]{:S(2)}, u32[]{:S(2)}) %all-to-all-start.5) | async-done | bytes 266400 | tf_op jit(solution)/shard_map/all_to_all | solution.py:290
  228.2 0.8 broadcast_in_dim.121
  229.1 8.6 %all-to-all-start.6 = ((f32[256,1,132]{2,1,0:T(1,128)}), f32[256,1,132]{2,1,0:T(1,128)S(1)}, u32[]{:S(2)}, u32[]{:S(2)}) async-start(f32[256,1,132]{2,1,0:T(1,128)} %broadcast_in_dim.121), calls=%async_computation.6 | async-start | bytes 524288 | tf_op jit(solution)/shard_map/all_to_all | solution.py:294
  237.7 0.6 slice_multiply_fusion.32
  238.3 15.0 %all-to-all-done.6 = f32[256,1,132]{2,1,0:T(1,128)S(1)} async-done(((f32[256,1,132]{2,1,0:T(1,128)}), f32[256,1,132]{2,1,0:T(1,128)S(1)}, u32[]{:S(2)}, u32[]{:S(2)}) %all-to-all-start.6) | async-done | bytes 135200 | tf_op jit(solution)/shard_map/all_to_all | solution.py:294
  253.3 0.6 reduce.2
  254.0 0.2 slice.497
  254.2 0.7 slice_multiply_fusion.31
  254.9 0.6 slice_multiply_fusion.33
  (114 shorter events, 2.4 us)
Async XLA Ops:
  1.7 1.2 copy-start.7
  2.9 0.6 copy-start.18
  3.5 0.6 copy-start.11
  8.0 22.0 %all-to-all-start = ((bf16[16,128,3,64]{1,3,2,0:T(8,128)(2,1)}), bf16[16,128,3,64]{1,3,2,0:T(8,128)(2,1)S(1)}, u32[]{:S(2)}, u32[]{:S(2)}) async-start(bf16[16,128,3,64]{1,3,2,0:T(8,128)(2,1)} %bitcast.7), calls=%async_computation | async-start | bytes 1572864 | tf_op jit(solution)/shard_map/all_to_all | solution.py:168
  32.4 4.4 %copy-start = (f32[1024,2048]{1,0:T(8,128)}, f32[1024,2048]{1,0:T(8,128)S(1)}, u32[]{:S(2)}) copy-start(f32[1024,2048]{1,0:T(8,128)S(1)} %get-tuple-element.85) | copy-start | bytes 25165828
  34.8 7.6 %copy-start.3 = (bf16[31,1024]{1,0:T(8,128)(2,1)S(1)}, bf16[31,1024]{1,0:T(8,128)(2,1)}, u32[]{:S(2)}) copy-start(bf16[31,1024]{1,0:T(8,128)(2,1)} %param.13) | copy-start | bytes 190468
  34.9 13.4 %copy-start.1 = (bf16[1,128,1024]{2,1,0:T(8,128)(2,1)S(1)}, bf16[1,128,1024]{2,1,0:T(8,128)(2,1)}, u32[]{:S(2)}) copy-start(bf16[1,128,1024]{2,1,0:T(8,128)(2,1)} %param.7) | copy-start | bytes 786436
  34.9 15.4 %copy-start.4 = (f32[1024]{0:T(1024)S(1)}, f32[1024]{0:T(1024)}, u32[]{:S(2)}) copy-start(f32[1024]{0:T(1024)} %param.12) | copy-start | bytes 12292
  34.9 25.8 %copy-start.2 = (bf16[1,128,1024]{2,1,0:T(8,128)(2,1)S(1)}, bf16[1,128,1024]{2,1,0:T(8,128)(2,1)}, u32[]{:S(2)}) copy-start(bf16[1,128,1024]{2,1,0:T(8,128)(2,1)} %param.8) | copy-start | bytes 786436
  37.5 10.8 %all-to-all-start.1 = ((bf16[8,128,64]{1,2,0:T(8,128)(2,1)}), bf16[8,128,64]{1,2,0:T(8,128)(2,1)S(1)}, u32[]{:S(2)}, u32[]{:S(2)}) async-start(bf16[8,128,64]{1,2,0:T(8,128)(2,1)} %copy_bitcast_fusion.2), calls=%async_computation.1 | async-start | bytes 262144 | tf_op jit(solution)/shard_map/all_to_all | solution.py:185
  50.5 5.3 %collective-permute-start = (bf16[15,1024]{1,0:T(8,128)(2,1)S(1)}, bf16[15,1024]{1,0:T(8,128)(2,1)S(1)}, u32[]{:S(2)}, u32[]{:S(2)}) collective-permute-start(bf16[15,1024]{1,0:T(8,128)(2,1)S(1)} %get-tuple-element.49), channel_id=1, source_target_pairs={{0,1},{1,2},{2,3},{3,4},{4,5},{5,6},{6,7},{7,8},{8,9},{9,10},{10,1... | collective-permute-start | bytes 92168 | tf_op jit(solution)/shard_map/ppermute | solution.py:24
  53.8 6.7 %collective-permute-start.1 = (bf16[15,1024]{1,0:T(8,128)(2,1)S(1)}, bf16[15,1024]{1,0:T(8,128)(2,1)S(1)}, u32[]{:S(2)}, u32[]{:S(2)}) collective-permute-start(bf16[15,1024]{1,0:T(8,128)(2,1)S(1)} %get-tuple-element.50), channel_id=1, source_target_pairs={{1,0},{2,1},{3,2},{4,3},{5,4},{6,5},{7,6},{8,7},{9,8},{10,9},{11,1... | collective-permute-start | bytes 92168 | tf_op jit(solution)/shard_map/ppermute | solution.py:25
  66.2 4.5 %collective-permute-start.2 = (bf16[15,1024]{1,0:T(8,128)(2,1)S(1)}, bf16[15,1024]{1,0:T(8,128)(2,1)S(1)}, u32[]{:S(2)}, u32[]{:S(2)}) collective-permute-start(bf16[15,1024]{1,0:T(8,128)(2,1)S(1)} %get-tuple-element.47), channel_id=1, source_target_pairs={{0,1},{1,2},{2,3},{3,4},{4,5},{5,6},{6,7},{7,8},{8,9},{9,10},{10,1... | collective-permute-start | bytes 92168 | tf_op jit(solution)/shard_map/ppermute | solution.py:24
  68.2 7.5 %collective-permute-start.3 = (bf16[15,1024]{1,0:T(8,128)(2,1)S(1)}, bf16[15,1024]{1,0:T(8,128)(2,1)S(1)}, u32[]{:S(2)}, u32[]{:S(2)}) collective-permute-start(bf16[15,1024]{1,0:T(8,128)(2,1)S(1)} %get-tuple-element.48), channel_id=1, source_target_pairs={{1,0},{2,1},{3,2},{4,3},{5,4},{6,5},{7,6},{8,7},{9,8},{10,9},{11,1... | collective-permute-start | bytes 92168 | tf_op jit(solution)/shard_map/ppermute | solution.py:25
  79.6 8.5 %copy-start.15 = (f32[128]{0:T(128)}, f32[128]{0:T(128)S(1)}, u32[]{:S(2)}) copy-start(f32[128]{0:T(128)S(1)} %negate_multiply_fusion.1) | copy-start | bytes 1540
  82.1 14.8 %all-to-all-start.2 = ((bf16[16,128,64]{1,2,0:T(8,128)(2,1)}), bf16[16,128,64]{1,2,0:T(8,128)(2,1)S(1)}, u32[]{:S(2)}, u32[]{:S(2)}) async-start(bf16[16,128,64]{1,2,0:T(8,128)(2,1)} %bitcast.45), calls=%async_computation.2 | async-start | bytes 524288 | tf_op jit(solution)/shard_map/all_to_all | solution.py:227
  88.1 18.7 %copy-start.17 = (pred[1024]{0:T(1024)(128)(4,1)}, pred[1024]{0:T(1024)(128)(4,1)S(1)}, u32[]{:S(2)}) copy-start(pred[1024]{0:T(1024)(128)(4,1)S(1)} %dynamic-slice.6) | copy-start | bytes 3076
  97.7 8.3 %collective-permute-start.4 = (f32[2,1024]{1,0:T(2,128)}, f32[2,1024]{1,0:T(2,128)}, u32[]{:S(2)}, u32[]{:S(2)}) collective-permute-start(f32[2,1024]{1,0:T(2,128)} %pad_maximum_fusion.1), channel_id=1, source_target_pairs={{0,8},{1,9},{2,10},{3,11},{4,12},{5,13},{6,14},{7,15},{8,0},{9,1},... | collective-permute-start | bytes 24584 | tf_op jit(solution)/shard_map/ppermute | solution.py:232
  113.5 15.5 %copy-start.5 = (f32[1024]{0:T(1024)S(1)}, f32[1024]{0:T(1024)}, u32[]{:S(2)}) copy-start(f32[1024]{0:T(1024)} %param.11) | copy-start | bytes 12292
  113.5 15.5 %copy-start.8 = (f32[128]{0:T(128)S(1)}, f32[128]{0:T(128)}, u32[]{:S(2)}) copy-start(f32[128]{0:T(128)} %copy-done.7) | copy-start | bytes 1540
  113.5 15.6 %copy-start.12 = (f32[128]{0:T(128)S(1)}, f32[128]{0:T(128)}, u32[]{:S(2)}) copy-start(f32[128]{0:T(128)} %copy-done.11) | copy-start | bytes 1540
  120.6 9.5 %copy-start.6 = (bf16[1024]{0:T(1024)(128)(2,1)S(1)}, bf16[1024]{0:T(1024)(128)(2,1)}, u32[]{:S(2)}) copy-start(bf16[1024]{0:T(1024)(128)(2,1)} %get-tuple-element.34) | copy-start | bytes 6148
  120.6 16.4 %copy-start.9 = (f32[128]{0:T(128)S(1)}, f32[128]{0:T(128)}, u32[]{:S(2)}) copy-start(f32[128]{0:T(128)} %copy-done.7) | copy-start | bytes 1540
  120.6 19.5 %copy-start.19 = (f32[128]{0:T(128)S(1)}, f32[128]{0:T(128)}, u32[]{:S(2)}) copy-start(f32[128]{0:T(128)} %copy-done.18) | copy-start | bytes 1540
  120.6 19.5 %copy-start.13 = (f32[128]{0:T(128)S(1)}, f32[128]{0:T(128)}, u32[]{:S(2)}) copy-start(f32[128]{0:T(128)} %copy-done.11) | copy-start | bytes 1540
  125.1 11.9 %all-to-all-start.3 = ((bf16[8,128,3,64]{1,3,2,0:T(8,128)(2,1)}), bf16[8,128,3,64]{1,3,2,0:T(8,128)(2,1)S(1)}, u32[]{:S(2)}, u32[]{:S(2)}) async-start(bf16[8,128,3,64]{1,3,2,0:T(8,128)(2,1)} %copy.118), calls=%async_computation.3 | async-start | bytes 786432 | tf_op jit(solution)/shard_map/all_to_all | solution.py:185
  146.1 72.7 %copy-start.10 = (f32[128]{0:T(128)S(1)}, f32[128]{0:T(128)}, u32[]{:S(2)}) copy-start(f32[128]{0:T(128)} %copy-done.7) | copy-start | bytes 1540
  146.1 72.7 %copy-start.14 = (f32[128]{0:T(128)S(1)}, f32[128]{0:T(128)}, u32[]{:S(2)}) copy-start(f32[128]{0:T(128)} %copy-done.11) | copy-start | bytes 1540
  146.1 72.7 %copy-start.16 = (f32[128]{0:T(128)S(1)}, f32[128]{0:T(128)}, u32[]{:S(2)}) copy-start(f32[128]{0:T(128)} %copy-done.15) | copy-start | bytes 1540
  210.3 17.7 %all-to-all-start.5 = ((bf16[16,4,2081]{2,1,0:T(4,128)(2,1)}), bf16[16,4,2081]{2,1,0:T(4,128)(2,1)S(1)}, u32[]{:S(2)}, u32[]{:S(2)}) async-start(bf16[16,4,2081]{2,1,0:T(4,128)(2,1)} %reduce_sum.491), calls=%async_computation.5 | async-start | bytes 557056 | tf_op jit(solution)/shard_map/all_to_all | solution.py:290
  229.1 24.3 %all-to-all-start.6 = ((f32[256,1,132]{2,1,0:T(1,128)}), f32[256,1,132]{2,1,0:T(1,128)S(1)}, u32[]{:S(2)}, u32[]{:S(2)}) async-start(f32[256,1,132]{2,1,0:T(1,128)} %broadcast_in_dim.121), calls=%async_computation.6 | async-start | bytes 524288 | tf_op jit(solution)/shard_map/all_to_all | solution.py:294

commit v5 on v4

--- a/solution.py
+++ b/solution.py
@@ -287,13 +287,22 @@
     packed = packed.reshape(outer_count, tm_count, rows // devices, packed.shape[1])
     packed = packed.transpose(1, 0, 2, 3).astype(jnp.bfloat16)
     reduced = lax.all_to_all(packed, "tm", 0, 0, tiled=True).astype(jnp.float32).sum(0)
-    reduced = lax.all_to_all(reduced.astype(jnp.bfloat16), "dp", 0, 0, tiled=True)
-    reduced = reduced.astype(jnp.float32).sum(0)
-    grad_proj = reduced[:, : 4 * width]
-    small_part = reduced[:, 4 * width :].reshape(1, -1)
+    big_cols = 4 * width
+    spare = reduced[:, :, big_cols:].reshape(-1)
+    spare_rows = -(-spare.size // big_cols)
+    spare = jnp.pad(spare, (0, spare_rows * big_cols - spare.size)).reshape(spare_rows, big_cols)
+    body = jnp.concatenate(
+        [reduced[:, :, :big_cols], jnp.broadcast_to(spare, (outer_count,) + spare.shape)], axis=1
+    )
+    body = lax.all_to_all(body.astype(jnp.bfloat16), "dp", 0, 0, tiled=True)
+    body = body.astype(jnp.float32).sum(0)
+    grad_proj = body[: rows // devices]
+    spread = rows // devices * small_width
+    small_part = body[rows // devices :].reshape(1, -1)[:, : outer_count * spread]
     small_all = lax.all_to_all(
-        jnp.broadcast_to(small_part, (devices, small_part.shape[1])), axes, 0, 0, tiled=True
-    )
+        jnp.broadcast_to(small_part, (tm_count, small_part.shape[1])), "tm", 0, 0, tiled=True
+    )
+    small_all = small_all.reshape(tm_count, outer_count, spread).transpose(1, 0, 2)
     small_sum = small_all.reshape(-1)[:small_count]
     conv_sum = small_sum[: conv_term.size].reshape(conv_term.shape)
     gains_sum = small_sum[conv_term.size :].reshape(2, -1)

time: 257 us -> 252 us (0.981)
  waiting for transfers between devices: 66.3 us -> 63 us
  local copies, waits for them, and re-layouts: 11.7 us -> 14.6 us
    all_to_all x2, waiting for transfers between devices: 23.3 us -> 19.7 us  [the longest x1 12.6 us: per_device(): body = lax.all_to_all(body.astype(jnp.bfloat16), 'dp', 0, 0, tiled=True)]
    reduce_sum x1, other arithmetic: 4.98 us -> 1.92 us  [per_device(): lax.all_to_all(packed, 'tm', 0, 0, tiled=True).astype(jnp.float32).sum(0)]
    concatenate x1, local copies, waits for them, and re-layouts: 0.29 us -> 3.28 us  [per_device(): jnp.concatenate([conv_term, gain_attn_term[None], gain_conv_term[None]],...]
where the time goes in v5:
time: 252 us; the launch traced here: 251 us
  waiting for transfers between devices  63 us (25%)
  blocking collectives  59.2 us (23%)
  starting transfers between devices  48.8 us (19%)
  matrix products  38.1 us (15%)
  other arithmetic  25 us (10%)
  local copies, waits for them, and re-layouts  14.6 us (6%)
  between operations  2.65 us (1%)
    all_to_all x1, blocking collectives, per_device(): lax.all_to_all(packed, 'tm', 0, 0, tiled=True).astype(jnp.float32).sum(0)  59.2 us
    all_to_all x1, waiting for transfers between devices, per_device(): lax.all_to_all(jnp.tile(qkv, (halves, 1, 1, 1)), 'tm', 0, 0, tiled=True)  12.9 us
    all_to_all x1, waiting for transfers between devices, per_device(): body = lax.all_to_all(body.astype(jnp.bfloat16), 'dp', 0, 0, tiled=True)  12.6 us
    all_to_all x2, waiting for transfers between devices, to_frames(): lax.all_to_all(blocks, 'tm', 0, 0, tiled=True, axis_index_groups=half_gro...  12 us
    ppermute x2, waiting for transfers between devices, padded_2(): after = lax.ppermute(first, axis, down)  9.62 us
    all_to_all x1, waiting for transfers between devices, per_device(): lax.all_to_all(jnp.tile(send_grad, (halves, 1, 1)), 'tm', 0, 0, tiled=True)  8.85 us
    all_to_all x2, starting transfers between devices, to_frames(): lax.all_to_all(blocks, 'tm', 0, 0, tiled=True, axis_index_groups=half_gro...  8.81 us
    all_to_all x1, starting transfers between devices, per_device(): lax.all_to_all(jnp.tile(qkv, (halves, 1, 1, 1)), 'tm', 0, 0, tiled=True)  8.44 us
  transfers between devices with their start and end apart: 11, of which 8 were waited for; matrix products, arithmetic and copies ran while one was open for 4% of the time, Pallas kernels for 0%

profile of v5, /device:TPU:1, one launch (start us, length us, event | category | flops | bytes accessed | tf_op | source)
XLA Modules:
  0.0 251.3 jit_solution(12152745738050438525)
XLA Ops:
  0.6 1.1 convert_reduce_fusion.2
  1.7 1.2 fusion.42
  2.9 2.6 %fusion.10 = bf16[128,1536]{1,0:T(8,128)(2,1)S(1)} fusion(bf16[1024,2048]{1,0:T(8,128)(2,1)} %param.10, bf16[1,128,1024]{2,1,0:T(8,128)(2,1)} %param.7, f32[1024]{0:T(1024)} %param.11, f32[128]{0:T(128)S(1)} %fusion.112, f32[128]{0:T(128)S(1)} %broadcast_multiply_fusion.1), kind=kOutput, calls=%fused_computation.17 | convolution fusion | flops 403505152 | bytes 3806208 | tf_op jit(solution)/shard_map/dot_general | solution.py:156
  5.6 0.2 copy.150
  5.8 1.1 tile.8
  6.9 8.4 %all-to-all-start = ((bf16[16,128,3,64]{1,3,2,0:T(8,128)(2,1)}), bf16[16,128,3,64]{1,3,2,0:T(8,128)(2,1)S(1)}, u32[]{:S(2)}, u32[]{:S(2)}) async-start(bf16[16,128,3,64]{1,3,2,0:T(8,128)(2,1)} %bitcast.7), calls=%async_computation | async-start | bytes 1572864 | tf_op jit(solution)/shard_map/all_to_all | solution.py:168
  16.0 12.9 %all-to-all-done = bf16[16,128,3,64]{1,3,2,0:T(8,128)(2,1)S(1)} async-done(((bf16[16,128,3,64]{1,3,2,0:T(8,128)(2,1)}), bf16[16,128,3,64]{1,3,2,0:T(8,128)(2,1)S(1)}, u32[]{:S(2)}, u32[]{:S(2)}) %all-to-all-start) | async-done | bytes 786464 | tf_op jit(solution)/shard_map/all_to_all | solution.py:168
  29.0 0.8 fusion.134
  29.8 1.4 fusion.3
  31.2 2.5 fusion
  33.8 1.9 fusion.27
  35.7 0.7 copy_bitcast_fusion.2
  36.4 4.9 %all-to-all-start.1 = ((bf16[8,128,64]{1,2,0:T(8,128)(2,1)}), bf16[8,128,64]{1,2,0:T(8,128)(2,1)S(1)}, u32[]{:S(2)}, u32[]{:S(2)}) async-start(bf16[8,128,64]{1,2,0:T(8,128)(2,1)} %copy_bitcast_fusion.2), calls=%async_computation.1 | async-start | bytes 262144 | tf_op jit(solution)/shard_map/all_to_all | solution.py:185
  41.4 5.8 %all-to-all-done.1 = bf16[8,128,64]{1,2,0:T(8,128)(2,1)S(1)} async-done(((bf16[8,128,64]{1,2,0:T(8,128)(2,1)}), bf16[8,128,64]{1,2,0:T(8,128)(2,1)S(1)}, u32[]{:S(2)}, u32[]{:S(2)}) %all-to-all-start.1) | async-done | bytes 131104 | tf_op jit(solution)/shard_map/all_to_all | solution.py:185
  47.1 1.8 fusion.140
  49.1 0.2 select_convert_fusion
  49.4 3.3 %collective-permute-start = (bf16[15,1024]{1,0:T(8,128)(2,1)S(1)}, bf16[15,1024]{1,0:T(8,128)(2,1)S(1)}, u32[]{:S(2)}, u32[]{:S(2)}) collective-permute-start(bf16[15,1024]{1,0:T(8,128)(2,1)S(1)} %get-tuple-element.49), channel_id=1, source_target_pairs={{0,1},{1,2},{2,3},{3,4},{4,5},{5,6},{6,7},{7,8},{8,9},{9,10},{10,1... | collective-permute-start | bytes 92168 | tf_op jit(solution)/shard_map/ppermute | solution.py:24
  52.7 1.9 collective-permute-start.1
  54.7 4.8 %collective-permute-done.1 = bf16[15,1024]{1,0:T(8,128)(2,1)S(1)} collective-permute-done((bf16[15,1024]{1,0:T(8,128)(2,1)S(1)}, bf16[15,1024]{1,0:T(8,128)(2,1)S(1)}, u32[]{:S(2)}, u32[]{:S(2)}) %collective-permute-start.1) | collective-permute-done | bytes 30752 | tf_op jit(solution)/shard_map/ppermute | solution.py:25
  59.5 4.8 %multiply_reduce_fusion.1 = (bf16[1024]{0:T(1024)(128)(2,1)S(1)}, bf16[1024]{0:T(1024)(128)(2,1)S(1)}, bf16[1024]{0:T(1024)(128)(2,1)S(1)}, bf16[1024]{0:T(1024)...) fusion(f32[158,1024]{1,0:T(8,128)S(1)} %maximum_convert_fusion,, ...), kind=kLoop, calls=%fused_computation.126 | loop fusion | flops 13875200 | bytes 17203200 | tf_op jit(solution)/shard_map/reduce_sum | solution.py:207
  64.3 1.4 multiply_reduce_fusion.19
  65.8 1.9 collective-permute-start.2
  67.7 2.6 %collective-permute-start.3 = (bf16[15,1024]{1,0:T(8,128)(2,1)S(1)}, bf16[15,1024]{1,0:T(8,128)(2,1)S(1)}, u32[]{:S(2)}, u32[]{:S(2)}) collective-permute-start(bf16[15,1024]{1,0:T(8,128)(2,1)S(1)} %get-tuple-element.48), channel_id=1, source_target_pairs={{1,0},{2,1},{3,2},{4,3},{5,4},{6,5},{7,6},{8,7},{9,8},{10,9},{11,1... | collective-permute-start | bytes 92168 | tf_op jit(solution)/shard_map/ppermute | solution.py:25
  70.3 4.9 %collective-permute-done.3 = bf16[15,1024]{1,0:T(8,128)(2,1)S(1)} collective-permute-done((bf16[15,1024]{1,0:T(8,128)(2,1)S(1)}, bf16[15,1024]{1,0:T(8,128)(2,1)S(1)}, u32[]{:S(2)}, u32[]{:S(2)}) %collective-permute-start.3) | collective-permute-done | bytes 30752 | tf_op jit(solution)/shard_map/ppermute | solution.py:25
  75.2 4.1 %multiply_reduce_fusion = (bf16[1024]{0:T(1024)(128)(2,1)}, f32[128]{0:T(128)S(1)}, f32[128,1024]{1,0:T(8,128)S(1)}) fusion(f32[128,1024]{1,0:T(8,128)S(1)} %get-tuple-element.87, f32[128]{0:T(128)S(1)} %fusion.113, f32[128]{0:T(128)S(1)} %broadcast_multiply_fusion, f32[1024]{0:T(1024)S(1)} %copy-done.4, f32[158,1024]{1,0:T(8,128)S(1)} %maximum_convert_fusion.1, ...), kind=kLoop, calls=%fused_computation.125 | loop fusion | flops 9042816 | bytes 17436288 | tf_op jit(solution)/shard_map/transpose(jvp())/reduce_sum | solution.py:33
  79.4 0.3 fusion.132
  79.8 1.5 convolution_convert_fusion.3
  81.5 0.8 tile.20
  82.2 6.0 %all-to-all-start.2 = ((bf16[16,128,64]{1,2,0:T(8,128)(2,1)}), bf16[16,128,64]{1,2,0:T(8,128)(2,1)S(1)}, u32[]{:S(2)}, u32[]{:S(2)}) async-start(bf16[16,128,64]{1,2,0:T(8,128)(2,1)} %bitcast.45), calls=%async_computation.2 | async-start | bytes 524288 | tf_op jit(solution)/shard_map/all_to_all | solution.py:227
  88.2 8.9 %all-to-all-done.2 = bf16[16,128,64]{1,2,0:T(8,128)(2,1)S(1)} async-done(((bf16[16,128,64]{1,2,0:T(8,128)(2,1)}), bf16[16,128,64]{1,2,0:T(8,128)(2,1)S(1)}, u32[]{:S(2)}, u32[]{:S(2)}) %all-to-all-start.2) | async-done | bytes 262176 | tf_op jit(solution)/shard_map/all_to_all | solution.py:227
  97.2 1.2 collective-permute-start.4
  98.3 6.9 %fusion.23 = bf16[8,8,8,128]{3,1,2,0:T(8,128)(2,1)S(1)} fusion(f32[1024,2048]{1,0:T(8,128)} %copy-done, f32[1024]{0:T(1024)S(1)} %multiply_reduce_fusion.34, f32[1024]{0:T(1024)S(1)} %log_add_fusion, pred[2048]{0:T(1024)(128)(4,1)S(1)} %iota_compare_fusion, bf16[2048,64]{0,1:T(8,128)(2,1)S(1)} %copy_bitcast_fusion.1, s32[]{:T(128)S(6)} %select_n.51, ...), kind=kOutput, calls=%fused_computation.32 | convolution fusion | flops 551682048 | bytes 9185284 | tf_op jit(solution)/shard_map/dot_general | solution.py:247
  105.6 6.7 %fusion.2 = (bf16[2048,1024]{0,1:T(8,128)(2,1)}, f32[2048,1024]{0,1:T(8,128)}) fusion(f32[2048]{0:T(1024)S(1)} %bitcast.273, pred[1024]{0:T(1024)(128)(4,1)S(1)} %dynamic-slice.6, bf16[2048,1,64]{0,2,1:T(8,128)(2,1)} %get-tuple-element.44, s32[]{:T(128)S(6)} %select_n.51, bf16[2048,3,64]{0,2,1:T(8,128)(2,1)S(1)} %copy_bitcast_fusion), kind=kOutput, calls=%fused_computation.8 | convolution fusion | flops 278921216 | bytes 12985348 | tf_op jit(solution)/shard_map/dot_general | solution.py:250
  112.3 7.1 %fusion.22 = bf16[8,8,8,128]{3,1,2,0:T(8,128)(2,1)S(1)} fusion(f32[2048,1024]{0,1:T(8,128)} %get-tuple-element.89, f32[2048]{0:T(1024)S(1)} %bitcast.272, f32[2048]{0:T(1024)S(1)} %bitcast.274, pred[1024]{0:T(1024)(128)(4,1)S(1)} %dynamic-slice.6, bf16[2048,1,64]{0,2,1:T(8,128)(2,1)S(1)} %get-tuple-element.43, s32[]{:T(128)S(6)} %select_n.51, ...), kind=kOutput, calls=%fused_computation.31 | convolution fusion | flops 551682048 | bytes 9192452 | tf_op jit(solution)/shard_map/dot_general | solution.py:256
  119.8 3.6 %fusion.21 = bf16[8,128,1,64]{1,3,0,2:T(8,128)(2,1)S(1)} fusion(bf16[8,128,2048]{2,1,0:T(8,128)(2,1)} %bitcast.192, bf16[2048,64,1]{0,1,2:T(8,128)(2,1)S(1)} %reshape.228), kind=kOutput, calls=%fused_computation.30 | convolution fusion | flops 268500992 | bytes 4587520 | tf_op jit(solution)/shard_map/dot_general | solution.py:259
  123.4 0.8 copy.159
  124.2 3.9 %all-to-all-start.3 = ((bf16[8,128,3,64]{1,3,2,0:T(8,128)(2,1)}), bf16[8,128,3,64]{1,3,2,0:T(8,128)(2,1)S(1)}, u32[]{:S(2)}, u32[]{:S(2)}) async-start(bf16[8,128,3,64]{1,3,2,0:T(8,128)(2,1)} %copy.159), calls=%async_computation.3 | async-start | bytes 786432 | tf_op jit(solution)/shard_map/all_to_all | solution.py:185
  128.1 0.2 fusion.80
  129.4 0.4 convolution_convert_fusion.1
  129.8 6.2 %all-to-all-done.3 = bf16[8,128,3,64]{1,3,2,0:T(8,128)(2,1)S(1)} async-done(((bf16[8,128,3,64]{1,3,2,0:T(8,128)(2,1)}), bf16[8,128,3,64]{1,3,2,0:T(8,128)(2,1)S(1)}, u32[]{:S(2)}, u32[]{:S(2)}) %all-to-all-start.3) | async-done | bytes 393248 | tf_op jit(solution)/shard_map/all_to_all | solution.py:185
  136.0 3.1 %fusion.43 = (f32[128]{0:T(128)S(1)}, f32[128,1024]{1,0:T(8,128)S(1)}) fusion(bf16[1,128,1024]{2,1,0:T(8,128)(2,1)S(1)} %copy-done.1, f32[1024]{0:T(1024)S(1)} %copy-done.5, f32[128]{0:T(128)} %copy-done.35, bf16[128,1536]{0,1:T(8,128)(2,1)S(1)} %bitcast.193, bf16[1024,2048]{1,0:T(8,128)(2,1)} %param.10), kind=kOutput, calls=%fused_computation.57 | convolution fusion | flops 403308416 | bytes 4330496 | tf_op jit(solution)/shard_map/dot_general | solution.py:264
  139.2 0.6 multiply_multiply_fusion
  139.8 0.9 fusion.40
  140.8 3.3 %concatenate.33 = bf16[33,1024]{1,0:T(8,128)(2,1)} concatenate(bf16[1,1024]{1,0:T(2,128)(2,1)S(1)} %stack.146, bf16[1,1024]{1,0:T(2,128)(2,1)S(1)} %stack.147, bf16[1,1024]{1,0:T(2,128)(2,1)S(1)} %stack.148, bf16[1,1024]{1,0:T(2,128)(2,1)S(1)} %stack.149, bf16[1,1024]{1,0:T(2,128)(2,1)S(1)} %stack.150, bf16[1,1024]{1,0:T(2,128)(2,1)S(1)} %stack.151, bf16[1,1024]{1,0:T(2,128)(2,1)S(1)} %stack.152, ...), dimensions={0} | concatenate | bytes 135168 | tf_op jit(solution)/shard_map/concatenate | solution.py:279
  144.0 1.5 concatenate.34
  145.6 1.0 convolution_convert_fusion
  146.6 0.5 maximum_bitcast_fusion
  147.1 2.1 copy.168
  149.3 59.2 %all_to_all.36 = bf16[16,16,4,2081]{3,2,1,0:T(4,128)(2,1)S(1)} all-to-all(bf16[16,16,4,2081]{3,2,1,0:T(4,128)(2,1)S(1)} %copy.168), channel_id=1, replica_groups=mesh['dp'=16,'tm'=16] {'tm'}, dimensions={0} | all-to-all | bytes 8523776 | tf_op jit(solution)/shard_map/all_to_all | solution.py:289
  208.4 1.9 convert_reduce_fusion
  210.8 1.0 pad_maximum_fusion
  211.8 8.4 %all-to-all-start.5 = ((bf16[16,6,2048]{2,1,0:T(8,128)(2,1)}), bf16[16,6,2048]{2,1,0:T(8,128)(2,1)S(1)}, u32[]{:S(2)}, u32[]{:S(2)}) async-start(bf16[16,6,2048]{2,1,0:T(8,128)(2,1)} %pad_maximum_fusion), calls=%async_computation.5 | async-start | bytes 1048576 | tf_op jit(solution)/shard_map/all_to_all | solution.py:297
  220.3 1.0 fusion.79
  221.3 12.6 %all-to-all-done.5 = bf16[16,6,2048]{2,1,0:T(8,128)(2,1)S(1)} async-done(((bf16[16,6,2048]{2,1,0:T(8,128)(2,1)}), bf16[16,6,2048]{2,1,0:T(8,128)(2,1)S(1)}, u32[]{:S(2)}, u32[]{:S(2)}) %all-to-all-start.5) | async-done | bytes 393248 | tf_op jit(solution)/shard_map/all_to_all | solution.py:297
  233.8 0.3 convert_reduce_fusion.1
  234.2 0.7 broadcast_in_dim.122
  234.9 6.3 %all-to-all-start.6 = ((f32[16,1,2112]{2,1,0:T(1,128)}), f32[16,1,2112]{2,1,0:T(1,128)S(1)}, u32[]{:S(2)}, u32[]{:S(2)}) async-start(f32[16,1,2112]{2,1,0:T(1,128)} %broadcast_in_dim.122), calls=%async_computation.6 | async-start | bytes 278528 | tf_op jit(solution)/shard_map/all_to_all | solution.py:302
  241.2 0.6 slice_multiply_fusion.32
  241.9 7.1 %all-to-all-done.6 = f32[16,1,2112]{2,1,0:T(1,128)S(1)} async-done(((f32[16,1,2112]{2,1,0:T(1,128)}), f32[16,1,2112]{2,1,0:T(1,128)S(1)}, u32[]{:S(2)}, u32[]{:S(2)}) %all-to-all-start.6) | async-done | bytes 135200 | tf_op jit(solution)/shard_map/all_to_all | solution.py:302
  249.0 0.3 reduce.2
  249.3 0.3 reshape.225
  249.8 0.2 slice.513
  250.0 0.7 slice_multiply_fusion.31
  250.7 0.6 slice_multiply_fusion.33
  (172 shorter events, 2.8 us)
Async XLA Ops:
  1.7 27.2 %copy-start.35 = (f32[128]{0:T(128)}, f32[128]{0:T(128)S(1)}, u32[]{:S(2)}) copy-start(f32[128]{0:T(128)S(1)} %broadcast_multiply_fusion.1) | copy-start | bytes 1540
  2.9 26.0 %copy-start.43 = (f32[128]{0:T(128)}, f32[128]{0:T(128)S(1)}, u32[]{:S(2)}) copy-start(f32[128]{0:T(128)S(1)} %fusion.42) | copy-start | bytes 1540
  2.9 26.0 %copy-start.38 = (f32[128]{0:T(128)}, f32[128]{0:T(128)S(1)}, u32[]{:S(2)}) copy-start(f32[128]{0:T(128)S(1)} %fusion.112) | copy-start | bytes 1540
  6.9 22.0 %all-to-all-start = ((bf16[16,128,3,64]{1,3,2,0:T(8,128)(2,1)}), bf16[16,128,3,64]{1,3,2,0:T(8,128)(2,1)S(1)}, u32[]{:S(2)}, u32[]{:S(2)}) async-start(bf16[16,128,3,64]{1,3,2,0:T(8,128)(2,1)} %bitcast.7), calls=%async_computation | async-start | bytes 1572864 | tf_op jit(solution)/shard_map/all_to_all | solution.py:168
  31.2 4.4 %copy-start = (f32[1024,2048]{1,0:T(8,128)}, f32[1024,2048]{1,0:T(8,128)S(1)}, u32[]{:S(2)}) copy-start(f32[1024,2048]{1,0:T(8,128)S(1)} %get-tuple-element.85) | copy-start | bytes 25165828
  33.7 7.6 %copy-start.3 = (bf16[31,1024]{1,0:T(8,128)(2,1)S(1)}, bf16[31,1024]{1,0:T(8,128)(2,1)}, u32[]{:S(2)}) copy-start(bf16[31,1024]{1,0:T(8,128)(2,1)} %param.13) | copy-start | bytes 190468
  33.7 13.4 %copy-start.1 = (bf16[1,128,1024]{2,1,0:T(8,128)(2,1)S(1)}, bf16[1,128,1024]{2,1,0:T(8,128)(2,1)}, u32[]{:S(2)}) copy-start(bf16[1,128,1024]{2,1,0:T(8,128)(2,1)} %param.7) | copy-start | bytes 786436
  33.7 15.4 %copy-start.4 = (f32[1024]{0:T(1024)S(1)}, f32[1024]{0:T(1024)}, u32[]{:S(2)}) copy-start(f32[1024]{0:T(1024)} %param.12) | copy-start | bytes 12292
  33.8 25.8 %copy-start.2 = (bf16[1,128,1024]{2,1,0:T(8,128)(2,1)S(1)}, bf16[1,128,1024]{2,1,0:T(8,128)(2,1)}, u32[]{:S(2)}) copy-start(bf16[1,128,1024]{2,1,0:T(8,128)(2,1)} %param.8) | copy-start | bytes 786436
  36.4 10.8 %all-to-all-start.1 = ((bf16[8,128,64]{1,2,0:T(8,128)(2,1)}), bf16[8,128,64]{1,2,0:T(8,128)(2,1)S(1)}, u32[]{:S(2)}, u32[]{:S(2)}) async-start(bf16[8,128,64]{1,2,0:T(8,128)(2,1)} %copy_bitcast_fusion.2), calls=%async_computation.1 | async-start | bytes 262144 | tf_op jit(solution)/shard_map/all_to_all | solution.py:185
  49.4 5.3 %collective-permute-start = (bf16[15,1024]{1,0:T(8,128)(2,1)S(1)}, bf16[15,1024]{1,0:T(8,128)(2,1)S(1)}, u32[]{:S(2)}, u32[]{:S(2)}) collective-permute-start(bf16[15,1024]{1,0:T(8,128)(2,1)S(1)} %get-tuple-element.49), channel_id=1, source_target_pairs={{0,1},{1,2},{2,3},{3,4},{4,5},{5,6},{6,7},{7,8},{8,9},{9,10},{10,1... | collective-permute-start | bytes 92168 | tf_op jit(solution)/shard_map/ppermute | solution.py:24
  52.7 6.7 %collective-permute-start.1 = (bf16[15,1024]{1,0:T(8,128)(2,1)S(1)}, bf16[15,1024]{1,0:T(8,128)(2,1)S(1)}, u32[]{:S(2)}, u32[]{:S(2)}) collective-permute-start(bf16[15,1024]{1,0:T(8,128)(2,1)S(1)} %get-tuple-element.50), channel_id=1, source_target_pairs={{1,0},{2,1},{3,2},{4,3},{5,4},{6,5},{7,6},{8,7},{9,8},{10,9},{11,1... | collective-permute-start | bytes 92168 | tf_op jit(solution)/shard_map/ppermute | solution.py:25
  65.8 4.5 %collective-permute-start.2 = (bf16[15,1024]{1,0:T(8,128)(2,1)S(1)}, bf16[15,1024]{1,0:T(8,128)(2,1)S(1)}, u32[]{:S(2)}, u32[]{:S(2)}) collective-permute-start(bf16[15,1024]{1,0:T(8,128)(2,1)S(1)} %get-tuple-element.47), channel_id=1, source_target_pairs={{0,1},{1,2},{2,3},{3,4},{4,5},{5,6},{6,7},{7,8},{8,9},{9,10},{10,1... | collective-permute-start | bytes 92168 | tf_op jit(solution)/shard_map/ppermute | solution.py:24
  67.7 7.5 %collective-permute-start.3 = (bf16[15,1024]{1,0:T(8,128)(2,1)S(1)}, bf16[15,1024]{1,0:T(8,128)(2,1)S(1)}, u32[]{:S(2)}, u32[]{:S(2)}) collective-permute-start(bf16[15,1024]{1,0:T(8,128)(2,1)S(1)} %get-tuple-element.48), channel_id=1, source_target_pairs={{1,0},{2,1},{3,2},{4,3},{5,4},{6,5},{7,6},{8,7},{9,8},{10,9},{11,1... | collective-permute-start | bytes 92168 | tf_op jit(solution)/shard_map/ppermute | solution.py:25
  79.6 25.5 %copy-start.41 = (f32[128]{0:T(128)}, f32[128]{0:T(128)S(1)}, u32[]{:S(2)}) copy-start(f32[128]{0:T(128)S(1)} %negate_multiply_fusion.1) | copy-start | bytes 1540
  82.2 14.8 %all-to-all-start.2 = ((bf16[16,128,64]{1,2,0:T(8,128)(2,1)}), bf16[16,128,64]{1,2,0:T(8,128)(2,1)S(1)}, u32[]{:S(2)}, u32[]{:S(2)}) async-start(bf16[16,128,64]{1,2,0:T(8,128)(2,1)} %bitcast.45), calls=%async_computation.2 | async-start | bytes 524288 | tf_op jit(solution)/shard_map/all_to_all | solution.py:227
  97.2 8.4 %collective-permute-start.4 = (f32[2,1024]{1,0:T(2,128)S(1)}, f32[2,1024]{1,0:T(2,128)S(1)}, u32[]{:S(2)}, u32[]{:S(2)}) collective-permute-start(f32[2,1024]{1,0:T(2,128)S(1)} %pad_maximum_fusion.2), channel_id=1, source_target_pairs={{0,8},{1,9},{2,10},{3,11},{4,12},{5,13},{6,14},{7,15},{8,0},{9,1},... | collective-permute-start | bytes 24584 | tf_op jit(solution)/shard_map/ppermute | solution.py:232
  112.3 15.8 %copy-start.5 = (f32[1024]{0:T(1024)S(1)}, f32[1024]{0:T(1024)}, u32[]{:S(2)}) copy-start(f32[1024]{0:T(1024)} %param.11) | copy-start | bytes 12292
  112.3 15.8 %copy-start.36 = (f32[128]{0:T(128)S(1)}, f32[128]{0:T(128)}, u32[]{:S(2)}) copy-start(f32[128]{0:T(128)} %copy-done.35) | copy-start | bytes 1540
  112.3 15.8 %copy-start.39 = (f32[128]{0:T(128)S(1)}, f32[128]{0:T(128)}, u32[]{:S(2)}) copy-start(f32[128]{0:T(128)} %copy-done.38) | copy-start | bytes 1540
  119.4 9.1 %copy-start.34 = (bf16[1024]{0:T(1024)(128)(2,1)S(1)}, bf16[1024]{0:T(1024)(128)(2,1)}, u32[]{:S(2)}) copy-start(bf16[1024]{0:T(1024)(128)(2,1)} %get-tuple-element.34) | copy-start | bytes 6148
  119.4 9.1 %copy-start.33 = (bf16[1024]{0:T(1024)(128)(2,1)S(1)}, bf16[1024]{0:T(1024)(128)(2,1)}, u32[]{:S(2)}) copy-start(bf16[1024]{0:T(1024)(128)(2,1)} %get-tuple-element.33) | copy-start | bytes 6148
  119.4 9.1 %copy-start.32 = (bf16[1024]{0:T(1024)(128)(2,1)S(1)}, bf16[1024]{0:T(1024)(128)(2,1)}, u32[]{:S(2)}) copy-start(bf16[1024]{0:T(1024)(128)(2,1)} %get-tuple-element.32) | copy-start | bytes 6148
  119.4 9.1 %copy-start.31 = (bf16[1024]{0:T(1024)(128)(2,1)S(1)}, bf16[1024]{0:T(1024)(128)(2,1)}, u32[]{:S(2)}) copy-start(bf16[1024]{0:T(1024)(128)(2,1)} %get-tuple-element.31) | copy-start | bytes 6148
  119.5 9.1 %copy-start.30 = (bf16[1024]{0:T(1024)(128)(2,1)S(1)}, bf16[1024]{0:T(1024)(128)(2,1)}, u32[]{:S(2)}) copy-start(bf16[1024]{0:T(1024)(128)(2,1)} %get-tuple-element.30) | copy-start | bytes 6148
  119.5 9.1 %copy-start.29 = (bf16[1024]{0:T(1024)(128)(2,1)S(1)}, bf16[1024]{0:T(1024)(128)(2,1)}, u32[]{:S(2)}) copy-start(bf16[1024]{0:T(1024)(128)(2,1)} %get-tuple-element.29) | copy-start | bytes 6148
  119.5 9.1 %copy-start.28 = (bf16[1024]{0:T(1024)(128)(2,1)S(1)}, bf16[1024]{0:T(1024)(128)(2,1)}, u32[]{:S(2)}) copy-start(bf16[1024]{0:T(1024)(128)(2,1)} %get-tuple-element.28) | copy-start | bytes 6148
  119.5 9.2 %copy-start.27 = (bf16[1024]{0:T(1024)(128)(2,1)S(1)}, bf16[1024]{0:T(1024)(128)(2,1)}, u32[]{:S(2)}) copy-start(bf16[1024]{0:T(1024)(128)(2,1)} %get-tuple-element.27) | copy-start | bytes 6148
  119.5 9.2 %copy-start.26 = (bf16[1024]{0:T(1024)(128)(2,1)S(1)}, bf16[1024]{0:T(1024)(128)(2,1)}, u32[]{:S(2)}) copy-start(bf16[1024]{0:T(1024)(128)(2,1)} %get-tuple-element.26) | copy-start | bytes 6148
  119.5 9.2 %copy-start.25 = (bf16[1024]{0:T(1024)(128)(2,1)S(1)}, bf16[1024]{0:T(1024)(128)(2,1)}, u32[]{:S(2)}) copy-start(bf16[1024]{0:T(1024)(128)(2,1)} %get-tuple-element.25) | copy-start | bytes 6148
  119.5 9.2 %copy-start.24 = (bf16[1024]{0:T(1024)(128)(2,1)S(1)}, bf16[1024]{0:T(1024)(128)(2,1)}, u32[]{:S(2)}) copy-start(bf16[1024]{0:T(1024)(128)(2,1)} %get-tuple-element.24) | copy-start | bytes 6148
  119.5 9.2 %copy-start.23 = (bf16[1024]{0:T(1024)(128)(2,1)S(1)}, bf16[1024]{0:T(1024)(128)(2,1)}, u32[]{:S(2)}) copy-start(bf16[1024]{0:T(1024)(128)(2,1)} %get-tuple-element.23) | copy-start | bytes 6148
  119.5 9.2 %copy-start.22 = (bf16[1024]{0:T(1024)(128)(2,1)S(1)}, bf16[1024]{0:T(1024)(128)(2,1)}, u32[]{:S(2)}) copy-start(bf16[1024]{0:T(1024)(128)(2,1)} %get-tuple-element.22) | copy-start | bytes 6148
  119.5 9.2 %copy-start.20 = (bf16[1024]{0:T(1024)(128)(2,1)S(1)}, bf16[1024]{0:T(1024)(128)(2,1)}, u32[]{:S(2)}) copy-start(bf16[1024]{0:T(1024)(128)(2,1)} %get-tuple-element.21) | copy-start | bytes 6148
  119.6 9.2 %copy-start.19 = (bf16[1024]{0:T(1024)(128)(2,1)S(1)}, bf16[1024]{0:T(1024)(128)(2,1)}, u32[]{:S(2)}) copy-start(bf16[1024]{0:T(1024)(128)(2,1)} %get-tuple-element.20) | copy-start | bytes 6148
  119.6 9.3 %copy-start.18 = (bf16[1024]{0:T(1024)(128)(2,1)S(1)}, bf16[1024]{0:T(1024)(128)(2,1)}, u32[]{:S(2)}) copy-start(bf16[1024]{0:T(1024)(128)(2,1)} %get-tuple-element.19) | copy-start | bytes 6148
  119.6 9.3 %copy-start.17 = (bf16[1024]{0:T(1024)(128)(2,1)S(1)}, bf16[1024]{0:T(1024)(128)(2,1)}, u32[]{:S(2)}) copy-start(bf16[1024]{0:T(1024)(128)(2,1)} %get-tuple-element.18) | copy-start | bytes 6148
  119.6 9.3 %copy-start.16 = (bf16[1024]{0:T(1024)(128)(2,1)S(1)}, bf16[1024]{0:T(1024)(128)(2,1)}, u32[]{:S(2)}) copy-start(bf16[1024]{0:T(1024)(128)(2,1)} %get-tuple-element.17) | copy-start | bytes 6148
  119.6 9.3 %copy-start.15 = (bf16[1024]{0:T(1024)(128)(2,1)S(1)}, bf16[1024]{0:T(1024)(128)(2,1)}, u32[]{:S(2)}) copy-start(bf16[1024]{0:T(1024)(128)(2,1)} %get-tuple-element.16) | copy-start | bytes 6148
  119.6 9.3 %copy-start.14 = (bf16[1024]{0:T(1024)(128)(2,1)S(1)}, bf16[1024]{0:T(1024)(128)(2,1)}, u32[]{:S(2)}) copy-start(bf16[1024]{0:T(1024)(128)(2,1)} %get-tuple-element.15) | copy-start | bytes 6148
  119.6 9.3 %copy-start.13 = (bf16[1024]{0:T(1024)(128)(2,1)S(1)}, bf16[1024]{0:T(1024)(128)(2,1)}, u32[]{:S(2)}) copy-start(bf16[1024]{0:T(1024)(128)(2,1)} %get-tuple-element.14) | copy-start | bytes 6148
  119.6 9.3 %copy-start.12 = (bf16[1024]{0:T(1024)(128)(2,1)S(1)}, bf16[1024]{0:T(1024)(128)(2,1)}, u32[]{:S(2)}) copy-start(bf16[1024]{0:T(1024)(128)(2,1)} %get-tuple-element.13) | copy-start | bytes 6148
  119.6 9.4 %copy-start.11 = (bf16[1024]{0:T(1024)(128)(2,1)S(1)}, bf16[1024]{0:T(1024)(128)(2,1)}, u32[]{:S(2)}) copy-start(bf16[1024]{0:T(1024)(128)(2,1)} %get-tuple-element.12) | copy-start | bytes 6148
  119.6 9.4 %copy-start.10 = (bf16[1024]{0:T(1024)(128)(2,1)S(1)}, bf16[1024]{0:T(1024)(128)(2,1)}, u32[]{:S(2)}) copy-start(bf16[1024]{0:T(1024)(128)(2,1)} %get-tuple-element.11) | copy-start | bytes 6148
  119.7 9.4 %copy-start.9 = (bf16[1024]{0:T(1024)(128)(2,1)S(1)}, bf16[1024]{0:T(1024)(128)(2,1)}, u32[]{:S(2)}) copy-start(bf16[1024]{0:T(1024)(128)(2,1)} %get-tuple-element.10) | copy-start | bytes 6148
  119.7 9.4 %copy-start.8 = (bf16[1024]{0:T(1024)(128)(2,1)S(1)}, bf16[1024]{0:T(1024)(128)(2,1)}, u32[]{:S(2)}) copy-start(bf16[1024]{0:T(1024)(128)(2,1)} %get-tuple-element.9) | copy-start | bytes 6148
  119.7 9.4 %copy-start.7 = (bf16[1024]{0:T(1024)(128)(2,1)S(1)}, bf16[1024]{0:T(1024)(128)(2,1)}, u32[]{:S(2)}) copy-start(bf16[1024]{0:T(1024)(128)(2,1)} %get-tuple-element.8) | copy-start | bytes 6148
  119.7 9.4 %copy-start.6 = (bf16[1024]{0:T(1024)(128)(2,1)S(1)}, bf16[1024]{0:T(1024)(128)(2,1)}, u32[]{:S(2)}) copy-start(bf16[1024]{0:T(1024)(128)(2,1)} %get-tuple-element.7) | copy-start | bytes 6148
  119.7 9.5 %copy-start.21 = (bf16[1024]{0:T(1024)(128)(2,1)S(1)}, bf16[1024]{0:T(1024)(128)(2,1)}, u32[]{:S(2)}) copy-start(bf16[1024]{0:T(1024)(128)(2,1)} %get-tuple-element.35) | copy-start | bytes 6148
  124.2 11.8 %all-to-all-start.3 = ((bf16[8,128,3,64]{1,3,2,0:T(8,128)(2,1)}), bf16[8,128,3,64]{1,3,2,0:T(8,128)(2,1)S(1)}, u32[]{:S(2)}, u32[]{:S(2)}) async-start(bf16[8,128,3,64]{1,3,2,0:T(8,128)(2,1)} %copy.159), calls=%async_computation.3 | async-start | bytes 786432 | tf_op jit(solution)/shard_map/all_to_all | solution.py:185
  149.2 71.0 %copy-start.37 = (f32[128]{0:T(128)S(1)}, f32[128]{0:T(128)}, u32[]{:S(2)}) copy-start(f32[128]{0:T(128)} %copy-done.35) | copy-start | bytes 1540
  149.3 71.0 %copy-start.40 = (f32[128]{0:T(128)S(1)}, f32[128]{0:T(128)}, u32[]{:S(2)}) copy-start(f32[128]{0:T(128)} %copy-done.38) | copy-start | bytes 1540
  149.3 71.0 %copy-start.42 = (f32[128]{0:T(128)S(1)}, f32[128]{0:T(128)}, u32[]{:S(2)}) copy-start(f32[128]{0:T(128)} %copy-done.41) | copy-start | bytes 1540
  211.8 22.0 %all-to-all-start.5 = ((bf16[16,6,2048]{2,1,0:T(8,128)(2,1)}), bf16[16,6,2048]{2,1,0:T(8,128)(2,1)S(1)}, u32[]{:S(2)}, u32[]{:S(2)}) async-start(bf16[16,6,2048]{2,1,0:T(8,128)(2,1)} %pad_maximum_fusion), calls=%async_computation.5 | async-start | bytes 1048576 | tf_op jit(solution)/shard_map/all_to_all | solution.py:297
  234.9 14.0 %all-to-all-start.6 = ((f32[16,1,2112]{2,1,0:T(1,128)}), f32[16,1,2112]{2,1,0:T(1,128)S(1)}, u32[]{:S(2)}, u32[]{:S(2)}) async-start(f32[16,1,2112]{2,1,0:T(1,128)} %broadcast_in_dim.122), calls=%async_computation.6 | async-start | bytes 278528 | tf_op jit(solution)/shard_map/all_to_all | solution.py:302

commit v6 on v5

--- a/solution.py
+++ b/solution.py
@@ -276,7 +276,8 @@
     axes = ("dp", "tm")
     devices = lax.axis_size(axes)
     rows = inner_part.shape[0]
-    small = jnp.concatenate([conv_term, gain_attn_term[None], gain_conv_term[None]], axis=0)
+    rows_per = rows // devices
+    small = jnp.concatenate([conv_term, gain_conv_term[None]], axis=0)
     small_count = small.size
     small_width = -(-small_count // rows)
     small_flat = jnp.pad(small.reshape(-1), (0, small_width * rows - small_count))
@@ -284,28 +285,41 @@
         [inner_part, outer_part, small_flat.reshape(rows, small_width)], axis=1
     )
     outer_count = lax.axis_size("dp")
-    packed = packed.reshape(outer_count, tm_count, rows // devices, packed.shape[1])
+    packed = packed.reshape(outer_count, tm_count, rows_per, packed.shape[1])
     packed = packed.transpose(1, 0, 2, 3).astype(jnp.bfloat16)
     reduced = lax.all_to_all(packed, "tm", 0, 0, tiled=True).astype(jnp.float32).sum(0)
+    w_rows = w_proj.reshape(outer_count, tm_count, rows_per, 4 * width)
+    w_rows = lax.dynamic_index_in_dim(w_rows, me, 1, keepdims=False)[:, :, : 3 * width]
+    g_rows = lax.dynamic_index_in_dim(
+        gain_attn.reshape(outer_count, tm_count, rows_per), me, 1, keepdims=False
+    )
+    gain_attn_part = (
+        jnp.sum(w_rows.astype(jnp.float32) * reduced[:, :, : 3 * width], axis=-1) / g_rows
+    )
     big_cols = 4 * width
-    spare = reduced[:, :, big_cols:].reshape(-1)
-    spare_rows = -(-spare.size // big_cols)
-    spare = jnp.pad(spare, (0, spare_rows * big_cols - spare.size)).reshape(spare_rows, big_cols)
+    spare = jnp.concatenate(
+        [reduced[:, :, big_cols:].reshape(-1), gain_attn_part.reshape(-1)]
+    )
+    spare_size = spare.size
+    spare_rows = -(-spare_size // big_cols)
+    spare = jnp.pad(spare, (0, spare_rows * big_cols - spare_size)).reshape(spare_rows, big_cols)
     body = jnp.concatenate(
         [reduced[:, :, :big_cols], jnp.broadcast_to(spare, (outer_count,) + spare.shape)], axis=1
     )
     body = lax.all_to_all(body.astype(jnp.bfloat16), "dp", 0, 0, tiled=True)
     body = body.astype(jnp.float32).sum(0)
-    grad_proj = body[: rows // devices]
-    spread = rows // devices * small_width
-    small_part = body[rows // devices :].reshape(1, -1)[:, : outer_count * spread]
+    grad_proj = body[:rows_per]
+    small_part = body[rows_per:].reshape(1, -1)[:, :spare_size]
     small_all = lax.all_to_all(
-        jnp.broadcast_to(small_part, (tm_count, small_part.shape[1])), "tm", 0, 0, tiled=True
-    )
-    small_all = small_all.reshape(tm_count, outer_count, spread).transpose(1, 0, 2)
-    small_sum = small_all.reshape(-1)[:small_count]
+        jnp.broadcast_to(small_part, (tm_count, spare_size)), "tm", 0, 0, tiled=True
+    )
+    spread = outer_count * rows_per * small_width
+    small_sum = small_all[:, :spread].reshape(tm_count, outer_count, rows_per * small_width)
+    small_sum = small_sum.transpose(1, 0, 2).reshape(-1)[:small_count]
+    gain_attn_sum = small_all[:, spread:].reshape(tm_count, outer_count, rows_per)
+    gain_attn_sum = gain_attn_sum.transpose(1, 0, 2).reshape(-1)
     conv_sum = small_sum[: conv_term.size].reshape(conv_term.shape)
-    gains_sum = small_sum[conv_term.size :].reshape(2, -1)
+    gains_sum = jnp.stack([gain_attn_sum, small_sum[conv_term.size :]])
     return (grad_frames, grad_proj * grad_scale, conv_sum * grad_scale, gains_sum * grad_scale)
 
 

time: 252 us -> 261 us (1.036)
  blocking collectives: 59.2 us -> 0 us
  waiting for transfers between devices: 63 us -> 109 us
  starting transfers between devices: 48.8 us -> 64.6 us
  local copies, waits for them, and re-layouts: 14.6 us -> 21.7 us
    all_to_all x1 -> x0, blocking collectives: 59.2 us -> none  [per_device(): lax.all_to_all(packed, 'tm', 0, 0, tiled=True).astype(jnp.float32).sum(0)]
    all_to_all x1 -> x2, waiting for transfers between devices: 7.1 us -> 53.4 us  [the longest x1 46.3 us: per_device(): lax.all_to_all(packed, 'tm', 0, 0, tiled=True).astype(jnp.float32).sum(0)]
    all_to_all x1 -> x2, starting transfers between devices: 6.29 us -> 22.1 us  [the longest x1 16.6 us: per_device(): lax.all_to_all(jnp.broadcast_to(small_part, (tm_count, spare_size)), 'tm'...]
    reshape x2 -> x3, local copies, waits for them, and re-layouts: 0.45 us -> 7.42 us  [the longest x1 7.21 us: per_device(): w_rows = w_proj.reshape(outer_count, tm_count, rows_per, 4 * width)]
    concatenate x1, local copies, waits for them, and re-layouts: 3.28 us -> 0.27 us  [per_device(): small = jnp.concatenate([conv_term, gain_conv_term[None]], axis=0)]
  transfers between devices with their start and end apart: 11 -> 12, of which waited for: 8 -> 9; matrix products, arithmetic and copies ran while one was open for 4% -> 9% of each run, Pallas kernels for 0% -> 0%
where the time goes in v6:
time: 261 us; the launch traced here: 260 us
  waiting for transfers between devices  109 us (42%)
  starting transfers between devices  64.6 us (25%)
  matrix products  39 us (15%)
  other arithmetic  24 us (9%)
  local copies, waits for them, and re-layouts  21.7 us (8%)
    all_to_all x1, waiting for transfers between devices, per_device(): lax.all_to_all(packed, 'tm', 0, 0, tiled=True).astype(jnp.float32).sum(0)  46.3 us
    all_to_all x1, starting transfers between devices, per_device(): lax.all_to_all(jnp.broadcast_to(small_part, (tm_count, spare_size)), 'tm'...  16.6 us
    all_to_all x1, waiting for transfers between devices, per_device(): lax.all_to_all(jnp.tile(qkv, (halves, 1, 1, 1)), 'tm', 0, 0, tiled=True)  12.9 us
    all_to_all x1, waiting for transfers between devices, per_device(): body = lax.all_to_all(body.astype(jnp.bfloat16), 'dp', 0, 0, tiled=True)  12.7 us
    all_to_all x2, waiting for transfers between devices, to_frames(): lax.all_to_all(blocks, 'tm', 0, 0, tiled=True, axis_index_groups=half_gro...  11.1 us
    ppermute x2, waiting for transfers between devices, padded_2(): after = lax.ppermute(first, axis, down)  9.62 us
    all_to_all x1, waiting for transfers between devices, per_device(): lax.all_to_all(jnp.tile(send_grad, (halves, 1, 1)), 'tm', 0, 0, tiled=True)  8.84 us
    all_to_all x2, starting transfers between devices, to_frames(): lax.all_to_all(blocks, 'tm', 0, 0, tiled=True, axis_index_groups=half_gro...  8.82 us
  transfers between devices with their start and end apart: 12, of which 9 were waited for; matrix products, arithmetic and copies ran while one was open for 9% of the time, Pallas kernels for 0%

profile of v6, /device:TPU:1, one launch (start us, length us, event | category | flops | bytes accessed | tf_op | source)
XLA Modules:
  0.0 260.1 jit_solution(15524626967542192064)
XLA Ops:
  0.6 1.1 convert_reduce_fusion.2
  1.7 1.2 fusion.41
  2.9 2.6 %fusion.10 = bf16[128,1536]{1,0:T(8,128)(2,1)S(1)} fusion(bf16[1024,2048]{1,0:T(8,128)(2,1)} %param.10, bf16[1,128,1024]{2,1,0:T(8,128)(2,1)} %param.7, f32[1024]{0:T(1024)} %param.11, f32[128]{0:T(128)S(1)} %fusion.115, f32[128]{0:T(128)S(1)} %broadcast_multiply_fusion.1), kind=kOutput, calls=%fused_computation.17 | convolution fusion | flops 403505152 | bytes 3806208 | tf_op jit(solution)/shard_map/dot_general | solution.py:156
  5.6 0.2 copy.77
  5.8 1.1 tile.8
  6.9 8.4 %all-to-all-start = ((bf16[16,128,3,64]{1,3,2,0:T(8,128)(2,1)}), bf16[16,128,3,64]{1,3,2,0:T(8,128)(2,1)S(1)}, u32[]{:S(2)}, u32[]{:S(2)}) async-start(bf16[16,128,3,64]{1,3,2,0:T(8,128)(2,1)} %bitcast.7), calls=%async_computation | async-start | bytes 1572864 | tf_op jit(solution)/shard_map/all_to_all | solution.py:168
  16.0 12.9 %all-to-all-done = bf16[16,128,3,64]{1,3,2,0:T(8,128)(2,1)S(1)} async-done(((bf16[16,128,3,64]{1,3,2,0:T(8,128)(2,1)}), bf16[16,128,3,64]{1,3,2,0:T(8,128)(2,1)S(1)}, u32[]{:S(2)}, u32[]{:S(2)}) %all-to-all-start) | async-done | bytes 786464 | tf_op jit(solution)/shard_map/all_to_all | solution.py:168
  29.0 0.8 fusion.137
  29.9 1.4 fusion.3
  31.3 2.5 fusion
  33.8 1.9 fusion.30
  35.7 0.7 copy_bitcast_fusion.2
  36.4 4.9 %all-to-all-start.1 = ((bf16[8,128,64]{1,2,0:T(8,128)(2,1)}), bf16[8,128,64]{1,2,0:T(8,128)(2,1)S(1)}, u32[]{:S(2)}, u32[]{:S(2)}) async-start(bf16[8,128,64]{1,2,0:T(8,128)(2,1)} %copy_bitcast_fusion.2), calls=%async_computation.1 | async-start | bytes 262144 | tf_op jit(solution)/shard_map/all_to_all | solution.py:185
  41.4 5.8 %all-to-all-done.1 = bf16[8,128,64]{1,2,0:T(8,128)(2,1)S(1)} async-done(((bf16[8,128,64]{1,2,0:T(8,128)(2,1)}), bf16[8,128,64]{1,2,0:T(8,128)(2,1)S(1)}, u32[]{:S(2)}, u32[]{:S(2)}) %all-to-all-start.1) | async-done | bytes 131104 | tf_op jit(solution)/shard_map/all_to_all | solution.py:185
  47.2 1.8 fusion.143
  49.2 0.2 select_convert_fusion
  49.5 3.3 %collective-permute-start = (bf16[15,1024]{1,0:T(8,128)(2,1)S(1)}, bf16[15,1024]{1,0:T(8,128)(2,1)S(1)}, u32[]{:S(2)}, u32[]{:S(2)}) collective-permute-start(bf16[15,1024]{1,0:T(8,128)(2,1)S(1)} %get-tuple-element.47), channel_id=1, source_target_pairs={{0,1},{1,2},{2,3},{3,4},{4,5},{5,6},{6,7},{7,8},{8,9},{9,10},{10,1... | collective-permute-start | bytes 92168 | tf_op jit(solution)/shard_map/ppermute | solution.py:24
  52.8 1.9 collective-permute-start.1
  54.7 4.8 %collective-permute-done.1 = bf16[15,1024]{1,0:T(8,128)(2,1)S(1)} collective-permute-done((bf16[15,1024]{1,0:T(8,128)(2,1)S(1)}, bf16[15,1024]{1,0:T(8,128)(2,1)S(1)}, u32[]{:S(2)}, u32[]{:S(2)}) %collective-permute-start.1) | collective-permute-done | bytes 30752 | tf_op jit(solution)/shard_map/ppermute | solution.py:25
  59.6 4.2 %multiply_reduce_fusion.1 = (bf16[1024]{0:T(1024)(128)(2,1)S(1)}, bf16[1024]{0:T(1024)(128)(2,1)S(1)}, bf16[1024]{0:T(1024)(128)(2,1)S(1)}, bf16[1024]{0:T(1024)...) fusion(f32[158,1024]{1,0:T(8,128)S(1)} %maximum_convert_fusion,, ...), kind=kLoop, calls=%fused_computation.125 | loop fusion | flops 13875200 | bytes 17203200 | tf_op jit(solution)/shard_map/reduce_sum | solution.py:207
  63.8 0.8 multiply_reduce_fusion.19
  64.6 1.9 collective-permute-start.2
  66.5 2.6 collective-permute-start.3
  69.1 4.9 %collective-permute-done.3 = bf16[15,1024]{1,0:T(8,128)(2,1)S(1)} collective-permute-done((bf16[15,1024]{1,0:T(8,128)(2,1)S(1)}, bf16[15,1024]{1,0:T(8,128)(2,1)S(1)}, u32[]{:S(2)}, u32[]{:S(2)}) %collective-permute-start.3) | collective-permute-done | bytes 30752 | tf_op jit(solution)/shard_map/ppermute | solution.py:25
  74.1 3.6 %multiply_reduce_fusion = (bf16[1024]{0:T(1024)(128)(2,1)S(1)}, f32[128]{0:T(128)S(1)}, f32[128,1024]{1,0:T(8,128)S(1)}) fusion(f32[128,1024]{1,0:T(8,128)S(1)} %get-tuple-element.85, f32[128]{0:T(128)S(1)} %fusion.116, f32[128]{0:T(128)S(1)} %broadcast_multiply_fusion, f32[1024]{0:T(1024)S(1)} %copy-done.5, f32[158,1024]{1,0:T(8,128)S(1)} %maximum_convert_fusion.1, ...), kind=kLoop, calls=%fused_computation.124 | loop fusion | flops 9042816 | bytes 17436288 | tf_op jit(solution)/shard_map/transpose(jvp())/reduce_sum | solution.py:33
  77.7 0.3 fusion.135
  78.1 1.5 convolution_convert_fusion.3
  79.8 0.8 tile.20
  80.5 6.0 %all-to-all-start.2 = ((bf16[16,128,64]{1,2,0:T(8,128)(2,1)}), bf16[16,128,64]{1,2,0:T(8,128)(2,1)S(1)}, u32[]{:S(2)}, u32[]{:S(2)}) async-start(bf16[16,128,64]{1,2,0:T(8,128)(2,1)} %bitcast.45), calls=%async_computation.2 | async-start | bytes 524288 | tf_op jit(solution)/shard_map/all_to_all | solution.py:227
  86.5 8.8 %all-to-all-done.2 = bf16[16,128,64]{1,2,0:T(8,128)(2,1)S(1)} async-done(((bf16[16,128,64]{1,2,0:T(8,128)(2,1)}), bf16[16,128,64]{1,2,0:T(8,128)(2,1)S(1)}, u32[]{:S(2)}, u32[]{:S(2)}) %all-to-all-start.2) | async-done | bytes 262176 | tf_op jit(solution)/shard_map/all_to_all | solution.py:227
  95.5 1.2 collective-permute-start.4
  96.6 6.9 %fusion.26 = bf16[8,8,8,128]{3,1,2,0:T(8,128)(2,1)S(1)} fusion(f32[1024,2048]{1,0:T(8,128)} %copy-done, f32[1024]{0:T(1024)S(1)} %multiply_reduce_fusion.34, f32[1024]{0:T(1024)S(1)} %log_add_fusion, pred[2048]{0:T(1024)(128)(4,1)S(1)} %iota_compare_fusion.1, bf16[2048,64]{0,1:T(8,128)(2,1)S(1)} %copy_bitcast_fusion.1, s32[]{:T(128)S(6)} %select_n.57, ...), kind=kOutput, calls=%fused_computation.33 | convolution fusion | flops 551682048 | bytes 9185284 | tf_op jit(solution)/shard_map/dot_general | solution.py:247
  103.9 6.7 %fusion.2 = (bf16[2048,1024]{0,1:T(8,128)(2,1)}, f32[2048,1024]{0,1:T(8,128)}) fusion(f32[2048]{0:T(1024)S(1)} %bitcast.286, pred[1024]{0:T(1024)(128)(4,1)S(1)} %dynamic-slice.6, bf16[2048,1,64]{0,2,1:T(8,128)(2,1)} %get-tuple-element.42, s32[]{:T(128)S(6)} %select_n.57, bf16[2048,3,64]{0,2,1:T(8,128)(2,1)S(1)} %copy_bitcast_fusion), kind=kOutput, calls=%fused_computation.8 | convolution fusion | flops 278921216 | bytes 12985348 | tf_op jit(solution)/shard_map/dot_general | solution.py:250
  110.6 7.1 %fusion.25 = bf16[8,8,8,128]{3,1,2,0:T(8,128)(2,1)S(1)} fusion(f32[2048,1024]{0,1:T(8,128)} %get-tuple-element.87, f32[2048]{0:T(1024)S(1)} %bitcast.285, f32[2048]{0:T(1024)S(1)} %bitcast.287, pred[1024]{0:T(1024)(128)(4,1)} %copy-done.7, bf16[2048,1,64]{0,2,1:T(8,128)(2,1)S(1)} %copy-done.3, s32[]{:T(128)S(6)} %select_n.57, ...), kind=kOutput, calls=%fused_computation.32 | convolution fusion | flops 551682048 | bytes 9192452 | tf_op jit(solution)/shard_map/dot_general | solution.py:256
  117.8 3.6 %fusion.24 = bf16[8,128,1,64]{1,3,0,2:T(8,128)(2,1)S(1)} fusion(bf16[8,128,2048]{2,1,0:T(8,128)(2,1)} %bitcast.202, bf16[2048,64,1]{0,1,2:T(8,128)(2,1)S(1)} %reshape.236), kind=kOutput, calls=%fused_computation.31 | convolution fusion | flops 268500992 | bytes 4587520 | tf_op jit(solution)/shard_map/dot_general | solution.py:259
  121.5 0.8 copy.86
  122.2 3.9 %all-to-all-start.3 = ((bf16[8,128,3,64]{1,3,2,0:T(8,128)(2,1)}), bf16[8,128,3,64]{1,3,2,0:T(8,128)(2,1)S(1)}, u32[]{:S(2)}, u32[]{:S(2)}) async-start(bf16[8,128,3,64]{1,3,2,0:T(8,128)(2,1)} %copy.86), calls=%async_computation.3 | async-start | bytes 786432 | tf_op jit(solution)/shard_map/all_to_all | solution.py:185
  126.1 0.2 fusion.82
  126.3 0.8 copy.88
  127.6 0.3 concatenate.36
  128.3 0.4 convolution_convert_fusion.1
  128.7 5.4 %all-to-all-done.3 = bf16[8,128,3,64]{1,3,2,0:T(8,128)(2,1)S(1)} async-done(((bf16[8,128,3,64]{1,3,2,0:T(8,128)(2,1)}), bf16[8,128,3,64]{1,3,2,0:T(8,128)(2,1)S(1)}, u32[]{:S(2)}, u32[]{:S(2)}) %all-to-all-start.3) | async-done | bytes 393248 | tf_op jit(solution)/shard_map/all_to_all | solution.py:185
  134.1 1.9 convolution_convert_fusion
  136.0 0.5 maximum_bitcast_fusion
  136.6 4.1 %copy.95 = bf16[16,16,4,2080]{3,2,1,0:T(4,128)(2,1)} copy(bf16[16,16,4,2080]{3,0,2,1:T(8,128)(2,1)S(1)} %maximum_bitcast_fusion) | data formatting | bytes 8519680 | tf_op jit(solution)/shard_map/convert_element_type | solution.py:289
  140.7 5.6 %all-to-all-start.4 = ((bf16[16,16,4,2080]{3,2,1,0:T(4,128)(2,1)}), bf16[16,16,4,2080]{3,2,1,0:T(4,128)(2,1)}, u32[]{:S(2)}, u32[]{:S(2)}) async-start(bf16[16,16,4,2080]{3,2,1,0:T(4,128)(2,1)} %copy.95), calls=%async_computation.4 | async-start | bytes 8912896 | tf_op jit(solution)/shard_map/all_to_all | solution.py:290
  146.3 7.2 %reshape.227 = bf16[16,16,4,2048]{3,2,1,0:T(4,128)(2,1)} reshape(bf16[1024,2048]{1,0:T(8,128)(2,1)} %param.10) | data formatting | bytes 8388608 | tf_op jit(solution)/shard_map/reshape | solution.py:291
  153.7 1.1 dynamic-slice_bitcast_fusion
  154.8 3.1 %fusion.44 = (f32[128]{0:T(128)S(1)}, f32[128,1024]{1,0:T(8,128)S(1)}) fusion(bf16[1,128,1024]{2,1,0:T(8,128)(2,1)S(1)} %copy-done.1, f32[128]{0:T(128)S(1)} %broadcast_multiply_fusion.1, f32[1024]{0:T(1024)S(1)} %copy-done.6, bf16[128,1536]{0,1:T(8,128)(2,1)S(1)} %bitcast.205, bf16[1024,2048]{1,0:T(8,128)(2,1)} %param.10), kind=kOutput, calls=%fused_computation.56 | convolution fusion | flops 403308416 | bytes 4330496 | tf_op jit(solution)/shard_map/dot_general | solution.py:264
  157.9 46.3 %all-to-all-done.4 = bf16[16,16,4,2080]{3,2,1,0:T(4,128)(2,1)} async-done(((bf16[16,16,4,2080]{3,2,1,0:T(4,128)(2,1)}), bf16[16,16,4,2080]{3,2,1,0:T(4,128)(2,1)}, u32[]{:S(2)}, u32[]{:S(2)}) %all-to-all-start.4) | async-done | bytes 4259872 | tf_op jit(solution)/shard_map/all_to_all | solution.py:290
  204.2 4.3 %convert_reduce_fusion = f32[16,4,2080]{2,1,0:T(4,128)S(1)} fusion(bf16[16,16,4,2080]{3,2,1,0:T(4,128)(2,1)} %all-to-all-done.4), kind=kLoop, calls=%fused_computation | loop fusion | flops 4126720 | bytes 4792320 | tf_op jit(solution)/shard_map/reduce_sum | solution.py:290
  209.1 1.0 pad_maximum_fusion
  210.2 8.4 %all-to-all-start.5 = ((bf16[16,6,2048]{2,1,0:T(8,128)(2,1)}), bf16[16,6,2048]{2,1,0:T(8,128)(2,1)S(1)}, u32[]{:S(2)}, u32[]{:S(2)}) async-start(bf16[16,6,2048]{2,1,0:T(8,128)(2,1)} %pad_maximum_fusion), calls=%async_computation.5 | async-start | bytes 1048576 | tf_op jit(solution)/shard_map/all_to_all | solution.py:309
  218.6 0.3 fusion.133
  218.9 1.0 fusion.81
  219.9 12.7 %all-to-all-done.5 = bf16[16,6,2048]{2,1,0:T(8,128)(2,1)S(1)} async-done(((bf16[16,6,2048]{2,1,0:T(8,128)(2,1)}), bf16[16,6,2048]{2,1,0:T(8,128)(2,1)S(1)}, u32[]{:S(2)}, u32[]{:S(2)}) %all-to-all-start.5) | async-done | bytes 393248 | tf_op jit(solution)/shard_map/all_to_all | solution.py:309
  232.7 0.7 broadcast_in_dim.120
  233.4 16.6 %all-to-all-start.6 = ((f32[16,1,2112]{2,1,0:T(1,128)}), f32[16,1,2112]{2,1,0:T(1,128)S(1)}, u32[]{:S(2)}, u32[]{:S(2)}) async-start(f32[16,1,2112]{2,1,0:T(1,128)} %broadcast_in_dim.120), calls=%async_computation.6 | async-start | bytes 278528 | tf_op jit(solution)/shard_map/all_to_all | solution.py:313
  250.0 0.6 slice_multiply_fusion.33
  250.6 7.1 %all-to-all-done.6 = f32[16,1,2112]{2,1,0:T(1,128)S(1)} async-done(((f32[16,1,2112]{2,1,0:T(1,128)}), f32[16,1,2112]{2,1,0:T(1,128)S(1)}, u32[]{:S(2)}, u32[]{:S(2)}) %all-to-all-start.6) | async-done | bytes 135200 | tf_op jit(solution)/shard_map/all_to_all | solution.py:313
  257.7 0.4 copy.96
  258.2 0.3 copy.98
  258.8 0.7 slice_multiply_fusion.32
  259.5 0.6 maximum_multiply_fusion
  (116 shorter events, 3.6 us)
Async XLA Ops:
  2.9 26.0 %copy-start.8 = (f32[128]{0:T(128)}, f32[128]{0:T(128)S(1)}, u32[]{:S(2)}) copy-start(f32[128]{0:T(128)S(1)} %fusion.41) | copy-start | bytes 1540
  6.9 22.0 %all-to-all-start = ((bf16[16,128,3,64]{1,3,2,0:T(8,128)(2,1)}), bf16[16,128,3,64]{1,3,2,0:T(8,128)(2,1)S(1)}, u32[]{:S(2)}, u32[]{:S(2)}) async-start(bf16[16,128,3,64]{1,3,2,0:T(8,128)(2,1)} %bitcast.7), calls=%async_computation | async-start | bytes 1572864 | tf_op jit(solution)/shard_map/all_to_all | solution.py:168
  31.3 4.4 %copy-start = (f32[1024,2048]{1,0:T(8,128)}, f32[1024,2048]{1,0:T(8,128)S(1)}, u32[]{:S(2)}) copy-start(f32[1024,2048]{1,0:T(8,128)S(1)} %get-tuple-element.83) | copy-start | bytes 25165828
  33.8 7.6 %copy-start.4 = (bf16[31,1024]{1,0:T(8,128)(2,1)S(1)}, bf16[31,1024]{1,0:T(8,128)(2,1)}, u32[]{:S(2)}) copy-start(bf16[31,1024]{1,0:T(8,128)(2,1)} %param.13) | copy-start | bytes 190468
  33.8 13.4 %copy-start.1 = (bf16[1,128,1024]{2,1,0:T(8,128)(2,1)S(1)}, bf16[1,128,1024]{2,1,0:T(8,128)(2,1)}, u32[]{:S(2)}) copy-start(bf16[1,128,1024]{2,1,0:T(8,128)(2,1)} %param.7) | copy-start | bytes 786436
  33.8 15.4 %copy-start.5 = (f32[1024]{0:T(1024)S(1)}, f32[1024]{0:T(1024)}, u32[]{:S(2)}) copy-start(f32[1024]{0:T(1024)} %param.12) | copy-start | bytes 12292
  33.8 25.8 %copy-start.2 = (bf16[1,128,1024]{2,1,0:T(8,128)(2,1)S(1)}, bf16[1,128,1024]{2,1,0:T(8,128)(2,1)}, u32[]{:S(2)}) copy-start(bf16[1,128,1024]{2,1,0:T(8,128)(2,1)} %param.8) | copy-start | bytes 786436
  36.4 10.8 %all-to-all-start.1 = ((bf16[8,128,64]{1,2,0:T(8,128)(2,1)}), bf16[8,128,64]{1,2,0:T(8,128)(2,1)S(1)}, u32[]{:S(2)}, u32[]{:S(2)}) async-start(bf16[8,128,64]{1,2,0:T(8,128)(2,1)} %copy_bitcast_fusion.2), calls=%async_computation.1 | async-start | bytes 262144 | tf_op jit(solution)/shard_map/all_to_all | solution.py:185
  49.5 5.3 %collective-permute-start = (bf16[15,1024]{1,0:T(8,128)(2,1)S(1)}, bf16[15,1024]{1,0:T(8,128)(2,1)S(1)}, u32[]{:S(2)}, u32[]{:S(2)}) collective-permute-start(bf16[15,1024]{1,0:T(8,128)(2,1)S(1)} %get-tuple-element.47), channel_id=1, source_target_pairs={{0,1},{1,2},{2,3},{3,4},{4,5},{5,6},{6,7},{7,8},{8,9},{9,10},{10,1... | collective-permute-start | bytes 92168 | tf_op jit(solution)/shard_map/ppermute | solution.py:24
  52.8 6.7 %collective-permute-start.1 = (bf16[15,1024]{1,0:T(8,128)(2,1)S(1)}, bf16[15,1024]{1,0:T(8,128)(2,1)S(1)}, u32[]{:S(2)}, u32[]{:S(2)}) collective-permute-start(bf16[15,1024]{1,0:T(8,128)(2,1)S(1)} %get-tuple-element.48), channel_id=1, source_target_pairs={{1,0},{2,1},{3,2},{4,3},{5,4},{6,5},{7,6},{8,7},{9,8},{10,9},{11,1... | collective-permute-start | bytes 92168 | tf_op jit(solution)/shard_map/ppermute | solution.py:25
  64.6 4.5 %collective-permute-start.2 = (bf16[15,1024]{1,0:T(8,128)(2,1)S(1)}, bf16[15,1024]{1,0:T(8,128)(2,1)S(1)}, u32[]{:S(2)}, u32[]{:S(2)}) collective-permute-start(bf16[15,1024]{1,0:T(8,128)(2,1)S(1)} %get-tuple-element.45), channel_id=1, source_target_pairs={{0,1},{1,2},{2,3},{3,4},{4,5},{5,6},{6,7},{7,8},{8,9},{9,10},{10,1... | collective-permute-start | bytes 92168 | tf_op jit(solution)/shard_map/ppermute | solution.py:24
  66.5 7.5 %collective-permute-start.3 = (bf16[15,1024]{1,0:T(8,128)(2,1)S(1)}, bf16[15,1024]{1,0:T(8,128)(2,1)S(1)}, u32[]{:S(2)}, u32[]{:S(2)}) collective-permute-start(bf16[15,1024]{1,0:T(8,128)(2,1)S(1)} %get-tuple-element.46), channel_id=1, source_target_pairs={{1,0},{2,1},{3,2},{4,3},{5,4},{6,5},{7,6},{8,7},{9,8},{10,9},{11,1... | collective-permute-start | bytes 92168 | tf_op jit(solution)/shard_map/ppermute | solution.py:25
  80.5 14.8 %all-to-all-start.2 = ((bf16[16,128,64]{1,2,0:T(8,128)(2,1)}), bf16[16,128,64]{1,2,0:T(8,128)(2,1)S(1)}, u32[]{:S(2)}, u32[]{:S(2)}) async-start(bf16[16,128,64]{1,2,0:T(8,128)(2,1)} %bitcast.45), calls=%async_computation.2 | async-start | bytes 524288 | tf_op jit(solution)/shard_map/all_to_all | solution.py:227
  86.5 17.4 %copy-start.7 = (pred[1024]{0:T(1024)(128)(4,1)}, pred[1024]{0:T(1024)(128)(4,1)S(1)}, u32[]{:S(2)}) copy-start(pred[1024]{0:T(1024)(128)(4,1)S(1)} %dynamic-slice.6) | copy-start | bytes 3076
  95.5 8.4 %collective-permute-start.4 = (f32[2,1024]{1,0:T(2,128)S(1)}, f32[2,1024]{1,0:T(2,128)S(1)}, u32[]{:S(2)}, u32[]{:S(2)}) collective-permute-start(f32[2,1024]{1,0:T(2,128)S(1)} %pad_maximum_fusion.2), channel_id=1, source_target_pairs={{0,8},{1,9},{2,10},{3,11},{4,12},{5,13},{6,14},{7,15},{8,0},{9,1},... | collective-permute-start | bytes 24584 | tf_op jit(solution)/shard_map/ppermute | solution.py:232
  103.9 6.7 %copy-start.3 = (bf16[2048,1,64]{0,2,1:T(8,128)(2,1)S(1)}, bf16[2048,1,64]{0,2,1:T(8,128)(2,1)}, u32[]{:S(2)}) copy-start(bf16[2048,1,64]{0,2,1:T(8,128)(2,1)} %get-tuple-element.41) | copy-start | bytes 786436
  110.6 15.5 %copy-start.6 = (f32[1024]{0:T(1024)S(1)}, f32[1024]{0:T(1024)}, u32[]{:S(2)}) copy-start(f32[1024]{0:T(1024)} %param.11) | copy-start | bytes 12292
  122.2 11.8 %all-to-all-start.3 = ((bf16[8,128,3,64]{1,3,2,0:T(8,128)(2,1)}), bf16[8,128,3,64]{1,3,2,0:T(8,128)(2,1)S(1)}, u32[]{:S(2)}, u32[]{:S(2)}) async-start(bf16[8,128,3,64]{1,3,2,0:T(8,128)(2,1)} %copy.86), calls=%async_computation.3 | async-start | bytes 786432 | tf_op jit(solution)/shard_map/all_to_all | solution.py:185
  140.7 63.5 %all-to-all-start.4 = ((bf16[16,16,4,2080]{3,2,1,0:T(4,128)(2,1)}), bf16[16,16,4,2080]{3,2,1,0:T(4,128)(2,1)}, u32[]{:S(2)}, u32[]{:S(2)}) async-start(bf16[16,16,4,2080]{3,2,1,0:T(4,128)(2,1)} %copy.95), calls=%async_computation.4 | async-start | bytes 8912896 | tf_op jit(solution)/shard_map/all_to_all | solution.py:290
  153.5 65.1 %copy-start.9 = (f32[128]{0:T(128)S(1)}, f32[128]{0:T(128)}, u32[]{:S(2)}) copy-start(f32[128]{0:T(128)} %copy-done.8) | copy-start | bytes 1540
  210.2 22.4 %all-to-all-start.5 = ((bf16[16,6,2048]{2,1,0:T(8,128)(2,1)}), bf16[16,6,2048]{2,1,0:T(8,128)(2,1)S(1)}, u32[]{:S(2)}, u32[]{:S(2)}) async-start(bf16[16,6,2048]{2,1,0:T(8,128)(2,1)} %pad_maximum_fusion), calls=%async_computation.5 | async-start | bytes 1048576 | tf_op jit(solution)/shard_map/all_to_all | solution.py:309
  233.4 24.3 %all-to-all-start.6 = ((f32[16,1,2112]{2,1,0:T(1,128)}), f32[16,1,2112]{2,1,0:T(1,128)S(1)}, u32[]{:S(2)}, u32[]{:S(2)}) async-start(f32[16,1,2112]{2,1,0:T(1,128)} %broadcast_in_dim.120), calls=%async_computation.6 | async-start | bytes 278528 | tf_op jit(solution)/shard_map/all_to_all | solution.py:313

commit v7 on v5

--- a/solution.py
+++ b/solution.py
@@ -284,9 +284,17 @@
         [inner_part, outer_part, small_flat.reshape(rows, small_width)], axis=1
     )
     outer_count = lax.axis_size("dp")
-    packed = packed.reshape(outer_count, tm_count, rows // devices, packed.shape[1])
-    packed = packed.transpose(1, 0, 2, 3).astype(jnp.bfloat16)
-    reduced = lax.all_to_all(packed, "tm", 0, 0, tiled=True).astype(jnp.float32).sum(0)
+    cores = 2
+    chips = tm_count // cores
+    pairs = [[cores * k + c for c in range(cores)] for k in range(chips)]
+    same_core = [[cores * k + c for k in range(chips)] for c in range(cores)]
+    cols = packed.shape[1]
+    packed = packed.reshape(outer_count, chips, cores, rows // devices, cols)
+    packed = packed.transpose(2, 0, 1, 3, 4).astype(jnp.bfloat16)
+    reduced = lax.all_to_all(packed, "tm", 0, 0, tiled=True, axis_index_groups=pairs)
+    reduced = reduced.astype(jnp.float32).sum(0).transpose(1, 0, 2, 3).astype(jnp.bfloat16)
+    reduced = lax.all_to_all(reduced, "tm", 0, 0, tiled=True, axis_index_groups=same_core)
+    reduced = reduced.astype(jnp.float32).sum(0)
     big_cols = 4 * width
     spare = reduced[:, :, big_cols:].reshape(-1)
     spare_rows = -(-spare.size // big_cols)

time: 252 us -> 235 us (0.933)
  blocking collectives: 59.2 us -> 41.7 us
  local copies, waits for them, and re-layouts: 14.6 us -> 11.1 us
  other arithmetic: 25 us -> 28.3 us
    all_to_all x1 -> x2, blocking collectives: 59.2 us -> 41.7 us  [the longest x1 32.7 us: per_device(): lax.all_to_all(reduced, 'tm', 0, 0, tiled=True, axis_index_groups=same_core)]
    reduce_sum x1 -> x2, other arithmetic: 1.92 us -> 5.09 us  [the longest x1 4.07 us: per_device(): reduced.astype(jnp.float32).sum(0).transpose(1, 0, 2, 3)]
    concatenate x1, local copies, waits for them, and re-layouts: 3.28 us -> 0.29 us  [per_device(): jnp.concatenate([conv_term, gain_attn_term[None], gain_conv_term[None]],...]
  transfers between devices with their start and end apart: 11 -> 11, of which waited for: 8 -> 8; matrix products, arithmetic and copies ran while one was open for 4% -> 5% of each run, Pallas kernels for 0% -> 0%
where the time goes in v7:
time: 235 us; the launch traced here: 234 us
  waiting for transfers between devices  60.8 us (26%)
  starting transfers between devices  50 us (21%)
  blocking collectives  41.7 us (18%)
  matrix products  38.9 us (17%)
  other arithmetic  28.3 us (12%)
  local copies, waits for them, and re-layouts  11.1 us (5%)
  between operations  2.74 us (1%)
    all_to_all x1, blocking collectives, per_device(): lax.all_to_all(reduced, 'tm', 0, 0, tiled=True, axis_index_groups=same_core)  32.7 us
    all_to_all x1, waiting for transfers between devices, per_device(): lax.all_to_all(jnp.tile(qkv, (halves, 1, 1, 1)), 'tm', 0, 0, tiled=True)  12.9 us
    all_to_all x1, waiting for transfers between devices, per_device(): body = lax.all_to_all(body.astype(jnp.bfloat16), 'dp', 0, 0, tiled=True)  11.6 us
    all_to_all x2, waiting for transfers between devices, to_frames(): lax.all_to_all(blocks, 'tm', 0, 0, tiled=True, axis_index_groups=half_gro...  11.3 us
    ppermute x2, waiting for transfers between devices, padded_2(): after = lax.ppermute(first, axis, down)  9.62 us
    all_to_all x1, blocking collectives, per_device(): lax.all_to_all(packed, 'tm', 0, 0, tiled=True, axis_index_groups=pairs)  8.99 us
    all_to_all x2, starting transfers between devices, to_frames(): lax.all_to_all(blocks, 'tm', 0, 0, tiled=True, axis_index_groups=half_gro...  8.82 us
    all_to_all x1, starting transfers between devices, per_device(): lax.all_to_all(jnp.tile(qkv, (halves, 1, 1, 1)), 'tm', 0, 0, tiled=True)  8.43 us
  transfers between devices with their start and end apart: 11, of which 8 were waited for; matrix products, arithmetic and copies ran while one was open for 5% of the time, Pallas kernels for 0%

profile of v7, /device:TPU:1, one launch (start us, length us, event | category | flops | bytes accessed | tf_op | source)
XLA Modules:
  0.0 233.5 jit_solution(14086191151388264246)
XLA Ops:
  0.6 1.1 convert_reduce_fusion.2
  1.7 1.2 fusion.42
  2.9 2.7 %fusion.10 = bf16[128,1536]{1,0:T(8,128)(2,1)S(1)} fusion(bf16[1024,2048]{1,0:T(8,128)(2,1)} %param.10, bf16[1,128,1024]{2,1,0:T(8,128)(2,1)} %param.7, f32[1024]{0:T(1024)} %param.11, f32[128]{0:T(128)S(1)} %fusion.112, f32[128]{0:T(128)S(1)} %broadcast_multiply_fusion.1), kind=kOutput, calls=%fused_computation.17 | convolution fusion | flops 403505152 | bytes 3806208 | tf_op jit(solution)/shard_map/dot_general | solution.py:156
  5.8 1.1 tile.8
  6.9 8.4 %all-to-all-start = ((bf16[16,128,3,64]{1,3,2,0:T(8,128)(2,1)}), bf16[16,128,3,64]{1,3,2,0:T(8,128)(2,1)S(1)}, u32[]{:S(2)}, u32[]{:S(2)}) async-start(bf16[16,128,3,64]{1,3,2,0:T(8,128)(2,1)} %bitcast.7), calls=%async_computation | async-start | bytes 1572864 | tf_op jit(solution)/shard_map/all_to_all | solution.py:168
  16.0 12.9 %all-to-all-done = bf16[16,128,3,64]{1,3,2,0:T(8,128)(2,1)S(1)} async-done(((bf16[16,128,3,64]{1,3,2,0:T(8,128)(2,1)}), bf16[16,128,3,64]{1,3,2,0:T(8,128)(2,1)S(1)}, u32[]{:S(2)}, u32[]{:S(2)}) %all-to-all-start) | async-done | bytes 786464 | tf_op jit(solution)/shard_map/all_to_all | solution.py:168
  29.0 0.8 fusion.134
  29.9 1.4 fusion.3
  31.3 2.5 %fusion = f32[1024]{0:T(1024)S(1)} fusion(f32[1024,2048]{1,0:T(8,128)S(1)} %get-tuple-element.85, f32[1024]{0:T(1024)S(1)} %get-tuple-element.84, pred[2048]{0:T(1024)(128)(4,1)S(1)} %iota_compare_fusion), kind=kLoop, calls=%fused_computation.5 | loop fusion | flops 10484736 | bytes 8398848 | tf_op jit(solution)/shard_map/reduce_sum | solution.py:176
  33.8 1.9 fusion.27
  35.8 0.7 copy_bitcast_fusion.2
  36.4 4.9 %all-to-all-start.1 = ((bf16[8,128,64]{1,2,0:T(8,128)(2,1)}), bf16[8,128,64]{1,2,0:T(8,128)(2,1)S(1)}, u32[]{:S(2)}, u32[]{:S(2)}) async-start(bf16[8,128,64]{1,2,0:T(8,128)(2,1)} %copy_bitcast_fusion.2), calls=%async_computation.1 | async-start | bytes 262144 | tf_op jit(solution)/shard_map/all_to_all | solution.py:185
  41.5 5.8 %all-to-all-done.1 = bf16[8,128,64]{1,2,0:T(8,128)(2,1)S(1)} async-done(((bf16[8,128,64]{1,2,0:T(8,128)(2,1)}), bf16[8,128,64]{1,2,0:T(8,128)(2,1)S(1)}, u32[]{:S(2)}, u32[]{:S(2)}) %all-to-all-start.1) | async-done | bytes 131104 | tf_op jit(solution)/shard_map/all_to_all | solution.py:185
  47.2 1.8 fusion.140
  49.5 3.3 %collective-permute-start = (bf16[15,1024]{1,0:T(8,128)(2,1)S(1)}, bf16[15,1024]{1,0:T(8,128)(2,1)S(1)}, u32[]{:S(2)}, u32[]{:S(2)}) collective-permute-start(bf16[15,1024]{1,0:T(8,128)(2,1)S(1)} %get-tuple-element.49), channel_id=1, source_target_pairs={{0,1},{1,2},{2,3},{3,4},{4,5},{5,6},{6,7},{7,8},{8,9},{9,10},{10,1... | collective-permute-start | bytes 92168 | tf_op jit(solution)/shard_map/ppermute | solution.py:24
  52.8 1.9 collective-permute-start.1
  54.8 4.8 %collective-permute-done.1 = bf16[15,1024]{1,0:T(8,128)(2,1)S(1)} collective-permute-done((bf16[15,1024]{1,0:T(8,128)(2,1)S(1)}, bf16[15,1024]{1,0:T(8,128)(2,1)S(1)}, u32[]{:S(2)}, u32[]{:S(2)}) %collective-permute-start.1) | collective-permute-done | bytes 30752 | tf_op jit(solution)/shard_map/ppermute | solution.py:25
  59.6 4.8 %multiply_reduce_fusion.1 = (bf16[1024]{0:T(1024)(128)(2,1)S(1)}, bf16[1024]{0:T(1024)(128)(2,1)}, bf16[1024]{0:T(1024)(128)(2,1)}, bf16[1024]{0:T(1024)(128)(2,...) fusion(f32[158,1024]{1,0:T(8,128)S(1)} %maximum_convert_fusion,, ...), kind=kLoop, calls=%fused_computation.126 | loop fusion | flops 13875200 | bytes 17203200 | tf_op jit(solution)/shard_map/reduce_sum | solution.py:207
  64.4 1.4 multiply_reduce_fusion.19
  65.9 1.9 collective-permute-start.2
  67.8 2.6 %collective-permute-start.3 = (bf16[15,1024]{1,0:T(8,128)(2,1)S(1)}, bf16[15,1024]{1,0:T(8,128)(2,1)S(1)}, u32[]{:S(2)}, u32[]{:S(2)}) collective-permute-start(bf16[15,1024]{1,0:T(8,128)(2,1)S(1)} %get-tuple-element.48), channel_id=1, source_target_pairs={{1,0},{2,1},{3,2},{4,3},{5,4},{6,5},{7,6},{8,7},{9,8},{10,9},{11,1... | collective-permute-start | bytes 92168 | tf_op jit(solution)/shard_map/ppermute | solution.py:25
  70.4 4.9 %collective-permute-done.3 = bf16[15,1024]{1,0:T(8,128)(2,1)S(1)} collective-permute-done((bf16[15,1024]{1,0:T(8,128)(2,1)S(1)}, bf16[15,1024]{1,0:T(8,128)(2,1)S(1)}, u32[]{:S(2)}, u32[]{:S(2)}) %collective-permute-start.3) | collective-permute-done | bytes 30752 | tf_op jit(solution)/shard_map/ppermute | solution.py:25
  75.3 4.1 %multiply_reduce_fusion = (bf16[1024]{0:T(1024)(128)(2,1)}, f32[128]{0:T(128)S(1)}, f32[128,1024]{1,0:T(8,128)S(1)}) fusion(f32[128,1024]{1,0:T(8,128)S(1)} %get-tuple-element.87, f32[128]{0:T(128)S(1)} %fusion.113, f32[128]{0:T(128)S(1)} %broadcast_multiply_fusion, f32[1024]{0:T(1024)S(1)} %copy-done.8, f32[158,1024]{1,0:T(8,128)S(1)} %maximum_convert_fusion.1, ...), kind=kLoop, calls=%fused_computation.125 | loop fusion | flops 9042816 | bytes 17436288 | tf_op jit(solution)/shard_map/transpose(jvp())/reduce_sum | solution.py:33
  79.9 1.5 convolution_convert_fusion.3
  81.5 0.8 tile.20
  82.3 6.0 %all-to-all-start.2 = ((bf16[16,128,64]{1,2,0:T(8,128)(2,1)}), bf16[16,128,64]{1,2,0:T(8,128)(2,1)S(1)}, u32[]{:S(2)}, u32[]{:S(2)}) async-start(bf16[16,128,64]{1,2,0:T(8,128)(2,1)} %bitcast.45), calls=%async_computation.2 | async-start | bytes 524288 | tf_op jit(solution)/shard_map/all_to_all | solution.py:227
  88.3 0.6 dynamic-slice.6
  88.8 8.3 %all-to-all-done.2 = bf16[16,128,64]{1,2,0:T(8,128)(2,1)S(1)} async-done(((bf16[16,128,64]{1,2,0:T(8,128)(2,1)}), bf16[16,128,64]{1,2,0:T(8,128)(2,1)S(1)}, u32[]{:S(2)}, u32[]{:S(2)}) %all-to-all-start.2) | async-done | bytes 262176 | tf_op jit(solution)/shard_map/all_to_all | solution.py:227
  97.2 0.6 pad_maximum_fusion.2
  97.8 1.1 collective-permute-start.4
  98.9 6.9 %fusion.23 = bf16[8,8,8,128]{3,1,2,0:T(8,128)(2,1)S(1)} fusion(f32[1024,2048]{1,0:T(8,128)} %copy-done, f32[1024]{0:T(1024)S(1)} %multiply_reduce_fusion.34, f32[1024]{0:T(1024)S(1)} %log_add_fusion, pred[2048]{0:T(1024)(128)(4,1)S(1)} %iota_compare_fusion, bf16[2048,64]{0,1:T(8,128)(2,1)S(1)} %copy_bitcast_fusion.1, s32[]{:T(128)S(6)} %select_n.51, ...), kind=kOutput, calls=%fused_computation.32 | convolution fusion | flops 551682048 | bytes 9185284 | tf_op jit(solution)/shard_map/dot_general | solution.py:247
  106.2 0.8 maximum_select_fusion
  107.0 6.5 %fusion.2 = (bf16[2048,1024]{0,1:T(8,128)(2,1)}, f32[2048,1024]{0,1:T(8,128)}) fusion(f32[2048]{0:T(1024)S(1)} %bitcast.275, pred[1024]{0:T(1024)(128)(4,1)} %dynamic-slice.6, bf16[2048,1,64]{0,2,1:T(8,128)(2,1)S(1)} %copy-done.6, s32[]{:T(128)S(6)} %select_n.51, bf16[2048,3,64]{0,2,1:T(8,128)(2,1)S(1)} %copy_bitcast_fusion), kind=kOutput, calls=%fused_computation.7 | convolution fusion | flops 278921216 | bytes 12985348 | tf_op jit(solution)/shard_map/dot_general | solution.py:250
  113.6 7.1 %fusion.22 = bf16[8,8,8,128]{3,1,2,0:T(8,128)(2,1)S(1)} fusion(f32[2048,1024]{0,1:T(8,128)} %get-tuple-element.89, f32[2048]{0:T(1024)S(1)} %bitcast.274, f32[2048]{0:T(1024)} %bitcast.276, pred[1024]{0:T(1024)(128)(4,1)} %dynamic-slice.6, bf16[2048,1,64]{0,2,1:T(8,128)(2,1)S(1)} %copy-done.5, s32[]{:T(128)S(6)} %select_n.51, ...), kind=kOutput, calls=%fused_computation.31 | convolution fusion | flops 551682048 | bytes 9192452 | tf_op jit(solution)/shard_map/dot_general | solution.py:256
  121.1 3.6 %fusion.21 = bf16[8,128,1,64]{1,3,0,2:T(8,128)(2,1)S(1)} fusion(bf16[8,128,2048]{2,1,0:T(8,128)(2,1)} %bitcast.194, bf16[2048,64,1]{0,1,2:T(8,128)(2,1)S(1)} %reshape.228), kind=kOutput, calls=%fused_computation.30 | convolution fusion | flops 268500992 | bytes 4587520 | tf_op jit(solution)/shard_map/dot_general | solution.py:259
  124.7 0.8 copy.169
  125.5 3.9 %all-to-all-start.3 = ((bf16[8,128,3,64]{1,3,2,0:T(8,128)(2,1)}), bf16[8,128,3,64]{1,3,2,0:T(8,128)(2,1)S(1)}, u32[]{:S(2)}, u32[]{:S(2)}) async-start(bf16[8,128,3,64]{1,3,2,0:T(8,128)(2,1)} %copy.169), calls=%async_computation.3 | async-start | bytes 786432 | tf_op jit(solution)/shard_map/all_to_all | solution.py:185
  129.6 0.8 copy.171
  131.3 0.4 convolution_convert_fusion.1
  131.8 5.5 %all-to-all-done.3 = bf16[8,128,3,64]{1,3,2,0:T(8,128)(2,1)S(1)} async-done(((bf16[8,128,3,64]{1,3,2,0:T(8,128)(2,1)}), bf16[8,128,3,64]{1,3,2,0:T(8,128)(2,1)S(1)}, u32[]{:S(2)}, u32[]{:S(2)}) %all-to-all-start.3) | async-done | bytes 393248 | tf_op jit(solution)/shard_map/all_to_all | solution.py:185
  137.3 3.1 %fusion.43 = (f32[128]{0:T(128)S(1)}, f32[128,1024]{1,0:T(8,128)S(1)}) fusion(bf16[1,128,1024]{2,1,0:T(8,128)(2,1)S(1)} %copy-done.1, f32[1024]{0:T(1024)S(1)} %copy-done.9, f32[128]{0:T(128)S(1)} %copy-done.43, bf16[128,1536]{0,1:T(8,128)(2,1)S(1)} %bitcast.195, bf16[1024,2048]{1,0:T(8,128)(2,1)} %param.10), kind=kOutput, calls=%fused_computation.57 | convolution fusion | flops 403308416 | bytes 4330496 | tf_op jit(solution)/shard_map/dot_general | solution.py:264
  140.5 0.3 fusion.40
  141.1 0.6 concatenate.34
  141.8 1.9 convolution_convert_fusion
  143.7 0.5 maximum_bitcast_fusion
  144.2 0.4 copy.178
  144.6 9.0 %all_to_all.41 = bf16[2,16,8,4,2081]{4,2,3,1,0:T(8,128)(2,1)} all-to-all(bf16[2,16,8,4,2081]{4,2,3,1,0:T(8,128)(2,1)S(1)} %copy.178), channel_id=1, replica_groups={{0,1},{2,3},{4,5},{6,7},{8,9},{10,11},{12,13},{14,15},{16,17},{18,19},{..., dimensions={0} | all-to-all | bytes 8523776 | tf_op jit(solution)/shard_map/all_to_all | solution.py:294
  153.6 4.1 %reduce_sum.500 = bf16[16,8,4,2081]{3,1,2,0:T(8,128)(2,1)S(1)} reduce(bf16[2,16,8,4,2081]{4,2,3,1,0:T(8,128)(2,1)} %all_to_all.41, bf16[]{:T(256)} %constant.61.clone.1), dimensions={0}, to_apply=%region_44.45 | reduce | flops 1065472 | bytes 6392834 | tf_op jit(solution)/shard_map/reduce_sum | solution.py:295
  157.7 0.9 copy.180
  158.6 32.7 %all_to_all.42 = bf16[8,16,4,2081]{3,2,1,0:T(4,128)(2,1)S(1)} all-to-all(bf16[8,16,4,2081]{3,2,1,0:T(4,128)(2,1)S(1)} %copy.180), channel_id=1, replica_groups={{0,2,4,6,8,10,12,14},{1,3,5,7,9,11,13,15},{16,18,20,22,24,26,28,30},{17..., dimensions={0} | all-to-all | bytes 4261888 | tf_op jit(solution)/shard_map/all_to_all | solution.py:296
  191.3 1.0 convert_reduce_fusion
  192.7 1.0 pad_maximum_fusion
  193.7 8.4 %all-to-all-start.6 = ((bf16[16,6,2048]{2,1,0:T(8,128)(2,1)}), bf16[16,6,2048]{2,1,0:T(8,128)(2,1)S(1)}, u32[]{:S(2)}, u32[]{:S(2)}) async-start(bf16[16,6,2048]{2,1,0:T(8,128)(2,1)} %pad_maximum_fusion), calls=%async_computation.6 | async-start | bytes 1048576 | tf_op jit(solution)/shard_map/all_to_all | solution.py:305
  202.2 1.0 fusion.79
  203.2 11.6 %all-to-all-done.6 = bf16[16,6,2048]{2,1,0:T(8,128)(2,1)S(1)} async-done(((bf16[16,6,2048]{2,1,0:T(8,128)(2,1)}), bf16[16,6,2048]{2,1,0:T(8,128)(2,1)S(1)}, u32[]{:S(2)}, u32[]{:S(2)}) %all-to-all-start.6) | async-done | bytes 393248 | tf_op jit(solution)/shard_map/all_to_all | solution.py:305
  214.8 0.3 convert_reduce_fusion.1
  215.2 0.7 broadcast_in_dim.122
  215.9 7.6 %all-to-all-start.7 = ((f32[16,1,2112]{2,1,0:T(1,128)}), f32[16,1,2112]{2,1,0:T(1,128)S(1)}, u32[]{:S(2)}, u32[]{:S(2)}) async-start(f32[16,1,2112]{2,1,0:T(1,128)} %broadcast_in_dim.122), calls=%async_computation.7 | async-start | bytes 278528 | tf_op jit(solution)/shard_map/all_to_all | solution.py:310
  223.5 0.6 slice_multiply_fusion.32
  224.1 7.1 %all-to-all-done.7 = f32[16,1,2112]{2,1,0:T(1,128)S(1)} async-done(((f32[16,1,2112]{2,1,0:T(1,128)}), f32[16,1,2112]{2,1,0:T(1,128)S(1)}, u32[]{:S(2)}, u32[]{:S(2)}) %all-to-all-start.7) | async-done | bytes 135200 | tf_op jit(solution)/shard_map/all_to_all | solution.py:310
  231.2 0.3 reduce.3
  231.5 0.3 reshape.225
  232.3 0.7 slice_multiply_fusion.31
  232.9 0.6 slice_multiply_fusion.33
  (191 shorter events, 4.2 us)
Async XLA Ops:
  1.7 27.2 %copy-start.42 = (f32[128]{0:T(128)}, f32[128]{0:T(128)S(1)}, u32[]{:S(2)}) copy-start(f32[128]{0:T(128)S(1)} %broadcast_multiply_fusion.1) | copy-start | bytes 1540
  2.9 26.0 %copy-start.50 = (f32[128]{0:T(128)}, f32[128]{0:T(128)S(1)}, u32[]{:S(2)}) copy-start(f32[128]{0:T(128)S(1)} %fusion.42) | copy-start | bytes 1540
  2.9 26.0 %copy-start.45 = (f32[128]{0:T(128)}, f32[128]{0:T(128)S(1)}, u32[]{:S(2)}) copy-start(f32[128]{0:T(128)S(1)} %fusion.112) | copy-start | bytes 1540
  6.9 22.0 %all-to-all-start = ((bf16[16,128,3,64]{1,3,2,0:T(8,128)(2,1)}), bf16[16,128,3,64]{1,3,2,0:T(8,128)(2,1)S(1)}, u32[]{:S(2)}, u32[]{:S(2)}) async-start(bf16[16,128,3,64]{1,3,2,0:T(8,128)(2,1)} %bitcast.7), calls=%async_computation | async-start | bytes 1572864 | tf_op jit(solution)/shard_map/all_to_all | solution.py:168
  31.3 4.4 %copy-start = (f32[1024,2048]{1,0:T(8,128)}, f32[1024,2048]{1,0:T(8,128)S(1)}, u32[]{:S(2)}) copy-start(f32[1024,2048]{1,0:T(8,128)S(1)} %get-tuple-element.85) | copy-start | bytes 25165828
  33.8 7.6 %copy-start.7 = (bf16[31,1024]{1,0:T(8,128)(2,1)S(1)}, bf16[31,1024]{1,0:T(8,128)(2,1)}, u32[]{:S(2)}) copy-start(bf16[31,1024]{1,0:T(8,128)(2,1)} %param.13) | copy-start | bytes 190468
  33.8 13.4 %copy-start.1 = (bf16[1,128,1024]{2,1,0:T(8,128)(2,1)S(1)}, bf16[1,128,1024]{2,1,0:T(8,128)(2,1)}, u32[]{:S(2)}) copy-start(bf16[1,128,1024]{2,1,0:T(8,128)(2,1)} %param.7) | copy-start | bytes 786436
  33.8 15.4 %copy-start.8 = (f32[1024]{0:T(1024)S(1)}, f32[1024]{0:T(1024)}, u32[]{:S(2)}) copy-start(f32[1024]{0:T(1024)} %param.12) | copy-start | bytes 12292
  33.8 25.8 %copy-start.2 = (bf16[1,128,1024]{2,1,0:T(8,128)(2,1)S(1)}, bf16[1,128,1024]{2,1,0:T(8,128)(2,1)}, u32[]{:S(2)}) copy-start(bf16[1,128,1024]{2,1,0:T(8,128)(2,1)} %param.8) | copy-start | bytes 786436
  36.4 10.8 %all-to-all-start.1 = ((bf16[8,128,64]{1,2,0:T(8,128)(2,1)}), bf16[8,128,64]{1,2,0:T(8,128)(2,1)S(1)}, u32[]{:S(2)}, u32[]{:S(2)}) async-start(bf16[8,128,64]{1,2,0:T(8,128)(2,1)} %copy_bitcast_fusion.2), calls=%async_computation.1 | async-start | bytes 262144 | tf_op jit(solution)/shard_map/all_to_all | solution.py:185
  49.5 5.3 %collective-permute-start = (bf16[15,1024]{1,0:T(8,128)(2,1)S(1)}, bf16[15,1024]{1,0:T(8,128)(2,1)S(1)}, u32[]{:S(2)}, u32[]{:S(2)}) collective-permute-start(bf16[15,1024]{1,0:T(8,128)(2,1)S(1)} %get-tuple-element.49), channel_id=1, source_target_pairs={{0,1},{1,2},{2,3},{3,4},{4,5},{5,6},{6,7},{7,8},{8,9},{9,10},{10,1... | collective-permute-start | bytes 92168 | tf_op jit(solution)/shard_map/ppermute | solution.py:24
  52.8 6.7 %collective-permute-start.1 = (bf16[15,1024]{1,0:T(8,128)(2,1)S(1)}, bf16[15,1024]{1,0:T(8,128)(2,1)S(1)}, u32[]{:S(2)}, u32[]{:S(2)}) collective-permute-start(bf16[15,1024]{1,0:T(8,128)(2,1)S(1)} %get-tuple-element.50), channel_id=1, source_target_pairs={{1,0},{2,1},{3,2},{4,3},{5,4},{6,5},{7,6},{8,7},{9,8},{10,9},{11,1... | collective-permute-start | bytes 92168 | tf_op jit(solution)/shard_map/ppermute | solution.py:25
  65.9 4.5 %collective-permute-start.2 = (bf16[15,1024]{1,0:T(8,128)(2,1)S(1)}, bf16[15,1024]{1,0:T(8,128)(2,1)S(1)}, u32[]{:S(2)}, u32[]{:S(2)}) collective-permute-start(bf16[15,1024]{1,0:T(8,128)(2,1)S(1)} %get-tuple-element.47), channel_id=1, source_target_pairs={{0,1},{1,2},{2,3},{3,4},{4,5},{5,6},{6,7},{7,8},{8,9},{9,10},{10,1... | collective-permute-start | bytes 92168 | tf_op jit(solution)/shard_map/ppermute | solution.py:24
  67.8 7.5 %collective-permute-start.3 = (bf16[15,1024]{1,0:T(8,128)(2,1)S(1)}, bf16[15,1024]{1,0:T(8,128)(2,1)S(1)}, u32[]{:S(2)}, u32[]{:S(2)}) collective-permute-start(bf16[15,1024]{1,0:T(8,128)(2,1)S(1)} %get-tuple-element.48), channel_id=1, source_target_pairs={{1,0},{2,1},{3,2},{4,3},{5,4},{6,5},{7,6},{8,7},{9,8},{10,9},{11,1... | collective-permute-start | bytes 92168 | tf_op jit(solution)/shard_map/ppermute | solution.py:25
  79.7 17.5 %copy-start.48 = (f32[128]{0:T(128)}, f32[128]{0:T(128)S(1)}, u32[]{:S(2)}) copy-start(f32[128]{0:T(128)S(1)} %negate_multiply_fusion.1) | copy-start | bytes 1540
  82.3 14.8 %all-to-all-start.2 = ((bf16[16,128,64]{1,2,0:T(8,128)(2,1)}), bf16[16,128,64]{1,2,0:T(8,128)(2,1)S(1)}, u32[]{:S(2)}, u32[]{:S(2)}) async-start(bf16[16,128,64]{1,2,0:T(8,128)(2,1)} %bitcast.45), calls=%async_computation.2 | async-start | bytes 524288 | tf_op jit(solution)/shard_map/all_to_all | solution.py:227
  97.8 9.1 %copy-start.6 = (bf16[2048,1,64]{0,2,1:T(8,128)(2,1)S(1)}, bf16[2048,1,64]{0,2,1:T(8,128)(2,1)}, u32[]{:S(2)}) copy-start(bf16[2048,1,64]{0,2,1:T(8,128)(2,1)} %get-tuple-element.44) | copy-start | bytes 786436
  97.8 8.3 %collective-permute-start.4 = (f32[2,1024]{1,0:T(2,128)}, f32[2,1024]{1,0:T(2,128)}, u32[]{:S(2)}, u32[]{:S(2)}) collective-permute-start(f32[2,1024]{1,0:T(2,128)} %pad_maximum_fusion.2), channel_id=1, source_target_pairs={{0,8},{1,9},{2,10},{3,11},{4,12},{5,13},{6,14},{7,15},{8,0},{9,1},... | collective-permute-start | bytes 24584 | tf_op jit(solution)/shard_map/ppermute | solution.py:232
  107.0 6.5 %copy-start.41 = (f32[1,2048]{1,0:T(1,128)}, f32[1,2048]{1,0:T(1,128)S(1)}, u32[]{:S(2)}) copy-start(f32[1,2048]{1,0:T(1,128)S(1)} %get-tuple-element.83) | copy-start | bytes 24580
  107.0 6.5 %copy-start.5 = (bf16[2048,1,64]{0,2,1:T(8,128)(2,1)S(1)}, bf16[2048,1,64]{0,2,1:T(8,128)(2,1)}, u32[]{:S(2)}) copy-start(bf16[2048,1,64]{0,2,1:T(8,128)(2,1)} %get-tuple-element.43) | copy-start | bytes 786436
  113.5 15.8 %copy-start.9 = (f32[1024]{0:T(1024)S(1)}, f32[1024]{0:T(1024)}, u32[]{:S(2)}) copy-start(f32[1024]{0:T(1024)} %param.11) | copy-start | bytes 12292
  113.5 15.8 %copy-start.43 = (f32[128]{0:T(128)S(1)}, f32[128]{0:T(128)}, u32[]{:S(2)}) copy-start(f32[128]{0:T(128)} %copy-done.42) | copy-start | bytes 1540
  113.5 15.8 %copy-start.46 = (f32[128]{0:T(128)S(1)}, f32[128]{0:T(128)}, u32[]{:S(2)}) copy-start(f32[128]{0:T(128)} %copy-done.45) | copy-start | bytes 1540
  120.7 9.8 %copy-start.40 = (bf16[1024]{0:T(1024)(128)(2,1)S(1)}, bf16[1024]{0:T(1024)(128)(2,1)}, u32[]{:S(2)}) copy-start(bf16[1024]{0:T(1024)(128)(2,1)} %get-tuple-element.34) | copy-start | bytes 6148
  120.7 9.8 %copy-start.39 = (bf16[1024]{0:T(1024)(128)(2,1)S(1)}, bf16[1024]{0:T(1024)(128)(2,1)}, u32[]{:S(2)}) copy-start(bf16[1024]{0:T(1024)(128)(2,1)} %get-tuple-element.33) | copy-start | bytes 6148
  120.7 9.8 %copy-start.38 = (bf16[1024]{0:T(1024)(128)(2,1)S(1)}, bf16[1024]{0:T(1024)(128)(2,1)}, u32[]{:S(2)}) copy-start(bf16[1024]{0:T(1024)(128)(2,1)} %get-tuple-element.32) | copy-start | bytes 6148
  120.7 9.8 %copy-start.37 = (bf16[1024]{0:T(1024)(128)(2,1)S(1)}, bf16[1024]{0:T(1024)(128)(2,1)}, u32[]{:S(2)}) copy-start(bf16[1024]{0:T(1024)(128)(2,1)} %get-tuple-element.31) | copy-start | bytes 6148
  120.7 9.8 %copy-start.36 = (bf16[1024]{0:T(1024)(128)(2,1)S(1)}, bf16[1024]{0:T(1024)(128)(2,1)}, u32[]{:S(2)}) copy-start(bf16[1024]{0:T(1024)(128)(2,1)} %get-tuple-element.30) | copy-start | bytes 6148
  120.7 9.8 %copy-start.35 = (bf16[1024]{0:T(1024)(128)(2,1)S(1)}, bf16[1024]{0:T(1024)(128)(2,1)}, u32[]{:S(2)}) copy-start(bf16[1024]{0:T(1024)(128)(2,1)} %get-tuple-element.29) | copy-start | bytes 6148
  120.7 9.8 %copy-start.34 = (bf16[1024]{0:T(1024)(128)(2,1)S(1)}, bf16[1024]{0:T(1024)(128)(2,1)}, u32[]{:S(2)}) copy-start(bf16[1024]{0:T(1024)(128)(2,1)} %get-tuple-element.28) | copy-start | bytes 6148
  120.8 9.8 %copy-start.33 = (bf16[1024]{0:T(1024)(128)(2,1)S(1)}, bf16[1024]{0:T(1024)(128)(2,1)}, u32[]{:S(2)}) copy-start(bf16[1024]{0:T(1024)(128)(2,1)} %get-tuple-element.27) | copy-start | bytes 6148
  120.8 9.8 %copy-start.32 = (bf16[1024]{0:T(1024)(128)(2,1)S(1)}, bf16[1024]{0:T(1024)(128)(2,1)}, u32[]{:S(2)}) copy-start(bf16[1024]{0:T(1024)(128)(2,1)} %get-tuple-element.26) | copy-start | bytes 6148
  120.8 9.9 %copy-start.31 = (bf16[1024]{0:T(1024)(128)(2,1)S(1)}, bf16[1024]{0:T(1024)(128)(2,1)}, u32[]{:S(2)}) copy-start(bf16[1024]{0:T(1024)(128)(2,1)} %get-tuple-element.25) | copy-start | bytes 6148
  120.8 9.9 %copy-start.30 = (bf16[1024]{0:T(1024)(128)(2,1)S(1)}, bf16[1024]{0:T(1024)(128)(2,1)}, u32[]{:S(2)}) copy-start(bf16[1024]{0:T(1024)(128)(2,1)} %get-tuple-element.24) | copy-start | bytes 6148
  120.8 9.9 %copy-start.29 = (bf16[1024]{0:T(1024)(128)(2,1)S(1)}, bf16[1024]{0:T(1024)(128)(2,1)}, u32[]{:S(2)}) copy-start(bf16[1024]{0:T(1024)(128)(2,1)} %get-tuple-element.23) | copy-start | bytes 6148
  120.8 9.9 %copy-start.28 = (bf16[1024]{0:T(1024)(128)(2,1)S(1)}, bf16[1024]{0:T(1024)(128)(2,1)}, u32[]{:S(2)}) copy-start(bf16[1024]{0:T(1024)(128)(2,1)} %get-tuple-element.22) | copy-start | bytes 6148
  120.8 9.9 %copy-start.26 = (bf16[1024]{0:T(1024)(128)(2,1)S(1)}, bf16[1024]{0:T(1024)(128)(2,1)}, u32[]{:S(2)}) copy-start(bf16[1024]{0:T(1024)(128)(2,1)} %get-tuple-element.21) | copy-start | bytes 6148
  120.8 9.9 %copy-start.25 = (bf16[1024]{0:T(1024)(128)(2,1)S(1)}, bf16[1024]{0:T(1024)(128)(2,1)}, u32[]{:S(2)}) copy-start(bf16[1024]{0:T(1024)(128)(2,1)} %get-tuple-element.20) | copy-start | bytes 6148
  120.8 9.9 %copy-start.24 = (bf16[1024]{0:T(1024)(128)(2,1)S(1)}, bf16[1024]{0:T(1024)(128)(2,1)}, u32[]{:S(2)}) copy-start(bf16[1024]{0:T(1024)(128)(2,1)} %get-tuple-element.19) | copy-start | bytes 6148
  120.8 9.9 %copy-start.23 = (bf16[1024]{0:T(1024)(128)(2,1)S(1)}, bf16[1024]{0:T(1024)(128)(2,1)}, u32[]{:S(2)}) copy-start(bf16[1024]{0:T(1024)(128)(2,1)} %get-tuple-element.18) | copy-start | bytes 6148
  120.9 10.0 %copy-start.22 = (bf16[1024]{0:T(1024)(128)(2,1)S(1)}, bf16[1024]{0:T(1024)(128)(2,1)}, u32[]{:S(2)}) copy-start(bf16[1024]{0:T(1024)(128)(2,1)} %get-tuple-element.17) | copy-start | bytes 6148
  120.9 10.0 %copy-start.21 = (bf16[1024]{0:T(1024)(128)(2,1)S(1)}, bf16[1024]{0:T(1024)(128)(2,1)}, u32[]{:S(2)}) copy-start(bf16[1024]{0:T(1024)(128)(2,1)} %get-tuple-element.16) | copy-start | bytes 6148
  120.9 10.0 %copy-start.20 = (bf16[1024]{0:T(1024)(128)(2,1)S(1)}, bf16[1024]{0:T(1024)(128)(2,1)}, u32[]{:S(2)}) copy-start(bf16[1024]{0:T(1024)(128)(2,1)} %get-tuple-element.15) | copy-start | bytes 6148
  120.9 10.0 %copy-start.19 = (bf16[1024]{0:T(1024)(128)(2,1)S(1)}, bf16[1024]{0:T(1024)(128)(2,1)}, u32[]{:S(2)}) copy-start(bf16[1024]{0:T(1024)(128)(2,1)} %get-tuple-element.14) | copy-start | bytes 6148
  120.9 10.0 %copy-start.18 = (bf16[1024]{0:T(1024)(128)(2,1)S(1)}, bf16[1024]{0:T(1024)(128)(2,1)}, u32[]{:S(2)}) copy-start(bf16[1024]{0:T(1024)(128)(2,1)} %get-tuple-element.13) | copy-start | bytes 6148
  120.9 10.0 %copy-start.17 = (bf16[1024]{0:T(1024)(128)(2,1)S(1)}, bf16[1024]{0:T(1024)(128)(2,1)}, u32[]{:S(2)}) copy-start(bf16[1024]{0:T(1024)(128)(2,1)} %get-tuple-element.12) | copy-start | bytes 6148
  120.9 10.0 %copy-start.16 = (bf16[1024]{0:T(1024)(128)(2,1)S(1)}, bf16[1024]{0:T(1024)(128)(2,1)}, u32[]{:S(2)}) copy-start(bf16[1024]{0:T(1024)(128)(2,1)} %get-tuple-element.11) | copy-start | bytes 6148
  120.9 10.1 %copy-start.15 = (bf16[1024]{0:T(1024)(128)(2,1)S(1)}, bf16[1024]{0:T(1024)(128)(2,1)}, u32[]{:S(2)}) copy-start(bf16[1024]{0:T(1024)(128)(2,1)} %get-tuple-element.10) | copy-start | bytes 6148
  120.9 10.1 %copy-start.14 = (bf16[1024]{0:T(1024)(128)(2,1)S(1)}, bf16[1024]{0:T(1024)(128)(2,1)}, u32[]{:S(2)}) copy-start(bf16[1024]{0:T(1024)(128)(2,1)} %get-tuple-element.9) | copy-start | bytes 6148
  120.9 10.1 %copy-start.13 = (bf16[1024]{0:T(1024)(128)(2,1)S(1)}, bf16[1024]{0:T(1024)(128)(2,1)}, u32[]{:S(2)}) copy-start(bf16[1024]{0:T(1024)(128)(2,1)} %get-tuple-element.8) | copy-start | bytes 6148
  121.0 10.1 %copy-start.12 = (bf16[1024]{0:T(1024)(128)(2,1)S(1)}, bf16[1024]{0:T(1024)(128)(2,1)}, u32[]{:S(2)}) copy-start(bf16[1024]{0:T(1024)(128)(2,1)} %get-tuple-element.7) | copy-start | bytes 6148
  121.0 10.1 %copy-start.11 = (bf16[1024]{0:T(1024)(128)(2,1)S(1)}, bf16[1024]{0:T(1024)(128)(2,1)}, u32[]{:S(2)}) copy-start(bf16[1024]{0:T(1024)(128)(2,1)} %get-tuple-element.6) | copy-start | bytes 6148
  121.0 10.1 %copy-start.10 = (bf16[1024]{0:T(1024)(128)(2,1)S(1)}, bf16[1024]{0:T(1024)(128)(2,1)}, u32[]{:S(2)}) copy-start(bf16[1024]{0:T(1024)(128)(2,1)} %get-tuple-element.5) | copy-start | bytes 6148
  121.0 10.1 %copy-start.27 = (bf16[1024]{0:T(1024)(128)(2,1)S(1)}, bf16[1024]{0:T(1024)(128)(2,1)}, u32[]{:S(2)}) copy-start(bf16[1024]{0:T(1024)(128)(2,1)} %get-tuple-element.35) | copy-start | bytes 6148
  121.0 19.5 %copy-start.51 = (f32[128]{0:T(128)S(1)}, f32[128]{0:T(128)}, u32[]{:S(2)}) copy-start(f32[128]{0:T(128)} %copy-done.50) | copy-start | bytes 1540
  125.5 11.8 %all-to-all-start.3 = ((bf16[8,128,3,64]{1,3,2,0:T(8,128)(2,1)}), bf16[8,128,3,64]{1,3,2,0:T(8,128)(2,1)S(1)}, u32[]{:S(2)}, u32[]{:S(2)}) async-start(bf16[8,128,3,64]{1,3,2,0:T(8,128)(2,1)} %copy.169), calls=%async_computation.3 | async-start | bytes 786432 | tf_op jit(solution)/shard_map/all_to_all | solution.py:185
  140.5 4.1 %copy-start.3 = (f32[128,1024]{1,0:T(8,128)}, f32[128,1024]{1,0:T(8,128)S(1)}, u32[]{:S(2)}) copy-start(f32[128,1024]{1,0:T(8,128)S(1)} %get-tuple-element.91) | copy-start | bytes 1572868
  157.7 44.5 %copy-start.44 = (f32[128]{0:T(128)S(1)}, f32[128]{0:T(128)}, u32[]{:S(2)}) copy-start(f32[128]{0:T(128)} %copy-done.42) | copy-start | bytes 1540
  157.7 44.5 %copy-start.47 = (f32[128]{0:T(128)S(1)}, f32[128]{0:T(128)}, u32[]{:S(2)}) copy-start(f32[128]{0:T(128)} %copy-done.45) | copy-start | bytes 1540
  157.7 44.5 %copy-start.49 = (f32[128]{0:T(128)S(1)}, f32[128]{0:T(128)}, u32[]{:S(2)}) copy-start(f32[128]{0:T(128)} %copy-done.48) | copy-start | bytes 1540
  158.6 43.6 %copy-start.4 = (f32[128,1024]{1,0:T(8,128)S(1)}, f32[128,1024]{1,0:T(8,128)}, u32[]{:S(2)}) copy-start(f32[128,1024]{1,0:T(8,128)} %copy-done.3) | copy-start | bytes 1572868
  193.7 21.0 %all-to-all-start.6 = ((bf16[16,6,2048]{2,1,0:T(8,128)(2,1)}), bf16[16,6,2048]{2,1,0:T(8,128)(2,1)S(1)}, u32[]{:S(2)}, u32[]{:S(2)}) async-start(bf16[16,6,2048]{2,1,0:T(8,128)(2,1)} %pad_maximum_fusion), calls=%async_computation.6 | async-start | bytes 1048576 | tf_op jit(solution)/shard_map/all_to_all | solution.py:305
  215.9 15.3 %all-to-all-start.7 = ((f32[16,1,2112]{2,1,0:T(1,128)}), f32[16,1,2112]{2,1,0:T(1,128)S(1)}, u32[]{:S(2)}, u32[]{:S(2)}) async-start(f32[16,1,2112]{2,1,0:T(1,128)} %broadcast_in_dim.122), calls=%async_computation.7 | async-start | bytes 278528 | tf_op jit(solution)/shard_map/all_to_all | solution.py:310

commit v8 on v7

--- a/solution.py
+++ b/solution.py
@@ -302,7 +302,14 @@
     body = jnp.concatenate(
         [reduced[:, :, :big_cols], jnp.broadcast_to(spare, (outer_count,) + spare.shape)], axis=1
     )
-    body = lax.all_to_all(body.astype(jnp.bfloat16), "dp", 0, 0, tiled=True)
+    rings = 2
+    ring_size = outer_count // rings
+    across = [[r * ring_size + z for r in range(rings)] for z in range(ring_size)]
+    along = [[r * ring_size + z for z in range(ring_size)] for r in range(rings)]
+    body = body.reshape((rings, ring_size) + body.shape[1:]).astype(jnp.bfloat16)
+    body = lax.all_to_all(body, "dp", 0, 0, tiled=True, axis_index_groups=across)
+    body = body.astype(jnp.float32).sum(0).astype(jnp.bfloat16)
+    body = lax.all_to_all(body, "dp", 0, 0, tiled=True, axis_index_groups=along)
     body = body.astype(jnp.float32).sum(0)
     grad_proj = body[: rows // devices]
     spread = rows // devices * small_width

time: 235 us -> 239 us (1.017)
  blocking collectives: 41.7 us -> 48.8 us
  waiting for transfers between devices: 60.8 us -> 57.7 us
    all_to_all x0 -> x1, blocking collectives: none -> 7.13 us  [per_device(): lax.all_to_all(body, 'dp', 0, 0, tiled=True, axis_index_groups=across)]
    all_to_all x1, waiting for transfers between devices: 11.6 us -> 8.46 us  [per_device(): body = lax.all_to_all(body, 'dp', 0, 0, tiled=True, axis_index_groups=along)]
where the time goes in v8:
time: 239 us; the launch traced here: 238 us
  waiting for transfers between devices  57.7 us (24%)
  starting transfers between devices  50.1 us (21%)
  blocking collectives  48.8 us (20%)
  matrix products  38.9 us (16%)
  other arithmetic  27.3 us (11%)
  local copies, waits for them, and re-layouts  12.2 us (5%)
  between operations  2.74 us (1%)
    all_to_all x1, blocking collectives, per_device(): lax.all_to_all(reduced, 'tm', 0, 0, tiled=True, axis_index_groups=same_core)  32.7 us
    all_to_all x1, waiting for transfers between devices, per_device(): lax.all_to_all(jnp.tile(qkv, (halves, 1, 1, 1)), 'tm', 0, 0, tiled=True)  12.9 us
    all_to_all x2, waiting for transfers between devices, to_frames(): lax.all_to_all(blocks, 'tm', 0, 0, tiled=True, axis_index_groups=half_gro...  11.3 us
    ppermute x2, waiting for transfers between devices, padded_2(): after = lax.ppermute(first, axis, down)  9.62 us
    all_to_all x1, blocking collectives, per_device(): lax.all_to_all(packed, 'tm', 0, 0, tiled=True, axis_index_groups=pairs)  8.99 us
    all_to_all x2, starting transfers between devices, to_frames(): lax.all_to_all(blocks, 'tm', 0, 0, tiled=True, axis_index_groups=half_gro...  8.82 us
    all_to_all x1, waiting for transfers between devices, per_device(): body = lax.all_to_all(body, 'dp', 0, 0, tiled=True, axis_index_groups=along)  8.46 us
    all_to_all x1, starting transfers between devices, per_device(): lax.all_to_all(jnp.tile(qkv, (halves, 1, 1, 1)), 'tm', 0, 0, tiled=True)  8.43 us
  transfers between devices with their start and end apart: 11, of which 8 were waited for; matrix products, arithmetic and copies ran while one was open for 5% of the time, Pallas kernels for 0%

profile of v8, /device:TPU:1, one launch (start us, length us, event | category | flops | bytes accessed | tf_op | source)
XLA Modules:
  0.0 237.7 jit_solution(15663453686381918802)
XLA Ops:
  0.6 1.1 convert_reduce_fusion.1
  1.7 1.2 fusion.42
  2.9 2.7 %fusion.10 = bf16[128,1536]{1,0:T(8,128)(2,1)S(1)} fusion(bf16[1024,2048]{1,0:T(8,128)(2,1)} %param.10, bf16[1,128,1024]{2,1,0:T(8,128)(2,1)} %param.7, f32[1024]{0:T(1024)} %param.11, f32[128]{0:T(128)S(1)} %fusion.112, f32[128]{0:T(128)S(1)} %broadcast_multiply_fusion.1), kind=kOutput, calls=%fused_computation.17 | convolution fusion | flops 403505152 | bytes 3806208 | tf_op jit(solution)/shard_map/dot_general | solution.py:156
  5.8 1.1 tile.8
  6.9 8.4 %all-to-all-start = ((bf16[16,128,3,64]{1,3,2,0:T(8,128)(2,1)}), bf16[16,128,3,64]{1,3,2,0:T(8,128)(2,1)S(1)}, u32[]{:S(2)}, u32[]{:S(2)}) async-start(bf16[16,128,3,64]{1,3,2,0:T(8,128)(2,1)} %bitcast.7), calls=%async_computation | async-start | bytes 1572864 | tf_op jit(solution)/shard_map/all_to_all | solution.py:168
  16.0 12.9 %all-to-all-done = bf16[16,128,3,64]{1,3,2,0:T(8,128)(2,1)S(1)} async-done(((bf16[16,128,3,64]{1,3,2,0:T(8,128)(2,1)}), bf16[16,128,3,64]{1,3,2,0:T(8,128)(2,1)S(1)}, u32[]{:S(2)}, u32[]{:S(2)}) %all-to-all-start) | async-done | bytes 786464 | tf_op jit(solution)/shard_map/all_to_all | solution.py:168
  29.0 0.8 fusion.134
  29.9 1.4 fusion.3
  31.3 2.5 %fusion = f32[1024]{0:T(1024)S(1)} fusion(f32[1024,2048]{1,0:T(8,128)S(1)} %get-tuple-element.85, f32[1024]{0:T(1024)S(1)} %get-tuple-element.84, pred[2048]{0:T(1024)(128)(4,1)S(1)} %iota_compare_fusion), kind=kLoop, calls=%fused_computation.5 | loop fusion | flops 10484736 | bytes 8398848 | tf_op jit(solution)/shard_map/reduce_sum | solution.py:176
  33.8 1.9 fusion.27
  35.8 0.7 copy_bitcast_fusion.2
  36.4 4.9 %all-to-all-start.1 = ((bf16[8,128,64]{1,2,0:T(8,128)(2,1)}), bf16[8,128,64]{1,2,0:T(8,128)(2,1)S(1)}, u32[]{:S(2)}, u32[]{:S(2)}) async-start(bf16[8,128,64]{1,2,0:T(8,128)(2,1)} %copy_bitcast_fusion.2), calls=%async_computation.1 | async-start | bytes 262144 | tf_op jit(solution)/shard_map/all_to_all | solution.py:185
  41.5 5.8 %all-to-all-done.1 = bf16[8,128,64]{1,2,0:T(8,128)(2,1)S(1)} async-done(((bf16[8,128,64]{1,2,0:T(8,128)(2,1)}), bf16[8,128,64]{1,2,0:T(8,128)(2,1)S(1)}, u32[]{:S(2)}, u32[]{:S(2)}) %all-to-all-start.1) | async-done | bytes 131104 | tf_op jit(solution)/shard_map/all_to_all | solution.py:185
  47.2 1.8 fusion.140
  49.5 3.3 %collective-permute-start = (bf16[15,1024]{1,0:T(8,128)(2,1)S(1)}, bf16[15,1024]{1,0:T(8,128)(2,1)S(1)}, u32[]{:S(2)}, u32[]{:S(2)}) collective-permute-start(bf16[15,1024]{1,0:T(8,128)(2,1)S(1)} %get-tuple-element.49), channel_id=1, source_target_pairs={{0,1},{1,2},{2,3},{3,4},{4,5},{5,6},{6,7},{7,8},{8,9},{9,10},{10,1... | collective-permute-start | bytes 92168 | tf_op jit(solution)/shard_map/ppermute | solution.py:24
  52.8 1.9 collective-permute-start.1
  54.8 4.8 %collective-permute-done.1 = bf16[15,1024]{1,0:T(8,128)(2,1)S(1)} collective-permute-done((bf16[15,1024]{1,0:T(8,128)(2,1)S(1)}, bf16[15,1024]{1,0:T(8,128)(2,1)S(1)}, u32[]{:S(2)}, u32[]{:S(2)}) %collective-permute-start.1) | collective-permute-done | bytes 30752 | tf_op jit(solution)/shard_map/ppermute | solution.py:25
  59.6 4.8 %multiply_reduce_fusion.1 = (bf16[1024]{0:T(1024)(128)(2,1)S(1)}, bf16[1024]{0:T(1024)(128)(2,1)}, bf16[1024]{0:T(1024)(128)(2,1)}, bf16[1024]{0:T(1024)(128)(2,...) fusion(f32[158,1024]{1,0:T(8,128)S(1)} %maximum_convert_fusion,, ...), kind=kLoop, calls=%fused_computation.126 | loop fusion | flops 13875200 | bytes 17203200 | tf_op jit(solution)/shard_map/reduce_sum | solution.py:207
  64.4 1.4 multiply_reduce_fusion.19
  65.9 1.9 collective-permute-start.2
  67.8 2.6 %collective-permute-start.3 = (bf16[15,1024]{1,0:T(8,128)(2,1)S(1)}, bf16[15,1024]{1,0:T(8,128)(2,1)S(1)}, u32[]{:S(2)}, u32[]{:S(2)}) collective-permute-start(bf16[15,1024]{1,0:T(8,128)(2,1)S(1)} %get-tuple-element.48), channel_id=1, source_target_pairs={{1,0},{2,1},{3,2},{4,3},{5,4},{6,5},{7,6},{8,7},{9,8},{10,9},{11,1... | collective-permute-start | bytes 92168 | tf_op jit(solution)/shard_map/ppermute | solution.py:25
  70.4 4.9 %collective-permute-done.3 = bf16[15,1024]{1,0:T(8,128)(2,1)S(1)} collective-permute-done((bf16[15,1024]{1,0:T(8,128)(2,1)S(1)}, bf16[15,1024]{1,0:T(8,128)(2,1)S(1)}, u32[]{:S(2)}, u32[]{:S(2)}) %collective-permute-start.3) | collective-permute-done | bytes 30752 | tf_op jit(solution)/shard_map/ppermute | solution.py:25
  75.3 4.1 %multiply_reduce_fusion = (bf16[1024]{0:T(1024)(128)(2,1)}, f32[128]{0:T(128)S(1)}, f32[128,1024]{1,0:T(8,128)S(1)}) fusion(f32[128,1024]{1,0:T(8,128)S(1)} %get-tuple-element.87, f32[128]{0:T(128)S(1)} %fusion.113, f32[128]{0:T(128)S(1)} %broadcast_multiply_fusion, f32[1024]{0:T(1024)S(1)} %copy-done.8, f32[158,1024]{1,0:T(8,128)S(1)} %maximum_convert_fusion.1, ...), kind=kLoop, calls=%fused_computation.125 | loop fusion | flops 9042816 | bytes 17436288 | tf_op jit(solution)/shard_map/transpose(jvp())/reduce_sum | solution.py:33
  79.9 1.5 convolution_convert_fusion.3
  81.5 0.8 tile.20
  82.3 6.0 %all-to-all-start.2 = ((bf16[16,128,64]{1,2,0:T(8,128)(2,1)}), bf16[16,128,64]{1,2,0:T(8,128)(2,1)S(1)}, u32[]{:S(2)}, u32[]{:S(2)}) async-start(bf16[16,128,64]{1,2,0:T(8,128)(2,1)} %bitcast.45), calls=%async_computation.2 | async-start | bytes 524288 | tf_op jit(solution)/shard_map/all_to_all | solution.py:227
  88.3 0.6 dynamic-slice.6
  88.8 8.3 %all-to-all-done.2 = bf16[16,128,64]{1,2,0:T(8,128)(2,1)S(1)} async-done(((bf16[16,128,64]{1,2,0:T(8,128)(2,1)}), bf16[16,128,64]{1,2,0:T(8,128)(2,1)S(1)}, u32[]{:S(2)}, u32[]{:S(2)}) %all-to-all-start.2) | async-done | bytes 262176 | tf_op jit(solution)/shard_map/all_to_all | solution.py:227
  97.2 0.6 pad_maximum_fusion.2
  97.8 1.1 collective-permute-start.4
  98.9 6.9 %fusion.23 = bf16[8,8,8,128]{3,1,2,0:T(8,128)(2,1)S(1)} fusion(f32[1024,2048]{1,0:T(8,128)} %copy-done, f32[1024]{0:T(1024)S(1)} %multiply_reduce_fusion.34, f32[1024]{0:T(1024)S(1)} %log_add_fusion, pred[2048]{0:T(1024)(128)(4,1)S(1)} %iota_compare_fusion, bf16[2048,64]{0,1:T(8,128)(2,1)S(1)} %copy_bitcast_fusion.1, s32[]{:T(128)S(6)} %select_n.51, ...), kind=kOutput, calls=%fused_computation.32 | convolution fusion | flops 551682048 | bytes 9185284 | tf_op jit(solution)/shard_map/dot_general | solution.py:247
  106.2 0.8 maximum_select_fusion
  107.0 6.5 %fusion.2 = (bf16[2048,1024]{0,1:T(8,128)(2,1)}, f32[2048,1024]{0,1:T(8,128)}) fusion(f32[2048]{0:T(1024)S(1)} %bitcast.277, pred[1024]{0:T(1024)(128)(4,1)} %dynamic-slice.6, bf16[2048,1,64]{0,2,1:T(8,128)(2,1)S(1)} %copy-done.6, s32[]{:T(128)S(6)} %select_n.51, bf16[2048,3,64]{0,2,1:T(8,128)(2,1)S(1)} %copy_bitcast_fusion), kind=kOutput, calls=%fused_computation.7 | convolution fusion | flops 278921216 | bytes 12985348 | tf_op jit(solution)/shard_map/dot_general | solution.py:250
  113.6 7.1 %fusion.22 = bf16[8,8,8,128]{3,1,2,0:T(8,128)(2,1)S(1)} fusion(f32[2048,1024]{0,1:T(8,128)} %get-tuple-element.89, f32[2048]{0:T(1024)S(1)} %bitcast.276, f32[2048]{0:T(1024)} %bitcast.278, pred[1024]{0:T(1024)(128)(4,1)} %dynamic-slice.6, bf16[2048,1,64]{0,2,1:T(8,128)(2,1)S(1)} %copy-done.5, s32[]{:T(128)S(6)} %select_n.51, ...), kind=kOutput, calls=%fused_computation.31 | convolution fusion | flops 551682048 | bytes 9192452 | tf_op jit(solution)/shard_map/dot_general | solution.py:256
  121.1 3.6 %fusion.21 = bf16[8,128,1,64]{1,3,0,2:T(8,128)(2,1)S(1)} fusion(bf16[8,128,2048]{2,1,0:T(8,128)(2,1)} %bitcast.195, bf16[2048,64,1]{0,1,2:T(8,128)(2,1)S(1)} %reshape.230), kind=kOutput, calls=%fused_computation.30 | convolution fusion | flops 268500992 | bytes 4587520 | tf_op jit(solution)/shard_map/dot_general | solution.py:259
  124.7 0.8 copy.150
  125.5 3.9 %all-to-all-start.3 = ((bf16[8,128,3,64]{1,3,2,0:T(8,128)(2,1)}), bf16[8,128,3,64]{1,3,2,0:T(8,128)(2,1)S(1)}, u32[]{:S(2)}, u32[]{:S(2)}) async-start(bf16[8,128,3,64]{1,3,2,0:T(8,128)(2,1)} %copy.150), calls=%async_computation.3 | async-start | bytes 786432 | tf_op jit(solution)/shard_map/all_to_all | solution.py:185
  129.6 0.8 copy.152
  131.3 0.4 convolution_convert_fusion.1
  131.8 5.5 %all-to-all-done.3 = bf16[8,128,3,64]{1,3,2,0:T(8,128)(2,1)S(1)} async-done(((bf16[8,128,3,64]{1,3,2,0:T(8,128)(2,1)}), bf16[8,128,3,64]{1,3,2,0:T(8,128)(2,1)S(1)}, u32[]{:S(2)}, u32[]{:S(2)}) %all-to-all-start.3) | async-done | bytes 393248 | tf_op jit(solution)/shard_map/all_to_all | solution.py:185
  137.3 3.1 %fusion.43 = (f32[128]{0:T(128)S(1)}, f32[128,1024]{1,0:T(8,128)S(1)}) fusion(bf16[1,128,1024]{2,1,0:T(8,128)(2,1)S(1)} %copy-done.1, f32[1024]{0:T(1024)S(1)} %copy-done.9, f32[128]{0:T(128)S(1)} %copy-done.43, bf16[128,1536]{0,1:T(8,128)(2,1)S(1)} %bitcast.197, bf16[1024,2048]{1,0:T(8,128)(2,1)} %param.10), kind=kOutput, calls=%fused_computation.56 | convolution fusion | flops 403308416 | bytes 4330496 | tf_op jit(solution)/shard_map/dot_general | solution.py:264
  140.5 0.3 fusion.40
  141.1 0.6 concatenate.34
  141.8 1.9 convolution_convert_fusion
  143.7 0.5 maximum_bitcast_fusion
  144.2 0.4 copy.159
  144.6 9.0 %all_to_all.46 = bf16[2,16,8,4,2081]{4,2,3,1,0:T(8,128)(2,1)} all-to-all(bf16[2,16,8,4,2081]{4,2,3,1,0:T(8,128)(2,1)S(1)} %copy.159), channel_id=1, replica_groups={{0,1},{2,3},{4,5},{6,7},{8,9},{10,11},{12,13},{14,15},{16,17},{18,19},{..., dimensions={0} | all-to-all | bytes 8523776 | tf_op jit(solution)/shard_map/all_to_all | solution.py:294
  153.6 4.1 %reduce_sum.512 = bf16[16,8,4,2081]{3,1,2,0:T(8,128)(2,1)S(1)} reduce(bf16[2,16,8,4,2081]{4,2,3,1,0:T(8,128)(2,1)} %all_to_all.46, bf16[]{:T(256)} %constant.62.clone.1), dimensions={0}, to_apply=%region_44.45 | reduce | flops 1065472 | bytes 6392834 | tf_op jit(solution)/shard_map/reduce_sum | solution.py:295
  157.7 0.9 copy.161
  158.6 32.7 %all_to_all.47 = bf16[8,16,4,2081]{3,2,1,0:T(4,128)(2,1)S(1)} all-to-all(bf16[8,16,4,2081]{3,2,1,0:T(4,128)(2,1)S(1)} %copy.161), channel_id=1, replica_groups={{0,2,4,6,8,10,12,14},{1,3,5,7,9,11,13,15},{16,18,20,22,24,26,28,30},{17..., dimensions={0} | all-to-all | bytes 4261888 | tf_op jit(solution)/shard_map/all_to_all | solution.py:296
  191.3 1.0 convert_reduce_fusion
  193.2 7.1 %all_to_all.48 = bf16[2,8,6,2048]{3,1,2,0:T(8,128)(2,1)S(1)} all-to-all(bf16[2,8,6,2048]{3,1,2,0:T(8,128)(2,1)S(1)} %copy.163), channel_id=1, replica_groups={{0,128},{16,144},{32,160},{48,176},{64,192},{80,208},{96,224},{112,240}..., dimensions={0} | all-to-all | bytes 786432 | tf_op jit(solution)/shard_map/all_to_all | solution.py:310
  200.4 0.8 copy.164
  201.2 8.2 %all-to-all-start.7 = ((bf16[8,6,2048]{2,1,0:T(8,128)(2,1)}), bf16[8,6,2048]{2,1,0:T(8,128)(2,1)S(1)}, u32[]{:S(2)}, u32[]{:S(2)}) async-start(bf16[8,6,2048]{2,1,0:T(8,128)(2,1)} %copy.164), calls=%async_computation.7 | async-start | bytes 524288 | tf_op jit(solution)/shard_map/all_to_all | solution.py:312
  209.4 1.0 fusion.79
  210.4 8.5 %all-to-all-done.7 = bf16[8,6,2048]{2,1,0:T(8,128)(2,1)S(1)} async-done(((bf16[8,6,2048]{2,1,0:T(8,128)(2,1)}), bf16[8,6,2048]{2,1,0:T(8,128)(2,1)S(1)}, u32[]{:S(2)}, u32[]{:S(2)}) %all-to-all-start.7) | async-done | bytes 196640 | tf_op jit(solution)/shard_map/all_to_all | solution.py:312
  219.0 0.7 broadcast_in_dim.122
  219.7 7.9 %all-to-all-start.8 = ((f32[16,1,2112]{2,1,0:T(1,128)}), f32[16,1,2112]{2,1,0:T(1,128)S(1)}, u32[]{:S(2)}, u32[]{:S(2)}) async-start(f32[16,1,2112]{2,1,0:T(1,128)} %broadcast_in_dim.122), calls=%async_computation.8 | async-start | bytes 278528 | tf_op jit(solution)/shard_map/all_to_all | solution.py:317
  227.6 0.6 slice_multiply_fusion.32
  228.2 7.2 %all-to-all-done.8 = f32[16,1,2112]{2,1,0:T(1,128)S(1)} async-done(((f32[16,1,2112]{2,1,0:T(1,128)}), f32[16,1,2112]{2,1,0:T(1,128)S(1)}, u32[]{:S(2)}, u32[]{:S(2)}) %all-to-all-start.8) | async-done | bytes 135200 | tf_op jit(solution)/shard_map/all_to_all | solution.py:317
  235.4 0.3 reduce.4
  235.7 0.3 reshape.227
  236.5 0.7 slice_multiply_fusion.31
  237.1 0.6 slice_multiply_fusion.33
  (195 shorter events, 4.8 us)
Async XLA Ops:
  1.7 27.2 %copy-start.42 = (f32[128]{0:T(128)}, f32[128]{0:T(128)S(1)}, u32[]{:S(2)}) copy-start(f32[128]{0:T(128)S(1)} %broadcast_multiply_fusion.1) | copy-start | bytes 1540
  2.9 26.0 %copy-start.50 = (f32[128]{0:T(128)}, f32[128]{0:T(128)S(1)}, u32[]{:S(2)}) copy-start(f32[128]{0:T(128)S(1)} %fusion.42) | copy-start | bytes 1540
  2.9 26.0 %copy-start.45 = (f32[128]{0:T(128)}, f32[128]{0:T(128)S(1)}, u32[]{:S(2)}) copy-start(f32[128]{0:T(128)S(1)} %fusion.112) | copy-start | bytes 1540
  6.9 22.0 %all-to-all-start = ((bf16[16,128,3,64]{1,3,2,0:T(8,128)(2,1)}), bf16[16,128,3,64]{1,3,2,0:T(8,128)(2,1)S(1)}, u32[]{:S(2)}, u32[]{:S(2)}) async-start(bf16[16,128,3,64]{1,3,2,0:T(8,128)(2,1)} %bitcast.7), calls=%async_computation | async-start | bytes 1572864 | tf_op jit(solution)/shard_map/all_to_all | solution.py:168
  31.3 4.4 %copy-start = (f32[1024,2048]{1,0:T(8,128)}, f32[1024,2048]{1,0:T(8,128)S(1)}, u32[]{:S(2)}) copy-start(f32[1024,2048]{1,0:T(8,128)S(1)} %get-tuple-element.85) | copy-start | bytes 25165828
  33.8 7.6 %copy-start.7 = (bf16[31,1024]{1,0:T(8,128)(2,1)S(1)}, bf16[31,1024]{1,0:T(8,128)(2,1)}, u32[]{:S(2)}) copy-start(bf16[31,1024]{1,0:T(8,128)(2,1)} %param.13) | copy-start | bytes 190468
  33.8 13.4 %copy-start.1 = (bf16[1,128,1024]{2,1,0:T(8,128)(2,1)S(1)}, bf16[1,128,1024]{2,1,0:T(8,128)(2,1)}, u32[]{:S(2)}) copy-start(bf16[1,128,1024]{2,1,0:T(8,128)(2,1)} %param.7) | copy-start | bytes 786436
  33.8 15.4 %copy-start.8 = (f32[1024]{0:T(1024)S(1)}, f32[1024]{0:T(1024)}, u32[]{:S(2)}) copy-start(f32[1024]{0:T(1024)} %param.12) | copy-start | bytes 12292
  33.8 25.8 %copy-start.2 = (bf16[1,128,1024]{2,1,0:T(8,128)(2,1)S(1)}, bf16[1,128,1024]{2,1,0:T(8,128)(2,1)}, u32[]{:S(2)}) copy-start(bf16[1,128,1024]{2,1,0:T(8,128)(2,1)} %param.8) | copy-start | bytes 786436
  36.4 10.8 %all-to-all-start.1 = ((bf16[8,128,64]{1,2,0:T(8,128)(2,1)}), bf16[8,128,64]{1,2,0:T(8,128)(2,1)S(1)}, u32[]{:S(2)}, u32[]{:S(2)}) async-start(bf16[8,128,64]{1,2,0:T(8,128)(2,1)} %copy_bitcast_fusion.2), calls=%async_computation.1 | async-start | bytes 262144 | tf_op jit(solution)/shard_map/all_to_all | solution.py:185
  49.5 5.3 %collective-permute-start = (bf16[15,1024]{1,0:T(8,128)(2,1)S(1)}, bf16[15,1024]{1,0:T(8,128)(2,1)S(1)}, u32[]{:S(2)}, u32[]{:S(2)}) collective-permute-start(bf16[15,1024]{1,0:T(8,128)(2,1)S(1)} %get-tuple-element.49), channel_id=1, source_target_pairs={{0,1},{1,2},{2,3},{3,4},{4,5},{5,6},{6,7},{7,8},{8,9},{9,10},{10,1... | collective-permute-start | bytes 92168 | tf_op jit(solution)/shard_map/ppermute | solution.py:24
  52.8 6.7 %collective-permute-start.1 = (bf16[15,1024]{1,0:T(8,128)(2,1)S(1)}, bf16[15,1024]{1,0:T(8,128)(2,1)S(1)}, u32[]{:S(2)}, u32[]{:S(2)}) collective-permute-start(bf16[15,1024]{1,0:T(8,128)(2,1)S(1)} %get-tuple-element.50), channel_id=1, source_target_pairs={{1,0},{2,1},{3,2},{4,3},{5,4},{6,5},{7,6},{8,7},{9,8},{10,9},{11,1... | collective-permute-start | bytes 92168 | tf_op jit(solution)/shard_map/ppermute | solution.py:25
  65.9 4.5 %collective-permute-start.2 = (bf16[15,1024]{1,0:T(8,128)(2,1)S(1)}, bf16[15,1024]{1,0:T(8,128)(2,1)S(1)}, u32[]{:S(2)}, u32[]{:S(2)}) collective-permute-start(bf16[15,1024]{1,0:T(8,128)(2,1)S(1)} %get-tuple-element.47), channel_id=1, source_target_pairs={{0,1},{1,2},{2,3},{3,4},{4,5},{5,6},{6,7},{7,8},{8,9},{9,10},{10,1... | collective-permute-start | bytes 92168 | tf_op jit(solution)/shard_map/ppermute | solution.py:24
  67.8 7.5 %collective-permute-start.3 = (bf16[15,1024]{1,0:T(8,128)(2,1)S(1)}, bf16[15,1024]{1,0:T(8,128)(2,1)S(1)}, u32[]{:S(2)}, u32[]{:S(2)}) collective-permute-start(bf16[15,1024]{1,0:T(8,128)(2,1)S(1)} %get-tuple-element.48), channel_id=1, source_target_pairs={{1,0},{2,1},{3,2},{4,3},{5,4},{6,5},{7,6},{8,7},{9,8},{10,9},{11,1... | collective-permute-start | bytes 92168 | tf_op jit(solution)/shard_map/ppermute | solution.py:25
  79.7 17.5 %copy-start.48 = (f32[128]{0:T(128)}, f32[128]{0:T(128)S(1)}, u32[]{:S(2)}) copy-start(f32[128]{0:T(128)S(1)} %negate_multiply_fusion.1) | copy-start | bytes 1540
  82.3 14.8 %all-to-all-start.2 = ((bf16[16,128,64]{1,2,0:T(8,128)(2,1)}), bf16[16,128,64]{1,2,0:T(8,128)(2,1)S(1)}, u32[]{:S(2)}, u32[]{:S(2)}) async-start(bf16[16,128,64]{1,2,0:T(8,128)(2,1)} %bitcast.45), calls=%async_computation.2 | async-start | bytes 524288 | tf_op jit(solution)/shard_map/all_to_all | solution.py:227
  97.8 9.1 %copy-start.6 = (bf16[2048,1,64]{0,2,1:T(8,128)(2,1)S(1)}, bf16[2048,1,64]{0,2,1:T(8,128)(2,1)}, u32[]{:S(2)}) copy-start(bf16[2048,1,64]{0,2,1:T(8,128)(2,1)} %get-tuple-element.44) | copy-start | bytes 786436
  97.8 8.3 %collective-permute-start.4 = (f32[2,1024]{1,0:T(2,128)}, f32[2,1024]{1,0:T(2,128)}, u32[]{:S(2)}, u32[]{:S(2)}) collective-permute-start(f32[2,1024]{1,0:T(2,128)} %pad_maximum_fusion.2), channel_id=1, source_target_pairs={{0,8},{1,9},{2,10},{3,11},{4,12},{5,13},{6,14},{7,15},{8,0},{9,1},... | collective-permute-start | bytes 24584 | tf_op jit(solution)/shard_map/ppermute | solution.py:232
  107.0 6.5 %copy-start.41 = (f32[1,2048]{1,0:T(1,128)}, f32[1,2048]{1,0:T(1,128)S(1)}, u32[]{:S(2)}) copy-start(f32[1,2048]{1,0:T(1,128)S(1)} %get-tuple-element.83) | copy-start | bytes 24580
  107.0 6.5 %copy-start.5 = (bf16[2048,1,64]{0,2,1:T(8,128)(2,1)S(1)}, bf16[2048,1,64]{0,2,1:T(8,128)(2,1)}, u32[]{:S(2)}) copy-start(bf16[2048,1,64]{0,2,1:T(8,128)(2,1)} %get-tuple-element.43) | copy-start | bytes 786436
  113.5 15.8 %copy-start.9 = (f32[1024]{0:T(1024)S(1)}, f32[1024]{0:T(1024)}, u32[]{:S(2)}) copy-start(f32[1024]{0:T(1024)} %param.11) | copy-start | bytes 12292
  113.5 15.8 %copy-start.43 = (f32[128]{0:T(128)S(1)}, f32[128]{0:T(128)}, u32[]{:S(2)}) copy-start(f32[128]{0:T(128)} %copy-done.42) | copy-start | bytes 1540
  113.5 15.8 %copy-start.46 = (f32[128]{0:T(128)S(1)}, f32[128]{0:T(128)}, u32[]{:S(2)}) copy-start(f32[128]{0:T(128)} %copy-done.45) | copy-start | bytes 1540
  120.7 9.8 %copy-start.40 = (bf16[1024]{0:T(1024)(128)(2,1)S(1)}, bf16[1024]{0:T(1024)(128)(2,1)}, u32[]{:S(2)}) copy-start(bf16[1024]{0:T(1024)(128)(2,1)} %get-tuple-element.34) | copy-start | bytes 6148
  120.7 9.8 %copy-start.39 = (bf16[1024]{0:T(1024)(128)(2,1)S(1)}, bf16[1024]{0:T(1024)(128)(2,1)}, u32[]{:S(2)}) copy-start(bf16[1024]{0:T(1024)(128)(2,1)} %get-tuple-element.33) | copy-start | bytes 6148
  120.7 9.8 %copy-start.38 = (bf16[1024]{0:T(1024)(128)(2,1)S(1)}, bf16[1024]{0:T(1024)(128)(2,1)}, u32[]{:S(2)}) copy-start(bf16[1024]{0:T(1024)(128)(2,1)} %get-tuple-element.32) | copy-start | bytes 6148
  120.7 9.8 %copy-start.37 = (bf16[1024]{0:T(1024)(128)(2,1)S(1)}, bf16[1024]{0:T(1024)(128)(2,1)}, u32[]{:S(2)}) copy-start(bf16[1024]{0:T(1024)(128)(2,1)} %get-tuple-element.31) | copy-start | bytes 6148
  120.7 9.8 %copy-start.36 = (bf16[1024]{0:T(1024)(128)(2,1)S(1)}, bf16[1024]{0:T(1024)(128)(2,1)}, u32[]{:S(2)}) copy-start(bf16[1024]{0:T(1024)(128)(2,1)} %get-tuple-element.30) | copy-start | bytes 6148
  120.7 9.8 %copy-start.35 = (bf16[1024]{0:T(1024)(128)(2,1)S(1)}, bf16[1024]{0:T(1024)(128)(2,1)}, u32[]{:S(2)}) copy-start(bf16[1024]{0:T(1024)(128)(2,1)} %get-tuple-element.29) | copy-start | bytes 6148
  120.7 9.8 %copy-start.34 = (bf16[1024]{0:T(1024)(128)(2,1)S(1)}, bf16[1024]{0:T(1024)(128)(2,1)}, u32[]{:S(2)}) copy-start(bf16[1024]{0:T(1024)(128)(2,1)} %get-tuple-element.28) | copy-start | bytes 6148
  120.8 9.8 %copy-start.33 = (bf16[1024]{0:T(1024)(128)(2,1)S(1)}, bf16[1024]{0:T(1024)(128)(2,1)}, u32[]{:S(2)}) copy-start(bf16[1024]{0:T(1024)(128)(2,1)} %get-tuple-element.27) | copy-start | bytes 6148
  120.8 9.8 %copy-start.32 = (bf16[1024]{0:T(1024)(128)(2,1)S(1)}, bf16[1024]{0:T(1024)(128)(2,1)}, u32[]{:S(2)}) copy-start(bf16[1024]{0:T(1024)(128)(2,1)} %get-tuple-element.26) | copy-start | bytes 6148
  120.8 9.9 %copy-start.31 = (bf16[1024]{0:T(1024)(128)(2,1)S(1)}, bf16[1024]{0:T(1024)(128)(2,1)}, u32[]{:S(2)}) copy-start(bf16[1024]{0:T(1024)(128)(2,1)} %get-tuple-element.25) | copy-start | bytes 6148
  120.8 9.9 %copy-start.30 = (bf16[1024]{0:T(1024)(128)(2,1)S(1)}, bf16[1024]{0:T(1024)(128)(2,1)}, u32[]{:S(2)}) copy-start(bf16[1024]{0:T(1024)(128)(2,1)} %get-tuple-element.24) | copy-start | bytes 6148
  120.8 9.9 %copy-start.29 = (bf16[1024]{0:T(1024)(128)(2,1)S(1)}, bf16[1024]{0:T(1024)(128)(2,1)}, u32[]{:S(2)}) copy-start(bf16[1024]{0:T(1024)(128)(2,1)} %get-tuple-element.23) | copy-start | bytes 6148
  120.8 9.9 %copy-start.28 = (bf16[1024]{0:T(1024)(128)(2,1)S(1)}, bf16[1024]{0:T(1024)(128)(2,1)}, u32[]{:S(2)}) copy-start(bf16[1024]{0:T(1024)(128)(2,1)} %get-tuple-element.22) | copy-start | bytes 6148
  120.8 9.9 %copy-start.26 = (bf16[1024]{0:T(1024)(128)(2,1)S(1)}, bf16[1024]{0:T(1024)(128)(2,1)}, u32[]{:S(2)}) copy-start(bf16[1024]{0:T(1024)(128)(2,1)} %get-tuple-element.21) | copy-start | bytes 6148
  120.8 9.9 %copy-start.25 = (bf16[1024]{0:T(1024)(128)(2,1)S(1)}, bf16[1024]{0:T(1024)(128)(2,1)}, u32[]{:S(2)}) copy-start(bf16[1024]{0:T(1024)(128)(2,1)} %get-tuple-element.20) | copy-start | bytes 6148
  120.8 9.9 %copy-start.24 = (bf16[1024]{0:T(1024)(128)(2,1)S(1)}, bf16[1024]{0:T(1024)(128)(2,1)}, u32[]{:S(2)}) copy-start(bf16[1024]{0:T(1024)(128)(2,1)} %get-tuple-element.19) | copy-start | bytes 6148
  120.8 9.9 %copy-start.23 = (bf16[1024]{0:T(1024)(128)(2,1)S(1)}, bf16[1024]{0:T(1024)(128)(2,1)}, u32[]{:S(2)}) copy-start(bf16[1024]{0:T(1024)(128)(2,1)} %get-tuple-element.18) | copy-start | bytes 6148
  120.9 10.0 %copy-start.22 = (bf16[1024]{0:T(1024)(128)(2,1)S(1)}, bf16[1024]{0:T(1024)(128)(2,1)}, u32[]{:S(2)}) copy-start(bf16[1024]{0:T(1024)(128)(2,1)} %get-tuple-element.17) | copy-start | bytes 6148
  120.9 10.0 %copy-start.21 = (bf16[1024]{0:T(1024)(128)(2,1)S(1)}, bf16[1024]{0:T(1024)(128)(2,1)}, u32[]{:S(2)}) copy-start(bf16[1024]{0:T(1024)(128)(2,1)} %get-tuple-element.16) | copy-start | bytes 6148
  120.9 10.0 %copy-start.20 = (bf16[1024]{0:T(1024)(128)(2,1)S(1)}, bf16[1024]{0:T(1024)(128)(2,1)}, u32[]{:S(2)}) copy-start(bf16[1024]{0:T(1024)(128)(2,1)} %get-tuple-element.15) | copy-start | bytes 6148
  120.9 10.0 %copy-start.19 = (bf16[1024]{0:T(1024)(128)(2,1)S(1)}, bf16[1024]{0:T(1024)(128)(2,1)}, u32[]{:S(2)}) copy-start(bf16[1024]{0:T(1024)(128)(2,1)} %get-tuple-element.14) | copy-start | bytes 6148
  120.9 10.0 %copy-start.18 = (bf16[1024]{0:T(1024)(128)(2,1)S(1)}, bf16[1024]{0:T(1024)(128)(2,1)}, u32[]{:S(2)}) copy-start(bf16[1024]{0:T(1024)(128)(2,1)} %get-tuple-element.13) | copy-start | bytes 6148
  120.9 10.0 %copy-start.17 = (bf16[1024]{0:T(1024)(128)(2,1)S(1)}, bf16[1024]{0:T(1024)(128)(2,1)}, u32[]{:S(2)}) copy-start(bf16[1024]{0:T(1024)(128)(2,1)} %get-tuple-element.12) | copy-start | bytes 6148
  120.9 10.0 %copy-start.16 = (bf16[1024]{0:T(1024)(128)(2,1)S(1)}, bf16[1024]{0:T(1024)(128)(2,1)}, u32[]{:S(2)}) copy-start(bf16[1024]{0:T(1024)(128)(2,1)} %get-tuple-element.11) | copy-start | bytes 6148
  120.9 10.1 %copy-start.15 = (bf16[1024]{0:T(1024)(128)(2,1)S(1)}, bf16[1024]{0:T(1024)(128)(2,1)}, u32[]{:S(2)}) copy-start(bf16[1024]{0:T(1024)(128)(2,1)} %get-tuple-element.10) | copy-start | bytes 6148
  120.9 10.1 %copy-start.14 = (bf16[1024]{0:T(1024)(128)(2,1)S(1)}, bf16[1024]{0:T(1024)(128)(2,1)}, u32[]{:S(2)}) copy-start(bf16[1024]{0:T(1024)(128)(2,1)} %get-tuple-element.9) | copy-start | bytes 6148
  120.9 10.1 %copy-start.13 = (bf16[1024]{0:T(1024)(128)(2,1)S(1)}, bf16[1024]{0:T(1024)(128)(2,1)}, u32[]{:S(2)}) copy-start(bf16[1024]{0:T(1024)(128)(2,1)} %get-tuple-element.8) | copy-start | bytes 6148
  121.0 10.1 %copy-start.12 = (bf16[1024]{0:T(1024)(128)(2,1)S(1)}, bf16[1024]{0:T(1024)(128)(2,1)}, u32[]{:S(2)}) copy-start(bf16[1024]{0:T(1024)(128)(2,1)} %get-tuple-element.7) | copy-start | bytes 6148
  121.0 10.1 %copy-start.11 = (bf16[1024]{0:T(1024)(128)(2,1)S(1)}, bf16[1024]{0:T(1024)(128)(2,1)}, u32[]{:S(2)}) copy-start(bf16[1024]{0:T(1024)(128)(2,1)} %get-tuple-element.6) | copy-start | bytes 6148
  121.0 10.1 %copy-start.10 = (bf16[1024]{0:T(1024)(128)(2,1)S(1)}, bf16[1024]{0:T(1024)(128)(2,1)}, u32[]{:S(2)}) copy-start(bf16[1024]{0:T(1024)(128)(2,1)} %get-tuple-element.5) | copy-start | bytes 6148
  121.0 10.1 %copy-start.27 = (bf16[1024]{0:T(1024)(128)(2,1)S(1)}, bf16[1024]{0:T(1024)(128)(2,1)}, u32[]{:S(2)}) copy-start(bf16[1024]{0:T(1024)(128)(2,1)} %get-tuple-element.35) | copy-start | bytes 6148
  121.0 19.5 %copy-start.51 = (f32[128]{0:T(128)S(1)}, f32[128]{0:T(128)}, u32[]{:S(2)}) copy-start(f32[128]{0:T(128)} %copy-done.50) | copy-start | bytes 1540
  125.5 11.8 %all-to-all-start.3 = ((bf16[8,128,3,64]{1,3,2,0:T(8,128)(2,1)}), bf16[8,128,3,64]{1,3,2,0:T(8,128)(2,1)S(1)}, u32[]{:S(2)}, u32[]{:S(2)}) async-start(bf16[8,128,3,64]{1,3,2,0:T(8,128)(2,1)} %copy.150), calls=%async_computation.3 | async-start | bytes 786432 | tf_op jit(solution)/shard_map/all_to_all | solution.py:185
  140.5 4.1 %copy-start.3 = (f32[128,1024]{1,0:T(8,128)}, f32[128,1024]{1,0:T(8,128)S(1)}, u32[]{:S(2)}) copy-start(f32[128,1024]{1,0:T(8,128)S(1)} %get-tuple-element.91) | copy-start | bytes 1572868
  157.7 51.7 %copy-start.44 = (f32[128]{0:T(128)S(1)}, f32[128]{0:T(128)}, u32[]{:S(2)}) copy-start(f32[128]{0:T(128)} %copy-done.42) | copy-start | bytes 1540
  157.7 51.7 %copy-start.47 = (f32[128]{0:T(128)S(1)}, f32[128]{0:T(128)}, u32[]{:S(2)}) copy-start(f32[128]{0:T(128)} %copy-done.45) | copy-start | bytes 1540
  157.7 51.7 %copy-start.49 = (f32[128]{0:T(128)S(1)}, f32[128]{0:T(128)}, u32[]{:S(2)}) copy-start(f32[128]{0:T(128)} %copy-done.48) | copy-start | bytes 1540
  158.6 50.9 %copy-start.4 = (f32[128,1024]{1,0:T(8,128)S(1)}, f32[128,1024]{1,0:T(8,128)}, u32[]{:S(2)}) copy-start(f32[128,1024]{1,0:T(8,128)} %copy-done.3) | copy-start | bytes 1572868
  201.2 17.7 %all-to-all-start.7 = ((bf16[8,6,2048]{2,1,0:T(8,128)(2,1)}), bf16[8,6,2048]{2,1,0:T(8,128)(2,1)S(1)}, u32[]{:S(2)}, u32[]{:S(2)}) async-start(bf16[8,6,2048]{2,1,0:T(8,128)(2,1)} %copy.164), calls=%async_computation.7 | async-start | bytes 524288 | tf_op jit(solution)/shard_map/all_to_all | solution.py:312
  219.7 15.7 %all-to-all-start.8 = ((f32[16,1,2112]{2,1,0:T(1,128)}), f32[16,1,2112]{2,1,0:T(1,128)S(1)}, u32[]{:S(2)}, u32[]{:S(2)}) async-start(f32[16,1,2112]{2,1,0:T(1,128)} %broadcast_in_dim.122), calls=%async_computation.8 | async-start | bytes 278528 | tf_op jit(solution)/shard_map/all_to_all | solution.py:317

commit v9 on v7

--- a/solution.py
+++ b/solution.py
@@ -296,17 +296,15 @@
     reduced = lax.all_to_all(reduced, "tm", 0, 0, tiled=True, axis_index_groups=same_core)
     reduced = reduced.astype(jnp.float32).sum(0)
     big_cols = 4 * width
-    spare = reduced[:, :, big_cols:].reshape(-1)
-    spare_rows = -(-spare.size // big_cols)
-    spare = jnp.pad(spare, (0, spare_rows * big_cols - spare.size)).reshape(spare_rows, big_cols)
+    spare = reduced[:, :, big_cols:].reshape(rows // devices, -1)
     body = jnp.concatenate(
-        [reduced[:, :, :big_cols], jnp.broadcast_to(spare, (outer_count,) + spare.shape)], axis=1
+        [reduced[:, :, :big_cols], jnp.broadcast_to(spare, (outer_count,) + spare.shape)], axis=2
     )
     body = lax.all_to_all(body.astype(jnp.bfloat16), "dp", 0, 0, tiled=True)
     body = body.astype(jnp.float32).sum(0)
-    grad_proj = body[: rows // devices]
+    grad_proj = body[:, :big_cols]
     spread = rows // devices * small_width
-    small_part = body[rows // devices :].reshape(1, -1)[:, : outer_count * spread]
+    small_part = body[:, big_cols:].reshape(1, -1)
     small_all = lax.all_to_all(
         jnp.broadcast_to(small_part, (tm_count, small_part.shape[1])), "tm", 0, 0, tiled=True
     )

time: 235 us -> 231 us (0.983)
  waiting for transfers between devices: 60.8 us -> 57 us
    all_to_all x1, waiting for transfers between devices: 11.6 us -> 7.81 us  [per_device(): body = lax.all_to_all(body.astype(jnp.bfloat16), 'dp', 0, 0, tiled=True)]
where the time goes in v9:
time: 231 us; the launch traced here: 230 us
  waiting for transfers between devices  57 us (25%)
  starting transfers between devices  50.2 us (22%)
  blocking collectives  41.7 us (18%)
  matrix products  38.9 us (17%)
  other arithmetic  27.9 us (12%)
  local copies, waits for them, and re-layouts  11.1 us (5%)
  between operations  2.72 us (1%)
    all_to_all x1, blocking collectives, per_device(): lax.all_to_all(reduced, 'tm', 0, 0, tiled=True, axis_index_groups=same_core)  32.7 us
    all_to_all x1, waiting for transfers between devices, per_device(): lax.all_to_all(jnp.tile(qkv, (halves, 1, 1, 1)), 'tm', 0, 0, tiled=True)  12.9 us
    all_to_all x2, waiting for transfers between devices, to_frames(): lax.all_to_all(blocks, 'tm', 0, 0, tiled=True, axis_index_groups=half_gro...  11.3 us
    ppermute x2, waiting for transfers between devices, padded_2(): after = lax.ppermute(first, axis, down)  9.62 us
    all_to_all x1, blocking collectives, per_device(): lax.all_to_all(packed, 'tm', 0, 0, tiled=True, axis_index_groups=pairs)  8.99 us
    all_to_all x2, starting transfers between devices, to_frames(): lax.all_to_all(blocks, 'tm', 0, 0, tiled=True, axis_index_groups=half_gro...  8.82 us
    all_to_all x1, starting transfers between devices, per_device(): lax.all_to_all(jnp.tile(qkv, (halves, 1, 1, 1)), 'tm', 0, 0, tiled=True)  8.43 us
    all_to_all x1, starting transfers between devices, per_device(): body = lax.all_to_all(body.astype(jnp.bfloat16), 'dp', 0, 0, tiled=True)  8.41 us
  transfers between devices with their start and end apart: 11, of which 8 were waited for; matrix products, arithmetic and copies ran while one was open for 5% of the time, Pallas kernels for 0%

profile of v9, /device:TPU:1, one launch (start us, length us, event | category | flops | bytes accessed | tf_op | source)
XLA Modules:
  0.0 229.5 jit_solution(9741046686046200288)
XLA Ops:
  0.6 1.1 convert_reduce_fusion.1
  1.7 1.2 fusion.42
  2.9 2.7 %fusion.10 = bf16[128,1536]{1,0:T(8,128)(2,1)S(1)} fusion(bf16[1024,2048]{1,0:T(8,128)(2,1)} %param.10, bf16[1,128,1024]{2,1,0:T(8,128)(2,1)} %param.7, f32[1024]{0:T(1024)} %param.11, f32[128]{0:T(128)S(1)} %fusion.112, f32[128]{0:T(128)S(1)} %broadcast_multiply_fusion.1), kind=kOutput, calls=%fused_computation.17 | convolution fusion | flops 403505152 | bytes 3806208 | tf_op jit(solution)/shard_map/dot_general | solution.py:156
  5.8 1.1 tile.8
  6.9 8.4 %all-to-all-start = ((bf16[16,128,3,64]{1,3,2,0:T(8,128)(2,1)}), bf16[16,128,3,64]{1,3,2,0:T(8,128)(2,1)S(1)}, u32[]{:S(2)}, u32[]{:S(2)}) async-start(bf16[16,128,3,64]{1,3,2,0:T(8,128)(2,1)} %bitcast.7), calls=%async_computation | async-start | bytes 1572864 | tf_op jit(solution)/shard_map/all_to_all | solution.py:168
  16.0 12.9 %all-to-all-done = bf16[16,128,3,64]{1,3,2,0:T(8,128)(2,1)S(1)} async-done(((bf16[16,128,3,64]{1,3,2,0:T(8,128)(2,1)}), bf16[16,128,3,64]{1,3,2,0:T(8,128)(2,1)S(1)}, u32[]{:S(2)}, u32[]{:S(2)}) %all-to-all-start) | async-done | bytes 786464 | tf_op jit(solution)/shard_map/all_to_all | solution.py:168
  29.0 0.8 fusion.134
  29.9 1.4 fusion.3
  31.3 2.5 %fusion = f32[1024]{0:T(1024)S(1)} fusion(f32[1024,2048]{1,0:T(8,128)S(1)} %get-tuple-element.85, f32[1024]{0:T(1024)S(1)} %get-tuple-element.84, pred[2048]{0:T(1024)(128)(4,1)S(1)} %iota_compare_fusion), kind=kLoop, calls=%fused_computation.5 | loop fusion | flops 10484736 | bytes 8398848 | tf_op jit(solution)/shard_map/reduce_sum | solution.py:176
  33.8 1.9 fusion.27
  35.8 0.7 copy_bitcast_fusion.2
  36.4 4.9 %all-to-all-start.1 = ((bf16[8,128,64]{1,2,0:T(8,128)(2,1)}), bf16[8,128,64]{1,2,0:T(8,128)(2,1)S(1)}, u32[]{:S(2)}, u32[]{:S(2)}) async-start(bf16[8,128,64]{1,2,0:T(8,128)(2,1)} %copy_bitcast_fusion.2), calls=%async_computation.1 | async-start | bytes 262144 | tf_op jit(solution)/shard_map/all_to_all | solution.py:185
  41.5 5.8 %all-to-all-done.1 = bf16[8,128,64]{1,2,0:T(8,128)(2,1)S(1)} async-done(((bf16[8,128,64]{1,2,0:T(8,128)(2,1)}), bf16[8,128,64]{1,2,0:T(8,128)(2,1)S(1)}, u32[]{:S(2)}, u32[]{:S(2)}) %all-to-all-start.1) | async-done | bytes 131104 | tf_op jit(solution)/shard_map/all_to_all | solution.py:185
  47.2 1.8 fusion.140
  49.5 3.3 %collective-permute-start = (bf16[15,1024]{1,0:T(8,128)(2,1)S(1)}, bf16[15,1024]{1,0:T(8,128)(2,1)S(1)}, u32[]{:S(2)}, u32[]{:S(2)}) collective-permute-start(bf16[15,1024]{1,0:T(8,128)(2,1)S(1)} %get-tuple-element.49), channel_id=1, source_target_pairs={{0,1},{1,2},{2,3},{3,4},{4,5},{5,6},{6,7},{7,8},{8,9},{9,10},{10,1... | collective-permute-start | bytes 92168 | tf_op jit(solution)/shard_map/ppermute | solution.py:24
  52.8 1.9 collective-permute-start.1
  54.8 4.8 %collective-permute-done.1 = bf16[15,1024]{1,0:T(8,128)(2,1)S(1)} collective-permute-done((bf16[15,1024]{1,0:T(8,128)(2,1)S(1)}, bf16[15,1024]{1,0:T(8,128)(2,1)S(1)}, u32[]{:S(2)}, u32[]{:S(2)}) %collective-permute-start.1) | collective-permute-done | bytes 30752 | tf_op jit(solution)/shard_map/ppermute | solution.py:25
  59.6 4.8 %multiply_reduce_fusion.1 = (bf16[1024]{0:T(1024)(128)(2,1)S(1)}, bf16[1024]{0:T(1024)(128)(2,1)}, bf16[1024]{0:T(1024)(128)(2,1)}, bf16[1024]{0:T(1024)(128)(2,...) fusion(f32[158,1024]{1,0:T(8,128)S(1)} %maximum_convert_fusion,, ...), kind=kLoop, calls=%fused_computation.125 | loop fusion | flops 13875200 | bytes 17203200 | tf_op jit(solution)/shard_map/reduce_sum | solution.py:207
  64.4 1.4 multiply_reduce_fusion.19
  65.9 1.9 collective-permute-start.2
  67.8 2.6 %collective-permute-start.3 = (bf16[15,1024]{1,0:T(8,128)(2,1)S(1)}, bf16[15,1024]{1,0:T(8,128)(2,1)S(1)}, u32[]{:S(2)}, u32[]{:S(2)}) collective-permute-start(bf16[15,1024]{1,0:T(8,128)(2,1)S(1)} %get-tuple-element.48), channel_id=1, source_target_pairs={{1,0},{2,1},{3,2},{4,3},{5,4},{6,5},{7,6},{8,7},{9,8},{10,9},{11,1... | collective-permute-start | bytes 92168 | tf_op jit(solution)/shard_map/ppermute | solution.py:25
  70.4 4.9 %collective-permute-done.3 = bf16[15,1024]{1,0:T(8,128)(2,1)S(1)} collective-permute-done((bf16[15,1024]{1,0:T(8,128)(2,1)S(1)}, bf16[15,1024]{1,0:T(8,128)(2,1)S(1)}, u32[]{:S(2)}, u32[]{:S(2)}) %collective-permute-start.3) | collective-permute-done | bytes 30752 | tf_op jit(solution)/shard_map/ppermute | solution.py:25
  75.3 4.1 %multiply_reduce_fusion = (bf16[1024]{0:T(1024)(128)(2,1)}, f32[128]{0:T(128)S(1)}, f32[128,1024]{1,0:T(8,128)S(1)}) fusion(f32[128,1024]{1,0:T(8,128)S(1)} %get-tuple-element.87, f32[128]{0:T(128)S(1)} %fusion.113, f32[128]{0:T(128)S(1)} %broadcast_multiply_fusion, f32[1024]{0:T(1024)S(1)} %copy-done.8, f32[158,1024]{1,0:T(8,128)S(1)} %maximum_convert_fusion.1, ...), kind=kLoop, calls=%fused_computation.124 | loop fusion | flops 9042816 | bytes 17436288 | tf_op jit(solution)/shard_map/transpose(jvp())/reduce_sum | solution.py:33
  79.9 1.5 convolution_convert_fusion.3
  81.5 0.8 tile.20
  82.3 6.0 %all-to-all-start.2 = ((bf16[16,128,64]{1,2,0:T(8,128)(2,1)}), bf16[16,128,64]{1,2,0:T(8,128)(2,1)S(1)}, u32[]{:S(2)}, u32[]{:S(2)}) async-start(bf16[16,128,64]{1,2,0:T(8,128)(2,1)} %bitcast.45), calls=%async_computation.2 | async-start | bytes 524288 | tf_op jit(solution)/shard_map/all_to_all | solution.py:227
  88.3 0.6 dynamic-slice.6
  88.8 8.3 %all-to-all-done.2 = bf16[16,128,64]{1,2,0:T(8,128)(2,1)S(1)} async-done(((bf16[16,128,64]{1,2,0:T(8,128)(2,1)}), bf16[16,128,64]{1,2,0:T(8,128)(2,1)S(1)}, u32[]{:S(2)}, u32[]{:S(2)}) %all-to-all-start.2) | async-done | bytes 262176 | tf_op jit(solution)/shard_map/all_to_all | solution.py:227
  97.2 0.6 pad_maximum_fusion.2
  97.8 1.1 collective-permute-start.4
  98.9 6.9 %fusion.23 = bf16[8,8,8,128]{3,1,2,0:T(8,128)(2,1)S(1)} fusion(f32[1024,2048]{1,0:T(8,128)} %copy-done, f32[1024]{0:T(1024)S(1)} %multiply_reduce_fusion.34, f32[1024]{0:T(1024)S(1)} %log_add_fusion, pred[2048]{0:T(1024)(128)(4,1)S(1)} %iota_compare_fusion, bf16[2048,64]{0,1:T(8,128)(2,1)S(1)} %copy_bitcast_fusion.1, s32[]{:T(128)S(6)} %select_n.51, ...), kind=kOutput, calls=%fused_computation.32 | convolution fusion | flops 551682048 | bytes 9185284 | tf_op jit(solution)/shard_map/dot_general | solution.py:247
  106.2 0.8 maximum_select_fusion
  107.0 6.5 %fusion.2 = (bf16[2048,1024]{0,1:T(8,128)(2,1)}, f32[2048,1024]{0,1:T(8,128)}) fusion(f32[2048]{0:T(1024)S(1)} %bitcast.270, pred[1024]{0:T(1024)(128)(4,1)} %dynamic-slice.6, bf16[2048,1,64]{0,2,1:T(8,128)(2,1)S(1)} %copy-done.6, s32[]{:T(128)S(6)} %select_n.51, bf16[2048,3,64]{0,2,1:T(8,128)(2,1)S(1)} %copy_bitcast_fusion), kind=kOutput, calls=%fused_computation.7 | convolution fusion | flops 278921216 | bytes 12985348 | tf_op jit(solution)/shard_map/dot_general | solution.py:250
  113.6 7.1 %fusion.22 = bf16[8,8,8,128]{3,1,2,0:T(8,128)(2,1)S(1)} fusion(f32[2048,1024]{0,1:T(8,128)} %get-tuple-element.89, f32[2048]{0:T(1024)S(1)} %bitcast.269, f32[2048]{0:T(1024)} %bitcast.271, pred[1024]{0:T(1024)(128)(4,1)} %dynamic-slice.6, bf16[2048,1,64]{0,2,1:T(8,128)(2,1)S(1)} %copy-done.5, s32[]{:T(128)S(6)} %select_n.51, ...), kind=kOutput, calls=%fused_computation.31 | convolution fusion | flops 551682048 | bytes 9192452 | tf_op jit(solution)/shard_map/dot_general | solution.py:256
  121.1 3.6 %fusion.21 = bf16[8,128,1,64]{1,3,0,2:T(8,128)(2,1)S(1)} fusion(bf16[8,128,2048]{2,1,0:T(8,128)(2,1)} %bitcast.190, bf16[2048,64,1]{0,1,2:T(8,128)(2,1)S(1)} %reshape.223), kind=kOutput, calls=%fused_computation.30 | convolution fusion | flops 268500992 | bytes 4587520 | tf_op jit(solution)/shard_map/dot_general | solution.py:259
  124.7 0.8 copy.169
  125.5 3.9 %all-to-all-start.3 = ((bf16[8,128,3,64]{1,3,2,0:T(8,128)(2,1)}), bf16[8,128,3,64]{1,3,2,0:T(8,128)(2,1)S(1)}, u32[]{:S(2)}, u32[]{:S(2)}) async-start(bf16[8,128,3,64]{1,3,2,0:T(8,128)(2,1)} %copy.169), calls=%async_computation.3 | async-start | bytes 786432 | tf_op jit(solution)/shard_map/all_to_all | solution.py:185
  129.6 0.8 copy.171
  131.3 0.4 convolution_convert_fusion.1
  131.8 5.5 %all-to-all-done.3 = bf16[8,128,3,64]{1,3,2,0:T(8,128)(2,1)S(1)} async-done(((bf16[8,128,3,64]{1,3,2,0:T(8,128)(2,1)}), bf16[8,128,3,64]{1,3,2,0:T(8,128)(2,1)S(1)}, u32[]{:S(2)}, u32[]{:S(2)}) %all-to-all-start.3) | async-done | bytes 393248 | tf_op jit(solution)/shard_map/all_to_all | solution.py:185
  137.3 3.1 %fusion.43 = (f32[128]{0:T(128)S(1)}, f32[128,1024]{1,0:T(8,128)S(1)}) fusion(bf16[1,128,1024]{2,1,0:T(8,128)(2,1)S(1)} %copy-done.1, f32[1024]{0:T(1024)S(1)} %copy-done.9, f32[128]{0:T(128)S(1)} %copy-done.43, bf16[128,1536]{0,1:T(8,128)(2,1)S(1)} %bitcast.191, bf16[1024,2048]{1,0:T(8,128)(2,1)} %param.10), kind=kOutput, calls=%fused_computation.57 | convolution fusion | flops 403308416 | bytes 4330496 | tf_op jit(solution)/shard_map/dot_general | solution.py:264
  140.5 0.3 fusion.40
  140.8 0.3 concatenate.33
  141.1 0.6 concatenate.34
  141.8 1.9 convolution_convert_fusion
  143.7 0.5 maximum_bitcast_fusion
  144.2 0.4 copy.178
  144.6 9.0 %all_to_all.41 = bf16[2,16,8,4,2081]{4,2,3,1,0:T(8,128)(2,1)} all-to-all(bf16[2,16,8,4,2081]{4,2,3,1,0:T(8,128)(2,1)S(1)} %copy.178), channel_id=1, replica_groups={{0,1},{2,3},{4,5},{6,7},{8,9},{10,11},{12,13},{14,15},{16,17},{18,19},{..., dimensions={0} | all-to-all | bytes 8523776 | tf_op jit(solution)/shard_map/all_to_all | solution.py:294
  153.6 4.1 %reduce_sum.500 = bf16[16,8,4,2081]{3,1,2,0:T(8,128)(2,1)S(1)} reduce(bf16[2,16,8,4,2081]{4,2,3,1,0:T(8,128)(2,1)} %all_to_all.41, bf16[]{:T(256)} %constant.60.clone.1), dimensions={0}, to_apply=%region_44.45 | reduce | flops 1065472 | bytes 6392834 | tf_op jit(solution)/shard_map/reduce_sum | solution.py:295
  157.7 0.9 copy.180
  158.6 32.7 %all_to_all.42 = bf16[8,16,4,2081]{3,2,1,0:T(4,128)(2,1)S(1)} all-to-all(bf16[8,16,4,2081]{3,2,1,0:T(4,128)(2,1)S(1)} %copy.180), channel_id=1, replica_groups={{0,2,4,6,8,10,12,14},{1,3,5,7,9,11,13,15},{16,18,20,22,24,26,28,30},{17..., dimensions={0} | all-to-all | bytes 4261888 | tf_op jit(solution)/shard_map/all_to_all | solution.py:296
  191.3 1.0 convert_reduce_fusion
  192.6 0.9 pad_maximum_fusion.1
  193.4 8.4 %all-to-all-start.6 = ((bf16[16,4,2576]{2,1,0:T(4,128)(2,1)}), bf16[16,4,2576]{2,1,0:T(4,128)(2,1)S(1)}, u32[]{:S(2)}, u32[]{:S(2)}) async-start(bf16[16,4,2576]{2,1,0:T(4,128)(2,1)} %pad_maximum_fusion.1), calls=%async_computation.6 | async-start | bytes 688128 | tf_op jit(solution)/shard_map/all_to_all | solution.py:303
  201.9 1.0 fusion.79
  202.9 7.8 %all-to-all-done.6 = bf16[16,4,2576]{2,1,0:T(4,128)(2,1)S(1)} async-done(((bf16[16,4,2576]{2,1,0:T(4,128)(2,1)}), bf16[16,4,2576]{2,1,0:T(4,128)(2,1)S(1)}, u32[]{:S(2)}, u32[]{:S(2)}) %all-to-all-start.6) | async-done | bytes 329760 | tf_op jit(solution)/shard_map/all_to_all | solution.py:303
  210.9 0.7 broadcast_in_dim.125
  211.6 7.8 %all-to-all-start.7 = ((f32[16,1,2112]{2,1,0:T(1,128)}), f32[16,1,2112]{2,1,0:T(1,128)S(1)}, u32[]{:S(2)}, u32[]{:S(2)}) async-start(f32[16,1,2112]{2,1,0:T(1,128)} %broadcast_in_dim.125), calls=%async_computation.7 | async-start | bytes 278528 | tf_op jit(solution)/shard_map/all_to_all | solution.py:308
  219.4 0.6 slice_multiply_fusion.32
  220.1 7.1 %all-to-all-done.7 = f32[16,1,2112]{2,1,0:T(1,128)S(1)} async-done(((f32[16,1,2112]{2,1,0:T(1,128)}), f32[16,1,2112]{2,1,0:T(1,128)S(1)}, u32[]{:S(2)}, u32[]{:S(2)}) %all-to-all-start.7) | async-done | bytes 135200 | tf_op jit(solution)/shard_map/all_to_all | solution.py:308
  227.2 0.3 reduce.2
  227.5 0.3 reshape.220
  228.2 0.7 slice_multiply_fusion.31
  228.9 0.6 slice_multiply_fusion.33
  (188 shorter events, 3.9 us)
Async XLA Ops:
  1.7 27.2 %copy-start.42 = (f32[128]{0:T(128)}, f32[128]{0:T(128)S(1)}, u32[]{:S(2)}) copy-start(f32[128]{0:T(128)S(1)} %broadcast_multiply_fusion.1) | copy-start | bytes 1540
  2.9 26.0 %copy-start.50 = (f32[128]{0:T(128)}, f32[128]{0:T(128)S(1)}, u32[]{:S(2)}) copy-start(f32[128]{0:T(128)S(1)} %fusion.42) | copy-start | bytes 1540
  2.9 26.0 %copy-start.45 = (f32[128]{0:T(128)}, f32[128]{0:T(128)S(1)}, u32[]{:S(2)}) copy-start(f32[128]{0:T(128)S(1)} %fusion.112) | copy-start | bytes 1540
  6.9 22.0 %all-to-all-start = ((bf16[16,128,3,64]{1,3,2,0:T(8,128)(2,1)}), bf16[16,128,3,64]{1,3,2,0:T(8,128)(2,1)S(1)}, u32[]{:S(2)}, u32[]{:S(2)}) async-start(bf16[16,128,3,64]{1,3,2,0:T(8,128)(2,1)} %bitcast.7), calls=%async_computation | async-start | bytes 1572864 | tf_op jit(solution)/shard_map/all_to_all | solution.py:168
  31.3 4.4 %copy-start = (f32[1024,2048]{1,0:T(8,128)}, f32[1024,2048]{1,0:T(8,128)S(1)}, u32[]{:S(2)}) copy-start(f32[1024,2048]{1,0:T(8,128)S(1)} %get-tuple-element.85) | copy-start | bytes 25165828
  33.8 7.6 %copy-start.7 = (bf16[31,1024]{1,0:T(8,128)(2,1)S(1)}, bf16[31,1024]{1,0:T(8,128)(2,1)}, u32[]{:S(2)}) copy-start(bf16[31,1024]{1,0:T(8,128)(2,1)} %param.13) | copy-start | bytes 190468
  33.8 13.4 %copy-start.1 = (bf16[1,128,1024]{2,1,0:T(8,128)(2,1)S(1)}, bf16[1,128,1024]{2,1,0:T(8,128)(2,1)}, u32[]{:S(2)}) copy-start(bf16[1,128,1024]{2,1,0:T(8,128)(2,1)} %param.7) | copy-start | bytes 786436
  33.8 15.4 %copy-start.8 = (f32[1024]{0:T(1024)S(1)}, f32[1024]{0:T(1024)}, u32[]{:S(2)}) copy-start(f32[1024]{0:T(1024)} %param.12) | copy-start | bytes 12292
  33.8 25.8 %copy-start.2 = (bf16[1,128,1024]{2,1,0:T(8,128)(2,1)S(1)}, bf16[1,128,1024]{2,1,0:T(8,128)(2,1)}, u32[]{:S(2)}) copy-start(bf16[1,128,1024]{2,1,0:T(8,128)(2,1)} %param.8) | copy-start | bytes 786436
  36.4 10.8 %all-to-all-start.1 = ((bf16[8,128,64]{1,2,0:T(8,128)(2,1)}), bf16[8,128,64]{1,2,0:T(8,128)(2,1)S(1)}, u32[]{:S(2)}, u32[]{:S(2)}) async-start(bf16[8,128,64]{1,2,0:T(8,128)(2,1)} %copy_bitcast_fusion.2), calls=%async_computation.1 | async-start | bytes 262144 | tf_op jit(solution)/shard_map/all_to_all | solution.py:185
  49.5 5.3 %collective-permute-start = (bf16[15,1024]{1,0:T(8,128)(2,1)S(1)}, bf16[15,1024]{1,0:T(8,128)(2,1)S(1)}, u32[]{:S(2)}, u32[]{:S(2)}) collective-permute-start(bf16[15,1024]{1,0:T(8,128)(2,1)S(1)} %get-tuple-element.49), channel_id=1, source_target_pairs={{0,1},{1,2},{2,3},{3,4},{4,5},{5,6},{6,7},{7,8},{8,9},{9,10},{10,1... | collective-permute-start | bytes 92168 | tf_op jit(solution)/shard_map/ppermute | solution.py:24
  52.8 6.7 %collective-permute-start.1 = (bf16[15,1024]{1,0:T(8,128)(2,1)S(1)}, bf16[15,1024]{1,0:T(8,128)(2,1)S(1)}, u32[]{:S(2)}, u32[]{:S(2)}) collective-permute-start(bf16[15,1024]{1,0:T(8,128)(2,1)S(1)} %get-tuple-element.50), channel_id=1, source_target_pairs={{1,0},{2,1},{3,2},{4,3},{5,4},{6,5},{7,6},{8,7},{9,8},{10,9},{11,1... | collective-permute-start | bytes 92168 | tf_op jit(solution)/shard_map/ppermute | solution.py:25
  65.9 4.5 %collective-permute-start.2 = (bf16[15,1024]{1,0:T(8,128)(2,1)S(1)}, bf16[15,1024]{1,0:T(8,128)(2,1)S(1)}, u32[]{:S(2)}, u32[]{:S(2)}) collective-permute-start(bf16[15,1024]{1,0:T(8,128)(2,1)S(1)} %get-tuple-element.47), channel_id=1, source_target_pairs={{0,1},{1,2},{2,3},{3,4},{4,5},{5,6},{6,7},{7,8},{8,9},{9,10},{10,1... | collective-permute-start | bytes 92168 | tf_op jit(solution)/shard_map/ppermute | solution.py:24
  67.8 7.5 %collective-permute-start.3 = (bf16[15,1024]{1,0:T(8,128)(2,1)S(1)}, bf16[15,1024]{1,0:T(8,128)(2,1)S(1)}, u32[]{:S(2)}, u32[]{:S(2)}) collective-permute-start(bf16[15,1024]{1,0:T(8,128)(2,1)S(1)} %get-tuple-element.48), channel_id=1, source_target_pairs={{1,0},{2,1},{3,2},{4,3},{5,4},{6,5},{7,6},{8,7},{9,8},{10,9},{11,1... | collective-permute-start | bytes 92168 | tf_op jit(solution)/shard_map/ppermute | solution.py:25
  79.7 17.5 %copy-start.48 = (f32[128]{0:T(128)}, f32[128]{0:T(128)S(1)}, u32[]{:S(2)}) copy-start(f32[128]{0:T(128)S(1)} %negate_multiply_fusion.1) | copy-start | bytes 1540
  82.3 14.8 %all-to-all-start.2 = ((bf16[16,128,64]{1,2,0:T(8,128)(2,1)}), bf16[16,128,64]{1,2,0:T(8,128)(2,1)S(1)}, u32[]{:S(2)}, u32[]{:S(2)}) async-start(bf16[16,128,64]{1,2,0:T(8,128)(2,1)} %bitcast.45), calls=%async_computation.2 | async-start | bytes 524288 | tf_op jit(solution)/shard_map/all_to_all | solution.py:227
  97.8 9.1 %copy-start.6 = (bf16[2048,1,64]{0,2,1:T(8,128)(2,1)S(1)}, bf16[2048,1,64]{0,2,1:T(8,128)(2,1)}, u32[]{:S(2)}) copy-start(bf16[2048,1,64]{0,2,1:T(8,128)(2,1)} %get-tuple-element.44) | copy-start | bytes 786436
  97.8 8.3 %collective-permute-start.4 = (f32[2,1024]{1,0:T(2,128)}, f32[2,1024]{1,0:T(2,128)}, u32[]{:S(2)}, u32[]{:S(2)}) collective-permute-start(f32[2,1024]{1,0:T(2,128)} %pad_maximum_fusion.2), channel_id=1, source_target_pairs={{0,8},{1,9},{2,10},{3,11},{4,12},{5,13},{6,14},{7,15},{8,0},{9,1},... | collective-permute-start | bytes 24584 | tf_op jit(solution)/shard_map/ppermute | solution.py:232
  107.0 6.5 %copy-start.41 = (f32[1,2048]{1,0:T(1,128)}, f32[1,2048]{1,0:T(1,128)S(1)}, u32[]{:S(2)}) copy-start(f32[1,2048]{1,0:T(1,128)S(1)} %get-tuple-element.83) | copy-start | bytes 24580
  107.0 6.5 %copy-start.5 = (bf16[2048,1,64]{0,2,1:T(8,128)(2,1)S(1)}, bf16[2048,1,64]{0,2,1:T(8,128)(2,1)}, u32[]{:S(2)}) copy-start(bf16[2048,1,64]{0,2,1:T(8,128)(2,1)} %get-tuple-element.43) | copy-start | bytes 786436
  113.5 15.8 %copy-start.9 = (f32[1024]{0:T(1024)S(1)}, f32[1024]{0:T(1024)}, u32[]{:S(2)}) copy-start(f32[1024]{0:T(1024)} %param.11) | copy-start | bytes 12292
  113.5 15.8 %copy-start.43 = (f32[128]{0:T(128)S(1)}, f32[128]{0:T(128)}, u32[]{:S(2)}) copy-start(f32[128]{0:T(128)} %copy-done.42) | copy-start | bytes 1540
  113.5 15.8 %copy-start.46 = (f32[128]{0:T(128)S(1)}, f32[128]{0:T(128)}, u32[]{:S(2)}) copy-start(f32[128]{0:T(128)} %copy-done.45) | copy-start | bytes 1540
  120.7 9.8 %copy-start.40 = (bf16[1024]{0:T(1024)(128)(2,1)S(1)}, bf16[1024]{0:T(1024)(128)(2,1)}, u32[]{:S(2)}) copy-start(bf16[1024]{0:T(1024)(128)(2,1)} %get-tuple-element.34) | copy-start | bytes 6148
  120.7 9.8 %copy-start.39 = (bf16[1024]{0:T(1024)(128)(2,1)S(1)}, bf16[1024]{0:T(1024)(128)(2,1)}, u32[]{:S(2)}) copy-start(bf16[1024]{0:T(1024)(128)(2,1)} %get-tuple-element.33) | copy-start | bytes 6148
  120.7 9.8 %copy-start.38 = (bf16[1024]{0:T(1024)(128)(2,1)S(1)}, bf16[1024]{0:T(1024)(128)(2,1)}, u32[]{:S(2)}) copy-start(bf16[1024]{0:T(1024)(128)(2,1)} %get-tuple-element.32) | copy-start | bytes 6148
  120.7 9.8 %copy-start.37 = (bf16[1024]{0:T(1024)(128)(2,1)S(1)}, bf16[1024]{0:T(1024)(128)(2,1)}, u32[]{:S(2)}) copy-start(bf16[1024]{0:T(1024)(128)(2,1)} %get-tuple-element.31) | copy-start | bytes 6148
  120.7 9.8 %copy-start.36 = (bf16[1024]{0:T(1024)(128)(2,1)S(1)}, bf16[1024]{0:T(1024)(128)(2,1)}, u32[]{:S(2)}) copy-start(bf16[1024]{0:T(1024)(128)(2,1)} %get-tuple-element.30) | copy-start | bytes 6148
  120.7 9.8 %copy-start.35 = (bf16[1024]{0:T(1024)(128)(2,1)S(1)}, bf16[1024]{0:T(1024)(128)(2,1)}, u32[]{:S(2)}) copy-start(bf16[1024]{0:T(1024)(128)(2,1)} %get-tuple-element.29) | copy-start | bytes 6148
  120.7 9.8 %copy-start.34 = (bf16[1024]{0:T(1024)(128)(2,1)S(1)}, bf16[1024]{0:T(1024)(128)(2,1)}, u32[]{:S(2)}) copy-start(bf16[1024]{0:T(1024)(128)(2,1)} %get-tuple-element.28) | copy-start | bytes 6148
  120.8 9.8 %copy-start.33 = (bf16[1024]{0:T(1024)(128)(2,1)S(1)}, bf16[1024]{0:T(1024)(128)(2,1)}, u32[]{:S(2)}) copy-start(bf16[1024]{0:T(1024)(128)(2,1)} %get-tuple-element.27) | copy-start | bytes 6148
  120.8 9.8 %copy-start.32 = (bf16[1024]{0:T(1024)(128)(2,1)S(1)}, bf16[1024]{0:T(1024)(128)(2,1)}, u32[]{:S(2)}) copy-start(bf16[1024]{0:T(1024)(128)(2,1)} %get-tuple-element.26) | copy-start | bytes 6148
  120.8 9.9 %copy-start.31 = (bf16[1024]{0:T(1024)(128)(2,1)S(1)}, bf16[1024]{0:T(1024)(128)(2,1)}, u32[]{:S(2)}) copy-start(bf16[1024]{0:T(1024)(128)(2,1)} %get-tuple-element.25) | copy-start | bytes 6148
  120.8 9.9 %copy-start.30 = (bf16[1024]{0:T(1024)(128)(2,1)S(1)}, bf16[1024]{0:T(1024)(128)(2,1)}, u32[]{:S(2)}) copy-start(bf16[1024]{0:T(1024)(128)(2,1)} %get-tuple-element.24) | copy-start | bytes 6148
  120.8 9.9 %copy-start.29 = (bf16[1024]{0:T(1024)(128)(2,1)S(1)}, bf16[1024]{0:T(1024)(128)(2,1)}, u32[]{:S(2)}) copy-start(bf16[1024]{0:T(1024)(128)(2,1)} %get-tuple-element.23) | copy-start | bytes 6148
  120.8 9.9 %copy-start.28 = (bf16[1024]{0:T(1024)(128)(2,1)S(1)}, bf16[1024]{0:T(1024)(128)(2,1)}, u32[]{:S(2)}) copy-start(bf16[1024]{0:T(1024)(128)(2,1)} %get-tuple-element.22) | copy-start | bytes 6148
  120.8 9.9 %copy-start.26 = (bf16[1024]{0:T(1024)(128)(2,1)S(1)}, bf16[1024]{0:T(1024)(128)(2,1)}, u32[]{:S(2)}) copy-start(bf16[1024]{0:T(1024)(128)(2,1)} %get-tuple-element.21) | copy-start | bytes 6148
  120.8 9.9 %copy-start.25 = (bf16[1024]{0:T(1024)(128)(2,1)S(1)}, bf16[1024]{0:T(1024)(128)(2,1)}, u32[]{:S(2)}) copy-start(bf16[1024]{0:T(1024)(128)(2,1)} %get-tuple-element.20) | copy-start | bytes 6148
  120.8 9.9 %copy-start.24 = (bf16[1024]{0:T(1024)(128)(2,1)S(1)}, bf16[1024]{0:T(1024)(128)(2,1)}, u32[]{:S(2)}) copy-start(bf16[1024]{0:T(1024)(128)(2,1)} %get-tuple-element.19) | copy-start | bytes 6148
  120.8 9.9 %copy-start.23 = (bf16[1024]{0:T(1024)(128)(2,1)S(1)}, bf16[1024]{0:T(1024)(128)(2,1)}, u32[]{:S(2)}) copy-start(bf16[1024]{0:T(1024)(128)(2,1)} %get-tuple-element.18) | copy-start | bytes 6148
  120.9 10.0 %copy-start.22 = (bf16[1024]{0:T(1024)(128)(2,1)S(1)}, bf16[1024]{0:T(1024)(128)(2,1)}, u32[]{:S(2)}) copy-start(bf16[1024]{0:T(1024)(128)(2,1)} %get-tuple-element.17) | copy-start | bytes 6148
  120.9 10.0 %copy-start.21 = (bf16[1024]{0:T(1024)(128)(2,1)S(1)}, bf16[1024]{0:T(1024)(128)(2,1)}, u32[]{:S(2)}) copy-start(bf16[1024]{0:T(1024)(128)(2,1)} %get-tuple-element.16) | copy-start | bytes 6148
  120.9 10.0 %copy-start.20 = (bf16[1024]{0:T(1024)(128)(2,1)S(1)}, bf16[1024]{0:T(1024)(128)(2,1)}, u32[]{:S(2)}) copy-start(bf16[1024]{0:T(1024)(128)(2,1)} %get-tuple-element.15) | copy-start | bytes 6148
  120.9 10.0 %copy-start.19 = (bf16[1024]{0:T(1024)(128)(2,1)S(1)}, bf16[1024]{0:T(1024)(128)(2,1)}, u32[]{:S(2)}) copy-start(bf16[1024]{0:T(1024)(128)(2,1)} %get-tuple-element.14) | copy-start | bytes 6148
  120.9 10.0 %copy-start.18 = (bf16[1024]{0:T(1024)(128)(2,1)S(1)}, bf16[1024]{0:T(1024)(128)(2,1)}, u32[]{:S(2)}) copy-start(bf16[1024]{0:T(1024)(128)(2,1)} %get-tuple-element.13) | copy-start | bytes 6148
  120.9 10.0 %copy-start.17 = (bf16[1024]{0:T(1024)(128)(2,1)S(1)}, bf16[1024]{0:T(1024)(128)(2,1)}, u32[]{:S(2)}) copy-start(bf16[1024]{0:T(1024)(128)(2,1)} %get-tuple-element.12) | copy-start | bytes 6148
  120.9 10.0 %copy-start.16 = (bf16[1024]{0:T(1024)(128)(2,1)S(1)}, bf16[1024]{0:T(1024)(128)(2,1)}, u32[]{:S(2)}) copy-start(bf16[1024]{0:T(1024)(128)(2,1)} %get-tuple-element.11) | copy-start | bytes 6148
  120.9 10.1 %copy-start.15 = (bf16[1024]{0:T(1024)(128)(2,1)S(1)}, bf16[1024]{0:T(1024)(128)(2,1)}, u32[]{:S(2)}) copy-start(bf16[1024]{0:T(1024)(128)(2,1)} %get-tuple-element.10) | copy-start | bytes 6148
  120.9 10.1 %copy-start.14 = (bf16[1024]{0:T(1024)(128)(2,1)S(1)}, bf16[1024]{0:T(1024)(128)(2,1)}, u32[]{:S(2)}) copy-start(bf16[1024]{0:T(1024)(128)(2,1)} %get-tuple-element.9) | copy-start | bytes 6148
  120.9 10.1 %copy-start.13 = (bf16[1024]{0:T(1024)(128)(2,1)S(1)}, bf16[1024]{0:T(1024)(128)(2,1)}, u32[]{:S(2)}) copy-start(bf16[1024]{0:T(1024)(128)(2,1)} %get-tuple-element.8) | copy-start | bytes 6148
  121.0 10.1 %copy-start.12 = (bf16[1024]{0:T(1024)(128)(2,1)S(1)}, bf16[1024]{0:T(1024)(128)(2,1)}, u32[]{:S(2)}) copy-start(bf16[1024]{0:T(1024)(128)(2,1)} %get-tuple-element.7) | copy-start | bytes 6148
  121.0 10.1 %copy-start.11 = (bf16[1024]{0:T(1024)(128)(2,1)S(1)}, bf16[1024]{0:T(1024)(128)(2,1)}, u32[]{:S(2)}) copy-start(bf16[1024]{0:T(1024)(128)(2,1)} %get-tuple-element.6) | copy-start | bytes 6148
  121.0 10.1 %copy-start.10 = (bf16[1024]{0:T(1024)(128)(2,1)S(1)}, bf16[1024]{0:T(1024)(128)(2,1)}, u32[]{:S(2)}) copy-start(bf16[1024]{0:T(1024)(128)(2,1)} %get-tuple-element.5) | copy-start | bytes 6148
  121.0 10.1 %copy-start.27 = (bf16[1024]{0:T(1024)(128)(2,1)S(1)}, bf16[1024]{0:T(1024)(128)(2,1)}, u32[]{:S(2)}) copy-start(bf16[1024]{0:T(1024)(128)(2,1)} %get-tuple-element.35) | copy-start | bytes 6148
  121.0 19.5 %copy-start.51 = (f32[128]{0:T(128)S(1)}, f32[128]{0:T(128)}, u32[]{:S(2)}) copy-start(f32[128]{0:T(128)} %copy-done.50) | copy-start | bytes 1540
  125.5 11.8 %all-to-all-start.3 = ((bf16[8,128,3,64]{1,3,2,0:T(8,128)(2,1)}), bf16[8,128,3,64]{1,3,2,0:T(8,128)(2,1)S(1)}, u32[]{:S(2)}, u32[]{:S(2)}) async-start(bf16[8,128,3,64]{1,3,2,0:T(8,128)(2,1)} %copy.169), calls=%async_computation.3 | async-start | bytes 786432 | tf_op jit(solution)/shard_map/all_to_all | solution.py:185
  140.5 4.1 %copy-start.3 = (f32[128,1024]{1,0:T(8,128)}, f32[128,1024]{1,0:T(8,128)S(1)}, u32[]{:S(2)}) copy-start(f32[128,1024]{1,0:T(8,128)S(1)} %get-tuple-element.91) | copy-start | bytes 1572868
  157.7 44.2 %copy-start.44 = (f32[128]{0:T(128)S(1)}, f32[128]{0:T(128)}, u32[]{:S(2)}) copy-start(f32[128]{0:T(128)} %copy-done.42) | copy-start | bytes 1540
  157.7 44.2 %copy-start.47 = (f32[128]{0:T(128)S(1)}, f32[128]{0:T(128)}, u32[]{:S(2)}) copy-start(f32[128]{0:T(128)} %copy-done.45) | copy-start | bytes 1540
  157.7 44.2 %copy-start.49 = (f32[128]{0:T(128)S(1)}, f32[128]{0:T(128)}, u32[]{:S(2)}) copy-start(f32[128]{0:T(128)} %copy-done.48) | copy-start | bytes 1540
  158.6 43.3 %copy-start.4 = (f32[128,1024]{1,0:T(8,128)S(1)}, f32[128,1024]{1,0:T(8,128)}, u32[]{:S(2)}) copy-start(f32[128,1024]{1,0:T(8,128)} %copy-done.3) | copy-start | bytes 1572868
  193.4 17.3 %all-to-all-start.6 = ((bf16[16,4,2576]{2,1,0:T(4,128)(2,1)}), bf16[16,4,2576]{2,1,0:T(4,128)(2,1)S(1)}, u32[]{:S(2)}, u32[]{:S(2)}) async-start(bf16[16,4,2576]{2,1,0:T(4,128)(2,1)} %pad_maximum_fusion.1), calls=%async_computation.6 | async-start | bytes 688128 | tf_op jit(solution)/shard_map/all_to_all | solution.py:303
  211.6 15.5 %all-to-all-start.7 = ((f32[16,1,2112]{2,1,0:T(1,128)}), f32[16,1,2112]{2,1,0:T(1,128)S(1)}, u32[]{:S(2)}, u32[]{:S(2)}) async-start(f32[16,1,2112]{2,1,0:T(1,128)} %broadcast_in_dim.125), calls=%async_computation.7 | async-start | bytes 278528 | tf_op jit(solution)/shard_map/all_to_all | solution.py:308

commit v10 on v9

--- a/solution.py
+++ b/solution.py
@@ -267,11 +267,20 @@
     unused_attn, pull_attn = jax.vjp(normalize, inputs, gain_attn)
     back_inputs, gain_attn_term = pull_attn(back_normed)
     grad_frames = (grad_resid + back_inputs).astype(jnp.bfloat16)[None]
+    order = (lax.axis_size("dp"), tm_count // 2, 2, normed_attn.shape[1] // (2 * tm_count * lax.axis_size("dp")))
+
+    def by_core(matrix):
+        lead = matrix.shape[:-1]
+        moved = matrix.reshape(lead + order + (-1,))
+        base = len(lead)
+        axes_order = tuple(range(base)) + (base + 2, base, base + 1, base + 3, base + 4)
+        return moved.transpose(axes_order).reshape(matrix.shape)
+
     inner_part = lax.dot_general(
-        normed_attn, grad_qkv, contract_first, preferred_element_type=jnp.float32
+        by_core(normed_attn), grad_qkv, contract_first, preferred_element_type=jnp.float32
     )
     outer_part = lax.dot_general(
-        grad_resid_low, attended, contract_first, preferred_element_type=jnp.float32
+        by_core(grad_resid_low), attended, contract_first, preferred_element_type=jnp.float32
     )
     axes = ("dp", "tm")
     devices = lax.axis_size(axes)
@@ -281,7 +290,7 @@
     small_width = -(-small_count // rows)
     small_flat = jnp.pad(small.reshape(-1), (0, small_width * rows - small_count))
     packed = jnp.concatenate(
-        [inner_part, outer_part, small_flat.reshape(rows, small_width)], axis=1
+        [inner_part, outer_part, by_core(small_flat.reshape(rows, small_width).T).T], axis=1
     )
     outer_count = lax.axis_size("dp")
     cores = 2
@@ -289,8 +298,7 @@
     pairs = [[cores * k + c for c in range(cores)] for k in range(chips)]
     same_core = [[cores * k + c for k in range(chips)] for c in range(cores)]
     cols = packed.shape[1]
-    packed = packed.reshape(outer_count, chips, cores, rows // devices, cols)
-    packed = packed.transpose(2, 0, 1, 3, 4).astype(jnp.bfloat16)
+    packed = packed.reshape(cores, outer_count, chips, rows // devices, cols).astype(jnp.bfloat16)
     reduced = lax.all_to_all(packed, "tm", 0, 0, tiled=True, axis_index_groups=pairs)
     reduced = reduced.astype(jnp.float32).sum(0).transpose(1, 0, 2, 3).astype(jnp.bfloat16)
     reduced = lax.all_to_all(reduced, "tm", 0, 0, tiled=True, axis_index_groups=same_core)

time: 231 us -> 271 us (1.17); the launches traced: 230 us -> 267 us
  local copies, waits for them, and re-layouts: 11.1 us -> 33.9 us
  starting transfers between devices: 50.2 us -> 59.9 us
  waiting for transfers between devices: 57 us -> 50.3 us
  other arithmetic: 27.9 us -> 33.3 us
  blocking collectives: 41.7 us -> 46.7 us
    all_to_all x2, starting transfers between devices: 8.82 us -> 18.3 us  [to_frames(): lax.all_to_all(blocks, 'tm', 0, 0, tiled=True, axis_index_groups=half_gro...]
    another operation x31, local copies, waits for them, and re-layouts: 0.16 us -> 9.59 us  [per_device(): jnp.stack([jnp.sum(grad_conv_in * padded[shift_index:shift_index + frame_...]
    convert_element_type x1 -> x3, local copies, waits for them, and re-layouts: 0.36 us -> 7.44 us  [the longest x1 7.14 us: per_device(): packed.reshape(cores, outer_count, chips, rows // devices, cols)]
    all_to_all x2, waiting for transfers between devices: 11.3 us -> 5.76 us  [to_frames(): lax.all_to_all(blocks, 'tm', 0, 0, tiled=True, axis_index_groups=half_gro...]
    all_to_all x1, blocking collectives: 8.99 us -> 12.4 us  [per_device(): lax.all_to_all(packed, 'tm', 0, 0, tiled=True, axis_index_groups=pairs)]
    concatenate x0 -> x1, other arithmetic: none -> 3.25 us  [per_device(): jnp.concatenate([inner_part, outer_part, by_core(small_flat.reshape(rows,...]
    concatenate x1, local copies, waits for them, and re-layouts: 0.29 us -> 3.1 us  [per_device(): jnp.concatenate([conv_term, gain_attn_term[None], gain_conv_term[None]],...]
  transfers between devices with their start and end apart: 11 -> 11, of which waited for: 8 -> 7; matrix products, arithmetic and copies ran while one was open for 5% -> 9% of each run, Pallas kernels for 0% -> 0%
where the time goes in v10:
time: 271 us; the launch traced here: 267 us
  starting transfers between devices  59.9 us (22%)
  waiting for transfers between devices  50.3 us (19%)
  blocking collectives  46.7 us (17%)
  matrix products  40.2 us (15%)
  local copies, waits for them, and re-layouts  33.9 us (13%)
  other arithmetic  33.3 us (12%)
    all_to_all x1, blocking collectives, per_device(): lax.all_to_all(reduced, 'tm', 0, 0, tiled=True, axis_index_groups=same_core)  34.3 us
    all_to_all x2, starting transfers between devices, to_frames(): lax.all_to_all(blocks, 'tm', 0, 0, tiled=True, axis_index_groups=half_gro...  18.3 us
    all_to_all x1, waiting for transfers between devices, per_device(): lax.all_to_all(jnp.tile(qkv, (halves, 1, 1, 1)), 'tm', 0, 0, tiled=True)  12.9 us
    all_to_all x1, blocking collectives, per_device(): lax.all_to_all(packed, 'tm', 0, 0, tiled=True, axis_index_groups=pairs)  12.4 us
    another operation x31, local copies, waits for them, and re-layouts, per_device(): jnp.stack([jnp.sum(grad_conv_in * padded[shift_index:shift_index + frame_...  9.59 us
    ppermute x2, waiting for transfers between devices, padded_2(): after = lax.ppermute(first, axis, down)  9.54 us
    all_to_all x1, starting transfers between devices, per_device(): lax.all_to_all(jnp.tile(qkv, (halves, 1, 1, 1)), 'tm', 0, 0, tiled=True)  8.44 us
    all_to_all x1, starting transfers between devices, per_device(): body = lax.all_to_all(body.astype(jnp.bfloat16), 'dp', 0, 0, tiled=True)  8.39 us
  transfers between devices with their start and end apart: 11, of which 7 were waited for; matrix products, arithmetic and copies ran while one was open for 9% of the time, Pallas kernels for 0%

profile of v10, /device:TPU:1, one launch (start us, length us, event | category | flops | bytes accessed | tf_op | source)
XLA Modules:
  0.0 266.7 jit_solution(15833602449249728876)
XLA Ops:
  0.6 1.1 convert_reduce_fusion.2
  1.7 1.2 multiply_reduce_fusion.36
  2.9 2.6 fusion.10
  5.8 1.1 tile.8
  6.9 8.4 %all-to-all-start = ((bf16[16,128,3,64]{1,3,2,0:T(8,128)(2,1)}), bf16[16,128,3,64]{1,3,2,0:T(8,128)(2,1)S(1)}, u32[]{:S(2)}, u32[]{:S(2)}) async-start(bf16[16,128,3,64]{1,3,2,0:T(8,128)(2,1)} %bitcast.7), calls=%async_computation | async-start | bytes 1572864 | tf_op jit(solution)/shard_map/all_to_all | solution.py:168
  16.0 12.9 %all-to-all-done = bf16[16,128,3,64]{1,3,2,0:T(8,128)(2,1)S(1)} async-done(((bf16[16,128,3,64]{1,3,2,0:T(8,128)(2,1)}), bf16[16,128,3,64]{1,3,2,0:T(8,128)(2,1)S(1)}, u32[]{:S(2)}, u32[]{:S(2)}) %all-to-all-start) | async-done | bytes 786464 | tf_op jit(solution)/shard_map/all_to_all | solution.py:168
  29.0 0.9 fusion.117
  29.9 1.4 fusion.3
  31.3 2.5 fusion
  33.9 1.9 fusion.27
  35.8 0.7 copy_bitcast_fusion.2
  36.5 4.9 %all-to-all-start.1 = ((bf16[8,128,64]{1,2,0:T(8,128)(2,1)}), bf16[8,128,64]{1,2,0:T(8,128)(2,1)S(1)}, u32[]{:S(2)}, u32[]{:S(2)}) async-start(bf16[8,128,64]{1,2,0:T(8,128)(2,1)} %copy_bitcast_fusion.2), calls=%async_computation.1 | async-start | bytes 262144 | tf_op jit(solution)/shard_map/all_to_all | solution.py:185
  41.5 5.8 %all-to-all-done.1 = bf16[8,128,64]{1,2,0:T(8,128)(2,1)S(1)} async-done(((bf16[8,128,64]{1,2,0:T(8,128)(2,1)}), bf16[8,128,64]{1,2,0:T(8,128)(2,1)S(1)}, u32[]{:S(2)}, u32[]{:S(2)}) %all-to-all-start.1) | async-done | bytes 131104 | tf_op jit(solution)/shard_map/all_to_all | solution.py:185
  47.2 1.8 fusion.123
  49.5 3.3 %collective-permute-start = (bf16[15,1024]{1,0:T(8,128)(2,1)S(1)}, bf16[15,1024]{1,0:T(8,128)(2,1)S(1)}, u32[]{:S(2)}, u32[]{:S(2)}) collective-permute-start(bf16[15,1024]{1,0:T(8,128)(2,1)S(1)} %get-tuple-element.49), channel_id=1, source_target_pairs={{0,1},{1,2},{2,3},{3,4},{4,5},{5,6},{6,7},{7,8},{8,9},{9,10},{10,1... | collective-permute-start | bytes 92168 | tf_op jit(solution)/shard_map/ppermute | solution.py:24
  52.8 1.9 collective-permute-start.1
  54.8 4.8 %collective-permute-done.1 = bf16[15,1024]{1,0:T(8,128)(2,1)S(1)} collective-permute-done((bf16[15,1024]{1,0:T(8,128)(2,1)S(1)}, bf16[15,1024]{1,0:T(8,128)(2,1)S(1)}, u32[]{:S(2)}, u32[]{:S(2)}) %collective-permute-start.1) | collective-permute-done | bytes 30752 | tf_op jit(solution)/shard_map/ppermute | solution.py:25
  59.6 4.8 %multiply_reduce_fusion.2 = (bf16[1024]{0:T(1024)(128)(2,1)}, bf16[1024]{0:T(1024)(128)(2,1)}, bf16[1024]{0:T(1024)(128)(2,1)}, bf16[1024]{0:T(1024)(128)(2,1)},...) fusion(f32[158,1024]{1,0:T(8,128)S(1)} %maximum_convert_fusion,, ...), kind=kLoop, calls=%fused_computation.110 | loop fusion | flops 13875200 | bytes 17203200 | tf_op jit(solution)/shard_map/reduce_sum | solution.py:207
  64.4 0.8 multiply_reduce_fusion.20
  65.2 1.9 collective-permute-start.2
  67.2 2.7 collective-permute-start.3
  69.9 4.8 %collective-permute-done.3 = bf16[15,1024]{1,0:T(8,128)(2,1)S(1)} collective-permute-done((bf16[15,1024]{1,0:T(8,128)(2,1)S(1)}, bf16[15,1024]{1,0:T(8,128)(2,1)S(1)}, u32[]{:S(2)}, u32[]{:S(2)}) %collective-permute-start.3) | collective-permute-done | bytes 30752 | tf_op jit(solution)/shard_map/ppermute | solution.py:25
  74.7 4.1 %multiply_reduce_fusion = (bf16[1024]{0:T(1024)(128)(2,1)}, f32[128]{0:T(128)S(1)}, f32[128,1024]{1,0:T(8,128)S(1)}) fusion(f32[128,1024]{1,0:T(8,128)S(1)} %get-tuple-element.87, f32[128]{0:T(128)S(1)} %fusion.96, f32[128]{0:T(128)S(1)} %broadcast_multiply_fusion, f32[1024]{0:T(1024)S(1)} %copy-done.9, f32[158,1024]{1,0:T(8,128)S(1)} %maximum_convert_fusion.1, ...), kind=kLoop, calls=%fused_computation.108 | loop fusion | flops 9042816 | bytes 17436288 | tf_op jit(solution)/shard_map/transpose(jvp())/reduce_sum | solution.py:33
  79.2 0.8 copy-done.2
  80.1 1.5 convolution_convert_fusion.3
  81.8 0.8 tile.20
  82.6 6.0 %all-to-all-start.2 = ((bf16[16,128,64]{1,2,0:T(8,128)(2,1)}), bf16[16,128,64]{1,2,0:T(8,128)(2,1)S(1)}, u32[]{:S(2)}, u32[]{:S(2)}) async-start(bf16[16,128,64]{1,2,0:T(8,128)(2,1)} %bitcast.45), calls=%async_computation.2 | async-start | bytes 524288 | tf_op jit(solution)/shard_map/all_to_all | solution.py:227
  89.1 8.3 %all-to-all-done.2 = bf16[16,128,64]{1,2,0:T(8,128)(2,1)S(1)} async-done(((bf16[16,128,64]{1,2,0:T(8,128)(2,1)}), bf16[16,128,64]{1,2,0:T(8,128)(2,1)S(1)}, u32[]{:S(2)}, u32[]{:S(2)}) %all-to-all-start.2) | async-done | bytes 262176 | tf_op jit(solution)/shard_map/all_to_all | solution.py:227
  97.5 1.2 collective-permute-start.4
  98.7 6.9 %fusion.23 = bf16[8,8,8,128]{3,1,2,0:T(8,128)(2,1)S(1)} fusion(f32[1024,2048]{1,0:T(8,128)} %copy-done, f32[1024]{0:T(1024)S(1)} %multiply_reduce_fusion.37, f32[1024]{0:T(1024)S(1)} %log_add_fusion, pred[2048]{0:T(1024)(128)(4,1)S(1)} %iota_compare_fusion, bf16[2048,64]{0,1:T(8,128)(2,1)S(1)} %copy_bitcast_fusion.1, s32[]{:T(128)S(6)} %select_n.51, ...), kind=kOutput, calls=%fused_computation.32 | convolution fusion | flops 551682048 | bytes 9185284 | tf_op jit(solution)/shard_map/dot_general | solution.py:247
  106.0 6.7 %fusion.2 = (bf16[2048,1024]{0,1:T(8,128)(2,1)}, f32[2048,1024]{0,1:T(8,128)}) fusion(f32[2048]{0:T(1024)S(1)} %bitcast.263, pred[1024]{0:T(1024)(128)(4,1)S(1)} %dynamic-slice.6, bf16[2048,1,64]{0,2,1:T(8,128)(2,1)} %get-tuple-element.44, s32[]{:T(128)S(6)} %select_n.51, bf16[2048,3,64]{0,2,1:T(8,128)(2,1)S(1)} %copy_bitcast_fusion), kind=kOutput, calls=%fused_computation.7 | convolution fusion | flops 278921216 | bytes 12985348 | tf_op jit(solution)/shard_map/dot_general | solution.py:250
  112.7 7.1 %fusion.22 = bf16[8,8,8,128]{3,1,2,0:T(8,128)(2,1)S(1)} fusion(f32[2048,1024]{0,1:T(8,128)} %get-tuple-element.89, f32[2048]{0:T(1024)S(1)} %bitcast.262, f32[2048]{0:T(1024)S(1)} %bitcast.264, pred[1024]{0:T(1024)(128)(4,1)S(1)} %dynamic-slice.6, bf16[2048,1,64]{0,2,1:T(8,128)(2,1)S(1)} %copy-done.7, s32[]{:T(128)S(6)} %select_n.51, ...), kind=kOutput, calls=%fused_computation.31 | convolution fusion | flops 551682048 | bytes 9192452 | tf_op jit(solution)/shard_map/dot_general | solution.py:256
  120.0 3.6 %fusion.21 = bf16[8,128,1,64]{1,3,0,2:T(8,128)(2,1)S(1)} fusion(bf16[8,128,2048]{2,1,0:T(8,128)(2,1)} %bitcast.180, bf16[2048,64,1]{0,1,2:T(8,128)(2,1)S(1)} %reshape.242), kind=kOutput, calls=%fused_computation.30 | convolution fusion | flops 268500992 | bytes 4587520 | tf_op jit(solution)/shard_map/dot_general | solution.py:259
  123.7 0.8 copy.166
  124.4 13.4 %all-to-all-start.3 = ((bf16[8,128,3,64]{1,3,2,0:T(8,128)(2,1)}), bf16[8,128,3,64]{1,3,2,0:T(8,128)(2,1)S(1)}, u32[]{:S(2)}, u32[]{:S(2)}) async-start(bf16[8,128,3,64]{1,3,2,0:T(8,128)(2,1)} %copy.166), calls=%async_computation.3 | async-start | bytes 786432 | tf_op jit(solution)/shard_map/all_to_all | solution.py:185
  137.8 0.7 fusion.78
  138.6 0.9 copy.169
  148.6 0.6 stack.176
  149.4 0.6 reshape.233
  150.2 1.4 convolution_convert_fusion.1
  151.6 3.1 %multiply_reduce_fusion.33 = (f32[128]{0:T(128)S(1)}, f32[128,1024]{1,0:T(8,128)S(1)}) fusion(bf16[1,128,1024]{2,1,0:T(8,128)(2,1)S(1)} %copy-done.1, f32[1024]{0:T(1024)S(1)} %copy-done.10, f32[128]{0:T(128)} %copy-done.11, bf16[128,1536]{0,1:T(8,128)(2,1)S(1)} %bitcast.182, bf16[1024,2048]{1,0:T(8,128)(2,1)} %param.10), kind=kOutput, calls=%fused_computation.143 | convolution fusion | flops 403308416 | bytes 4330496 | tf_op jit(solution)/shard_map/dot_general | solution.py:264
  154.7 2.1 convolution_convert_fusion
  156.9 0.6 multiply_multiply_fusion
  157.5 0.9 multiply_reduce_fusion.1
  158.9 3.1 %concatenate.30 = bf16[33,1024]{1,0:T(8,128)(2,1)S(1)} concatenate(bf16[1,1024]{1,0:T(2,128)(2,1)S(1)} %stack.146, bf16[1,1024]{1,0:T(2,128)(2,1)S(1)} %stack.147, bf16[1,1024]{1,0:T(2,128)(2,1)S(1)} %stack.148, bf16[1,1024]{1,0:T(2,128)(2,1)S(1)} %stack.149, bf16[1,1024]{1,0:T(2,128)(2,1)S(1)} %stack.150, bf16[1,1024]{1,0:T(2,128)(2,1)S(1)} %stack.151, ...), dimensions={0} | concatenate | bytes 135168 | tf_op jit(solution)/shard_map/concatenate | solution.py:288
  162.0 1.3 reshape.234
  163.3 1.1 copy.173
  164.5 3.2 %pad_maximum_fusion = bf16[1024,2081]{1,0:T(8,128)(2,1)} fusion(bf16[1024,33]{1,0:T(8,128)(2,1)S(1)} %bitcast.187, bf16[1024,512]{1,0:T(8,128)(2,1)} %convolution_convert_fusion.1, bf16[1024,1536]{1,0:T(8,128)(2,1)S(1)} %convolution_convert_fusion), kind=kLoop, calls=%fused_computation.9 | loop fusion | flops 12785664 | bytes 8523776 | tf_op jit(solution)/shard_map/concatenate | solution.py:292
  167.7 7.1 %convert_element_type.123 = bf16[2,16,8,4,2081]{4,3,2,1,0:T(4,128)(2,1)} reshape(bf16[1024,2081]{1,0:T(8,128)(2,1)} %pad_maximum_fusion) | data formatting | bytes 8523776 | tf_op jit(solution)/shard_map/convert_element_type | solution.py:301
  174.9 12.4 %all_to_all.41 = bf16[2,16,8,4,2081]{4,3,2,1,0:T(4,128)(2,1)} all-to-all(bf16[2,16,8,4,2081]{4,3,2,1,0:T(4,128)(2,1)} %convert_element_type.123), channel_id=1, replica_groups={{0,1},{2,3},{4,5},{6,7},{8,9},{10,11},{12,13},{14,15},{16,17},{18,19},{..., dimensions={0} | all-to-all | bytes 8523776 | tf_op jit(solution)/shard_map/all_to_all | solution.py:302
  187.2 5.9 %reduce_sum.500 = bf16[16,8,4,2081]{3,2,1,0:T(4,128)(2,1)S(1)} reduce(bf16[2,16,8,4,2081]{4,3,2,1,0:T(4,128)(2,1)} %all_to_all.41, bf16[]{:T(256)} %constant.60.clone.1), dimensions={0}, to_apply=%region_44.45 | reduce | flops 1065472 | bytes 6392834 | tf_op jit(solution)/shard_map/reduce_sum | solution.py:303
  193.2 0.8 copy.174
  194.0 34.3 %all_to_all.42 = bf16[8,16,4,2081]{3,2,1,0:T(4,128)(2,1)S(1)} all-to-all(bf16[8,16,4,2081]{3,2,1,0:T(4,128)(2,1)S(1)} %copy.174), channel_id=1, replica_groups={{0,2,4,6,8,10,12,14},{1,3,5,7,9,11,13,15},{16,18,20,22,24,26,28,30},{17..., dimensions={0} | all-to-all | bytes 4261888 | tf_op jit(solution)/shard_map/all_to_all | solution.py:304
  228.3 1.0 convert_reduce_fusion
  229.6 0.9 pad_maximum_fusion.2
  230.5 8.4 %all-to-all-start.6 = ((bf16[16,4,2576]{2,1,0:T(4,128)(2,1)}), bf16[16,4,2576]{2,1,0:T(4,128)(2,1)S(1)}, u32[]{:S(2)}, u32[]{:S(2)}) async-start(bf16[16,4,2576]{2,1,0:T(4,128)(2,1)} %pad_maximum_fusion.2), calls=%async_computation.6 | async-start | bytes 688128 | tf_op jit(solution)/shard_map/all_to_all | solution.py:311
  238.9 2.0 fusion.65
  241.0 6.7 %all-to-all-done.6 = bf16[16,4,2576]{2,1,0:T(4,128)(2,1)S(1)} async-done(((bf16[16,4,2576]{2,1,0:T(4,128)(2,1)}), bf16[16,4,2576]{2,1,0:T(4,128)(2,1)S(1)}, u32[]{:S(2)}, u32[]{:S(2)}) %all-to-all-start.6) | async-done | bytes 329760 | tf_op jit(solution)/shard_map/all_to_all | solution.py:311
  247.9 0.7 broadcast_in_dim.125
  248.6 7.8 %all-to-all-start.7 = ((f32[16,1,2112]{2,1,0:T(1,128)}), f32[16,1,2112]{2,1,0:T(1,128)S(1)}, u32[]{:S(2)}, u32[]{:S(2)}) async-start(f32[16,1,2112]{2,1,0:T(1,128)} %broadcast_in_dim.125), calls=%async_computation.7 | async-start | bytes 278528 | tf_op jit(solution)/shard_map/all_to_all | solution.py:316
  256.5 0.6 slice_multiply_fusion.32
  257.1 7.1 %all-to-all-done.7 = f32[16,1,2112]{2,1,0:T(1,128)S(1)} async-done(((f32[16,1,2112]{2,1,0:T(1,128)}), f32[16,1,2112]{2,1,0:T(1,128)S(1)}, u32[]{:S(2)}, u32[]{:S(2)}) %all-to-all-start.7) | async-done | bytes 135200 | tf_op jit(solution)/shard_map/all_to_all | solution.py:316
  265.2 0.7 slice_multiply_fusion.31
  265.9 0.6 slice_multiply_fusion.33
  (169 shorter events, 14.4 us)
Async XLA Ops:
  1.7 136.1 %copy-start.11 = (f32[128]{0:T(128)}, f32[128]{0:T(128)S(1)}, u32[]{:S(2)}) copy-start(f32[128]{0:T(128)S(1)} %broadcast_multiply_fusion.1) | copy-start | bytes 1540
  2.9 4.0 %copy-start.39 = (f32[128]{0:T(128)}, f32[128]{0:T(128)S(1)}, u32[]{:S(2)}) copy-start(f32[128]{0:T(128)S(1)} %multiply_reduce_fusion.36) | copy-start | bytes 1540
  2.9 4.0 %copy-start.32 = (f32[128]{0:T(128)}, f32[128]{0:T(128)S(1)}, u32[]{:S(2)}) copy-start(f32[128]{0:T(128)S(1)} %fusion.95) | copy-start | bytes 1540
  6.9 22.0 %all-to-all-start = ((bf16[16,128,3,64]{1,3,2,0:T(8,128)(2,1)}), bf16[16,128,3,64]{1,3,2,0:T(8,128)(2,1)S(1)}, u32[]{:S(2)}, u32[]{:S(2)}) async-start(bf16[16,128,3,64]{1,3,2,0:T(8,128)(2,1)} %bitcast.7), calls=%async_computation | async-start | bytes 1572864 | tf_op jit(solution)/shard_map/all_to_all | solution.py:168
  31.3 4.4 %copy-start = (f32[1024,2048]{1,0:T(8,128)}, f32[1024,2048]{1,0:T(8,128)S(1)}, u32[]{:S(2)}) copy-start(f32[1024,2048]{1,0:T(8,128)S(1)} %get-tuple-element.85) | copy-start | bytes 25165828
  33.8 7.6 %copy-start.8 = (bf16[31,1024]{1,0:T(8,128)(2,1)S(1)}, bf16[31,1024]{1,0:T(8,128)(2,1)}, u32[]{:S(2)}) copy-start(bf16[31,1024]{1,0:T(8,128)(2,1)} %param.13) | copy-start | bytes 190468
  33.8 13.4 %copy-start.1 = (bf16[1,128,1024]{2,1,0:T(8,128)(2,1)S(1)}, bf16[1,128,1024]{2,1,0:T(8,128)(2,1)}, u32[]{:S(2)}) copy-start(bf16[1,128,1024]{2,1,0:T(8,128)(2,1)} %param.7) | copy-start | bytes 786436
  33.8 15.4 %copy-start.9 = (f32[1024]{0:T(1024)S(1)}, f32[1024]{0:T(1024)}, u32[]{:S(2)}) copy-start(f32[1024]{0:T(1024)} %param.12) | copy-start | bytes 12292
  33.8 25.8 %copy-start.4 = (bf16[1,128,1024]{2,1,0:T(8,128)(2,1)S(1)}, bf16[1,128,1024]{2,1,0:T(8,128)(2,1)}, u32[]{:S(2)}) copy-start(bf16[1,128,1024]{2,1,0:T(8,128)(2,1)} %param.8) | copy-start | bytes 786436
  36.5 10.8 %all-to-all-start.1 = ((bf16[8,128,64]{1,2,0:T(8,128)(2,1)}), bf16[8,128,64]{1,2,0:T(8,128)(2,1)S(1)}, u32[]{:S(2)}, u32[]{:S(2)}) async-start(bf16[8,128,64]{1,2,0:T(8,128)(2,1)} %copy_bitcast_fusion.2), calls=%async_computation.1 | async-start | bytes 262144 | tf_op jit(solution)/shard_map/all_to_all | solution.py:185
  49.5 5.3 %collective-permute-start = (bf16[15,1024]{1,0:T(8,128)(2,1)S(1)}, bf16[15,1024]{1,0:T(8,128)(2,1)S(1)}, u32[]{:S(2)}, u32[]{:S(2)}) collective-permute-start(bf16[15,1024]{1,0:T(8,128)(2,1)S(1)} %get-tuple-element.49), channel_id=1, source_target_pairs={{0,1},{1,2},{2,3},{3,4},{4,5},{5,6},{6,7},{7,8},{8,9},{9,10},{10,1... | collective-permute-start | bytes 92168 | tf_op jit(solution)/shard_map/ppermute | solution.py:24
  52.8 6.7 %collective-permute-start.1 = (bf16[15,1024]{1,0:T(8,128)(2,1)S(1)}, bf16[15,1024]{1,0:T(8,128)(2,1)S(1)}, u32[]{:S(2)}, u32[]{:S(2)}) collective-permute-start(bf16[15,1024]{1,0:T(8,128)(2,1)S(1)} %get-tuple-element.50), channel_id=1, source_target_pairs={{1,0},{2,1},{3,2},{4,3},{5,4},{6,5},{7,6},{8,7},{9,8},{10,9},{11,1... | collective-permute-start | bytes 92168 | tf_op jit(solution)/shard_map/ppermute | solution.py:25
  65.2 4.6 %collective-permute-start.2 = (bf16[15,1024]{1,0:T(8,128)(2,1)S(1)}, bf16[15,1024]{1,0:T(8,128)(2,1)S(1)}, u32[]{:S(2)}, u32[]{:S(2)}) collective-permute-start(bf16[15,1024]{1,0:T(8,128)(2,1)S(1)} %get-tuple-element.47), channel_id=1, source_target_pairs={{0,1},{1,2},{2,3},{3,4},{4,5},{5,6},{6,7},{7,8},{8,9},{9,10},{10,1... | collective-permute-start | bytes 92168 | tf_op jit(solution)/shard_map/ppermute | solution.py:24
  67.2 7.5 %collective-permute-start.3 = (bf16[15,1024]{1,0:T(8,128)(2,1)S(1)}, bf16[15,1024]{1,0:T(8,128)(2,1)S(1)}, u32[]{:S(2)}, u32[]{:S(2)}) collective-permute-start(bf16[15,1024]{1,0:T(8,128)(2,1)S(1)} %get-tuple-element.48), channel_id=1, source_target_pairs={{1,0},{2,1},{3,2},{4,3},{5,4},{6,5},{7,6},{8,7},{9,8},{10,9},{11,1... | collective-permute-start | bytes 92168 | tf_op jit(solution)/shard_map/ppermute | solution.py:25
  74.7 14.0 %copy-start.10 = (f32[1024]{0:T(1024)S(1)}, f32[1024]{0:T(1024)}, u32[]{:S(2)}) copy-start(f32[1024]{0:T(1024)} %param.11) | copy-start | bytes 12292
  79.2 0.8 copy-start.2
  79.2 9.5 %copy-start.35 = (f32[128]{0:T(128)}, f32[128]{0:T(128)S(1)}, u32[]{:S(2)}) copy-start(f32[128]{0:T(128)S(1)} %negate_multiply_fusion.1) | copy-start | bytes 1540
  82.6 14.8 %all-to-all-start.2 = ((bf16[16,128,64]{1,2,0:T(8,128)(2,1)}), bf16[16,128,64]{1,2,0:T(8,128)(2,1)S(1)}, u32[]{:S(2)}, u32[]{:S(2)}) async-start(bf16[16,128,64]{1,2,0:T(8,128)(2,1)} %bitcast.45), calls=%async_computation.2 | async-start | bytes 524288 | tf_op jit(solution)/shard_map/all_to_all | solution.py:227
  97.5 8.4 %collective-permute-start.4 = (f32[2,1024]{1,0:T(2,128)S(1)}, f32[2,1024]{1,0:T(2,128)S(1)}, u32[]{:S(2)}, u32[]{:S(2)}) collective-permute-start(f32[2,1024]{1,0:T(2,128)S(1)} %pad_maximum_fusion.3), channel_id=1, source_target_pairs={{0,8},{1,9},{2,10},{3,11},{4,12},{5,13},{6,14},{7,15},{8,0},{9,1},... | collective-permute-start | bytes 24584 | tf_op jit(solution)/shard_map/ppermute | solution.py:232
  106.0 6.7 %copy-start.7 = (bf16[2048,1,64]{0,2,1:T(8,128)(2,1)S(1)}, bf16[2048,1,64]{0,2,1:T(8,128)(2,1)}, u32[]{:S(2)}) copy-start(bf16[2048,1,64]{0,2,1:T(8,128)(2,1)} %get-tuple-element.43) | copy-start | bytes 786436
  112.7 25.1 %copy-start.33 = (f32[128]{0:T(128)S(1)}, f32[128]{0:T(128)}, u32[]{:S(2)}) copy-start(f32[128]{0:T(128)} %copy-done.32) | copy-start | bytes 1540
  119.8 19.8 %copy-start.30 = (bf16[1024]{0:T(1024)(128)(2,1)S(1)}, bf16[1024]{0:T(1024)(128)(2,1)}, u32[]{:S(2)}) copy-start(bf16[1024]{0:T(1024)(128)(2,1)} %get-tuple-element.20) | copy-start | bytes 6148
  119.8 19.8 %copy-start.29 = (bf16[1024]{0:T(1024)(128)(2,1)S(1)}, bf16[1024]{0:T(1024)(128)(2,1)}, u32[]{:S(2)}) copy-start(bf16[1024]{0:T(1024)(128)(2,1)} %get-tuple-element.19) | copy-start | bytes 6148
  119.8 20.4 %copy-start.28 = (bf16[1024]{0:T(1024)(128)(2,1)S(1)}, bf16[1024]{0:T(1024)(128)(2,1)}, u32[]{:S(2)}) copy-start(bf16[1024]{0:T(1024)(128)(2,1)} %get-tuple-element.18) | copy-start | bytes 6148
  119.8 21.0 %copy-start.27 = (bf16[1024]{0:T(1024)(128)(2,1)S(1)}, bf16[1024]{0:T(1024)(128)(2,1)}, u32[]{:S(2)}) copy-start(bf16[1024]{0:T(1024)(128)(2,1)} %get-tuple-element.17) | copy-start | bytes 6148
  119.8 21.6 %copy-start.26 = (bf16[1024]{0:T(1024)(128)(2,1)S(1)}, bf16[1024]{0:T(1024)(128)(2,1)}, u32[]{:S(2)}) copy-start(bf16[1024]{0:T(1024)(128)(2,1)} %get-tuple-element.16) | copy-start | bytes 6148
  119.8 22.2 %copy-start.25 = (bf16[1024]{0:T(1024)(128)(2,1)S(1)}, bf16[1024]{0:T(1024)(128)(2,1)}, u32[]{:S(2)}) copy-start(bf16[1024]{0:T(1024)(128)(2,1)} %get-tuple-element.15) | copy-start | bytes 6148
  119.9 22.8 %copy-start.24 = (bf16[1024]{0:T(1024)(128)(2,1)S(1)}, bf16[1024]{0:T(1024)(128)(2,1)}, u32[]{:S(2)}) copy-start(bf16[1024]{0:T(1024)(128)(2,1)} %get-tuple-element.14) | copy-start | bytes 6148
  119.9 23.4 %copy-start.23 = (bf16[1024]{0:T(1024)(128)(2,1)S(1)}, bf16[1024]{0:T(1024)(128)(2,1)}, u32[]{:S(2)}) copy-start(bf16[1024]{0:T(1024)(128)(2,1)} %get-tuple-element.13) | copy-start | bytes 6148
  119.9 23.9 %copy-start.22 = (bf16[1024]{0:T(1024)(128)(2,1)S(1)}, bf16[1024]{0:T(1024)(128)(2,1)}, u32[]{:S(2)}) copy-start(bf16[1024]{0:T(1024)(128)(2,1)} %get-tuple-element.12) | copy-start | bytes 6148
  119.9 24.5 %copy-start.21 = (bf16[1024]{0:T(1024)(128)(2,1)S(1)}, bf16[1024]{0:T(1024)(128)(2,1)}, u32[]{:S(2)}) copy-start(bf16[1024]{0:T(1024)(128)(2,1)} %get-tuple-element.11) | copy-start | bytes 6148
  119.9 25.1 %copy-start.20 = (bf16[1024]{0:T(1024)(128)(2,1)S(1)}, bf16[1024]{0:T(1024)(128)(2,1)}, u32[]{:S(2)}) copy-start(bf16[1024]{0:T(1024)(128)(2,1)} %get-tuple-element.10) | copy-start | bytes 6148
  119.9 25.7 %copy-start.19 = (bf16[1024]{0:T(1024)(128)(2,1)S(1)}, bf16[1024]{0:T(1024)(128)(2,1)}, u32[]{:S(2)}) copy-start(bf16[1024]{0:T(1024)(128)(2,1)} %get-tuple-element.9) | copy-start | bytes 6148
  119.9 26.3 %copy-start.18 = (bf16[1024]{0:T(1024)(128)(2,1)S(1)}, bf16[1024]{0:T(1024)(128)(2,1)}, u32[]{:S(2)}) copy-start(bf16[1024]{0:T(1024)(128)(2,1)} %get-tuple-element.8) | copy-start | bytes 6148
  119.9 26.9 %copy-start.17 = (bf16[1024]{0:T(1024)(128)(2,1)S(1)}, bf16[1024]{0:T(1024)(128)(2,1)}, u32[]{:S(2)}) copy-start(bf16[1024]{0:T(1024)(128)(2,1)} %get-tuple-element.7) | copy-start | bytes 6148
  119.9 27.5 %copy-start.16 = (bf16[1024]{0:T(1024)(128)(2,1)S(1)}, bf16[1024]{0:T(1024)(128)(2,1)}, u32[]{:S(2)}) copy-start(bf16[1024]{0:T(1024)(128)(2,1)} %get-tuple-element.6) | copy-start | bytes 6148
  119.9 28.1 %copy-start.15 = (bf16[1024]{0:T(1024)(128)(2,1)S(1)}, bf16[1024]{0:T(1024)(128)(2,1)}, u32[]{:S(2)}) copy-start(bf16[1024]{0:T(1024)(128)(2,1)} %get-tuple-element.5) | copy-start | bytes 6148
  120.0 28.6 %copy-start.14 = (bf16[1024]{0:T(1024)(128)(2,1)S(1)}, bf16[1024]{0:T(1024)(128)(2,1)}, u32[]{:S(2)}) copy-start(bf16[1024]{0:T(1024)(128)(2,1)} %get-tuple-element.4) | copy-start | bytes 6148
  120.0 29.4 %copy-start.31 = (bf16[1024]{0:T(1024)(128)(2,1)S(1)}, bf16[1024]{0:T(1024)(128)(2,1)}, u32[]{:S(2)}) copy-start(bf16[1024]{0:T(1024)(128)(2,1)} %get-tuple-element.35) | copy-start | bytes 6148
  124.4 27.1 %all-to-all-start.3 = ((bf16[8,128,3,64]{1,3,2,0:T(8,128)(2,1)}), bf16[8,128,3,64]{1,3,2,0:T(8,128)(2,1)S(1)}, u32[]{:S(2)}, u32[]{:S(2)}) async-start(bf16[8,128,3,64]{1,3,2,0:T(8,128)(2,1)} %copy.166), calls=%async_computation.3 | async-start | bytes 786432 | tf_op jit(solution)/shard_map/all_to_all | solution.py:185
  138.5 18.9 %copy-start.12 = (f32[128]{0:T(128)S(1)}, f32[128]{0:T(128)}, u32[]{:S(2)}) copy-start(f32[128]{0:T(128)} %copy-done.11) | copy-start | bytes 1540
  154.7 2.7 %copy-start.6 = (f32[128,1024]{1,0:T(8,128)}, f32[128,1024]{1,0:T(8,128)S(1)}, u32[]{:S(2)}) copy-start(f32[128,1024]{1,0:T(8,128)S(1)} %get-tuple-element.91) | copy-start | bytes 1572868
  157.5 0.9 copy-start.37
  193.1 45.7 %copy-start.40 = (f32[128]{0:T(128)S(1)}, f32[128]{0:T(128)}, u32[]{:S(2)}) copy-start(f32[128]{0:T(128)} %get-tuple-element.38) | copy-start | bytes 1540
  193.1 45.7 %copy-start.3 = (f32[128,1024]{1,0:T(8,128)S(1)}, f32[128,1024]{1,0:T(8,128)}, u32[]{:S(2)}) copy-start(f32[128,1024]{1,0:T(8,128)} %copy-done.2) | copy-start | bytes 1572868
  193.1 45.7 %copy-start.5 = (bf16[1,128,1024]{2,1,0:T(8,128)(2,1)S(1)}, bf16[1,128,1024]{2,1,0:T(8,128)(2,1)}, u32[]{:S(2)}) copy-start(bf16[1,128,1024]{2,1,0:T(8,128)(2,1)} %param.8) | copy-start | bytes 786436
  193.2 45.7 %copy-start.13 = (f32[128]{0:T(128)S(1)}, f32[128]{0:T(128)}, u32[]{:S(2)}) copy-start(f32[128]{0:T(128)} %copy-done.11) | copy-start | bytes 1540
  193.2 45.7 %copy-start.34 = (f32[128]{0:T(128)S(1)}, f32[128]{0:T(128)}, u32[]{:S(2)}) copy-start(f32[128]{0:T(128)} %copy-done.32) | copy-start | bytes 1540
  193.2 45.7 %copy-start.36 = (f32[128]{0:T(128)S(1)}, f32[128]{0:T(128)}, u32[]{:S(2)}) copy-start(f32[128]{0:T(128)} %copy-done.35) | copy-start | bytes 1540
  193.2 45.7 %copy-start.38 = (f32[128]{0:T(128)S(1)}, f32[128]{0:T(128)}, u32[]{:S(2)}) copy-start(f32[128]{0:T(128)} %copy-done.37) | copy-start | bytes 1540
  230.5 17.3 %all-to-all-start.6 = ((bf16[16,4,2576]{2,1,0:T(4,128)(2,1)}), bf16[16,4,2576]{2,1,0:T(4,128)(2,1)S(1)}, u32[]{:S(2)}, u32[]{:S(2)}) async-start(bf16[16,4,2576]{2,1,0:T(4,128)(2,1)} %pad_maximum_fusion.2), calls=%async_computation.6 | async-start | bytes 688128 | tf_op jit(solution)/shard_map/all_to_all | solution.py:311
  248.6 15.5 %all-to-all-start.7 = ((f32[16,1,2112]{2,1,0:T(1,128)}), f32[16,1,2112]{2,1,0:T(1,128)S(1)}, u32[]{:S(2)}, u32[]{:S(2)}) async-start(f32[16,1,2112]{2,1,0:T(1,128)} %broadcast_in_dim.125), calls=%async_computation.7 | async-start | bytes 278528 | tf_op jit(solution)/shard_map/all_to_all | solution.py:316
